TPU v7x, 32 devices: a whole 2x2x4 slice. The times are simulated.
32 devices in a mesh: grp: 2 (over x), stretch: 8 (over z, y), req: 2 (over core).
Axes of the slice: x: 2, y: 2, z: 4, core: 2. Of those that a mesh axis runs over, the one named last changes fastest.
Arguments:
- queries: bfloat16 [16, 256, 4096], P(('grp', 'stretch'), None, 'req'), parts along dimension 0, may hold values from -32 to 32
- fresh_keys: bfloat16 [16, 256, 512], P(('grp', 'stretch'), None, 'req'), parts along dimension 0, may hold values from -32 to 32
- fresh_values: bfloat16 [16, 256, 512], P(('grp', 'stretch'), None, 'req'), parts along dimension 0, may hold values from -6 to 6
- stored_stretch_keys: bfloat16 [256, 128, 512], P(('grp', 'stretch'), None, 'req'), parts along dimension 0, may hold values from -6 to 6
- stored_stretch_values: bfloat16 [256, 128, 512], P(('grp', 'stretch'), None, 'req'), parts along dimension 0, may hold values from -6 to 6
- scales: bfloat16 [256, 2, 4], P(('grp', 'stretch'), None, 'req'), parts along dimension 0, may hold values from 0.29 to 3.02
- stretch_ids: int32 [16, 32], P(('grp', 'stretch')), parts along dimension 0, may hold values from 0 to 127, as said below
- counts: int32 [16], P(('grp', 'stretch')), parts along dimension 0, may hold values from 24 to 32
- stretch_pos: int32 [16, 32], P(('grp', 'stretch')), parts along dimension 0, may hold values from 0 to 4095
Outputs:
- attended: bfloat16 [16, 256, 4096], P(('grp', 'stretch'), None, 'req'), parts along dimension 0
There are 2 independent parts, one for each index of `grp`. A program takes and returns all parts, laid end to end along the dimension named above; each array names one. Nothing has to cross between parts.
Inputs may be any that keep to these rules, and one draw needn't show every extreme that they name: `stretch_ids`: the 32 stretch ids of a request are distinct; at most 8 of them lie on one owner (owner = id // 16); the first 8 of every request lie on one owner, the same for all requests of a group.
All inputs are finite; a program needn't handle non-finite values.
Results may differ from a plain program's by a relative error of at most 0.012.
Values may be sent and summed in bfloat16 or wider, within the bound.
No kernel may reach another device: no remote copies, remote signals or barrier semaphores. Data moves between devices by JAX's collectives and lax.ppermute only.
A program may use at most 64 MiB of HBM per device.

v0:
```python
import jax
import jax.numpy as jnp
from jax import lax
from jax.sharding import PartitionSpec as P

rope_base = 500000.0


def apply_rotary(x, pos):
    half = x.shape[-1] // 2
    inv = rope_base ** (-(jnp.arange(half, dtype=jnp.float32) * 2.0 / x.shape[-1]))
    angle = pos.astype(jnp.float32)[..., None] * inv
    cosine = jnp.cos(angle)
    sine = jnp.sin(angle)
    first = x[..., :half]
    second = x[..., half:]
    return jnp.concatenate(
        [first * cosine - second * sine, second * cosine + first * sine], axis=-1
    )


def slot_tables(slot_stretch_ids, counts, positions, owners, capacity, per_owner):
    rows, slots = slot_stretch_ids.shape
    owner = slot_stretch_ids // per_owner
    local = slot_stretch_ids % per_owner
    slot_iota = jnp.arange(slots, dtype=jnp.int32)
    live = slot_iota[None, :] < counts[:, None]
    same = owner[:, :, None] == owner[:, None, :]
    earlier = slot_iota[:, None] < slot_iota[None, :]
    rank = jnp.sum((same & earlier[None, :, :] & live[:, :, None]).astype(jnp.int32), axis=1)
    target = owner * capacity + rank
    hits = (
        target[:, :, None] == jnp.arange(owners * capacity, dtype=jnp.int32)[None, None, :]
    ) & live[:, :, None]
    hits = hits.astype(jnp.int32)
    local_table = jnp.sum(hits * (local + 1)[:, :, None], axis=1) - 1
    place_table = jnp.sum(hits * positions[:, :, None], axis=1)
    return (
        local_table.reshape(rows, owners, capacity),
        place_table.reshape(rows, owners, capacity),
        owner,
        rank,
        live,
    )


def shards(
    queries,
    fresh_keys,
    fresh_values,
    stored_stretch_keys,
    stored_stretch_values,
    scales,
    stretch_ids,
    counts,
    stretch_pos,
):
    owners = lax.axis_size("stretch")
    rows, slots = stretch_ids.shape
    per_owner, span, width = stored_stretch_keys.shape
    kv_heads = scales.shape[2]
    head_dim = width // kv_heads
    q_heads = queries.shape[2] // head_dim
    request_group = q_heads // kv_heads
    tokens = queries.shape[1]
    capacity = 2 * slots // owners
    mine = slot_tables(stretch_ids, counts, stretch_pos, owners, capacity, per_owner)
    owner, rank, live = (mine[2], mine[3], mine[4])
    wanted, starts = (
        lax.all_to_all(
            jnp.transpose(mine[0], (1, 0, 2)), "stretch", split_axis=0, concat_axis=0, tiled=True
        ),
        lax.all_to_all(
            jnp.transpose(mine[1], (1, 0, 2)), "stretch", split_axis=0, concat_axis=0, tiled=True
        ),
    )
    chosen = jnp.maximum(wanted, 0)
    raw_keys = stored_stretch_keys[chosen]
    raw_values = stored_stretch_values[chosen]
    flat = owners * rows * capacity
    index = (owner * rows + jnp.arange(rows, dtype=jnp.int32)[:, None]) * capacity + rank
    index = jnp.where(live, index, 0)
    stretch_iota = jnp.arange(span, dtype=jnp.int32)
    got_keys, got_vals, got_scales = (
        lax.all_to_all(raw_keys, "stretch", split_axis=0, concat_axis=0, tiled=True),
        lax.all_to_all(raw_values, "stretch", split_axis=0, concat_axis=0, tiled=True),
        lax.all_to_all(scales[chosen], "stretch", split_axis=0, concat_axis=0, tiled=True),
    )
    scale_factor = got_scales.reshape(flat, 2, kv_heads)[index].astype(jnp.float32)
    keys_wide = (
        got_keys.reshape(flat, span, width)[index]
        .reshape(rows, slots, span, kv_heads, head_dim)
        .astype(jnp.float32)
    )
    keys_wide = keys_wide * scale_factor[:, :, 0][:, :, None, :, None]
    stretch_placement = (stretch_pos[:, :, None] + stretch_iota)[..., None]
    cached_keys = (
        apply_rotary(keys_wide, stretch_placement)
        .astype(jnp.bfloat16)
        .reshape(rows, slots, span, width)
    )
    vals_wide = (
        got_vals.reshape(flat, span, width)[index]
        .reshape(rows, slots, span, kv_heads, head_dim)
        .astype(jnp.float32)
    )
    cached_vals = (
        (vals_wide * scale_factor[:, :, 1][:, :, None, :, None])
        .astype(jnp.bfloat16)
        .reshape(rows, slots, span, width)
    )
    block = min(tokens, 64)
    blocks = tokens // block
    cache_length = slots * span
    token_iota = jnp.arange(tokens, dtype=jnp.int32)
    token_positions = (cache_length + token_iota)[:, None]
    keys_all = jnp.concatenate(
        [
            cached_keys[0].reshape(cache_length, kv_heads, head_dim),
            apply_rotary(
                fresh_keys[0].reshape(tokens, kv_heads, head_dim).astype(jnp.float32),
                token_positions,
            ).astype(jnp.bfloat16),
        ],
        axis=0,
    )
    combined_values = jnp.concatenate(
        [
            cached_vals[0].reshape(cache_length, kv_heads, head_dim),
            fresh_values[0].reshape(tokens, kv_heads, head_dim),
        ],
        axis=0,
    )
    query_rot = (
        apply_rotary(
            queries[0].reshape(tokens, q_heads, head_dim).astype(jnp.float32), token_positions
        )
        * head_dim ** (-0.5)
    ).astype(jnp.bfloat16)
    query_rot = query_rot.reshape(tokens, kv_heads, request_group, head_dim)
    cache_ok = jnp.arange(cache_length, dtype=jnp.int32) // span < counts[0]

    def attend(step):
        head = step // blocks
        first = step % blocks * block
        query_block = lax.dynamic_index_in_dim(
            lax.dynamic_slice_in_dim(query_rot, first, block, 0), head, 1, keepdims=False
        )
        key_head = lax.dynamic_index_in_dim(keys_all, head, 1, keepdims=False)
        val_head = lax.dynamic_index_in_dim(combined_values, head, 1, keepdims=False)
        scores = jnp.einsum(
            "tgd,ld->tgl", query_block, key_head, preferred_element_type=jnp.float32
        )
        row_pos = first + jnp.arange(block, dtype=jnp.int32)
        own_ok = token_iota[None, :] <= row_pos[:, None]
        visible = jnp.concatenate(
            [jnp.broadcast_to(cache_ok[None, :], (block, cache_length)), own_ok], axis=1
        )[:, None, :]
        top = jnp.max(jnp.where(visible, scores, -1e30), axis=-1, keepdims=True)
        prob = jnp.where(visible, jnp.exp(scores - top), 0.0)
        total = jnp.sum(prob, axis=-1)
        mixed = jnp.einsum(
            "tgl,ld->tgd", prob.astype(jnp.bfloat16), val_head, preferred_element_type=jnp.float32
        )
        return (mixed / total[..., None]).astype(jnp.bfloat16)

    pieces = lax.map(attend, jnp.arange(kv_heads * blocks, dtype=jnp.int32))
    pieces = pieces.reshape(kv_heads, blocks, block, request_group, head_dim)
    results = [jnp.transpose(pieces, (1, 2, 0, 3, 4)).reshape(tokens, q_heads * head_dim)]
    return jnp.stack(results, axis=0)


def solution(mesh):
    return jax.shard_map(
        shards,
        mesh=mesh,
        in_specs=(
            P(("grp", "stretch"), None, "req"),
            P(("grp", "stretch"), None, "req"),
            P(("grp", "stretch"), None, "req"),
            P(("grp", "stretch"), None, "req"),
            P(("grp", "stretch"), None, "req"),
            P(("grp", "stretch"), None, "req"),
            P(("grp", "stretch"), None),
            P(("grp", "stretch")),
            P(("grp", "stretch"), None),
        ),
        out_specs=P(("grp", "stretch"), None, "req"),
        check_vma=False,
    )
```

profile of v0, /device:TPU:0, one launch (start us, length us, event | category | flops | bytes accessed | tf_op | source)
XLA Modules:
  0.0 343.1 jit_solution(17457417227891711137)
XLA Ops:
  0.0 0.8 and_select_fusion.1
  2.2 0.7 sub.51
  2.8 7.3 %all-to-all-start = ((s32[8,1,8]{2,1,0:T(1,128)}), s32[8,1,8]{2,1,0:T(1,128)S(1)}, u32[]{:S(2)}, u32[]{:S(2)}) async-start(s32[8,1,8]{2,1,0:T(1,128)} %bitcast.8), calls=%async_computation | async-start | bytes 8192 | tf_op jit(solution)/shard_map/all_to_all | solution.py:70
  10.1 0.8 copy.72
  10.9 5.6 %all-to-all-done = s32[8,1,8]{2,1,0:T(1,128)S(1)} async-done(((s32[8,1,8]{2,1,0:T(1,128)}), s32[8,1,8]{2,1,0:T(1,128)S(1)}, u32[]{:S(2)}, u32[]{:S(2)}) %all-to-all-start) | async-done | bytes 288 | tf_op jit(solution)/shard_map/all_to_all | solution.py:70
  17.3 0.8 copy.73
  18.0 3.3 all-to-all-start.2
  21.4 2.8 gather_fusion
  24.2 3.6 %all-to-all-done.2 = bf16[8,1,8,2,2]{2,4,3,1,0:T(2,128)(2,1)S(1)} async-done(((bf16[8,1,8,2,2]{2,4,3,1,0:T(2,128)(2,1)}), bf16[8,1,8,2,2]{2,4,3,1,0:T(2,128)(2,1)S(1)}, u32[]{:S(2)}, u32[]{:S(2)}) %all-to-all-start.2) | async-done | bytes 544 | tf_op jit(solution)/shard_map/all_to_all | solution.py:87
  27.8 4.7 %all-to-all-start.1 = ((bf16[8,1,8,128,256]{4,3,2,1,0:T(8,128)(2,1)}), bf16[8,1,8,128,256]{4,3,2,1,0:T(8,128)(2,1)}, u32[]{:S(2)}, u32[]{:S(2)}) async-start(bf16[8,1,8,128,256]{4,3,2,1,0:T(8,128)(2,1)} %bitcast.92), calls=%async_computation.1 | async-start | bytes 8388608 | tf_op jit(solution)/shard_map/all_to_all | solution.py:85
  32.6 2.8 gather_fusion.4
  35.4 88.1 %all-to-all-done.1 = bf16[8,1,8,128,256]{4,3,2,1,0:T(8,128)(2,1)} async-done(((bf16[8,1,8,128,256]{4,3,2,1,0:T(8,128)(2,1)}), bf16[8,1,8,128,256]{4,3,2,1,0:T(8,128)(2,1)}, u32[]{:S(2)}, u32[]{:S(2)}) %all-to-all-start.1) | async-done | bytes 4194336 | tf_op jit(solution)/shard_map/all_to_all | solution.py:85
  123.5 4.7 %all-to-all-start.3 = ((bf16[8,1,8,128,256]{4,3,2,1,0:T(8,128)(2,1)}), bf16[8,1,8,128,256]{4,3,2,1,0:T(8,128)(2,1)}, u32[]{:S(2)}, u32[]{:S(2)}) async-start(bf16[8,1,8,128,256]{4,3,2,1,0:T(8,128)(2,1)} %bitcast.91), calls=%async_computation.3 | async-start | bytes 8388608 | tf_op jit(solution)/shard_map/all_to_all | solution.py:86
  128.3 0.8 copy.81
  130.6 1.5 copy.82
  132.2 0.7 subtract_convert_fusion.1
  132.9 4.7 %multiply_cosine_fusion = (f32[32,128,64]{1,2,0:T(8,128)S(1)}, f32[32,128,64]{1,2,0:T(8,128)}) fusion(f32[64]{0:T(128)S(1)} %negate_power_fusion, f32[32,128]{1,0:T(8,128)S(1)} %add_convert_fusion.2), kind=kLoop, calls=%fused_computation.50 | loop fusion | flops 262144 | bytes 2113792 | tf_op jit(solution)/shard_map/cos | solution.py:13
  138.7 2.9 gather_fusion.1
  141.5 3.4 copy.71
  145.0 2.6 broadcast_multiply_fusion
  147.6 0.8 subtract_convert_fusion
  148.4 0.7 copy.77
  149.6 0.7 copy.78
  150.3 1.3 concatenate.40
  151.6 69.1 %all-to-all-done.3 = bf16[8,1,8,128,256]{4,3,2,1,0:T(8,128)(2,1)} async-done(((bf16[8,1,8,128,256]{4,3,2,1,0:T(8,128)(2,1)}), bf16[8,1,8,128,256]{4,3,2,1,0:T(8,128)(2,1)}, u32[]{:S(2)}, u32[]{:S(2)}) %all-to-all-start.3) | async-done | bytes 4194336 | tf_op jit(solution)/shard_map/all_to_all | solution.py:86
  220.7 2.9 gather_fusion.5
  223.6 3.6 %reshape.521 = f32[4096,2,128]{2,1,0:T(2,128)} reshape(bf16[32,128,256]{2,1,0:T(8,128)(2,1)S(1)} %gather_fusion.5) | data formatting | bytes 6291456 | tf_op jit(solution)/shard_map/convert_element_type | solution.py:105
  227.1 7.3 %copy.86 = f32[4096,2,128]{0,2,1:T(8,128)} copy(f32[4096,2,128]{2,1,0:T(2,128)} %reshape.521) | data formatting | bytes 8388608 | tf_op jit(solution)/shard_map/convert_element_type | solution.py:105
  234.4 2.7 multiply_convert_fusion
  237.1 1.6 maximum_maximum_fusion
  238.7 101.7 %while.14 = (s32[]{:T(128)}, bf16[8,64,8,128]{3,2,1,0:T(8,128)(2,1)}, s32[8]{0:T(128)S(1)}, bf16[256,2,8,128]{3,2,0,1:T(8,128)(2,1)}, bf16[4352,2,128]{0,2,1:T(8...) while((s32[]{:T(128)}, ...), condition=%wide.region_5.6_spmd.clone, body=%wide.region_2.5_spmd.clone.sunk | while | flops 1152459008 | bytes 38785032 | solution.py:167
  238.7 0.7 dynamic_slice.56
  242.1 2.2 fusion.60
  245.2 4.2 %fusion.62 = (f32[64,8]{1,0:T(8,128)S(1)}, bf16[64,8,4352]{2,1,0:T(8,128)(2,1)S(1)}) fusion(f32[64,8,4352]{2,1,0:T(8,128)S(1)} %fusion.60, pred[64,4352]{1,0:T(8,128)(4,1)S(1)} %pad_add_fusion.2), kind=kOutput, calls=%fused_computation.90.clone.1 | output fusion | flops 11145471 | bytes 13649920 | tf_op jit(solution)/shard_map/while/body/eval_jaxpr/sub | solution.py:160
  249.4 2.0 fusion.63
  251.4 0.7 dynamic_slice.56
  254.8 2.2 fusion.60
  257.9 4.2 %fusion.62 = (f32[64,8]{1,0:T(8,128)S(1)}, bf16[64,8,4352]{2,1,0:T(8,128)(2,1)S(1)}) fusion(f32[64,8,4352]{2,1,0:T(8,128)S(1)} %fusion.60, pred[64,4352]{1,0:T(8,128)(4,1)S(1)} %pad_add_fusion.2), kind=kOutput, calls=%fused_computation.90.clone.1 | output fusion | flops 11145471 | bytes 13649920 | tf_op jit(solution)/shard_map/while/body/eval_jaxpr/sub | solution.py:160
  262.1 2.0 fusion.63
  264.1 0.7 dynamic_slice.56
  267.5 2.2 fusion.60
  270.6 4.2 %fusion.62 = (f32[64,8]{1,0:T(8,128)S(1)}, bf16[64,8,4352]{2,1,0:T(8,128)(2,1)S(1)}) fusion(f32[64,8,4352]{2,1,0:T(8,128)S(1)} %fusion.60, pred[64,4352]{1,0:T(8,128)(4,1)S(1)} %pad_add_fusion.2), kind=kOutput, calls=%fused_computation.90.clone.1 | output fusion | flops 11145471 | bytes 13649920 | tf_op jit(solution)/shard_map/while/body/eval_jaxpr/sub | solution.py:160
  274.8 2.0 fusion.63
  276.8 0.7 dynamic_slice.56
  280.2 2.2 fusion.60
  283.3 4.2 %fusion.62 = (f32[64,8]{1,0:T(8,128)S(1)}, bf16[64,8,4352]{2,1,0:T(8,128)(2,1)S(1)}) fusion(f32[64,8,4352]{2,1,0:T(8,128)S(1)} %fusion.60, pred[64,4352]{1,0:T(8,128)(4,1)S(1)} %pad_add_fusion.2), kind=kOutput, calls=%fused_computation.90.clone.1 | output fusion | flops 11145471 | bytes 13649920 | tf_op jit(solution)/shard_map/while/body/eval_jaxpr/sub | solution.py:160
  287.5 2.0 fusion.63
  292.9 2.2 fusion.60
  296.0 4.2 %fusion.62 = (f32[64,8]{1,0:T(8,128)S(1)}, bf16[64,8,4352]{2,1,0:T(8,128)(2,1)S(1)}) fusion(f32[64,8,4352]{2,1,0:T(8,128)S(1)} %fusion.60, pred[64,4352]{1,0:T(8,128)(4,1)S(1)} %pad_add_fusion.2), kind=kOutput, calls=%fused_computation.90.clone.1 | output fusion | flops 11145471 | bytes 13649920 | tf_op jit(solution)/shard_map/while/body/eval_jaxpr/sub | solution.py:160
  300.2 2.0 fusion.63
  302.2 0.7 dynamic_slice.56
  305.6 2.2 fusion.60
  308.7 4.2 %fusion.62 = (f32[64,8]{1,0:T(8,128)S(1)}, bf16[64,8,4352]{2,1,0:T(8,128)(2,1)S(1)}) fusion(f32[64,8,4352]{2,1,0:T(8,128)S(1)} %fusion.60, pred[64,4352]{1,0:T(8,128)(4,1)S(1)} %pad_add_fusion.2), kind=kOutput, calls=%fused_computation.90.clone.1 | output fusion | flops 11145471 | bytes 13649920 | tf_op jit(solution)/shard_map/while/body/eval_jaxpr/sub | solution.py:160
  312.9 2.0 fusion.63
  314.9 0.7 dynamic_slice.56
  318.4 2.2 fusion.60
  321.4 4.2 %fusion.62 = (f32[64,8]{1,0:T(8,128)S(1)}, bf16[64,8,4352]{2,1,0:T(8,128)(2,1)S(1)}) fusion(f32[64,8,4352]{2,1,0:T(8,128)S(1)} %fusion.60, pred[64,4352]{1,0:T(8,128)(4,1)S(1)} %pad_add_fusion.2), kind=kOutput, calls=%fused_computation.90.clone.1 | output fusion | flops 11145471 | bytes 13649920 | tf_op jit(solution)/shard_map/while/body/eval_jaxpr/sub | solution.py:160
  325.6 2.0 fusion.63
  327.6 0.7 dynamic_slice.56
  331.1 2.2 fusion.60
  334.1 4.2 %fusion.62 = (f32[64,8]{1,0:T(8,128)S(1)}, bf16[64,8,4352]{2,1,0:T(8,128)(2,1)S(1)}) fusion(f32[64,8,4352]{2,1,0:T(8,128)S(1)} %fusion.60, pred[64,4352]{1,0:T(8,128)(4,1)S(1)} %pad_add_fusion.2), kind=kOutput, calls=%fused_computation.90.clone.1 | output fusion | flops 11145471 | bytes 13649920 | tf_op jit(solution)/shard_map/while/body/eval_jaxpr/sub | solution.py:160
  338.3 2.0 fusion.63
  340.3 1.5 copy.92
  341.8 1.3 stack_reshape.3
  (113 shorter events, 12.1 us)
Async XLA Ops:
  0.0 21.4 %copy-start = (bf16[16,128,256]{2,1,0:T(8,128)(2,1)S(1)}, bf16[16,128,256]{2,1,0:T(8,128)(2,1)}, u32[]{:S(2)}) copy-start(bf16[16,128,256]{2,1,0:T(8,128)(2,1)} %param.14) | copy-start | bytes 3145732
  2.8 13.7 %all-to-all-start = ((s32[8,1,8]{2,1,0:T(1,128)}), s32[8,1,8]{2,1,0:T(1,128)S(1)}, u32[]{:S(2)}, u32[]{:S(2)}) async-start(s32[8,1,8]{2,1,0:T(1,128)} %bitcast.8), calls=%async_computation | async-start | bytes 8192 | tf_op jit(solution)/shard_map/all_to_all | solution.py:70
  18.0 9.8 %all-to-all-start.2 = ((bf16[8,1,8,2,2]{2,4,3,1,0:T(2,128)(2,1)}), bf16[8,1,8,2,2]{2,4,3,1,0:T(2,128)(2,1)S(1)}, u32[]{:S(2)}, u32[]{:S(2)}) async-start(bf16[8,1,8,2,2]{2,4,3,1,0:T(2,128)(2,1)} %copy.73), calls=%async_computation.2 | async-start | bytes 16384 | tf_op jit(solution)/shard_map/all_to_all | solution.py:87
  27.8 4.7 %copy-start.2 = (bf16[16,128,256]{2,1,0:T(8,128)(2,1)S(1)}, bf16[16,128,256]{2,1,0:T(8,128)(2,1)}, u32[]{:S(2)}) copy-start(bf16[16,128,256]{2,1,0:T(8,128)(2,1)} %param.15) | copy-start | bytes 3145732
  27.8 95.6 %all-to-all-start.1 = ((bf16[8,1,8,128,256]{4,3,2,1,0:T(8,128)(2,1)}), bf16[8,1,8,128,256]{4,3,2,1,0:T(8,128)(2,1)}, u32[]{:S(2)}, u32[]{:S(2)}) async-start(bf16[8,1,8,128,256]{4,3,2,1,0:T(8,128)(2,1)} %bitcast.92), calls=%async_computation.1 | async-start | bytes 8388608 | tf_op jit(solution)/shard_map/all_to_all | solution.py:85
  123.5 4.7 %copy-start.10 = (bf16[1,256,256]{2,1,0:T(8,128)(2,1)S(1)}, bf16[1,256,256]{2,1,0:T(8,128)(2,1)}, u32[]{:S(2)}) copy-start(bf16[1,256,256]{2,1,0:T(8,128)(2,1)} %param.12) | copy-start | bytes 393220
  123.5 4.9 %copy-start.11 = (bf16[1,256,256]{2,1,0:T(8,128)(2,1)S(1)}, bf16[1,256,256]{2,1,0:T(8,128)(2,1)}, u32[]{:S(2)}) copy-start(bf16[1,256,256]{2,1,0:T(8,128)(2,1)} %param.13) | copy-start | bytes 393220
  123.5 5.6 %copy-start.6 = (bf16[1,256,2048]{2,1,0:T(8,128)(2,1)S(1)}, bf16[1,256,2048]{2,1,0:T(8,128)(2,1)}, u32[]{:S(2)}) copy-start(bf16[1,256,2048]{2,1,0:T(8,128)(2,1)} %param.11) | copy-start | bytes 3145732
  123.5 97.2 %all-to-all-start.3 = ((bf16[8,1,8,128,256]{4,3,2,1,0:T(8,128)(2,1)}), bf16[8,1,8,128,256]{4,3,2,1,0:T(8,128)(2,1)}, u32[]{:S(2)}, u32[]{:S(2)}) async-start(bf16[8,1,8,128,256]{4,3,2,1,0:T(8,128)(2,1)} %bitcast.91), calls=%async_computation.3 | async-start | bytes 8388608 | tf_op jit(solution)/shard_map/all_to_all | solution.py:86
  130.4 1.8 copy-start.12
  130.4 1.8 copy-start.13
  144.9 2.6 copy-start.4
  234.4 2.7 copy-start.3
  234.4 2.7 copy-start.7
  234.4 2.7 copy-start.8
  234.4 2.7 copy-start.9
  245.2 4.2 %copy-start.5 = (bf16[4352,2,128]{0,2,1:T(8,128)(2,1)S(1)}, bf16[4352,2,128]{0,2,1:T(8,128)(2,1)}, u32[]{:S(2)}) copy-start(bf16[4352,2,128]{0,2,1:T(8,128)(2,1)} %get-tuple-element.316) | copy-start | bytes 6684676 | tf_op jit(solution)/shard_map/while
  257.9 4.2 %copy-start.5 = (bf16[4352,2,128]{0,2,1:T(8,128)(2,1)S(1)}, bf16[4352,2,128]{0,2,1:T(8,128)(2,1)}, u32[]{:S(2)}) copy-start(bf16[4352,2,128]{0,2,1:T(8,128)(2,1)} %get-tuple-element.316) | copy-start | bytes 6684676 | tf_op jit(solution)/shard_map/while
  270.6 4.2 %copy-start.5 = (bf16[4352,2,128]{0,2,1:T(8,128)(2,1)S(1)}, bf16[4352,2,128]{0,2,1:T(8,128)(2,1)}, u32[]{:S(2)}) copy-start(bf16[4352,2,128]{0,2,1:T(8,128)(2,1)} %get-tuple-element.316) | copy-start | bytes 6684676 | tf_op jit(solution)/shard_map/while
  283.3 4.2 %copy-start.5 = (bf16[4352,2,128]{0,2,1:T(8,128)(2,1)S(1)}, bf16[4352,2,128]{0,2,1:T(8,128)(2,1)}, u32[]{:S(2)}) copy-start(bf16[4352,2,128]{0,2,1:T(8,128)(2,1)} %get-tuple-element.316) | copy-start | bytes 6684676 | tf_op jit(solution)/shard_map/while
  296.0 4.2 %copy-start.5 = (bf16[4352,2,128]{0,2,1:T(8,128)(2,1)S(1)}, bf16[4352,2,128]{0,2,1:T(8,128)(2,1)}, u32[]{:S(2)}) copy-start(bf16[4352,2,128]{0,2,1:T(8,128)(2,1)} %get-tuple-element.316) | copy-start | bytes 6684676 | tf_op jit(solution)/shard_map/while
  308.7 4.2 %copy-start.5 = (bf16[4352,2,128]{0,2,1:T(8,128)(2,1)S(1)}, bf16[4352,2,128]{0,2,1:T(8,128)(2,1)}, u32[]{:S(2)}) copy-start(bf16[4352,2,128]{0,2,1:T(8,128)(2,1)} %get-tuple-element.316) | copy-start | bytes 6684676 | tf_op jit(solution)/shard_map/while
  321.4 4.2 %copy-start.5 = (bf16[4352,2,128]{0,2,1:T(8,128)(2,1)S(1)}, bf16[4352,2,128]{0,2,1:T(8,128)(2,1)}, u32[]{:S(2)}) copy-start(bf16[4352,2,128]{0,2,1:T(8,128)(2,1)} %get-tuple-element.316) | copy-start | bytes 6684676 | tf_op jit(solution)/shard_map/while
  334.1 4.2 %copy-start.5 = (bf16[4352,2,128]{0,2,1:T(8,128)(2,1)S(1)}, bf16[4352,2,128]{0,2,1:T(8,128)(2,1)}, u32[]{:S(2)}) copy-start(bf16[4352,2,128]{0,2,1:T(8,128)(2,1)} %get-tuple-element.316) | copy-start | bytes 6684676 | tf_op jit(solution)/shard_map/while
  340.3 2.8 copy-start.1
where the time goes:
time: 344 us; the launch traced here: 343 us
  waiting for transfers between devices  166 us (48%)
  other arithmetic  55.5 us (16%)
  local copies, waits for them, and re-layouts  43.7 us (13%)
  matrix products  33.6 us (10%)
  loops' own time  22.8 us (7%)
  starting transfers between devices  20 us (6%)
    all_to_all x1, waiting for transfers between devices, shards(): lax.all_to_all(raw_keys, 'stretch', split_axis=0, concat_axis=0, tiled=True)  88.1 us
    all_to_all x1, waiting for transfers between devices, shards(): lax.all_to_all(raw_values, 'stretch', split_axis=0, concat_axis=0, tiled=...  69.1 us
    sub x8, other arithmetic, attend(): prob = jnp.where(visible, jnp.exp(scores - top), 0.0)  33.4 us
    another operation x1, loops' own time, shards(): pieces = lax.map(attend, jnp.arange(kv_heads * blocks, dtype=jnp.int32))  22.8 us
    dot_general x8, matrix products, attend(): jnp.einsum('tgd,ld->tgl', query_block, key_head, preferred_element_type=j...  17.7 us
    dot_general x8, matrix products, attend(): jnp.einsum('tgl,ld->tgd', prob.astype(jnp.bfloat16), val_head, preferred_...  15.9 us
    convert_element_type x2, local copies, waits for them, and re-layouts, shards(): vals_wide = got_vals.reshape(flat, span, width)[index].reshape(rows, slot...  10.8 us
    all_to_all x1, starting transfers between devices, shards(): lax.all_to_all(jnp.transpose(mine[0], (1, 0, 2)), 'stretch', split_axis=0...  7.28 us
  transfers between devices with their start and end apart: 4, of which 4 were waited for; matrix products, arithmetic and copies ran while one was open for 9% of the time, Pallas kernels for 0%

commit v1 on v0

--- a/solution.py
+++ b/solution.py
@@ -1,6 +1,10 @@
+import functools
+
 import jax
 import jax.numpy as jnp
 from jax import lax
+from jax.experimental import pallas as pl
+from jax.experimental.pallas import tpu as pltpu
 from jax.sharding import PartitionSpec as P
 
 rope_base = 500000.0
@@ -109,65 +113,97 @@
         .astype(jnp.bfloat16)
         .reshape(rows, slots, span, width)
     )
-    block = min(tokens, 64)
-    blocks = tokens // block
     cache_length = slots * span
     token_iota = jnp.arange(tokens, dtype=jnp.int32)
     token_positions = (cache_length + token_iota)[:, None]
+    new_keys = apply_rotary(
+        fresh_keys.reshape(rows, tokens, kv_heads, head_dim).astype(jnp.float32),
+        token_positions,
+    ).astype(jnp.bfloat16)
     keys_all = jnp.concatenate(
-        [
-            cached_keys[0].reshape(cache_length, kv_heads, head_dim),
-            apply_rotary(
-                fresh_keys[0].reshape(tokens, kv_heads, head_dim).astype(jnp.float32),
-                token_positions,
-            ).astype(jnp.bfloat16),
-        ],
-        axis=0,
-    )
-    combined_values = jnp.concatenate(
-        [
-            cached_vals[0].reshape(cache_length, kv_heads, head_dim),
-            fresh_values[0].reshape(tokens, kv_heads, head_dim),
-        ],
-        axis=0,
+        [cached_keys.reshape(rows, cache_length, width), new_keys.reshape(rows, tokens, width)],
+        axis=1,
+    )
+    values_all = jnp.concatenate(
+        [cached_vals.reshape(rows, cache_length, width), fresh_values], axis=1
     )
     query_rot = (
         apply_rotary(
-            queries[0].reshape(tokens, q_heads, head_dim).astype(jnp.float32), token_positions
+            queries.reshape(rows, tokens, q_heads, head_dim).astype(jnp.float32), token_positions
         )
         * head_dim ** (-0.5)
     ).astype(jnp.bfloat16)
-    query_rot = query_rot.reshape(tokens, kv_heads, request_group, head_dim)
-    cache_ok = jnp.arange(cache_length, dtype=jnp.int32) // span < counts[0]
-
-    def attend(step):
-        head = step // blocks
-        first = step % blocks * block
-        query_block = lax.dynamic_index_in_dim(
-            lax.dynamic_slice_in_dim(query_rot, first, block, 0), head, 1, keepdims=False
+    query_rot = query_rot.reshape(rows, tokens, q_heads * head_dim)
+    return flash(query_rot, keys_all, values_all, counts * span, request_group, cache_length)
+
+
+def flash_kernel(live_ref, q_ref, k_ref, v_ref, o_ref, m_sc, l_sc, acc_sc, *, cache_length, chunk):
+    tokens = q_ref.shape[0]
+    live = live_ref[pl.program_id(0)]
+    q = q_ref[...]
+    m_sc[...] = jnp.full(m_sc.shape, -1e30, jnp.float32)
+    l_sc[...] = jnp.zeros(l_sc.shape, jnp.float32)
+    acc_sc[...] = jnp.zeros(acc_sc.shape, jnp.float32)
+
+    def step(first, size, causal):
+        k = k_ref[pl.ds(first, size), :]
+        v = v_ref[pl.ds(first, size), :]
+        s = lax.dot_general(q, k, (((1,), (1,)), ((), ())), preferred_element_type=jnp.float32)
+        col = lax.broadcasted_iota(jnp.int32, s.shape, 1)
+        if causal:
+            visible = col <= lax.broadcasted_iota(jnp.int32, s.shape, 0)
+        else:
+            visible = first + col < live
+        s = jnp.where(visible, s, -1e30)
+        m_old = m_sc[...]
+        m_new = jnp.maximum(m_old, jnp.max(s, axis=1, keepdims=True))
+        alpha = jnp.exp(m_old - m_new)
+        p = jnp.where(visible, jnp.exp(s - m_new), 0.0)
+        l_sc[...] = alpha * l_sc[...] + jnp.sum(p, axis=1, keepdims=True)
+        acc_sc[...] = alpha * acc_sc[...] + lax.dot_general(
+            p.astype(jnp.bfloat16), v, (((1,), (0,)), ((), ())), preferred_element_type=jnp.float32
         )
-        key_head = lax.dynamic_index_in_dim(keys_all, head, 1, keepdims=False)
-        val_head = lax.dynamic_index_in_dim(combined_values, head, 1, keepdims=False)
-        scores = jnp.einsum(
-            "tgd,ld->tgl", query_block, key_head, preferred_element_type=jnp.float32
-        )
-        row_pos = first + jnp.arange(block, dtype=jnp.int32)
-        own_ok = token_iota[None, :] <= row_pos[:, None]
-        visible = jnp.concatenate(
-            [jnp.broadcast_to(cache_ok[None, :], (block, cache_length)), own_ok], axis=1
-        )[:, None, :]
-        top = jnp.max(jnp.where(visible, scores, -1e30), axis=-1, keepdims=True)
-        prob = jnp.where(visible, jnp.exp(scores - top), 0.0)
-        total = jnp.sum(prob, axis=-1)
-        mixed = jnp.einsum(
-            "tgl,ld->tgd", prob.astype(jnp.bfloat16), val_head, preferred_element_type=jnp.float32
-        )
-        return (mixed / total[..., None]).astype(jnp.bfloat16)
-
-    pieces = lax.map(attend, jnp.arange(kv_heads * blocks, dtype=jnp.int32))
-    pieces = pieces.reshape(kv_heads, blocks, block, request_group, head_dim)
-    results = [jnp.transpose(pieces, (1, 2, 0, 3, 4)).reshape(tokens, q_heads * head_dim)]
-    return jnp.stack(results, axis=0)
+        m_sc[...] = m_new
+
+    for index in range(cache_length // chunk):
+
+        @pl.when(index * chunk < live)
+        def _():
+            step(index * chunk, chunk, False)
+
+    step(cache_length, tokens, True)
+    o_ref[...] = (acc_sc[...] / l_sc[...]).astype(o_ref.dtype)
+
+
+def flash(query_rot, keys_all, values_all, live, request_group, cache_length):
+    rows, tokens, q_width = query_rot.shape
+    length, width = keys_all.shape[1:]
+    head_dim = 128
+    q_heads = q_width // head_dim
+    kv_heads = width // head_dim
+    chunk = 512 if cache_length % 512 == 0 else 128
+    kernel = functools.partial(flash_kernel, cache_length=cache_length, chunk=chunk)
+    return pl.pallas_call(
+        kernel,
+        grid_spec=pltpu.PrefetchScalarGridSpec(
+            num_scalar_prefetch=1,
+            grid=(rows, kv_heads, request_group),
+            in_specs=[
+                pl.BlockSpec((None, tokens, head_dim), lambda r, h, g, lv: (r, 0, h * request_group + g)),
+                pl.BlockSpec((None, length, head_dim), lambda r, h, g, lv: (r, 0, h)),
+                pl.BlockSpec((None, length, head_dim), lambda r, h, g, lv: (r, 0, h)),
+            ],
+            out_specs=pl.BlockSpec(
+                (None, tokens, head_dim), lambda r, h, g, lv: (r, 0, h * request_group + g)
+            ),
+            scratch_shapes=[
+                pltpu.VMEM((tokens, 1), jnp.float32),
+                pltpu.VMEM((tokens, 1), jnp.float32),
+                pltpu.VMEM((tokens, head_dim), jnp.float32),
+            ],
+        ),
+        out_shape=jax.ShapeDtypeStruct((rows, tokens, q_width), jnp.bfloat16),
+    )(live, query_rot, keys_all, values_all)
 
 
 def solution(mesh):

time: 344 us -> 318 us (0.924)
  the two profiles are of different devices: /device:TPU:0 before, /device:TPU:2 now
where the time goes in v1:
time: 318 us; the launch traced here: 316 us
  waiting for transfers between devices  138 us (43%)
  Pallas kernels  87.6 us (28%)
  other arithmetic  36.1 us (11%)
  local copies, waits for them, and re-layouts  34.9 us (11%)
  starting transfers between devices  18.6 us (6%)
    all_to_all x1, waiting for transfers between devices, shards(): lax.all_to_all(raw_keys, 'stretch', split_axis=0, concat_axis=0, tiled=True)  88.1 us
    pallas_call x1, Pallas kernels, flash(): pl.pallas_call(kernel, grid_spec=pltpu.PrefetchScalarGridSpec(num_scalar_...  87.6 us
    all_to_all x1, waiting for transfers between devices, shards(): lax.all_to_all(raw_values, 'stretch', split_axis=0, concat_axis=0, tiled=...  40.8 us
    mul x4, local copies, waits for them, and re-layouts, shards(): vals_wide * scale_factor[:, :, 1][:, :, None, :, None]  9.64 us
    cos x2, other arithmetic, apply_rotary(): cosine = jnp.cos(angle)  9.32 us
    another operation x2, other arithmetic  7.4 us
    concatenate x2, other arithmetic, apply_rotary(): jnp.concatenate([first * cosine - second * sine, second * cosine + first...  6.91 us
  transfers between devices with their start and end apart: 4, of which 4 were waited for; matrix products, arithmetic and copies ran while one was open for 18% of the time, Pallas kernels for 0%

profile of v1, /device:TPU:2, one launch (start us, length us, event | category | flops | bytes accessed | tf_op | source)
XLA Modules:
  0.0 316.3 jit_solution(4641415680473340106)
XLA Ops:
  0.0 0.0 copy-start
  0.8 0.7 and_select_fusion.1
  1.4 0.1 convert_reduce_fusion
  1.5 0.1 select_reduce_fusion
  1.6 0.7 sub.24
  2.3 5.8 %all-to-all-start = ((s32[8,1,8]{2,1,0:T(1,128)}), s32[8,1,8]{2,1,0:T(1,128)S(1)}, u32[]{:S(2)}, u32[]{:S(2)}) async-start(s32[8,1,8]{2,1,0:T(1,128)} %bitcast.5), calls=%async_computation | async-start | bytes 8192 | tf_op jit(solution)/shard_map/all_to_all | solution.py:74
  8.1 0.8 copy.31
  8.9 5.6 %all-to-all-done = s32[8,1,8]{2,1,0:T(1,128)S(1)} async-done(((s32[8,1,8]{2,1,0:T(1,128)}), s32[8,1,8]{2,1,0:T(1,128)S(1)}, u32[]{:S(2)}, u32[]{:S(2)}) %all-to-all-start) | async-done | bytes 288 | tf_op jit(solution)/shard_map/all_to_all | solution.py:74
  14.6 0.1 reshape.554
  14.6 0.6 gather_fusion.2
  15.3 0.8 copy.32
  16.1 3.3 %all-to-all-start.2 = ((bf16[8,1,8,2,2]{2,4,3,1,0:T(2,128)(2,1)}), bf16[8,1,8,2,2]{2,4,3,1,0:T(2,128)(2,1)S(1)}, u32[]{:S(2)}, u32[]{:S(2)}) async-start(bf16[8,1,8,2,2]{2,4,3,1,0:T(2,128)(2,1)} %copy.32), calls=%async_computation.2 | async-start | bytes 16384 | tf_op jit(solution)/shard_map/all_to_all | solution.py:91
  19.4 0.0 copy-done
  19.4 2.8 gather_fusion
  22.2 3.7 %all-to-all-done.2 = bf16[8,1,8,2,2]{2,4,3,1,0:T(2,128)(2,1)S(1)} async-done(((bf16[8,1,8,2,2]{2,4,3,1,0:T(2,128)(2,1)}), bf16[8,1,8,2,2]{2,4,3,1,0:T(2,128)(2,1)S(1)}, u32[]{:S(2)}, u32[]{:S(2)}) %all-to-all-start.2) | async-done | bytes 544 | tf_op jit(solution)/shard_map/all_to_all | solution.py:91
  25.9 0.0 copy-start.2
  25.9 4.7 %all-to-all-start.1 = ((bf16[8,1,8,128,256]{4,3,2,1,0:T(8,128)(2,1)}), bf16[8,1,8,128,256]{4,3,2,1,0:T(8,128)(2,1)}, u32[]{:S(2)}, u32[]{:S(2)}) async-start(bf16[8,1,8,128,256]{4,3,2,1,0:T(8,128)(2,1)} %bitcast.44), calls=%async_computation.1 | async-start | bytes 8388608 | tf_op jit(solution)/shard_map/all_to_all | solution.py:89
  30.6 0.0 copy-done.2
  30.6 2.8 gather_fusion.4
  33.4 88.1 %all-to-all-done.1 = bf16[8,1,8,128,256]{4,3,2,1,0:T(8,128)(2,1)} async-done(((bf16[8,1,8,128,256]{4,3,2,1,0:T(8,128)(2,1)}), bf16[8,1,8,128,256]{4,3,2,1,0:T(8,128)(2,1)}, u32[]{:S(2)}, u32[]{:S(2)}) %all-to-all-start.1) | async-done | bytes 4194336 | tf_op jit(solution)/shard_map/all_to_all | solution.py:89
  121.5 0.0 copy-start.7
  121.5 4.7 %all-to-all-start.3 = ((bf16[8,1,8,128,256]{4,3,2,1,0:T(8,128)(2,1)}), bf16[8,1,8,128,256]{4,3,2,1,0:T(8,128)(2,1)}, u32[]{:S(2)}, u32[]{:S(2)}) async-start(bf16[8,1,8,128,256]{4,3,2,1,0:T(8,128)(2,1)} %bitcast.43), calls=%async_computation.3 | async-start | bytes 8388608 | tf_op jit(solution)/shard_map/all_to_all | solution.py:90
  126.2 0.0 copy-done.7
  126.2 0.0 copy-start.5
  126.2 0.1 reshape.550
  126.3 0.5 multiply_cosine_fusion.1
  126.9 0.5 subtract_convert_fusion.1
  127.4 0.4 pad_maximum_fusion.3
  127.7 0.1 convert_element_type.179
  127.8 0.0 copy-done.5
  127.8 0.2 convert_bitcast_fusion
  128.1 0.4 copy.37
  128.5 0.7 multiply_subtract_fusion
  129.2 0.6 fusion.1
  129.8 0.0 copy-start.8
  129.8 1.3 convert_element_type.170.q_ref
  131.1 0.0 copy-done.8
  131.1 0.1 add_convert_fusion.2
  131.2 8.8 %multiply_cosine_fusion = (f32[32,128,64]{2,1,0:T(8,128)}, f32[32,128,64]{2,1,0:T(8,128)}) fusion(f32[64]{0:T(128)S(1)} %negate_power_fusion, f32[32,128]{1,0:T(8,128)S(1)} %add_convert_fusion.2), kind=kLoop, calls=%fused_computation.11 | loop fusion | flops 262144 | bytes 2113792 | tf_op jit(solution)/shard_map/cos | solution.py:17
  140.0 0.2 copy.33
  140.2 0.6 gather_fusion.3
  140.8 0.1 copy.34
  140.9 0.1 copy.35
  141.0 0.1 copy.36
  141.1 3.1 mul.294
  144.2 6.4 %mul.295 = f32[1,4096,256]{2,1,0:T(8,128)} reshape(f32[32,128,2,128]{3,2,1,0:T(2,128)} %mul.294) | data formatting | bytes 8388608 | tf_op jit(solution)/shard_map/mul | solution.py:112
  150.6 2.9 gather_fusion.1
  153.5 3.6 %reshape.549 = f32[1,32,128,2,128]{4,3,2,1,0:T(2,128)} reshape(bf16[32,128,256]{2,1,0:T(8,128)(2,1)S(1)} %gather_fusion.1) | data formatting | bytes 6291456 | tf_op jit(solution)/shard_map/convert_element_type | solution.py:97
  157.1 0.0 copy-start.3
  157.1 0.0 copy-start.4
  157.1 4.2 %broadcast_multiply_fusion = f32[1,32,128,2,128]{4,3,2,1,0:T(2,128)S(1)} fusion(f32[1,32,128,2,128]{4,3,2,1,0:T(2,128)} %reshape.549, f32[32,2]{1,0:T(8,128)S(1)} %copy.35), kind=kLoop, calls=%fused_computation.18 | loop fusion | flops 1048576 | bytes 8388864 | tf_op jit(solution)/shard_map/mul | solution.py:99
  161.2 0.0 copy-done.3
  161.2 0.0 copy-done.4
  161.3 6.9 %subtract_convert_fusion = (bf16[1,32,128,2,64]{4,3,2,1,0:T(2,128)(2,1)S(1)}, bf16[1,32,128,2,64]{4,3,2,1,0:T(2,128)(2,1)S(1)}) fusion(f32[1,32,128,2,128]{4,3,2,1,0:T(2,128)S(1)} %broadcast_multiply_fusion, f32[32,128,64]{2,1,0:T(8,128)S(1)} %copy-done.4, f32[32,128,64]{2,1,0:T(8,128)S(1)} %copy-done.3), kind=kLoop, calls=%fused_computation.9 | loop fusion | flops 4194304 | bytes 8388608 | tf_op jit(solution)/shard_map/convert.6
  168.2 6.5 %pad_maximum_fusion.2 = bf16[1,32,128,2,128]{4,3,2,1,0:T(2,128)(2,1)} fusion(bf16[1,32,128,2,64]{4,3,2,1,0:T(2,128)(2,1)S(1)} %get-tuple-element.6, bf16[1,32,128,2,64]{4,3,2,1,0:T(2,128)(2,1)S(1)} %get-tuple-element.5), kind=kLoop, calls=%fused_computation.16 | loop fusion | flops 4194304 | bytes 4194304 | tf_op jit(solution)/shard_map/concatenate | solution.py:21
  174.7 3.2 convert_element_type.176
  177.9 40.8 %all-to-all-done.3 = bf16[8,1,8,128,256]{4,3,2,1,0:T(8,128)(2,1)} async-done(((bf16[8,1,8,128,256]{4,3,2,1,0:T(8,128)(2,1)}), bf16[8,1,8,128,256]{4,3,2,1,0:T(8,128)(2,1)}, u32[]{:S(2)}, u32[]{:S(2)}) %all-to-all-start.3) | async-done | bytes 4194336 | tf_op jit(solution)/shard_map/all_to_all | solution.py:90
  218.7 4.2 %gather_fusion.5 = bf16[32,128,256]{2,1,0:T(8,128)(2,1)} fusion(bf16[64,128,256]{2,1,0:T(8,128)(2,1)} %bitcast.15, s32[1024]{0:T(1024)S(1)} %pad_clamp_fusion), kind=kCustom, calls=%fused_computation.5 | custom fusion | bytes 4194432 | tf_op jit(solution)/shard_map/gather | solution.py:107
  222.9 0.0 copy-start.6
  222.9 3.4 %fusion = bf16[1,4096,256]{2,1,0:T(8,128)(2,1)S(1)} fusion(f32[1,4096,256]{2,1,0:T(8,128)} %mul.295, bf16[1,4096,256]{2,1,0:T(8,128)(2,1)} %bitcast.45), kind=kLoop, calls=%fused_computation.7 | loop fusion | flops 3145728 | bytes 8388608 | tf_op jit(solution)/shard_map/convert_element_type | solution.py:113
  226.3 0.0 copy-done.6
  226.3 2.4 pad_maximum_fusion
  228.7 87.6 %shard_map.91 = bf16[1,256,2048]{2,1,0:T(8,128)(2,1)} custom-call(s32[1]{0:T(128)S(6)} %mul.260.live_ref, bf16[1,256,2048]{2,1,0:T(8,128)(2,1)} %convert_element_type.170.q_ref, bf16[1,4352,256]{2,1,0:T(8,128)(2,1)} %get-tuple-element.21.k_ref, bf16[1,4352,256]{2,1,0:T(8,128)(2,1)} %get-tuple-element.22.v_ref), custom_call_target="tpu_custom_call" | custom-call | tf_op jit(solution)/shard_map/pallas_call | solution.py:186
  316.3 0.0 copy-done.1
  (11 shorter events, 0.1 us)
Async XLA Ops:
  0.0 19.4 %copy-start = (bf16[16,128,256]{2,1,0:T(8,128)(2,1)S(1)}, bf16[16,128,256]{2,1,0:T(8,128)(2,1)}, u32[]{:S(2)}) copy-start(bf16[16,128,256]{2,1,0:T(8,128)(2,1)} %param.12) | copy-start | bytes 3145732
  2.3 12.2 %all-to-all-start = ((s32[8,1,8]{2,1,0:T(1,128)}), s32[8,1,8]{2,1,0:T(1,128)S(1)}, u32[]{:S(2)}, u32[]{:S(2)}) async-start(s32[8,1,8]{2,1,0:T(1,128)} %bitcast.5), calls=%async_computation | async-start | bytes 8192 | tf_op jit(solution)/shard_map/all_to_all | solution.py:74
  16.1 9.8 %all-to-all-start.2 = ((bf16[8,1,8,2,2]{2,4,3,1,0:T(2,128)(2,1)}), bf16[8,1,8,2,2]{2,4,3,1,0:T(2,128)(2,1)S(1)}, u32[]{:S(2)}, u32[]{:S(2)}) async-start(bf16[8,1,8,2,2]{2,4,3,1,0:T(2,128)(2,1)} %copy.32), calls=%async_computation.2 | async-start | bytes 16384 | tf_op jit(solution)/shard_map/all_to_all | solution.py:91
  25.9 4.7 %copy-start.2 = (bf16[16,128,256]{2,1,0:T(8,128)(2,1)S(1)}, bf16[16,128,256]{2,1,0:T(8,128)(2,1)}, u32[]{:S(2)}) copy-start(bf16[16,128,256]{2,1,0:T(8,128)(2,1)} %param.13) | copy-start | bytes 3145732
  25.9 95.6 %all-to-all-start.1 = ((bf16[8,1,8,128,256]{4,3,2,1,0:T(8,128)(2,1)}), bf16[8,1,8,128,256]{4,3,2,1,0:T(8,128)(2,1)}, u32[]{:S(2)}, u32[]{:S(2)}) async-start(bf16[8,1,8,128,256]{4,3,2,1,0:T(8,128)(2,1)} %bitcast.44), calls=%async_computation.1 | async-start | bytes 8388608 | tf_op jit(solution)/shard_map/all_to_all | solution.py:89
  121.5 4.7 %copy-start.7 = (bf16[1,256,256]{2,1,0:T(8,128)(2,1)S(1)}, bf16[1,256,256]{2,1,0:T(8,128)(2,1)}, u32[]{:S(2)}) copy-start(bf16[1,256,256]{2,1,0:T(8,128)(2,1)} %param.10) | copy-start | bytes 393220
  121.5 97.2 %all-to-all-start.3 = ((bf16[8,1,8,128,256]{4,3,2,1,0:T(8,128)(2,1)}), bf16[8,1,8,128,256]{4,3,2,1,0:T(8,128)(2,1)}, u32[]{:S(2)}, u32[]{:S(2)}) async-start(bf16[8,1,8,128,256]{4,3,2,1,0:T(8,128)(2,1)} %bitcast.43), calls=%async_computation.3 | async-start | bytes 8388608 | tf_op jit(solution)/shard_map/all_to_all | solution.py:90
  126.2 1.7 copy-start.5
  129.8 1.3 copy-start.8
  157.1 4.2 %copy-start.3 = (f32[32,128,64]{2,1,0:T(8,128)S(1)}, f32[32,128,64]{2,1,0:T(8,128)}, u32[]{:S(2)}) copy-start(f32[32,128,64]{2,1,0:T(8,128)} %get-tuple-element.11) | copy-start | bytes 3145732
  157.1 4.2 %copy-start.4 = (f32[32,128,64]{2,1,0:T(8,128)S(1)}, f32[32,128,64]{2,1,0:T(8,128)}, u32[]{:S(2)}) copy-start(f32[32,128,64]{2,1,0:T(8,128)} %get-tuple-element.12) | copy-start | bytes 3145732
  222.9 3.4 %copy-start.6 = (bf16[1,256,256]{2,1,0:T(8,128)(2,1)S(1)}, bf16[1,256,256]{2,1,0:T(8,128)(2,1)}, u32[]{:S(2)}) copy-start(bf16[1,256,256]{2,1,0:T(8,128)(2,1)} %param.11) | copy-start | bytes 393220
  228.7 87.6 %copy-start.1 = (bf16[16,128,256]{2,1,0:T(8,128)(2,1)S(1)}, bf16[16,128,256]{2,1,0:T(8,128)(2,1)}, u32[]{:S(2)}) copy-start(bf16[16,128,256]{2,1,0:T(8,128)(2,1)} %param.12) | copy-start | bytes 3145732

commit v2 on v1

--- a/solution.py
+++ b/solution.py
@@ -137,73 +137,84 @@
     return flash(query_rot, keys_all, values_all, counts * span, request_group, cache_length)
 
 
-def flash_kernel(live_ref, q_ref, k_ref, v_ref, o_ref, m_sc, l_sc, acc_sc, *, cache_length, chunk):
+def flash_kernel(bias_ref, q_ref, k_ref, v_ref, o_ref, *, cache_length, chunk, heads):
     tokens = q_ref.shape[0]
-    live = live_ref[pl.program_id(0)]
-    q = q_ref[...]
-    m_sc[...] = jnp.full(m_sc.shape, -1e30, jnp.float32)
-    l_sc[...] = jnp.zeros(l_sc.shape, jnp.float32)
-    acc_sc[...] = jnp.zeros(acc_sc.shape, jnp.float32)
-
-    def step(first, size, causal):
-        k = k_ref[pl.ds(first, size), :]
-        v = v_ref[pl.ds(first, size), :]
-        s = lax.dot_general(q, k, (((1,), (1,)), ((), ())), preferred_element_type=jnp.float32)
-        col = lax.broadcasted_iota(jnp.int32, s.shape, 1)
-        if causal:
-            visible = col <= lax.broadcasted_iota(jnp.int32, s.shape, 0)
-        else:
-            visible = first + col < live
-        s = jnp.where(visible, s, -1e30)
-        m_old = m_sc[...]
-        m_new = jnp.maximum(m_old, jnp.max(s, axis=1, keepdims=True))
-        alpha = jnp.exp(m_old - m_new)
-        p = jnp.where(visible, jnp.exp(s - m_new), 0.0)
-        l_sc[...] = alpha * l_sc[...] + jnp.sum(p, axis=1, keepdims=True)
-        acc_sc[...] = alpha * acc_sc[...] + lax.dot_general(
-            p.astype(jnp.bfloat16), v, (((1,), (0,)), ((), ())), preferred_element_type=jnp.float32
-        )
-        m_sc[...] = m_new
-
-    for index in range(cache_length // chunk):
-
-        @pl.when(index * chunk < live)
-        def _():
-            step(index * chunk, chunk, False)
-
-    step(cache_length, tokens, True)
-    o_ref[...] = (acc_sc[...] / l_sc[...]).astype(o_ref.dtype)
+    lanes = 128
+    new_mask = lax.broadcasted_iota(jnp.int32, (tokens, tokens), 1) <= lax.broadcasted_iota(
+        jnp.int32, (tokens, tokens), 0
+    )
+
+    def fold(acc, s, op):
+        for b in range(s.shape[1] // lanes):
+            acc = op(acc, s[:, b * lanes:(b + 1) * lanes])
+        return acc
+
+    for head in range(heads):
+        q = q_ref[:, head * lanes:(head + 1) * lanes]
+
+        def scores(first, size):
+            return lax.dot_general(
+                q, k_ref[:, first:first + size], (((1,), (0,)), ((), ())),
+                preferred_element_type=jnp.float32,
+            )
+
+        def masked(first, size):
+            return scores(first, size) + bias_ref[:, first:first + size]
+
+        fresh = jnp.where(new_mask, scores(cache_length, tokens), -1e30)
+        top = fold(jnp.full((tokens, lanes), -1e30, jnp.float32), fresh, jnp.maximum)
+        for first in range(0, cache_length, chunk):
+            top = fold(top, masked(first, chunk), jnp.maximum)
+        top = jnp.max(top, axis=1, keepdims=True)
+
+        def mix(s, first, size):
+            p = jnp.exp(s - top)
+            return p, lax.dot_general(
+                p.astype(jnp.bfloat16), v_ref[first:first + size, :], (((1,), (0,)), ((), ())),
+                preferred_element_type=jnp.float32,
+            )
+
+        p, acc = mix(fresh, cache_length, tokens)
+        total = fold(jnp.zeros((tokens, lanes), jnp.float32), p, jnp.add)
+        for first in range(0, cache_length, chunk):
+            p, part = mix(masked(first, chunk), first, chunk)
+            total = fold(total, p, jnp.add)
+            acc = acc + part
+        total = jnp.sum(total, axis=1, keepdims=True)
+        o_ref[:, head * lanes:(head + 1) * lanes] = (acc / total).astype(o_ref.dtype)
+
+
+CHUNK = 512
+HEADS = 4
 
 
 def flash(query_rot, keys_all, values_all, live, request_group, cache_length):
     rows, tokens, q_width = query_rot.shape
     length, width = keys_all.shape[1:]
     head_dim = 128
-    q_heads = q_width // head_dim
     kv_heads = width // head_dim
-    chunk = 512 if cache_length % 512 == 0 else 128
-    kernel = functools.partial(flash_kernel, cache_length=cache_length, chunk=chunk)
+    chunk = CHUNK if cache_length % CHUNK == 0 else 128
+    heads = HEADS
+    keys_t = jnp.swapaxes(keys_all, 1, 2)
+    bias = jnp.where(
+        jnp.arange(cache_length, dtype=jnp.int32)[None, :] < live[:, None], 0.0, -1e30
+    ).astype(jnp.float32)[:, None, :]
+    kernel = functools.partial(flash_kernel, cache_length=cache_length, chunk=chunk, heads=heads)
+    per = request_group // heads
     return pl.pallas_call(
         kernel,
-        grid_spec=pltpu.PrefetchScalarGridSpec(
-            num_scalar_prefetch=1,
-            grid=(rows, kv_heads, request_group),
-            in_specs=[
-                pl.BlockSpec((None, tokens, head_dim), lambda r, h, g, lv: (r, 0, h * request_group + g)),
-                pl.BlockSpec((None, length, head_dim), lambda r, h, g, lv: (r, 0, h)),
-                pl.BlockSpec((None, length, head_dim), lambda r, h, g, lv: (r, 0, h)),
-            ],
-            out_specs=pl.BlockSpec(
-                (None, tokens, head_dim), lambda r, h, g, lv: (r, 0, h * request_group + g)
-            ),
-            scratch_shapes=[
-                pltpu.VMEM((tokens, 1), jnp.float32),
-                pltpu.VMEM((tokens, 1), jnp.float32),
-                pltpu.VMEM((tokens, head_dim), jnp.float32),
-            ],
+        grid=(rows, kv_heads, per),
+        in_specs=[
+            pl.BlockSpec((None, 1, cache_length), lambda r, h, g: (r, 0, 0)),
+            pl.BlockSpec((None, tokens, head_dim * heads), lambda r, h, g: (r, 0, h * per + g)),
+            pl.BlockSpec((None, head_dim, length), lambda r, h, g: (r, h, 0)),
+            pl.BlockSpec((None, length, head_dim), lambda r, h, g: (r, 0, h)),
+        ],
+        out_specs=pl.BlockSpec(
+            (None, tokens, head_dim * heads), lambda r, h, g: (r, 0, h * per + g)
         ),
         out_shape=jax.ShapeDtypeStruct((rows, tokens, q_width), jnp.bfloat16),
-    )(live, query_rot, keys_all, values_all)
+    )(bias, query_rot, keys_t, values_all)
 
 
 def solution(mesh):

time: 318 us -> 263 us (0.83)
  the two profiles are of different devices: /device:TPU:2 before, /device:TPU:0 now
where the time goes in v2:
time: 263 us; the launch traced here: 262 us
  waiting for transfers between devices  156 us (59%)
  local copies, waits for them, and re-layouts  35.7 us (14%)
  Pallas kernels  30.6 us (12%)
  starting transfers between devices  20 us (8%)
  other arithmetic  18.8 us (7%)
    all_to_all x1, waiting for transfers between devices, shards(): lax.all_to_all(raw_keys, 'stretch', split_axis=0, concat_axis=0, tiled=True)  88.1 us
    all_to_all x1, waiting for transfers between devices, shards(): lax.all_to_all(raw_values, 'stretch', split_axis=0, concat_axis=0, tiled=...  58.4 us
    pallas_call x1, Pallas kernels, flash(): pl.pallas_call(kernel, grid=(rows, kv_heads, per), in_specs=[pl.BlockSpec...  30.6 us
    mul x4, local copies, waits for them, and re-layouts, shards(): vals_wide * scale_factor[:, :, 1][:, :, None, :, None]  9.64 us
    all_to_all x1, starting transfers between devices, shards(): lax.all_to_all(jnp.transpose(mine[0], (1, 0, 2)), 'stretch', split_axis=0...  7.28 us
    all_to_all x1, waiting for transfers between devices, shards(): lax.all_to_all(jnp.transpose(mine[0], (1, 0, 2)), 'stretch', split_axis=0...  5.61 us
  transfers between devices with their start and end apart: 4, of which 4 were waited for; matrix products, arithmetic and copies ran while one was open for 15% of the time, Pallas kernels for 0%

profile of v2, /device:TPU:0, one launch (start us, length us, event | category | flops | bytes accessed | tf_op | source)
XLA Modules:
  0.0 261.8 jit_solution(9508539694346670597)
XLA Ops:
  0.0 0.0 copy-start
  0.8 0.7 and_select_fusion.1
  1.4 0.1 convert_reduce_fusion
  1.5 0.1 select_reduce_fusion
  1.6 0.7 sub.24
  2.3 7.3 %all-to-all-start = ((s32[8,1,8]{2,1,0:T(1,128)}), s32[8,1,8]{2,1,0:T(1,128)S(1)}, u32[]{:S(2)}, u32[]{:S(2)}) async-start(s32[8,1,8]{2,1,0:T(1,128)} %bitcast.6), calls=%async_computation | async-start | bytes 8192 | tf_op jit(solution)/shard_map/all_to_all | solution.py:74
  9.6 0.8 copy.48
  10.4 5.6 %all-to-all-done = s32[8,1,8]{2,1,0:T(1,128)S(1)} async-done(((s32[8,1,8]{2,1,0:T(1,128)}), s32[8,1,8]{2,1,0:T(1,128)S(1)}, u32[]{:S(2)}, u32[]{:S(2)}) %all-to-all-start) | async-done | bytes 288 | tf_op jit(solution)/shard_map/all_to_all | solution.py:74
  16.0 0.1 reshape.570
  16.1 0.6 gather_fusion.2
  16.7 0.8 copy.49
  17.5 3.3 %all-to-all-start.2 = ((bf16[8,1,8,2,2]{2,4,3,1,0:T(2,128)(2,1)}), bf16[8,1,8,2,2]{2,4,3,1,0:T(2,128)(2,1)S(1)}, u32[]{:S(2)}, u32[]{:S(2)}) async-start(bf16[8,1,8,2,2]{2,4,3,1,0:T(2,128)(2,1)} %copy.49), calls=%async_computation.2 | async-start | bytes 16384 | tf_op jit(solution)/shard_map/all_to_all | solution.py:91
  20.9 0.0 copy-done
  20.9 2.8 %gather_fusion = bf16[64,128,256]{2,1,0:T(8,128)(2,1)} fusion(bf16[16,128,256]{2,1,0:T(8,128)(2,1)S(1)} %copy-done, s32[1024]{0:T(1024)S(1)} %pad_clamp_fusion.1), kind=kCustom, calls=%fused_computation | custom fusion | bytes 8388864 | tf_op jit(solution)/shard_map/gather | solution.py:82
  23.7 3.7 %all-to-all-done.2 = bf16[8,1,8,2,2]{2,4,3,1,0:T(2,128)(2,1)S(1)} async-done(((bf16[8,1,8,2,2]{2,4,3,1,0:T(2,128)(2,1)}), bf16[8,1,8,2,2]{2,4,3,1,0:T(2,128)(2,1)S(1)}, u32[]{:S(2)}, u32[]{:S(2)}) %all-to-all-start.2) | async-done | bytes 544 | tf_op jit(solution)/shard_map/all_to_all | solution.py:91
  27.3 4.7 %all-to-all-start.1 = ((bf16[8,1,8,128,256]{4,3,2,1,0:T(8,128)(2,1)}), bf16[8,1,8,128,256]{4,3,2,1,0:T(8,128)(2,1)}, u32[]{:S(2)}, u32[]{:S(2)}) async-start(bf16[8,1,8,128,256]{4,3,2,1,0:T(8,128)(2,1)} %bitcast.55), calls=%async_computation.1 | async-start | bytes 8388608 | tf_op jit(solution)/shard_map/all_to_all | solution.py:89
  32.0 0.0 copy-done.3
  32.0 2.8 %gather_fusion.4 = bf16[64,128,256]{2,1,0:T(8,128)(2,1)} fusion(bf16[16,128,256]{2,1,0:T(8,128)(2,1)S(1)} %copy-done.3, s32[1024]{0:T(1024)S(1)} %pad_clamp_fusion.1), kind=kCustom, calls=%fused_computation.4 | custom fusion | bytes 8388864 | tf_op jit(solution)/shard_map/gather | solution.py:83
  34.8 88.1 %all-to-all-done.1 = bf16[8,1,8,128,256]{4,3,2,1,0:T(8,128)(2,1)} async-done(((bf16[8,1,8,128,256]{4,3,2,1,0:T(8,128)(2,1)}), bf16[8,1,8,128,256]{4,3,2,1,0:T(8,128)(2,1)}, u32[]{:S(2)}, u32[]{:S(2)}) %all-to-all-start.1) | async-done | bytes 4194336 | tf_op jit(solution)/shard_map/all_to_all | solution.py:89
  122.9 0.0 copy-start.6
  122.9 0.0 copy-start.5
  122.9 4.7 %all-to-all-start.3 = ((bf16[8,1,8,128,256]{4,3,2,1,0:T(8,128)(2,1)}), bf16[8,1,8,128,256]{4,3,2,1,0:T(8,128)(2,1)}, u32[]{:S(2)}, u32[]{:S(2)}) async-start(bf16[8,1,8,128,256]{4,3,2,1,0:T(8,128)(2,1)} %bitcast.54), calls=%async_computation.3 | async-start | bytes 8388608 | tf_op jit(solution)/shard_map/all_to_all | solution.py:90
  127.6 0.0 copy-done.6
  127.6 0.1 copy.57
  127.8 0.3 multiply_cosine_fusion.1
  128.1 0.1 copy.45
  128.2 0.1 copy.46
  128.3 0.0 copy-done.5
  128.3 0.2 convert_bitcast_fusion
  128.5 0.4 copy.58
  128.9 0.7 multiply_subtract_fusion
  129.6 0.6 fusion.1
  130.2 0.0 copy-start.8
  130.2 1.3 convert_element_type.170.q_ref
  131.6 0.0 copy-done.8
  131.6 0.1 add_convert_fusion.2
  131.7 4.7 %multiply_cosine_fusion = (f32[32,128,64]{1,0,2:T(8,128)S(1)}, f32[32,128,64]{1,0,2:T(8,128)}) fusion(f32[64]{0:T(128)S(1)} %negate_power_fusion, f32[32,128]{1,0:T(8,128)S(1)} %add_convert_fusion.2), kind=kLoop, calls=%fused_computation.20 | loop fusion | flops 262144 | bytes 2113792 | tf_op jit(solution)/shard_map/cos | solution.py:17
  136.4 0.6 compare_select_fusion.bias_ref
  137.0 0.2 copy.50
  137.2 0.6 gather_fusion.3
  137.8 0.1 copy.51
  137.9 0.1 copy.55
  138.0 3.1 %mul.294 = f32[32,128,2,128]{3,2,1,0:T(2,128)} broadcast(f32[32,2]{1,0:T(8,128)S(1)} %copy.55), dimensions={0,2} | broadcast | bytes 4194560 | tf_op jit(solution)/shard_map/mul | solution.py:112
  141.1 6.4 %mul.295 = f32[1,4096,256]{2,1,0:T(8,128)} reshape(f32[32,128,2,128]{3,2,1,0:T(2,128)} %mul.294) | data formatting | bytes 8388608 | tf_op jit(solution)/shard_map/mul | solution.py:112
  147.5 2.9 %gather_fusion.1 = bf16[32,128,256]{2,1,0:T(8,128)(2,1)S(1)} fusion(bf16[64,128,256]{2,1,0:T(8,128)(2,1)} %bitcast.8, s32[1024]{0:T(1024)S(1)} %pad_clamp_fusion), kind=kCustom, calls=%fused_computation.1 | custom fusion | bytes 4194432 | tf_op jit(solution)/shard_map/gather | solution.py:95
  150.4 3.3 %copy.56 = f32[32,128,256]{1,0,2:T(8,128)} copy(bf16[32,128,256]{2,1,0:T(8,128)(2,1)S(1)} %gather_fusion.1) | data formatting | bytes 6291456 | tf_op jit(solution)/shard_map/convert_element_type | solution.py:97
  153.7 0.0 copy-start.4
  153.7 2.8 %broadcast_multiply_fusion = f32[1,32,128,2,128]{2,1,4,3,0:T(8,128)S(1)} fusion(f32[1,32,128,2,128]{2,1,4,3,0:T(8,128)} %bitcast.53, f32[32,2]{0,1:T(2,128)S(1)} %get-tuple-element.14), kind=kLoop, calls=%fused_computation.16 | loop fusion | flops 1048576 | bytes 8388864 | tf_op jit(solution)/shard_map/mul | solution.py:99
  156.6 0.0 copy-done.4
  156.6 0.8 subtract_convert_fusion
  157.4 1.6 pad_maximum_fusion.1
  158.9 2.8 %convert_element_type.176 = bf16[1,4096,256]{1,2,0:T(8,128)(2,1)S(1)} reshape(bf16[1,32,128,2,128]{2,1,4,3,0:T(8,128)(2,1)} %pad_maximum_fusion.1) | data formatting | bytes 4194304 | tf_op jit(solution)/shard_map/convert_element_type | solution.py:103
  161.8 58.4 %all-to-all-done.3 = bf16[8,1,8,128,256]{4,3,2,1,0:T(8,128)(2,1)} async-done(((bf16[8,1,8,128,256]{4,3,2,1,0:T(8,128)(2,1)}), bf16[8,1,8,128,256]{4,3,2,1,0:T(8,128)(2,1)}, u32[]{:S(2)}, u32[]{:S(2)}) %all-to-all-start.3) | async-done | bytes 4194336 | tf_op jit(solution)/shard_map/all_to_all | solution.py:90
  220.1 4.2 %gather_fusion.5 = bf16[32,128,256]{2,1,0:T(8,128)(2,1)} fusion(bf16[64,128,256]{2,1,0:T(8,128)(2,1)} %bitcast.20, s32[1024]{0:T(1024)S(1)} %pad_clamp_fusion), kind=kCustom, calls=%fused_computation.5 | custom fusion | bytes 4194432 | tf_op jit(solution)/shard_map/gather | solution.py:107
  224.4 0.0 copy-start.2
  224.4 1.5 maximum_bitcast_fusion.k_ref
  225.9 1.4 copy-done.2
  227.4 0.0 copy-start.7
  227.4 2.3 fusion
  229.7 0.0 copy-done.7
  229.7 0.0 copy-start.1
  229.7 1.5 pad_maximum_fusion.v_ref
  231.2 30.6 %shard_map.91 = bf16[1,256,2048]{2,1,0:T(8,128)(2,1)} custom-call(f32[1,1,4096]{2,1,0:T(1,128)} %compare_select_fusion.bias_ref, bf16[1,256,2048]{2,1,0:T(8,128)(2,1)} %convert_element_type.170.q_ref, bf16[1,256,4352]{2,1,0:T(8,128)(2,1)} %maximum_bitcast_fusion.k_ref, bf16[1,4352,256]{2,1,0:T(8,128)(2,1)} %pad_maximum_fusion.v_ref), custom_call_target="tpu_custom_call" | custom-call | tf_op jit(solution)/shard_map/pallas_call | solution.py:204
  261.8 0.0 copy-done.1
  (13 shorter events, 0.1 us)
Async XLA Ops:
  0.0 20.9 %copy-start = (bf16[16,128,256]{2,1,0:T(8,128)(2,1)S(1)}, bf16[16,128,256]{2,1,0:T(8,128)(2,1)}, u32[]{:S(2)}) copy-start(bf16[16,128,256]{2,1,0:T(8,128)(2,1)} %param.12) | copy-start | bytes 3145732
  2.3 13.7 %all-to-all-start = ((s32[8,1,8]{2,1,0:T(1,128)}), s32[8,1,8]{2,1,0:T(1,128)S(1)}, u32[]{:S(2)}, u32[]{:S(2)}) async-start(s32[8,1,8]{2,1,0:T(1,128)} %bitcast.6), calls=%async_computation | async-start | bytes 8192 | tf_op jit(solution)/shard_map/all_to_all | solution.py:74
  17.5 9.8 %all-to-all-start.2 = ((bf16[8,1,8,2,2]{2,4,3,1,0:T(2,128)(2,1)}), bf16[8,1,8,2,2]{2,4,3,1,0:T(2,128)(2,1)S(1)}, u32[]{:S(2)}, u32[]{:S(2)}) async-start(bf16[8,1,8,2,2]{2,4,3,1,0:T(2,128)(2,1)} %copy.49), calls=%async_computation.2 | async-start | bytes 16384 | tf_op jit(solution)/shard_map/all_to_all | solution.py:91
  27.3 4.7 %copy-start.3 = (bf16[16,128,256]{2,1,0:T(8,128)(2,1)S(1)}, bf16[16,128,256]{2,1,0:T(8,128)(2,1)}, u32[]{:S(2)}) copy-start(bf16[16,128,256]{2,1,0:T(8,128)(2,1)} %param.13) | copy-start | bytes 3145732
  27.3 95.6 %all-to-all-start.1 = ((bf16[8,1,8,128,256]{4,3,2,1,0:T(8,128)(2,1)}), bf16[8,1,8,128,256]{4,3,2,1,0:T(8,128)(2,1)}, u32[]{:S(2)}, u32[]{:S(2)}) async-start(bf16[8,1,8,128,256]{4,3,2,1,0:T(8,128)(2,1)} %bitcast.55), calls=%async_computation.1 | async-start | bytes 8388608 | tf_op jit(solution)/shard_map/all_to_all | solution.py:89
  122.9 4.7 %copy-start.6 = (bf16[1,256,256]{2,1,0:T(8,128)(2,1)S(1)}, bf16[1,256,256]{2,1,0:T(8,128)(2,1)}, u32[]{:S(2)}) copy-start(bf16[1,256,256]{2,1,0:T(8,128)(2,1)} %param.10) | copy-start | bytes 393220
  122.9 5.3 %copy-start.5 = (bf16[1,256,2048]{2,1,0:T(8,128)(2,1)S(1)}, bf16[1,256,2048]{2,1,0:T(8,128)(2,1)}, u32[]{:S(2)}) copy-start(bf16[1,256,2048]{2,1,0:T(8,128)(2,1)} %param.9) | copy-start | bytes 3145732
  122.9 97.2 %all-to-all-start.3 = ((bf16[8,1,8,128,256]{4,3,2,1,0:T(8,128)(2,1)}), bf16[8,1,8,128,256]{4,3,2,1,0:T(8,128)(2,1)}, u32[]{:S(2)}, u32[]{:S(2)}) async-start(bf16[8,1,8,128,256]{4,3,2,1,0:T(8,128)(2,1)} %bitcast.54), calls=%async_computation.3 | async-start | bytes 8388608 | tf_op jit(solution)/shard_map/all_to_all | solution.py:90
  130.2 1.4 copy-start.8
  153.7 2.9 %copy-start.4 = (f32[32,128,64]{1,0,2:T(8,128)S(1)}, f32[32,128,64]{1,0,2:T(8,128)}, u32[]{:S(2)}) copy-start(f32[32,128,64]{1,0,2:T(8,128)} %get-tuple-element.12) | copy-start | bytes 3145732
  224.4 3.0 %copy-start.2 = (f32[1,4096,256]{2,1,0:T(8,128)S(1)}, f32[1,4096,256]{2,1,0:T(8,128)}, u32[]{:S(2)}) copy-start(f32[1,4096,256]{2,1,0:T(8,128)} %mul.295) | copy-start | bytes 12582916
  227.4 2.3 copy-start.7
  229.7 32.1 %copy-start.1 = (bf16[16,128,256]{2,1,0:T(8,128)(2,1)S(1)}, bf16[16,128,256]{2,1,0:T(8,128)(2,1)}, u32[]{:S(2)}) copy-start(bf16[16,128,256]{2,1,0:T(8,128)(2,1)} %param.12) | copy-start | bytes 3145732

commit v3 on v2

--- a/solution.py
+++ b/solution.py
@@ -68,15 +68,12 @@
     request_group = q_heads // kv_heads
     tokens = queries.shape[1]
     capacity = 2 * slots // owners
+    cache_length = slots * span
     mine = slot_tables(stretch_ids, counts, stretch_pos, owners, capacity, per_owner)
     owner, rank, live = (mine[2], mine[3], mine[4])
-    wanted, starts = (
-        lax.all_to_all(
-            jnp.transpose(mine[0], (1, 0, 2)), "stretch", split_axis=0, concat_axis=0, tiled=True
-        ),
-        lax.all_to_all(
-            jnp.transpose(mine[1], (1, 0, 2)), "stretch", split_axis=0, concat_axis=0, tiled=True
-        ),
+    all_scales = lax.all_gather(scales, "stretch", axis=0, tiled=True)
+    wanted = lax.all_to_all(
+        jnp.transpose(mine[0], (1, 0, 2)), "stretch", split_axis=0, concat_axis=0, tiled=True
     )
     chosen = jnp.maximum(wanted, 0)
     raw_keys = stored_stretch_keys[chosen]
@@ -84,57 +81,44 @@
     flat = owners * rows * capacity
     index = (owner * rows + jnp.arange(rows, dtype=jnp.int32)[:, None]) * capacity + rank
     index = jnp.where(live, index, 0)
-    stretch_iota = jnp.arange(span, dtype=jnp.int32)
-    got_keys, got_vals, got_scales = (
-        lax.all_to_all(raw_keys, "stretch", split_axis=0, concat_axis=0, tiled=True),
-        lax.all_to_all(raw_values, "stretch", split_axis=0, concat_axis=0, tiled=True),
-        lax.all_to_all(scales[chosen], "stretch", split_axis=0, concat_axis=0, tiled=True),
-    )
-    scale_factor = got_scales.reshape(flat, 2, kv_heads)[index].astype(jnp.float32)
-    keys_wide = (
-        got_keys.reshape(flat, span, width)[index]
-        .reshape(rows, slots, span, kv_heads, head_dim)
-        .astype(jnp.float32)
-    )
-    keys_wide = keys_wide * scale_factor[:, :, 0][:, :, None, :, None]
-    stretch_placement = (stretch_pos[:, :, None] + stretch_iota)[..., None]
-    cached_keys = (
-        apply_rotary(keys_wide, stretch_placement)
-        .astype(jnp.bfloat16)
-        .reshape(rows, slots, span, width)
-    )
-    vals_wide = (
-        got_vals.reshape(flat, span, width)[index]
-        .reshape(rows, slots, span, kv_heads, head_dim)
-        .astype(jnp.float32)
-    )
-    cached_vals = (
-        (vals_wide * scale_factor[:, :, 1][:, :, None, :, None])
-        .astype(jnp.bfloat16)
-        .reshape(rows, slots, span, width)
-    )
-    cache_length = slots * span
-    token_iota = jnp.arange(tokens, dtype=jnp.int32)
-    token_positions = (cache_length + token_iota)[:, None]
-    new_keys = apply_rotary(
-        fresh_keys.reshape(rows, tokens, kv_heads, head_dim).astype(jnp.float32),
-        token_positions,
-    ).astype(jnp.bfloat16)
-    keys_all = jnp.concatenate(
-        [cached_keys.reshape(rows, cache_length, width), new_keys.reshape(rows, tokens, width)],
-        axis=1,
-    )
-    values_all = jnp.concatenate(
-        [cached_vals.reshape(rows, cache_length, width), fresh_values], axis=1
-    )
+    slot_scale = all_scales[stretch_ids].astype(jnp.float32)
+    placement = stretch_pos[:, :, None] + jnp.arange(span, dtype=jnp.int32)
+    token_positions = cache_length + jnp.arange(tokens, dtype=jnp.int32)
     query_rot = (
         apply_rotary(
-            queries.reshape(rows, tokens, q_heads, head_dim).astype(jnp.float32), token_positions
+            queries.reshape(rows, tokens, q_heads, head_dim).astype(jnp.float32),
+            token_positions[:, None],
         )
         * head_dim ** (-0.5)
     ).astype(jnp.bfloat16)
     query_rot = query_rot.reshape(rows, tokens, q_heads * head_dim)
-    return flash(query_rot, keys_all, values_all, counts * span, request_group, cache_length)
+    results = []
+    for head in range(kv_heads):
+        cols = slice(head * head_dim, (head + 1) * head_dim)
+        sent = jnp.concatenate([raw_keys[..., cols], raw_values[..., cols]], axis=-1)
+        got = lax.all_to_all(sent, "stretch", split_axis=0, concat_axis=0, tiled=True)
+        if results:
+            got, earlier = lax.optimization_barrier((got, results[-1]))
+            results[-1] = earlier
+        got = got.reshape(flat, span, 2 * head_dim)[index]
+        keys = got[..., :head_dim].astype(jnp.float32) * slot_scale[:, :, 0, head][:, :, None, None]
+        keys = apply_rotary(keys, placement).astype(jnp.bfloat16)
+        vals = got[..., head_dim:].astype(jnp.float32) * slot_scale[:, :, 1, head][:, :, None, None]
+        vals = vals.astype(jnp.bfloat16)
+        new_keys = apply_rotary(
+            fresh_keys[..., cols].astype(jnp.float32), token_positions
+        ).astype(jnp.bfloat16)
+        keys_all = jnp.concatenate(
+            [keys.reshape(rows, cache_length, head_dim), new_keys], axis=1
+        )
+        values_all = jnp.concatenate(
+            [vals.reshape(rows, cache_length, head_dim), fresh_values[..., cols]], axis=1
+        )
+        group_cols = slice(head * request_group * head_dim, (head + 1) * request_group * head_dim)
+        results.append(
+            flash(query_rot[..., group_cols], keys_all, values_all, counts * span, request_group, cache_length)
+        )
+    return jnp.concatenate(results, axis=-1)
 
 
 def flash_kernel(bias_ref, q_ref, k_ref, v_ref, o_ref, *, cache_length, chunk, heads):
@@ -214,6 +198,11 @@
             (None, tokens, head_dim * heads), lambda r, h, g: (r, 0, h * per + g)
         ),
         out_shape=jax.ShapeDtypeStruct((rows, tokens, q_width), jnp.bfloat16),
+        cost_estimate=pl.CostEstimate(
+            flops=6 * rows * tokens * q_width * length,
+            transcendentals=rows * tokens * (q_width // head_dim) * length,
+            bytes_accessed=2 * rows * (2 * tokens * q_width + 2 * length * width),
+        ),
     )(bias, query_rot, keys_t, values_all)
 
 

time: 263 us -> 316 us (1.20)
  blocking collectives: 0 us -> 126 us
  waiting for transfers between devices: 156 us -> 87.9 us
  starting transfers between devices: 20 us -> 9.17 us
  other arithmetic: 18.8 us -> 28.6 us
  local copies, waits for them, and re-layouts: 35.7 us -> 30.3 us
    all_gather x0 -> x1, blocking collectives: none -> 112 us  [shards(): all_scales = lax.all_gather(scales, 'stretch', axis=0, tiled=True)]
    all_to_all x4 -> x2, waiting for transfers between devices: 156 us -> 87.9 us  [shards(): lax.all_to_all(sent, 'stretch', split_axis=0, concat_axis=0, tiled=True)]
    all_to_all x0 -> x1, blocking collectives: none -> 13.5 us  [shards(): lax.all_to_all(jnp.transpose(mine[0], (1, 0, 2)), 'stretch', split_axis=0...]
    all_to_all x4 -> x2, starting transfers between devices: 20 us -> 9.17 us  [shards(): lax.all_to_all(sent, 'stretch', split_axis=0, concat_axis=0, tiled=True)]
    mul x4 -> x1, local copies, waits for them, and re-layouts: 9.64 us -> 0.01 us  [shards(): got[..., head_dim:].astype(jnp.float32)]
    unnamed x1 -> x3, other arithmetic: 0.23 us -> 8.73 us
    concatenate x3 -> x5, other arithmetic: 3.07 us -> 11.1 us  [the longest x2 6.83 us: shards(): jnp.concatenate([raw_keys[..., cols], raw_values[..., cols]], axis=-1)]
    gather x6, local copies, waits for them, and re-layouts: 9.21 us -> 15.5 us  [the longest x4 14.8 us: shards(): got = got.reshape(flat, span, 2 * head_dim)[index]]
  transfers between devices with their start and end apart: 4 -> 2, of which waited for: 4 -> 1; matrix products, arithmetic and copies ran while one was open for 15% -> 8% of each run, Pallas kernels for 0% -> 5%
where the time goes in v3:
time: 316 us
  blocking collectives  126 us (40%)
  waiting for transfers between devices  87.9 us (28%)
  Pallas kernels  33 us (10%)
  local copies, waits for them, and re-layouts  30.3 us (10%)
  other arithmetic  28.6 us (9%)
  starting transfers between devices  9.17 us (3%)
    all_gather x1, blocking collectives, shards(): all_scales = lax.all_gather(scales, 'stretch', axis=0, tiled=True)  112 us
    all_to_all x2, waiting for transfers between devices, shards(): lax.all_to_all(sent, 'stretch', split_axis=0, concat_axis=0, tiled=True)  87.9 us
    pallas_call x2, Pallas kernels, flash(): pl.pallas_call(kernel, grid=(rows, kv_heads, per), in_specs=[pl.BlockSpec...  33 us
    gather x4, local copies, waits for them, and re-layouts, shards(): got = got.reshape(flat, span, 2 * head_dim)[index]  14.8 us
    all_to_all x1, blocking collectives, shards(): lax.all_to_all(jnp.transpose(mine[0], (1, 0, 2)), 'stretch', split_axis=0...  13.5 us
    all_to_all x2, starting transfers between devices, shards(): lax.all_to_all(sent, 'stretch', split_axis=0, concat_axis=0, tiled=True)  9.17 us
    unnamed x3, other arithmetic  8.73 us
    concatenate x2, other arithmetic, shards(): jnp.concatenate([raw_keys[..., cols], raw_values[..., cols]], axis=-1)  6.83 us
  transfers between devices with their start and end apart: 2, of which 1 were waited for; matrix products, arithmetic and copies ran while one was open for 8% of the time, Pallas kernels for 5%

profile of v3, /device:TPU:0, one launch (start us, length us, event | category | flops | bytes accessed | tf_op | source)
XLA Modules:
  0.0 315.8 jit_solution(13354257061460260468)
XLA Ops:
  0.0 0.0 copy-start
  0.0 0.8 fusion.40
  1.4 0.1 convert_reduce_fusion
  1.5 0.1 select_reduce_fusion
  1.6 0.1 sub.29
  1.7 13.5 %all_to_all.15 = s32[8,1,8]{2,1,0:T(1,128)S(1)} all-to-all(s32[8,1,8]{2,1,0:T(1,128)S(1)} %bitcast.82), channel_id=1, replica_groups=mesh['grp'=2,'stretch'=8,'req'=2] {'stretch'}, dimensions={0} | all-to-all | bytes 512 | tf_op jit(solution)/shard_map/all_to_all | solution.py:75
  15.3 0.1 reshape.700
  15.4 0.0 copy-done
  15.4 0.0 copy-start.2
  15.4 2.8 gather_fusion
  18.1 0.0 copy-done.2
  18.1 2.8 gather_fusion.1
  20.9 4.8 %fusion.45 = (bf16[8,1,8,128,128]{4,3,2,1,0:T(8,128)(2,1)S(1)}, bf16[8,1,8,128,128]{4,3,2,1,0:T(8,128)(2,1)S(1)}, bf16[8,1,8,128,128]{4,3,2,1,0:T(8,128)(2,1)}, bf16[8,1,8,128,128]{4,3,2,1,0:T(8,128)(2,1)S(1)}) fusion(bf16[8,1,8,128,256]{4,3,2,1,0:T(8,128)(2,1)} %bitcast.72, bf16[8,1,8,128,256]{4,3,2,1,0:T(8,128)(2,1)} %bitcast.73), kind=kLoop, calls=%fused_computation.103 | loop fusion | bytes 16777216 | tf_op jit(solution)/shard_map/slice | solution.py:98
  25.7 2.7 pad_maximum_fusion.1
  28.4 4.6 %all-to-all-start.2 = ((bf16[8,1,8,128,256]{4,3,2,1,0:T(8,128)(2,1)}), bf16[8,1,8,128,256]{4,3,2,1,0:T(8,128)(2,1)}, u32[]{:S(2)}, u32[]{:S(2)}) async-start(bf16[8,1,8,128,256]{4,3,2,1,0:T(8,128)(2,1)} %pad_maximum_fusion.1), calls=%async_computation.2 | async-start | bytes 8388608 | tf_op jit(solution)/shard_map/all_to_all | solution.py:99
  33.0 4.2 %pad_maximum_fusion = bf16[8,1,8,128,256]{4,3,2,1,0:T(8,128)(2,1)} fusion(bf16[8,1,8,128,128]{4,3,2,1,0:T(8,128)(2,1)} %get-tuple-element.46, bf16[8,1,8,128,128]{4,3,2,1,0:T(8,128)(2,1)S(1)} %get-tuple-element.10), kind=kLoop, calls=%fused_computation.5 | loop fusion | flops 8388608 | bytes 8388608 | tf_op jit(solution)/shard_map/concatenate | solution.py:98
  37.2 87.9 %all-to-all-done.2 = bf16[8,1,8,128,256]{4,3,2,1,0:T(8,128)(2,1)} async-done(((bf16[8,1,8,128,256]{4,3,2,1,0:T(8,128)(2,1)}), bf16[8,1,8,128,256]{4,3,2,1,0:T(8,128)(2,1)}, u32[]{:S(2)}, u32[]{:S(2)}) %all-to-all-start.2) | async-done | bytes 4194336 | tf_op jit(solution)/shard_map/all_to_all | solution.py:99
  125.0 4.6 %all-to-all-start.1 = ((bf16[8,1,8,128,256]{4,3,2,1,0:T(8,128)(2,1)}), bf16[8,1,8,128,256]{4,3,2,1,0:T(8,128)(2,1)}, u32[]{:S(2)}, u32[]{:S(2)}) async-start(bf16[8,1,8,128,256]{4,3,2,1,0:T(8,128)(2,1)} %pad_maximum_fusion), calls=%async_computation.1 | async-start | bytes 8388608 | tf_op jit(solution)/shard_map/all_to_all | solution.py:99
  129.6 0.0 copy-done.9
  129.6 0.1 copy.55
  129.7 112.3 %all_gather.3 = bf16[128,2,2]{2,1,0:T(2,128)(2,1)S(1)} all-gather(bf16[16,2,2]{2,1,0:T(2,128)(2,1)S(1)} %copy.55), channel_id=1, replica_groups=mesh['grp'=2,'stretch'=8,'req'=2] {'stretch'}, dimensions={0}, use_global_device_ids=true | all-gather | bytes 1152 | tf_op jit(solution)/shard_map/all_gather | solution.py:74
  242.0 0.6 gather_fusion.3
  242.6 0.1 copy.56
  242.7 0.0 copy-done.7
  242.8 0.1 copy.66
  242.9 0.1 copy.67
  243.0 0.0 copy-done.5
  243.0 0.2 convert_bitcast_fusion
  243.3 0.4 copy.72
  243.7 0.5 multiply_cosine_fusion.1
  244.2 0.7 multiply_subtract_fusion
  245.0 0.6 fusion
  245.6 0.0 copy-start.10
  245.6 0.0 copy-start.8
  245.6 0.7 convert_element_type.166
  246.3 0.1 add_convert_fusion
  246.4 0.1 copy-done.8
  246.5 0.3 fusion.30
  246.9 1.1 fusion.47
  247.9 0.6 compare_select_fusion.bias_ref
  248.5 4.2 %gather_fusion.2 = bf16[32,128,256]{2,1,0:T(8,128)(2,1)} fusion(bf16[64,128,256]{2,1,0:T(8,128)(2,1)} %bitcast.9, s32[1024]{0:T(1024)S(1)} %pad_clamp_fusion.1), kind=kCustom, calls=%fused_computation.2 | custom fusion | bytes 4194432 | tf_op jit(solution)/shard_map/gather | solution.py:103
  252.7 3.2 %copy.54 = bf16[32,128,256]{1,2,0:T(8,128)(2,1)S(1)} copy(bf16[32,128,256]{2,1,0:T(8,128)(2,1)} %gather_fusion.2) | data formatting | bytes 4194304 | tf_op jit(solution)/shard_map/gather | solution.py:103
  256.0 1.3 multiply_convert_fusion.1
  257.3 4.2 %fusion.20 = (bf16[1,32,8,8,128]{4,3,2,1,0:T(8,128)(2,1)S(1)}, bf16[1,32,8,8,128]{4,3,2,1,0:T(8,128)(2,1)S(1)}) fusion(f32[1,32,128,128]{2,3,1,0:T(8,128)S(1)} %get-tuple-element.22, f32[64]{0:T(128)S(1)} %negate_power_fusion, f32[32,128]{1,0:T(8,128)S(1)} %add_convert_fusion), kind=kLoop, calls=%fused_computation.46 | loop fusion | flops 2359296 | bytes 3162368
  261.5 0.1 copy.79
  261.6 0.1 copy.80
  261.7 0.0 copy-done.4
  261.7 0.7 copy.60
  262.4 1.1 pad_maximum_fusion.2.v_ref
  263.5 1.1 maximum_bitcast_fusion.k_ref
  264.7 16.4 %shard_map.91 = bf16[1,256,1024]{2,1,0:T(8,128)(2,1)} custom-call(f32[1,1,4096]{2,1,0:T(1,128)} %compare_select_fusion.bias_ref, bf16[1,256,1024]{2,1,0:T(8,128)(2,1)} %get-tuple-element.23.q_ref, bf16[1,128,4352]{2,1,0:T(8,128)(2,1)} %maximum_bitcast_fusion.k_ref, bf16[1,4352,128]{2,1,0:T(8,128)(2,1)} %pad_maximum_fusion.2.v_ref), custom_call_target="tpu_custom_call" | custom-call | flops 6845104128 | bytes 3276800 | tf_op jit(solution)/shard_map/pallas_call | solution.py:188
  281.1 0.0 all-to-all-done.1
  281.1 4.2 %gather_fusion.4 = bf16[32,128,256]{2,1,0:T(8,128)(2,1)} fusion(bf16[64,128,256]{2,1,0:T(8,128)(2,1)} %bitcast.20, s32[1024]{0:T(1024)S(1)} %pad_clamp_fusion.1), kind=kCustom, calls=%fused_computation.4 | custom fusion | bytes 4194432 | tf_op jit(solution)/shard_map/gather | solution.py:103
  285.3 3.2 %copy.61 = bf16[32,128,256]{1,2,0:T(8,128)(2,1)S(1)} copy(bf16[32,128,256]{2,1,0:T(8,128)(2,1)} %gather_fusion.4) | data formatting | bytes 4194304 | tf_op jit(solution)/shard_map/gather | solution.py:103
  288.5 1.3 multiply_convert_fusion
  289.8 4.2 %fusion.18 = (bf16[1,32,8,8,128]{4,3,2,1,0:T(8,128)(2,1)S(1)}, bf16[1,32,8,8,128]{4,3,2,1,0:T(8,128)(2,1)S(1)}) fusion(f32[1,32,128,128]{2,3,1,0:T(8,128)S(1)} %get-tuple-element.20, f32[64]{0:T(128)S(1)} %negate_power_fusion, f32[32,128]{1,0:T(8,128)S(1)} %add_convert_fusion), kind=kLoop, calls=%fused_computation.44 | loop fusion | flops 2359296 | bytes 3162368
  294.1 0.1 copy.77
  294.2 0.1 copy.78
  294.3 0.0 copy-done.3
  294.3 0.7 copy.65
  295.0 1.1 pad_maximum_fusion.3.v_ref
  296.0 1.1 maximum_bitcast_fusion.1.k_ref
  297.1 16.6 %shard_map.92 = bf16[1,256,1024]{2,1,0:T(8,128)(2,1)} custom-call(f32[1,1,4096]{2,1,0:T(1,128)} %compare_select_fusion.bias_ref, bf16[1,256,1024]{2,1,0:T(8,128)(2,1)} %get-tuple-element.24.q_ref, bf16[1,128,4352]{2,1,0:T(8,128)(2,1)} %maximum_bitcast_fusion.1.k_ref, bf16[1,4352,128]{2,1,0:T(8,128)(2,1)} %pad_maximum_fusion.3.v_ref), custom_call_target="tpu_custom_call" | custom-call | flops 6845104128 | bytes 3276800 | tf_op jit(solution)/shard_map/pallas_call | solution.py:188
  313.7 2.1 pad_maximum_fusion.4
  (25 shorter events, 0.1 us)
Async XLA Ops:
  0.0 15.4 %copy-start = (bf16[16,128,256]{2,1,0:T(8,128)(2,1)S(1)}, bf16[16,128,256]{2,1,0:T(8,128)(2,1)}, u32[]{:S(2)}) copy-start(bf16[16,128,256]{2,1,0:T(8,128)(2,1)} %param.12) | copy-start | bytes 3145732
  15.4 2.8 copy-start.2
  28.4 96.6 %all-to-all-start.2 = ((bf16[8,1,8,128,256]{4,3,2,1,0:T(8,128)(2,1)}), bf16[8,1,8,128,256]{4,3,2,1,0:T(8,128)(2,1)}, u32[]{:S(2)}, u32[]{:S(2)}) async-start(bf16[8,1,8,128,256]{4,3,2,1,0:T(8,128)(2,1)} %pad_maximum_fusion.1), calls=%async_computation.2 | async-start | bytes 8388608 | tf_op jit(solution)/shard_map/all_to_all | solution.py:99
  37.2 92.4 %copy-start.9 = (bf16[16,2,2]{0,2,1:T(2,128)(2,1)S(1)}, bf16[16,2,2]{0,2,1:T(2,128)(2,1)}, u32[]{:S(2)}) copy-start(bf16[16,2,2]{0,2,1:T(2,128)(2,1)} %param.14) | copy-start | bytes 388
  37.2 205.6 %copy-start.7 = (bf16[1,256,256]{2,1,0:T(8,128)(2,1)S(1)}, bf16[1,256,256]{2,1,0:T(8,128)(2,1)}, u32[]{:S(2)}) copy-start(bf16[1,256,256]{2,1,0:T(8,128)(2,1)} %param.10) | copy-start | bytes 393220
  37.2 205.9 %copy-start.5 = (bf16[1,256,2048]{2,1,0:T(8,128)(2,1)S(1)}, bf16[1,256,2048]{2,1,0:T(8,128)(2,1)}, u32[]{:S(2)}) copy-start(bf16[1,256,2048]{2,1,0:T(8,128)(2,1)} %param.9) | copy-start | bytes 3145732
  125.0 156.1 %all-to-all-start.1 = ((bf16[8,1,8,128,256]{4,3,2,1,0:T(8,128)(2,1)}), bf16[8,1,8,128,256]{4,3,2,1,0:T(8,128)(2,1)}, u32[]{:S(2)}, u32[]{:S(2)}) async-start(bf16[8,1,8,128,256]{4,3,2,1,0:T(8,128)(2,1)} %pad_maximum_fusion), calls=%async_computation.1 | async-start | bytes 8388608 | tf_op jit(solution)/shard_map/all_to_all | solution.py:99
  245.6 0.7 copy-start.10
  245.6 0.9 copy-start.8
  257.3 4.5 %copy-start.4 = (bf16[1,32,128,128]{2,3,1,0:T(8,128)(2,1)S(1)}, bf16[1,32,128,128]{2,3,1,0:T(8,128)(2,1)}, u32[]{:S(2)}) copy-start(bf16[1,32,128,128]{2,3,1,0:T(8,128)(2,1)} %get-tuple-element.21) | copy-start | bytes 3145732
  289.8 4.5 %copy-start.3 = (bf16[1,32,128,128]{2,3,1,0:T(8,128)(2,1)S(1)}, bf16[1,32,128,128]{2,3,1,0:T(8,128)(2,1)}, u32[]{:S(2)}) copy-start(bf16[1,32,128,128]{2,3,1,0:T(8,128)(2,1)} %get-tuple-element.19) | copy-start | bytes 3145732
  297.1 16.6 %copy-start.6 = (bf16[1,256,1024]{2,1,0:T(8,128)(2,1)S(1)}, bf16[1,256,1024]{2,1,0:T(8,128)(2,1)}, u32[]{:S(2)}) copy-start(bf16[1,256,1024]{2,1,0:T(8,128)(2,1)} %shard_map.91) | copy-start | bytes 1572868
  297.1 18.7 %copy-start.1 = (bf16[16,128,256]{2,1,0:T(8,128)(2,1)S(1)}, bf16[16,128,256]{2,1,0:T(8,128)(2,1)}, u32[]{:S(2)}) copy-start(bf16[16,128,256]{2,1,0:T(8,128)(2,1)} %param.12) | copy-start | bytes 3145732

commit v4 on v3

--- a/solution.py
+++ b/solution.py
@@ -72,9 +72,8 @@
     mine = slot_tables(stretch_ids, counts, stretch_pos, owners, capacity, per_owner)
     owner, rank, live = (mine[2], mine[3], mine[4])
     all_scales = lax.all_gather(scales, "stretch", axis=0, tiled=True)
-    wanted = lax.all_to_all(
-        jnp.transpose(mine[0], (1, 0, 2)), "stretch", split_axis=0, concat_axis=0, tiled=True
-    )
+    all_scales, table = lax.optimization_barrier((all_scales, jnp.transpose(mine[0], (1, 0, 2))))
+    wanted = lax.all_to_all(table, "stretch", split_axis=0, concat_axis=0, tiled=True)
     chosen = jnp.maximum(wanted, 0)
     raw_keys = stored_stretch_keys[chosen]
     raw_values = stored_stretch_values[chosen]

time: 316 us -> 282 us (0.89)
  blocking collectives: 126 us -> 44 us
  waiting for transfers between devices: 87.9 us -> 135 us
    all_gather x1, blocking collectives: 112 us -> 32.3 us  [shards(): all_scales = lax.all_gather(scales, 'stretch', axis=0, tiled=True)]
    all_to_all x2, waiting for transfers between devices: 87.9 us -> 135 us  [shards(): lax.all_to_all(sent, 'stretch', split_axis=0, concat_axis=0, tiled=True)]
  transfers between devices with their start and end apart: 2 -> 2, of which waited for: 1 -> 2; matrix products, arithmetic and copies ran while one was open for 8% -> 9% of each run, Pallas kernels for 5% -> 6%
where the time goes in v4:
time: 282 us
  waiting for transfers between devices  135 us (48%)
  blocking collectives  44 us (16%)
  Pallas kernels  33 us (12%)
  local copies, waits for them, and re-layouts  31 us (11%)
  other arithmetic  28.6 us (10%)
  starting transfers between devices  9.14 us (3%)
    all_to_all x2, waiting for transfers between devices, shards(): lax.all_to_all(sent, 'stretch', split_axis=0, concat_axis=0, tiled=True)  135 us
    pallas_call x2, Pallas kernels, flash(): pl.pallas_call(kernel, grid=(rows, kv_heads, per), in_specs=[pl.BlockSpec...  33 us
    all_gather x1, blocking collectives, shards(): all_scales = lax.all_gather(scales, 'stretch', axis=0, tiled=True)  32.3 us
    gather x4, local copies, waits for them, and re-layouts, shards(): got = got.reshape(flat, span, 2 * head_dim)[index]  14.9 us
    all_to_all x1, blocking collectives, shards(): lax.all_to_all(table, 'stretch', split_axis=0, concat_axis=0, tiled=True)  11.7 us
    all_to_all x2, starting transfers between devices, shards(): lax.all_to_all(sent, 'stretch', split_axis=0, concat_axis=0, tiled=True)  9.14 us
    unnamed x3, other arithmetic  8.72 us
    concatenate x2, other arithmetic, shards(): jnp.concatenate([raw_keys[..., cols], raw_values[..., cols]], axis=-1)  6.84 us
  transfers between devices with their start and end apart: 2, of which 2 were waited for; matrix products, arithmetic and copies ran while one was open for 9% of the time, Pallas kernels for 6%

profile of v4, /device:TPU:0, one launch (start us, length us, event | category | flops | bytes accessed | tf_op | source)
XLA Modules:
  0.0 281.8 jit_solution(14041348134612095221)
XLA Ops:
  0.0 0.0 copy-start
  0.0 0.8 fusion.40
  1.4 0.1 convert_reduce_fusion
  1.5 0.1 select_reduce_fusion
  1.6 0.1 sub.29
  1.7 0.8 copy.53
  2.5 32.3 %all_gather.3 = bf16[128,2,2]{2,1,0:T(2,128)(2,1)S(1)} all-gather(bf16[16,2,2]{2,1,0:T(2,128)(2,1)S(1)} %copy.53), channel_id=1, replica_groups=mesh['grp'=2,'stretch'=8,'req'=2] {'stretch'}, dimensions={0}, use_global_device_ids=true | all-gather | bytes 1152 | tf_op jit(solution)/shard_map/all_gather | solution.py:74
  34.8 11.7 %all_to_all.15 = s32[8,1,8]{2,1,0:T(1,128)S(1)} all-to-all(s32[8,1,8]{2,1,0:T(1,128)S(1)} %bitcast.82), channel_id=1, replica_groups=mesh['grp'=2,'stretch'=8,'req'=2] {'stretch'}, dimensions={0} | all-to-all | bytes 512 | tf_op jit(solution)/shard_map/all_to_all | solution.py:76
  46.5 0.1 reshape.700
  46.6 0.0 copy-done
  46.6 0.0 copy-start.2
  46.6 2.8 gather_fusion
  49.4 0.0 copy-done.2
  49.4 2.8 gather_fusion.1
  52.2 4.7 %fusion.45 = (bf16[8,1,8,128,128]{4,3,2,1,0:T(8,128)(2,1)S(1)}, bf16[8,1,8,128,128]{4,3,2,1,0:T(8,128)(2,1)S(1)}, bf16[8,1,8,128,128]{4,3,2,1,0:T(8,128)(2,1)}, bf16[8,1,8,128,128]{4,3,2,1,0:T(8,128)(2,1)S(1)}) fusion(bf16[8,1,8,128,256]{4,3,2,1,0:T(8,128)(2,1)} %bitcast.72, bf16[8,1,8,128,256]{4,3,2,1,0:T(8,128)(2,1)} %bitcast.73), kind=kLoop, calls=%fused_computation.103 | loop fusion | bytes 16777216 | tf_op jit(solution)/shard_map/slice | solution.py:97
  57.0 2.7 pad_maximum_fusion.1
  59.6 4.6 %all-to-all-start.2 = ((bf16[8,1,8,128,256]{4,3,2,1,0:T(8,128)(2,1)}), bf16[8,1,8,128,256]{4,3,2,1,0:T(8,128)(2,1)}, u32[]{:S(2)}, u32[]{:S(2)}) async-start(bf16[8,1,8,128,256]{4,3,2,1,0:T(8,128)(2,1)} %pad_maximum_fusion.1), calls=%async_computation.2 | async-start | bytes 8388608 | tf_op jit(solution)/shard_map/all_to_all | solution.py:98
  64.2 4.2 %pad_maximum_fusion = bf16[8,1,8,128,256]{4,3,2,1,0:T(8,128)(2,1)} fusion(bf16[8,1,8,128,128]{4,3,2,1,0:T(8,128)(2,1)} %get-tuple-element.50, bf16[8,1,8,128,128]{4,3,2,1,0:T(8,128)(2,1)S(1)} %get-tuple-element.14), kind=kLoop, calls=%fused_computation.5 | loop fusion | flops 8388608 | bytes 8388608 | tf_op jit(solution)/shard_map/concatenate | solution.py:97
  68.4 81.8 %all-to-all-done.2 = bf16[8,1,8,128,256]{4,3,2,1,0:T(8,128)(2,1)} async-done(((bf16[8,1,8,128,256]{4,3,2,1,0:T(8,128)(2,1)}), bf16[8,1,8,128,256]{4,3,2,1,0:T(8,128)(2,1)}, u32[]{:S(2)}, u32[]{:S(2)}) %all-to-all-start.2) | async-done | bytes 4194336 | tf_op jit(solution)/shard_map/all_to_all | solution.py:98
  150.2 4.5 %all-to-all-start.1 = ((bf16[8,1,8,128,256]{4,3,2,1,0:T(8,128)(2,1)}), bf16[8,1,8,128,256]{4,3,2,1,0:T(8,128)(2,1)}, u32[]{:S(2)}, u32[]{:S(2)}) async-start(bf16[8,1,8,128,256]{4,3,2,1,0:T(8,128)(2,1)} %pad_maximum_fusion), calls=%async_computation.1 | async-start | bytes 8388608 | tf_op jit(solution)/shard_map/all_to_all | solution.py:98
  154.7 0.6 gather_fusion.3
  155.3 0.1 copy.56
  155.4 0.0 copy-done.7
  155.5 0.1 copy.66
  155.6 0.1 copy.67
  155.7 0.0 copy-done.5
  155.7 0.2 convert_bitcast_fusion
  156.0 0.4 copy.72
  156.4 0.5 multiply_cosine_fusion.1
  156.9 0.7 multiply_subtract_fusion
  157.6 0.6 fusion
  158.3 0.0 copy-start.9
  158.3 0.0 copy-start.8
  158.3 0.5 convert_element_type.166
  158.8 0.1 copy-done.9
  158.9 0.1 add_convert_fusion
  159.0 0.2 copy-done.8
  159.2 0.3 fusion.30
  159.5 1.1 fusion.47
  160.6 0.6 compare_select_fusion.bias_ref
  161.2 4.2 %gather_fusion.2 = bf16[32,128,256]{2,1,0:T(8,128)(2,1)} fusion(bf16[64,128,256]{2,1,0:T(8,128)(2,1)} %bitcast.9, s32[1024]{0:T(1024)S(1)} %pad_clamp_fusion.1), kind=kCustom, calls=%fused_computation.2 | custom fusion | bytes 4194432 | tf_op jit(solution)/shard_map/gather | solution.py:102
  165.5 3.2 %copy.55 = bf16[32,128,256]{1,2,0:T(8,128)(2,1)S(1)} copy(bf16[32,128,256]{2,1,0:T(8,128)(2,1)} %gather_fusion.2) | data formatting | bytes 4194304 | tf_op jit(solution)/shard_map/gather | solution.py:102
  168.7 1.3 multiply_convert_fusion.1
  170.0 4.2 %fusion.20 = (bf16[1,32,8,8,128]{4,3,2,1,0:T(8,128)(2,1)S(1)}, bf16[1,32,8,8,128]{4,3,2,1,0:T(8,128)(2,1)S(1)}) fusion(f32[1,32,128,128]{2,3,1,0:T(8,128)S(1)} %get-tuple-element.26, f32[64]{0:T(128)S(1)} %negate_power_fusion, f32[32,128]{1,0:T(8,128)S(1)} %add_convert_fusion), kind=kLoop, calls=%fused_computation.46 | loop fusion | flops 2359296 | bytes 3162368
  174.2 0.1 copy.79
  174.3 0.1 copy.80
  174.4 0.0 copy-done.4
  174.4 0.7 copy.60
  175.1 1.1 pad_maximum_fusion.2.v_ref
  176.2 1.1 maximum_bitcast_fusion.k_ref
  177.4 16.4 %shard_map.91 = bf16[1,256,1024]{2,1,0:T(8,128)(2,1)} custom-call(f32[1,1,4096]{2,1,0:T(1,128)} %compare_select_fusion.bias_ref, bf16[1,256,1024]{2,1,0:T(8,128)(2,1)} %get-tuple-element.27.q_ref, bf16[1,128,4352]{2,1,0:T(8,128)(2,1)} %maximum_bitcast_fusion.k_ref, bf16[1,4352,128]{2,1,0:T(8,128)(2,1)} %pad_maximum_fusion.2.v_ref), custom_call_target="tpu_custom_call" | custom-call | flops 6845104128 | bytes 3276800 | tf_op jit(solution)/shard_map/pallas_call | solution.py:187
  193.8 53.3 %all-to-all-done.1 = bf16[8,1,8,128,256]{4,3,2,1,0:T(8,128)(2,1)} async-done(((bf16[8,1,8,128,256]{4,3,2,1,0:T(8,128)(2,1)}), bf16[8,1,8,128,256]{4,3,2,1,0:T(8,128)(2,1)}, u32[]{:S(2)}, u32[]{:S(2)}) %all-to-all-start.1) | async-done | bytes 4194336 | tf_op jit(solution)/shard_map/all_to_all | solution.py:98
  247.1 4.2 %gather_fusion.4 = bf16[32,128,256]{2,1,0:T(8,128)(2,1)} fusion(bf16[64,128,256]{2,1,0:T(8,128)(2,1)} %bitcast.20, s32[1024]{0:T(1024)S(1)} %pad_clamp_fusion.1), kind=kCustom, calls=%fused_computation.4 | custom fusion | bytes 4194432 | tf_op jit(solution)/shard_map/gather | solution.py:102
  251.3 3.2 %copy.61 = bf16[32,128,256]{1,2,0:T(8,128)(2,1)S(1)} copy(bf16[32,128,256]{2,1,0:T(8,128)(2,1)} %gather_fusion.4) | data formatting | bytes 4194304 | tf_op jit(solution)/shard_map/gather | solution.py:102
  254.5 1.3 multiply_convert_fusion
  255.8 4.2 %fusion.18 = (bf16[1,32,8,8,128]{4,3,2,1,0:T(8,128)(2,1)S(1)}, bf16[1,32,8,8,128]{4,3,2,1,0:T(8,128)(2,1)S(1)}) fusion(f32[1,32,128,128]{2,3,1,0:T(8,128)S(1)} %get-tuple-element.24, f32[64]{0:T(128)S(1)} %negate_power_fusion, f32[32,128]{1,0:T(8,128)S(1)} %add_convert_fusion), kind=kLoop, calls=%fused_computation.44 | loop fusion | flops 2359296 | bytes 3162368
  260.1 0.1 copy.77
  260.2 0.1 copy.78
  260.3 0.0 copy-done.3
  260.3 0.7 copy.65
  260.9 1.1 pad_maximum_fusion.3.v_ref
  262.0 1.1 maximum_bitcast_fusion.1.k_ref
  263.1 16.6 %shard_map.92 = bf16[1,256,1024]{2,1,0:T(8,128)(2,1)} custom-call(f32[1,1,4096]{2,1,0:T(1,128)} %compare_select_fusion.bias_ref, bf16[1,256,1024]{2,1,0:T(8,128)(2,1)} %get-tuple-element.28.q_ref, bf16[1,128,4352]{2,1,0:T(8,128)(2,1)} %maximum_bitcast_fusion.1.k_ref, bf16[1,4352,128]{2,1,0:T(8,128)(2,1)} %pad_maximum_fusion.3.v_ref), custom_call_target="tpu_custom_call" | custom-call | flops 6845104128 | bytes 3276800 | tf_op jit(solution)/shard_map/pallas_call | solution.py:187
  279.7 2.1 pad_maximum_fusion.4
  (23 shorter events, 0.1 us)
Async XLA Ops:
  0.0 46.6 %copy-start = (bf16[16,128,256]{2,1,0:T(8,128)(2,1)S(1)}, bf16[16,128,256]{2,1,0:T(8,128)(2,1)}, u32[]{:S(2)}) copy-start(bf16[16,128,256]{2,1,0:T(8,128)(2,1)} %param.12) | copy-start | bytes 3145732
  46.6 2.8 copy-start.2
  59.6 90.5 %all-to-all-start.2 = ((bf16[8,1,8,128,256]{4,3,2,1,0:T(8,128)(2,1)}), bf16[8,1,8,128,256]{4,3,2,1,0:T(8,128)(2,1)}, u32[]{:S(2)}, u32[]{:S(2)}) async-start(bf16[8,1,8,128,256]{4,3,2,1,0:T(8,128)(2,1)} %pad_maximum_fusion.1), calls=%async_computation.2 | async-start | bytes 8388608 | tf_op jit(solution)/shard_map/all_to_all | solution.py:98
  68.4 87.0 %copy-start.7 = (bf16[1,256,256]{2,1,0:T(8,128)(2,1)S(1)}, bf16[1,256,256]{2,1,0:T(8,128)(2,1)}, u32[]{:S(2)}) copy-start(bf16[1,256,256]{2,1,0:T(8,128)(2,1)} %param.10) | copy-start | bytes 393220
  68.4 87.3 %copy-start.5 = (bf16[1,256,2048]{2,1,0:T(8,128)(2,1)S(1)}, bf16[1,256,2048]{2,1,0:T(8,128)(2,1)}, u32[]{:S(2)}) copy-start(bf16[1,256,2048]{2,1,0:T(8,128)(2,1)} %param.9) | copy-start | bytes 3145732
  150.2 96.9 %all-to-all-start.1 = ((bf16[8,1,8,128,256]{4,3,2,1,0:T(8,128)(2,1)}), bf16[8,1,8,128,256]{4,3,2,1,0:T(8,128)(2,1)}, u32[]{:S(2)}, u32[]{:S(2)}) async-start(bf16[8,1,8,128,256]{4,3,2,1,0:T(8,128)(2,1)} %pad_maximum_fusion), calls=%async_computation.1 | async-start | bytes 8388608 | tf_op jit(solution)/shard_map/all_to_all | solution.py:98
  158.3 0.7 copy-start.9
  158.3 0.9 copy-start.8
  170.0 4.5 %copy-start.4 = (bf16[1,32,128,128]{2,3,1,0:T(8,128)(2,1)S(1)}, bf16[1,32,128,128]{2,3,1,0:T(8,128)(2,1)}, u32[]{:S(2)}) copy-start(bf16[1,32,128,128]{2,3,1,0:T(8,128)(2,1)} %get-tuple-element.25) | copy-start | bytes 3145732
  255.8 4.5 %copy-start.3 = (bf16[1,32,128,128]{2,3,1,0:T(8,128)(2,1)S(1)}, bf16[1,32,128,128]{2,3,1,0:T(8,128)(2,1)}, u32[]{:S(2)}) copy-start(bf16[1,32,128,128]{2,3,1,0:T(8,128)(2,1)} %get-tuple-element.23) | copy-start | bytes 3145732
  263.1 16.6 %copy-start.6 = (bf16[1,256,1024]{2,1,0:T(8,128)(2,1)S(1)}, bf16[1,256,1024]{2,1,0:T(8,128)(2,1)}, u32[]{:S(2)}) copy-start(bf16[1,256,1024]{2,1,0:T(8,128)(2,1)} %shard_map.91) | copy-start | bytes 1572868
  263.1 18.7 %copy-start.1 = (bf16[16,128,256]{2,1,0:T(8,128)(2,1)S(1)}, bf16[16,128,256]{2,1,0:T(8,128)(2,1)}, u32[]{:S(2)}) copy-start(bf16[16,128,256]{2,1,0:T(8,128)(2,1)} %param.12) | copy-start | bytes 3145732

commit v5 on v3

--- a/solution.py
+++ b/solution.py
@@ -71,17 +71,26 @@
     cache_length = slots * span
     mine = slot_tables(stretch_ids, counts, stretch_pos, owners, capacity, per_owner)
     owner, rank, live = (mine[2], mine[3], mine[4])
-    all_scales = lax.all_gather(scales, "stretch", axis=0, tiled=True)
-    wanted = lax.all_to_all(
-        jnp.transpose(mine[0], (1, 0, 2)), "stretch", split_axis=0, concat_axis=0, tiled=True
-    )
+    scale_code = (scales.astype(jnp.float32) * 65536.0).astype(jnp.int32).reshape(1, 1, -1)
+    requests = jnp.concatenate(
+        [
+            jnp.transpose(mine[0], (1, 0, 2)),
+            jnp.broadcast_to(scale_code, (owners, rows, scale_code.shape[2])),
+        ],
+        axis=2,
+    )
+    answers = lax.all_to_all(requests, "stretch", split_axis=0, concat_axis=0, tiled=True)
+    wanted = answers[:, :, :capacity]
     chosen = jnp.maximum(wanted, 0)
+    all_scales = (answers[:, 0, capacity:].astype(jnp.float32) * (1.0 / 65536.0)).reshape(
+        owners * per_owner, 2, scales.shape[2]
+    )
     raw_keys = stored_stretch_keys[chosen]
     raw_values = stored_stretch_values[chosen]
     flat = owners * rows * capacity
     index = (owner * rows + jnp.arange(rows, dtype=jnp.int32)[:, None]) * capacity + rank
     index = jnp.where(live, index, 0)
-    slot_scale = all_scales[stretch_ids].astype(jnp.float32)
+    slot_scale = all_scales[stretch_ids]
     placement = stretch_pos[:, :, None] + jnp.arange(span, dtype=jnp.int32)
     token_positions = cache_length + jnp.arange(tokens, dtype=jnp.int32)
     query_rot = (

time: 316 us -> 258 us (0.82)
  blocking collectives: 126 us -> 13.5 us
  waiting for transfers between devices: 87.9 us -> 141 us
    all_gather x1 -> x0, blocking collectives: 112 us -> none  [shards(): all_scales = lax.all_gather(scales, 'stretch', axis=0, tiled=True)]
    all_to_all x2, waiting for transfers between devices: 87.9 us -> 141 us  [shards(): lax.all_to_all(sent, 'stretch', split_axis=0, concat_axis=0, tiled=True)]
  transfers between devices with their start and end apart: 2 -> 2, of which waited for: 1 -> 2; matrix products, arithmetic and copies ran while one was open for 8% -> 10% of each run, Pallas kernels for 5% -> 6%
where the time goes in v5:
time: 258 us
  waiting for transfers between devices  141 us (55%)
  Pallas kernels  33 us (13%)
  local copies, waits for them, and re-layouts  30.8 us (12%)
  other arithmetic  29.4 us (11%)
  blocking collectives  13.5 us (5%)
  starting transfers between devices  9.14 us (4%)
    all_to_all x2, waiting for transfers between devices, shards(): lax.all_to_all(sent, 'stretch', split_axis=0, concat_axis=0, tiled=True)  141 us
    pallas_call x2, Pallas kernels, flash(): pl.pallas_call(kernel, grid=(rows, kv_heads, per), in_specs=[pl.BlockSpec...  33 us
    gather x4, local copies, waits for them, and re-layouts, shards(): got = got.reshape(flat, span, 2 * head_dim)[index]  14.8 us
    all_to_all x1, blocking collectives, shards(): lax.all_to_all(requests, 'stretch', split_axis=0, concat_axis=0, tiled=True)  13.5 us
    all_to_all x2, starting transfers between devices, shards(): lax.all_to_all(sent, 'stretch', split_axis=0, concat_axis=0, tiled=True)  9.14 us
    unnamed x3, other arithmetic  8.72 us
    concatenate x2, other arithmetic, shards(): jnp.concatenate([raw_keys[..., cols], raw_values[..., cols]], axis=-1)  6.85 us
  transfers between devices with their start and end apart: 2, of which 2 were waited for; matrix products, arithmetic and copies ran while one was open for 10% of the time, Pallas kernels for 6%

profile of v5, /device:TPU:0, one launch (start us, length us, event | category | flops | bytes accessed | tf_op | source)
XLA Modules:
  0.0 257.8 jit_solution(16669864933745967737)
XLA Ops:
  0.0 0.0 copy-start
  0.0 0.8 fusion.43
  1.4 0.1 convert_reduce_fusion
  1.5 0.1 select_reduce_fusion
  1.6 0.1 sub.29
  1.7 0.7 multiply_convert_fusion.2
  2.4 0.1 copy.54
  2.5 0.1 reshape.760
  2.6 0.1 pad.21.clone
  2.7 13.5 %all_to_all.15 = s32[8,1,72]{2,1,0:T(1,128)S(1)} all-to-all(s32[8,1,72]{2,1,0:T(1,128)S(1)} %pad_add_fusion), channel_id=1, replica_groups=mesh['grp'=2,'stretch'=8,'req'=2] {'stretch'}, dimensions={0} | all-to-all | bytes 4608 | tf_op jit(solution)/shard_map/all_to_all | solution.py:82
  16.3 0.1 reshape.701
  16.3 0.0 copy-done
  16.4 0.0 copy-start.2
  16.4 2.8 %gather_fusion = bf16[64,128,256]{2,1,0:T(8,128)(2,1)} fusion(bf16[16,128,256]{2,1,0:T(8,128)(2,1)S(1)} %copy-done, s32[1024]{0:T(1024)S(1)} %pad_clamp_fusion.2), kind=kCustom, calls=%fused_computation | custom fusion | bytes 8388864 | tf_op jit(solution)/shard_map/gather | solution.py:88
  19.2 0.0 copy-done.2
  19.2 2.8 %gather_fusion.1 = bf16[64,128,256]{2,1,0:T(8,128)(2,1)} fusion(bf16[16,128,256]{2,1,0:T(8,128)(2,1)S(1)} %copy-done.2, s32[1024]{0:T(1024)S(1)} %pad_clamp_fusion.2), kind=kCustom, calls=%fused_computation.1 | custom fusion | bytes 8388864 | tf_op jit(solution)/shard_map/gather | solution.py:89
  22.0 4.7 %fusion.48 = (bf16[8,1,8,128,128]{4,3,2,1,0:T(8,128)(2,1)S(1)}, bf16[8,1,8,128,128]{4,3,2,1,0:T(8,128)(2,1)S(1)}, bf16[8,1,8,128,128]{4,3,2,1,0:T(8,128)(2,1)}, bf16[8,1,8,128,128]{4,3,2,1,0:T(8,128)(2,1)S(1)}) fusion(bf16[8,1,8,128,256]{4,3,2,1,0:T(8,128)(2,1)} %bitcast.70, bf16[8,1,8,128,256]{4,3,2,1,0:T(8,128)(2,1)} %bitcast.71), kind=kLoop, calls=%fused_computation.108 | loop fusion | bytes 16777216 | tf_op jit(solution)/shard_map/slice | solution.py:107
  26.7 2.7 %pad_maximum_fusion.1 = bf16[8,1,8,128,256]{4,3,2,1,0:T(8,128)(2,1)} fusion(bf16[8,1,8,128,128]{4,3,2,1,0:T(8,128)(2,1)S(1)} %get-tuple-element.47, bf16[8,1,8,128,128]{4,3,2,1,0:T(8,128)(2,1)S(1)} %get-tuple-element.9), kind=kLoop, calls=%fused_computation.6 | loop fusion | flops 8388608 | bytes 8388608 | tf_op jit(solution)/shard_map/concatenate | solution.py:107
  29.4 4.6 %all-to-all-start.2 = ((bf16[8,1,8,128,256]{4,3,2,1,0:T(8,128)(2,1)}), bf16[8,1,8,128,256]{4,3,2,1,0:T(8,128)(2,1)}, u32[]{:S(2)}, u32[]{:S(2)}) async-start(bf16[8,1,8,128,256]{4,3,2,1,0:T(8,128)(2,1)} %pad_maximum_fusion.1), calls=%async_computation.2 | async-start | bytes 8388608 | tf_op jit(solution)/shard_map/all_to_all | solution.py:108
  33.9 4.2 %pad_maximum_fusion = bf16[8,1,8,128,256]{4,3,2,1,0:T(8,128)(2,1)} fusion(bf16[8,1,8,128,128]{4,3,2,1,0:T(8,128)(2,1)} %get-tuple-element.46, bf16[8,1,8,128,128]{4,3,2,1,0:T(8,128)(2,1)S(1)} %get-tuple-element.10), kind=kLoop, calls=%fused_computation.5 | loop fusion | flops 8388608 | bytes 8388608 | tf_op jit(solution)/shard_map/concatenate | solution.py:107
  38.1 87.8 %all-to-all-done.2 = bf16[8,1,8,128,256]{4,3,2,1,0:T(8,128)(2,1)} async-done(((bf16[8,1,8,128,256]{4,3,2,1,0:T(8,128)(2,1)}), bf16[8,1,8,128,256]{4,3,2,1,0:T(8,128)(2,1)}, u32[]{:S(2)}, u32[]{:S(2)}) %all-to-all-start.2) | async-done | bytes 4194336 | tf_op jit(solution)/shard_map/all_to_all | solution.py:108
  126.0 4.6 %all-to-all-start.1 = ((bf16[8,1,8,128,256]{4,3,2,1,0:T(8,128)(2,1)}), bf16[8,1,8,128,256]{4,3,2,1,0:T(8,128)(2,1)}, u32[]{:S(2)}, u32[]{:S(2)}) async-start(bf16[8,1,8,128,256]{4,3,2,1,0:T(8,128)(2,1)} %pad_maximum_fusion), calls=%async_computation.1 | async-start | bytes 8388608 | tf_op jit(solution)/shard_map/all_to_all | solution.py:108
  130.6 0.1 copy.67
  130.7 0.1 copy.68
  130.8 0.2 convert_bitcast_fusion
  131.1 0.4 copy.73
  131.5 0.5 multiply_cosine_fusion.1
  132.0 0.7 multiply_subtract_fusion
  132.8 0.6 fusion
  133.4 0.0 copy-start.9
  133.4 0.0 copy-start.8
  133.4 0.5 convert_element_type.168
  133.9 0.1 copy-done.9
  134.0 0.1 add_convert_fusion
  134.1 0.2 copy-done.8
  134.3 0.3 fusion.30
  134.7 1.1 fusion.50
  135.7 0.6 compare_select_fusion.bias_ref
  136.3 0.1 fusion.41
  136.4 0.2 mul.341
  136.7 0.6 gather_fusion.3
  137.3 0.1 copy.57
  137.4 4.2 %gather_fusion.2 = bf16[32,128,256]{2,1,0:T(8,128)(2,1)} fusion(bf16[64,128,256]{2,1,0:T(8,128)(2,1)} %bitcast.9, s32[1024]{0:T(1024)S(1)} %pad_clamp_fusion.1), kind=kCustom, calls=%fused_computation.2 | custom fusion | bytes 4194432 | tf_op jit(solution)/shard_map/gather | solution.py:112
  141.6 3.2 %copy.56 = bf16[32,128,256]{1,2,0:T(8,128)(2,1)S(1)} copy(bf16[32,128,256]{2,1,0:T(8,128)(2,1)} %gather_fusion.2) | data formatting | bytes 4194304 | tf_op jit(solution)/shard_map/gather | solution.py:112
  144.8 1.3 multiply_convert_fusion.1
  146.1 4.2 %fusion.20 = (bf16[1,32,8,8,128]{4,3,2,1,0:T(8,128)(2,1)S(1)}, bf16[1,32,8,8,128]{4,3,2,1,0:T(8,128)(2,1)S(1)}) fusion(f32[1,32,128,128]{2,3,1,0:T(8,128)S(1)} %get-tuple-element.22, f32[64]{0:T(128)S(1)} %negate_power_fusion, f32[32,128]{1,0:T(8,128)S(1)} %add_convert_fusion), kind=kLoop, calls=%fused_computation.46 | loop fusion | flops 2359296 | bytes 3162368
  150.4 0.1 copy.80
  150.5 0.1 copy.81
  150.6 0.7 copy.61
  151.3 1.1 pad_maximum_fusion.2.v_ref
  152.3 1.2 maximum_bitcast_fusion.k_ref
  153.5 16.4 %shard_map.91 = bf16[1,256,1024]{2,1,0:T(8,128)(2,1)} custom-call(f32[1,1,4096]{2,1,0:T(1,128)} %compare_select_fusion.bias_ref, bf16[1,256,1024]{2,1,0:T(8,128)(2,1)} %get-tuple-element.23.q_ref, bf16[1,128,4352]{2,1,0:T(8,128)(2,1)} %maximum_bitcast_fusion.k_ref, bf16[1,4352,128]{2,1,0:T(8,128)(2,1)} %pad_maximum_fusion.2.v_ref), custom_call_target="tpu_custom_call" | custom-call | flops 6845104128 | bytes 3276800 | tf_op jit(solution)/shard_map/pallas_call | solution.py:197
  170.0 53.1 %all-to-all-done.1 = bf16[8,1,8,128,256]{4,3,2,1,0:T(8,128)(2,1)} async-done(((bf16[8,1,8,128,256]{4,3,2,1,0:T(8,128)(2,1)}), bf16[8,1,8,128,256]{4,3,2,1,0:T(8,128)(2,1)}, u32[]{:S(2)}, u32[]{:S(2)}) %all-to-all-start.1) | async-done | bytes 4194336 | tf_op jit(solution)/shard_map/all_to_all | solution.py:108
  223.1 4.2 %gather_fusion.4 = bf16[32,128,256]{2,1,0:T(8,128)(2,1)} fusion(bf16[64,128,256]{2,1,0:T(8,128)(2,1)} %bitcast.19, s32[1024]{0:T(1024)S(1)} %pad_clamp_fusion.1), kind=kCustom, calls=%fused_computation.4 | custom fusion | bytes 4194432 | tf_op jit(solution)/shard_map/gather | solution.py:112
  227.3 3.2 %copy.62 = bf16[32,128,256]{1,2,0:T(8,128)(2,1)S(1)} copy(bf16[32,128,256]{2,1,0:T(8,128)(2,1)} %gather_fusion.4) | data formatting | bytes 4194304 | tf_op jit(solution)/shard_map/gather | solution.py:112
  230.5 1.3 multiply_convert_fusion
  231.8 4.2 %fusion.18 = (bf16[1,32,8,8,128]{4,3,2,1,0:T(8,128)(2,1)S(1)}, bf16[1,32,8,8,128]{4,3,2,1,0:T(8,128)(2,1)S(1)}) fusion(f32[1,32,128,128]{2,3,1,0:T(8,128)S(1)} %get-tuple-element.20, f32[64]{0:T(128)S(1)} %negate_power_fusion, f32[32,128]{1,0:T(8,128)S(1)} %add_convert_fusion), kind=kLoop, calls=%fused_computation.44 | loop fusion | flops 2359296 | bytes 3162368
  236.0 0.1 copy.78
  236.1 0.1 copy.79
  236.3 0.7 copy.66
  236.9 1.1 pad_maximum_fusion.3.v_ref
  238.0 1.1 maximum_bitcast_fusion.1.k_ref
  239.1 16.6 %shard_map.92 = bf16[1,256,1024]{2,1,0:T(8,128)(2,1)} custom-call(f32[1,1,4096]{2,1,0:T(1,128)} %compare_select_fusion.bias_ref, bf16[1,256,1024]{2,1,0:T(8,128)(2,1)} %get-tuple-element.24.q_ref, bf16[1,128,4352]{2,1,0:T(8,128)(2,1)} %maximum_bitcast_fusion.1.k_ref, bf16[1,4352,128]{2,1,0:T(8,128)(2,1)} %pad_maximum_fusion.3.v_ref), custom_call_target="tpu_custom_call" | custom-call | flops 6845104128 | bytes 3276800 | tf_op jit(solution)/shard_map/pallas_call | solution.py:197
  255.7 2.1 pad_maximum_fusion.4
  (27 shorter events, 0.2 us)
Async XLA Ops:
  0.0 16.4 %copy-start = (bf16[16,128,256]{2,1,0:T(8,128)(2,1)S(1)}, bf16[16,128,256]{2,1,0:T(8,128)(2,1)}, u32[]{:S(2)}) copy-start(bf16[16,128,256]{2,1,0:T(8,128)(2,1)} %param.12) | copy-start | bytes 3145732
  16.4 2.8 %copy-start.2 = (bf16[16,128,256]{2,1,0:T(8,128)(2,1)S(1)}, bf16[16,128,256]{2,1,0:T(8,128)(2,1)}, u32[]{:S(2)}) copy-start(bf16[16,128,256]{2,1,0:T(8,128)(2,1)} %param.13) | copy-start | bytes 3145732
  29.4 96.6 %all-to-all-start.2 = ((bf16[8,1,8,128,256]{4,3,2,1,0:T(8,128)(2,1)}), bf16[8,1,8,128,256]{4,3,2,1,0:T(8,128)(2,1)}, u32[]{:S(2)}, u32[]{:S(2)}) async-start(bf16[8,1,8,128,256]{4,3,2,1,0:T(8,128)(2,1)} %pad_maximum_fusion.1), calls=%async_computation.2 | async-start | bytes 8388608 | tf_op jit(solution)/shard_map/all_to_all | solution.py:108
  38.1 92.4 %copy-start.7 = (bf16[1,256,256]{2,1,0:T(8,128)(2,1)S(1)}, bf16[1,256,256]{2,1,0:T(8,128)(2,1)}, u32[]{:S(2)}) copy-start(bf16[1,256,256]{2,1,0:T(8,128)(2,1)} %param.10) | copy-start | bytes 393220
  38.1 92.7 %copy-start.5 = (bf16[1,256,2048]{2,1,0:T(8,128)(2,1)S(1)}, bf16[1,256,2048]{2,1,0:T(8,128)(2,1)}, u32[]{:S(2)}) copy-start(bf16[1,256,2048]{2,1,0:T(8,128)(2,1)} %param.9) | copy-start | bytes 3145732
  126.0 97.1 %all-to-all-start.1 = ((bf16[8,1,8,128,256]{4,3,2,1,0:T(8,128)(2,1)}), bf16[8,1,8,128,256]{4,3,2,1,0:T(8,128)(2,1)}, u32[]{:S(2)}, u32[]{:S(2)}) async-start(bf16[8,1,8,128,256]{4,3,2,1,0:T(8,128)(2,1)} %pad_maximum_fusion), calls=%async_computation.1 | async-start | bytes 8388608 | tf_op jit(solution)/shard_map/all_to_all | solution.py:108
  133.4 0.7 copy-start.9
  133.4 0.9 copy-start.8
  146.1 4.5 %copy-start.4 = (bf16[1,32,128,128]{2,3,1,0:T(8,128)(2,1)S(1)}, bf16[1,32,128,128]{2,3,1,0:T(8,128)(2,1)}, u32[]{:S(2)}) copy-start(bf16[1,32,128,128]{2,3,1,0:T(8,128)(2,1)} %get-tuple-element.21) | copy-start | bytes 3145732
  231.8 4.5 %copy-start.3 = (bf16[1,32,128,128]{2,3,1,0:T(8,128)(2,1)S(1)}, bf16[1,32,128,128]{2,3,1,0:T(8,128)(2,1)}, u32[]{:S(2)}) copy-start(bf16[1,32,128,128]{2,3,1,0:T(8,128)(2,1)} %get-tuple-element.19) | copy-start | bytes 3145732
  239.1 16.6 %copy-start.6 = (bf16[1,256,1024]{2,1,0:T(8,128)(2,1)S(1)}, bf16[1,256,1024]{2,1,0:T(8,128)(2,1)}, u32[]{:S(2)}) copy-start(bf16[1,256,1024]{2,1,0:T(8,128)(2,1)} %shard_map.91) | copy-start | bytes 1572868
  239.1 18.7 %copy-start.1 = (bf16[16,128,256]{2,1,0:T(8,128)(2,1)S(1)}, bf16[16,128,256]{2,1,0:T(8,128)(2,1)}, u32[]{:S(2)}) copy-start(bf16[16,128,256]{2,1,0:T(8,128)(2,1)} %param.12) | copy-start | bytes 3145732

commit v6 on v5

--- a/solution.py
+++ b/solution.py
@@ -85,8 +85,19 @@
     all_scales = (answers[:, 0, capacity:].astype(jnp.float32) * (1.0 / 65536.0)).reshape(
         owners * per_owner, 2, scales.shape[2]
     )
-    raw_keys = stored_stretch_keys[chosen]
-    raw_values = stored_stretch_values[chosen]
+    store = jnp.stack(
+        [
+            jnp.concatenate(
+                [
+                    stored_stretch_keys[..., h * head_dim:(h + 1) * head_dim],
+                    stored_stretch_values[..., h * head_dim:(h + 1) * head_dim],
+                ],
+                axis=-1,
+            )
+            for h in range(kv_heads)
+        ],
+        axis=0,
+    )
     flat = owners * rows * capacity
     index = (owner * rows + jnp.arange(rows, dtype=jnp.int32)[:, None]) * capacity + rank
     index = jnp.where(live, index, 0)
@@ -104,7 +115,7 @@
     results = []
     for head in range(kv_heads):
         cols = slice(head * head_dim, (head + 1) * head_dim)
-        sent = jnp.concatenate([raw_keys[..., cols], raw_values[..., cols]], axis=-1)
+        sent = store[head][chosen]
         got = lax.all_to_all(sent, "stretch", split_axis=0, concat_axis=0, tiled=True)
         if results:
             got, earlier = lax.optimization_barrier((got, results[-1]))
@@ -125,12 +136,16 @@
         )
         group_cols = slice(head * request_group * head_dim, (head + 1) * request_group * head_dim)
         results.append(
-            flash(query_rot[..., group_cols], keys_all, values_all, counts * span, request_group, cache_length)
-        )
-    return jnp.concatenate(results, axis=-1)
-
-
-def flash_kernel(bias_ref, q_ref, k_ref, v_ref, o_ref, *, cache_length, chunk, heads):
+            flash(
+                query_rot[..., group_cols], keys_all, values_all, counts * span, request_group,
+                cache_length, head * request_group, results[-1] if results else None, queries.shape[2],
+            )
+        )
+    return results[-1]
+
+
+def flash_kernel(bias_ref, q_ref, k_ref, v_ref, *refs, cache_length, chunk, heads):
+    o_ref = refs[-1]
     tokens = q_ref.shape[0]
     lanes = 128
     new_mask = lax.broadcasted_iota(jnp.int32, (tokens, tokens), 1) <= lax.broadcasted_iota(
@@ -181,7 +196,7 @@
 HEADS = 4
 
 
-def flash(query_rot, keys_all, values_all, live, request_group, cache_length):
+def flash(query_rot, keys_all, values_all, live, request_group, cache_length, offset, into, out_width):
     rows, tokens, q_width = query_rot.shape
     length, width = keys_all.shape[1:]
     head_dim = 128
@@ -194,25 +209,34 @@
     ).astype(jnp.float32)[:, None, :]
     kernel = functools.partial(flash_kernel, cache_length=cache_length, chunk=chunk, heads=heads)
     per = request_group // heads
+    block = offset // heads
+    in_specs = [
+        pl.BlockSpec((None, 1, cache_length), lambda r, h, g: (r, 0, 0)),
+        pl.BlockSpec((None, tokens, head_dim * heads), lambda r, h, g: (r, 0, h * per + g)),
+        pl.BlockSpec((None, head_dim, length), lambda r, h, g: (r, h, 0)),
+        pl.BlockSpec((None, length, head_dim), lambda r, h, g: (r, 0, h)),
+    ]
+    operands = [bias, query_rot, keys_t, values_all]
+    aliases = {}
+    if into is not None:
+        in_specs.append(pl.BlockSpec(memory_space=pl.ANY))
+        operands.append(into)
+        aliases = {4: 0}
     return pl.pallas_call(
         kernel,
         grid=(rows, kv_heads, per),
-        in_specs=[
-            pl.BlockSpec((None, 1, cache_length), lambda r, h, g: (r, 0, 0)),
-            pl.BlockSpec((None, tokens, head_dim * heads), lambda r, h, g: (r, 0, h * per + g)),
-            pl.BlockSpec((None, head_dim, length), lambda r, h, g: (r, h, 0)),
-            pl.BlockSpec((None, length, head_dim), lambda r, h, g: (r, 0, h)),
-        ],
+        in_specs=in_specs,
         out_specs=pl.BlockSpec(
-            (None, tokens, head_dim * heads), lambda r, h, g: (r, 0, h * per + g)
+            (None, tokens, head_dim * heads), lambda r, h, g: (r, 0, block + h * per + g)
         ),
-        out_shape=jax.ShapeDtypeStruct((rows, tokens, q_width), jnp.bfloat16),
+        out_shape=jax.ShapeDtypeStruct((rows, tokens, out_width), jnp.bfloat16),
+        input_output_aliases=aliases,
         cost_estimate=pl.CostEstimate(
             flops=6 * rows * tokens * q_width * length,
             transcendentals=rows * tokens * (q_width // head_dim) * length,
             bytes_accessed=2 * rows * (2 * tokens * q_width + 2 * length * width),
         ),
-    )(bias, query_rot, keys_t, values_all)
+    )(*operands)
 
 
 def solution(mesh):

time: 258 us -> 246 us (0.953)
  blocking collectives: 13.5 us -> 0 us
  other arithmetic: 29.4 us -> 19.5 us
  starting transfers between devices: 9.14 us -> 16.5 us
  waiting for transfers between devices: 141 us -> 148 us
  local copies, waits for them, and re-layouts: 30.8 us -> 27.5 us
    all_to_all x1 -> x0, blocking collectives: 13.5 us -> none  [shards(): lax.all_to_all(requests, 'stretch', split_axis=0, concat_axis=0, tiled=True)]
    concatenate x3 -> x1, other arithmetic: 8.96 us -> 0.27 us  [shards(): jnp.concatenate([stored_stretch_keys[..., h * head_dim:(h + 1) * head_dim...]
    all_to_all x0 -> x1, starting transfers between devices: none -> 7.28 us  [shards(): lax.all_to_all(requests, 'stretch', split_axis=0, concat_axis=0, tiled=True)]
    all_to_all x0 -> x1, waiting for transfers between devices: none -> 4.54 us  [shards(): lax.all_to_all(requests, 'stretch', split_axis=0, concat_axis=0, tiled=True)]
    slice x1 -> x2, local copies, waits for them, and re-layouts: 4.74 us -> 1.55 us  [the longest x1 1.27 us: shards(): stored_stretch_keys[..., h * head_dim:(h + 1) * head_dim]]
  transfers between devices with their start and end apart: 2 -> 3, of which waited for: 2 -> 3; matrix products, arithmetic and copies ran while one was open for 10% -> 11% of each run, Pallas kernels for 6% -> 7%
where the time goes in v6:
time: 246 us; the launch traced here: 245 us
  waiting for transfers between devices  148 us (60%)
  Pallas kernels  32.9 us (13%)
  local copies, waits for them, and re-layouts  27.5 us (11%)
  other arithmetic  19.5 us (8%)
  starting transfers between devices  16.5 us (7%)
    all_to_all x2, waiting for transfers between devices, shards(): lax.all_to_all(sent, 'stretch', split_axis=0, concat_axis=0, tiled=True)  143 us
    pallas_call x2, Pallas kernels, flash(): pl.pallas_call(kernel, grid=(rows, kv_heads, per), in_specs=in_specs, out...  32.9 us
    gather x4, local copies, waits for them, and re-layouts, shards(): got = got.reshape(flat, span, 2 * head_dim)[index]  14.8 us
    all_to_all x2, starting transfers between devices, shards(): lax.all_to_all(sent, 'stretch', split_axis=0, concat_axis=0, tiled=True)  9.27 us
    unnamed x3, other arithmetic  8.78 us
    all_to_all x1, starting transfers between devices, shards(): lax.all_to_all(requests, 'stretch', split_axis=0, concat_axis=0, tiled=True)  7.28 us
    gather x2, local copies, waits for them, and re-layouts, shards(): sent = store[head][chosen]  5.55 us
  transfers between devices with their start and end apart: 3, of which 3 were waited for; matrix products, arithmetic and copies ran while one was open for 11% of the time, Pallas kernels for 7%

profile of v6, /device:TPU:0, one launch (start us, length us, event | category | flops | bytes accessed | tf_op | source)
XLA Modules:
  0.0 245.3 jit_solution(2487315662521847087)
XLA Ops:
  0.0 0.8 fusion.43
  1.4 0.1 convert_reduce_fusion
  1.5 0.1 select_reduce_fusion
  1.6 0.1 sub.30
  1.7 0.7 multiply_convert_fusion.2
  2.4 0.1 copy.55
  2.5 0.1 reshape.760
  2.6 0.1 pad.15.clone
  2.7 0.6 pad_add_fusion
  3.3 7.3 %all-to-all-start = ((s32[8,1,72]{2,1,0:T(1,128)}), s32[8,1,72]{2,1,0:T(1,128)S(1)}, u32[]{:S(2)}, u32[]{:S(2)}) async-start(s32[8,1,72]{2,1,0:T(1,128)} %pad_add_fusion), calls=%async_computation | async-start | bytes 8192 | tf_op jit(solution)/shard_map/all_to_all | solution.py:82
  10.6 1.3 fusion.48
  11.9 0.0 copy-done.1
  11.9 0.3 fusion.49
  12.2 0.3 pad_maximum_fusion.2
  12.4 4.5 %all-to-all-done = s32[8,1,72]{2,1,0:T(1,128)S(1)} async-done(((s32[8,1,72]{2,1,0:T(1,128)}), s32[8,1,72]{2,1,0:T(1,128)S(1)}, u32[]{:S(2)}, u32[]{:S(2)}) %all-to-all-start) | async-done | bytes 2336 | tf_op jit(solution)/shard_map/all_to_all | solution.py:82
  17.0 0.1 reshape.701
  17.1 2.8 %gather_fusion.1 = bf16[64,128,256]{2,1,0:T(8,128)(2,1)} fusion(bf16[16,128,256]{2,1,0:T(8,128)(2,1)S(1)} %get-tuple-element.47, s32[1024]{0:T(1024)S(1)} %pad_clamp_fusion.2), kind=kCustom, calls=%fused_computation.1 | custom fusion | bytes 8388864 | tf_op jit(solution)/shard_map/gather | solution.py:118
  19.9 4.6 %all-to-all-start.2 = ((bf16[8,1,8,128,256]{4,3,2,1,0:T(8,128)(2,1)}), bf16[8,1,8,128,256]{4,3,2,1,0:T(8,128)(2,1)}, u32[]{:S(2)}, u32[]{:S(2)}) async-start(bf16[8,1,8,128,256]{4,3,2,1,0:T(8,128)(2,1)} %bitcast.71), calls=%async_computation.2 | async-start | bytes 8388608 | tf_op jit(solution)/shard_map/all_to_all | solution.py:119
  24.4 2.8 %gather_fusion = bf16[64,128,256]{2,1,0:T(8,128)(2,1)} fusion(bf16[16,128,256]{2,1,0:T(8,128)(2,1)S(1)} %get-tuple-element.46, s32[1024]{0:T(1024)S(1)} %pad_clamp_fusion.2), kind=kCustom, calls=%fused_computation | custom fusion | bytes 8388864 | tf_op jit(solution)/shard_map/gather | solution.py:118
  27.2 89.2 %all-to-all-done.2 = bf16[8,1,8,128,256]{4,3,2,1,0:T(8,128)(2,1)} async-done(((bf16[8,1,8,128,256]{4,3,2,1,0:T(8,128)(2,1)}), bf16[8,1,8,128,256]{4,3,2,1,0:T(8,128)(2,1)}, u32[]{:S(2)}, u32[]{:S(2)}) %all-to-all-start.2) | async-done | bytes 4194336 | tf_op jit(solution)/shard_map/all_to_all | solution.py:119
  116.5 4.7 %all-to-all-start.1 = ((bf16[8,1,8,128,256]{4,3,2,1,0:T(8,128)(2,1)}), bf16[8,1,8,128,256]{4,3,2,1,0:T(8,128)(2,1)}, u32[]{:S(2)}, u32[]{:S(2)}) async-start(bf16[8,1,8,128,256]{4,3,2,1,0:T(8,128)(2,1)} %bitcast.70), calls=%async_computation.1 | async-start | bytes 8388608 | tf_op jit(solution)/shard_map/all_to_all | solution.py:119
  121.2 0.0 copy-done.2
  121.2 0.1 copy.68
  121.3 0.1 copy.69
  121.5 0.0 copy-done
  121.5 0.2 convert_bitcast_fusion
  121.7 0.4 copy.74
  122.1 0.5 multiply_cosine_fusion.1
  122.7 0.6 multiply_subtract_fusion
  123.3 0.6 fusion
  123.9 0.0 copy-start.4
  123.9 0.0 copy-start.3
  123.9 0.5 convert_element_type.165
  124.5 0.1 copy-done.4
  124.6 0.1 add_convert_fusion
  124.6 0.2 copy-done.3
  124.8 0.3 fusion.30
  125.2 1.1 fusion.50
  126.3 0.6 compare_select_fusion.bias_ref
  126.9 0.1 fusion.41
  127.0 0.2 mul.341
  127.2 0.6 gather_fusion.3
  127.8 0.1 copy.58
  127.9 4.2 %gather_fusion.2 = bf16[32,128,256]{2,1,0:T(8,128)(2,1)} fusion(bf16[64,128,256]{2,1,0:T(8,128)(2,1)} %bitcast.9, s32[1024]{0:T(1024)S(1)} %pad_clamp_fusion.1), kind=kCustom, calls=%fused_computation.2 | custom fusion | bytes 4194432 | tf_op jit(solution)/shard_map/gather | solution.py:123
  132.1 3.2 %copy.57 = bf16[32,128,256]{1,2,0:T(8,128)(2,1)S(1)} copy(bf16[32,128,256]{2,1,0:T(8,128)(2,1)} %gather_fusion.2) | data formatting | bytes 4194304 | tf_op jit(solution)/shard_map/gather | solution.py:123
  135.3 0.4 multiply_convert_fusion.1
  135.8 4.3 %fusion.20 = (bf16[1,32,8,8,128]{4,3,2,1,0:T(8,128)(2,1)S(1)}, bf16[1,32,8,8,128]{4,3,2,1,0:T(8,128)(2,1)S(1)}) fusion(f32[1,32,128,128]{2,3,1,0:T(8,128)S(1)} %get-tuple-element.18, f32[64]{0:T(128)S(1)} %negate_power_fusion, f32[32,128]{1,0:T(8,128)S(1)} %add_convert_fusion), kind=kLoop, calls=%fused_computation.45 | loop fusion | flops 2359296 | bytes 3162368
  140.0 0.1 copy.81
  140.1 0.1 copy.82
  140.2 0.7 copy.62
  140.9 1.1 pad_maximum_fusion.v_ref
  142.0 1.2 maximum_bitcast_fusion.k_ref
  143.2 16.4 %shard_map.91.refs_0_ = bf16[1,256,2048]{2,1,0:T(8,128)(2,1)} custom-call(f32[1,1,4096]{2,1,0:T(1,128)} %compare_select_fusion.bias_ref, bf16[1,256,1024]{2,1,0:T(8,128)(2,1)} %get-tuple-element.23.q_ref, bf16[1,128,4352]{2,1,0:T(8,128)(2,1)} %maximum_bitcast_fusion.k_ref, bf16[1,4352,128]{2,1,0:T(8,128)(2,1)} %pad_maximum_fusion.v_ref), custom_call_target="tpu_custom_call" | custom-call | flops 6845104128 | bytes 3276800 | tf_op jit(solution)/shard_map/pallas_call | solution.py:225
  159.6 54.1 %all-to-all-done.1 = bf16[8,1,8,128,256]{4,3,2,1,0:T(8,128)(2,1)} async-done(((bf16[8,1,8,128,256]{4,3,2,1,0:T(8,128)(2,1)}), bf16[8,1,8,128,256]{4,3,2,1,0:T(8,128)(2,1)}, u32[]{:S(2)}, u32[]{:S(2)}) %all-to-all-start.1) | async-done | bytes 4194336 | tf_op jit(solution)/shard_map/all_to_all | solution.py:119
  213.7 4.2 %gather_fusion.4 = bf16[32,128,256]{2,1,0:T(8,128)(2,1)} fusion(bf16[64,128,256]{2,1,0:T(8,128)(2,1)} %bitcast.19, s32[1024]{0:T(1024)S(1)} %pad_clamp_fusion.1), kind=kCustom, calls=%fused_computation.4 | custom fusion | bytes 4194432 | tf_op jit(solution)/shard_map/gather | solution.py:123
  217.9 3.2 %copy.63 = bf16[32,128,256]{1,2,0:T(8,128)(2,1)S(1)} copy(bf16[32,128,256]{2,1,0:T(8,128)(2,1)} %gather_fusion.4) | data formatting | bytes 4194304 | tf_op jit(solution)/shard_map/gather | solution.py:123
  221.1 0.4 multiply_convert_fusion
  221.6 4.3 %fusion.18 = (bf16[1,32,8,8,128]{4,3,2,1,0:T(8,128)(2,1)S(1)}, bf16[1,32,8,8,128]{4,3,2,1,0:T(8,128)(2,1)S(1)}) fusion(f32[1,32,128,128]{2,3,1,0:T(8,128)S(1)} %get-tuple-element.16, f32[64]{0:T(128)S(1)} %negate_power_fusion, f32[32,128]{1,0:T(8,128)S(1)} %add_convert_fusion), kind=kLoop, calls=%fused_computation.43 | loop fusion | flops 2359296 | bytes 3162368
  225.8 0.1 copy.79
  225.9 0.1 copy.80
  226.0 0.7 copy.67
  226.7 1.1 pad_maximum_fusion.1.v_ref
  227.8 1.1 maximum_bitcast_fusion.1.k_ref
  228.9 16.5 %shard_map.92 = bf16[1,256,2048]{2,1,0:T(8,128)(2,1)} custom-call(f32[1,1,4096]{2,1,0:T(1,128)} %compare_select_fusion.bias_ref, bf16[1,256,1024]{2,1,0:T(8,128)(2,1)} %get-tuple-element.24.q_ref, bf16[1,128,4352]{2,1,0:T(8,128)(2,1)} %maximum_bitcast_fusion.1.k_ref, bf16[1,4352,128]{2,1,0:T(8,128)(2,1)} %pad_maximum_fusion.1.v_ref, ...), custom_call_target="tpu_custom_call", output_to_operand_aliasing={{}: (4, {})} | custom-call | flops 6845104128 | bytes 3276800 | tf_op jit(solution)/shard_map/pallas_call | solution.py:225
  (17 shorter events, 0.1 us)
Async XLA Ops:
  0.0 11.9 %copy-start.1 = (bf16[16,128,256]{2,1,0:T(8,128)(2,1)S(1)}, bf16[16,128,256]{2,1,0:T(8,128)(2,1)}, u32[]{:S(2)}) copy-start(bf16[16,128,256]{2,1,0:T(8,128)(2,1)} %param.13) | copy-start | bytes 3145732
  3.3 13.7 %all-to-all-start = ((s32[8,1,72]{2,1,0:T(1,128)}), s32[8,1,72]{2,1,0:T(1,128)S(1)}, u32[]{:S(2)}, u32[]{:S(2)}) async-start(s32[8,1,72]{2,1,0:T(1,128)} %pad_add_fusion), calls=%async_computation | async-start | bytes 8192 | tf_op jit(solution)/shard_map/all_to_all | solution.py:82
  19.9 96.6 %all-to-all-start.2 = ((bf16[8,1,8,128,256]{4,3,2,1,0:T(8,128)(2,1)}), bf16[8,1,8,128,256]{4,3,2,1,0:T(8,128)(2,1)}, u32[]{:S(2)}, u32[]{:S(2)}) async-start(bf16[8,1,8,128,256]{4,3,2,1,0:T(8,128)(2,1)} %bitcast.71), calls=%async_computation.2 | async-start | bytes 8388608 | tf_op jit(solution)/shard_map/all_to_all | solution.py:119
  116.5 4.7 %copy-start.2 = (bf16[1,256,256]{2,1,0:T(8,128)(2,1)S(1)}, bf16[1,256,256]{2,1,0:T(8,128)(2,1)}, u32[]{:S(2)}) copy-start(bf16[1,256,256]{2,1,0:T(8,128)(2,1)} %param.10) | copy-start | bytes 393220
  116.5 5.0 %copy-start = (bf16[1,256,2048]{2,1,0:T(8,128)(2,1)S(1)}, bf16[1,256,2048]{2,1,0:T(8,128)(2,1)}, u32[]{:S(2)}) copy-start(bf16[1,256,2048]{2,1,0:T(8,128)(2,1)} %param.9) | copy-start | bytes 3145732
  116.5 97.2 %all-to-all-start.1 = ((bf16[8,1,8,128,256]{4,3,2,1,0:T(8,128)(2,1)}), bf16[8,1,8,128,256]{4,3,2,1,0:T(8,128)(2,1)}, u32[]{:S(2)}, u32[]{:S(2)}) async-start(bf16[8,1,8,128,256]{4,3,2,1,0:T(8,128)(2,1)} %bitcast.70), calls=%async_computation.1 | async-start | bytes 8388608 | tf_op jit(solution)/shard_map/all_to_all | solution.py:119
  123.9 0.7 copy-start.4
  123.9 0.9 copy-start.3

commit v7 on v6

--- a/solution.py
+++ b/solution.py
@@ -115,36 +115,63 @@
     results = []
     for head in range(kv_heads):
         cols = slice(head * head_dim, (head + 1) * head_dim)
-        sent = store[head][chosen]
-        got = lax.all_to_all(sent, "stretch", split_axis=0, concat_axis=0, tiled=True)
-        if results:
-            got, earlier = lax.optimization_barrier((got, results[-1]))
-            results[-1] = earlier
-        got = got.reshape(flat, span, 2 * head_dim)[index]
-        keys = got[..., :head_dim].astype(jnp.float32) * slot_scale[:, :, 0, head][:, :, None, None]
-        keys = apply_rotary(keys, placement).astype(jnp.bfloat16)
-        vals = got[..., head_dim:].astype(jnp.float32) * slot_scale[:, :, 1, head][:, :, None, None]
-        vals = vals.astype(jnp.bfloat16)
+        last = head == kv_heads - 1
         new_keys = apply_rotary(
             fresh_keys[..., cols].astype(jnp.float32), token_positions
         ).astype(jnp.bfloat16)
-        keys_all = jnp.concatenate(
-            [keys.reshape(rows, cache_length, head_dim), new_keys], axis=1
-        )
+        group_cols = slice(head * request_group * head_dim, (head + 1) * request_group * head_dim)
+        query_head = query_rot[..., group_cols]
+        if last:
+            got_keys = lax.all_to_all(
+                store[head][chosen][..., :head_dim], "stretch", split_axis=0, concat_axis=0, tiled=True
+            )
+            if results:
+                got_keys, earlier = lax.optimization_barrier((got_keys, results[-1]))
+                results[-1] = earlier
+            got_vals = lax.all_to_all(
+                store[head][chosen][..., head_dim:], "stretch", split_axis=0, concat_axis=0, tiled=True
+            )
+            raw_k = got_keys.reshape(flat, span, head_dim)[index]
+        else:
+            got = lax.all_to_all(store[head][chosen], "stretch", split_axis=0, concat_axis=0, tiled=True)
+            if results:
+                got, earlier = lax.optimization_barrier((got, results[-1]))
+                results[-1] = earlier
+            got = got.reshape(flat, span, 2 * head_dim)[index]
+            raw_k = got[..., :head_dim]
+        keys = raw_k.astype(jnp.float32) * slot_scale[:, :, 0, head][:, :, None, None]
+        keys = apply_rotary(keys, placement).astype(jnp.bfloat16)
+        keys_t = jnp.swapaxes(
+            jnp.concatenate([keys.reshape(rows, cache_length, head_dim), new_keys], axis=1), 1, 2
+        )
+        top = None
+        if last:
+            top = flash(
+                query_head, keys_t, None, counts * span, request_group, cache_length, 0, None, 0, "top"
+            )
+            got_vals, top = lax.optimization_barrier((got_vals, top))
+            raw_v = got_vals.reshape(flat, span, head_dim)[index]
+        else:
+            raw_v = got[..., head_dim:]
+        vals = raw_v.astype(jnp.float32) * slot_scale[:, :, 1, head][:, :, None, None]
+        vals = vals.astype(jnp.bfloat16)
         values_all = jnp.concatenate(
             [vals.reshape(rows, cache_length, head_dim), fresh_values[..., cols]], axis=1
         )
-        group_cols = slice(head * request_group * head_dim, (head + 1) * request_group * head_dim)
         results.append(
             flash(
-                query_rot[..., group_cols], keys_all, values_all, counts * span, request_group,
+                query_head, keys_t, values_all, counts * span, request_group,
                 cache_length, head * request_group, results[-1] if results else None, queries.shape[2],
+                "mix" if last else "both", top,
             )
         )
     return results[-1]
 
 
-def flash_kernel(bias_ref, q_ref, k_ref, v_ref, *refs, cache_length, chunk, heads):
+def flash_kernel(*refs, cache_length, chunk, heads, mode):
+    bias_ref, q_ref, k_ref = refs[:3]
+    v_ref = refs[3] if mode != "top" else None
+    top_ref = refs[4] if mode == "mix" else None
     o_ref = refs[-1]
     tokens = q_ref.shape[0]
     lanes = 128
@@ -170,10 +197,16 @@
             return scores(first, size) + bias_ref[:, first:first + size]
 
         fresh = jnp.where(new_mask, scores(cache_length, tokens), -1e30)
-        top = fold(jnp.full((tokens, lanes), -1e30, jnp.float32), fresh, jnp.maximum)
-        for first in range(0, cache_length, chunk):
-            top = fold(top, masked(first, chunk), jnp.maximum)
-        top = jnp.max(top, axis=1, keepdims=True)
+        if mode == "mix":
+            top = top_ref[:, head * lanes:head * lanes + 1]
+        else:
+            top = fold(jnp.full((tokens, lanes), -1e30, jnp.float32), fresh, jnp.maximum)
+            for first in range(0, cache_length, chunk):
+                top = fold(top, masked(first, chunk), jnp.maximum)
+            top = jnp.max(top, axis=1, keepdims=True)
+        if mode == "top":
+            o_ref[:, head * lanes:(head + 1) * lanes] = jnp.broadcast_to(top, (tokens, lanes))
+            continue
 
         def mix(s, first, size):
             p = jnp.exp(s - top)
@@ -196,45 +229,58 @@
 HEADS = 4
 
 
-def flash(query_rot, keys_all, values_all, live, request_group, cache_length, offset, into, out_width):
+def flash(query_rot, keys_t, values_all, live, request_group, cache_length, offset, into, out_width,
+          mode="both", top=None):
     rows, tokens, q_width = query_rot.shape
-    length, width = keys_all.shape[1:]
-    head_dim = 128
-    kv_heads = width // head_dim
+    head_dim, length = keys_t.shape[1:]
+    kv_heads = 1
     chunk = CHUNK if cache_length % CHUNK == 0 else 128
     heads = HEADS
-    keys_t = jnp.swapaxes(keys_all, 1, 2)
     bias = jnp.where(
         jnp.arange(cache_length, dtype=jnp.int32)[None, :] < live[:, None], 0.0, -1e30
     ).astype(jnp.float32)[:, None, :]
-    kernel = functools.partial(flash_kernel, cache_length=cache_length, chunk=chunk, heads=heads)
+    kernel = functools.partial(
+        flash_kernel, cache_length=cache_length, chunk=chunk, heads=heads, mode=mode
+    )
     per = request_group // heads
     block = offset // heads
     in_specs = [
         pl.BlockSpec((None, 1, cache_length), lambda r, h, g: (r, 0, 0)),
         pl.BlockSpec((None, tokens, head_dim * heads), lambda r, h, g: (r, 0, h * per + g)),
         pl.BlockSpec((None, head_dim, length), lambda r, h, g: (r, h, 0)),
-        pl.BlockSpec((None, length, head_dim), lambda r, h, g: (r, 0, h)),
     ]
-    operands = [bias, query_rot, keys_t, values_all]
+    operands = [bias, query_rot, keys_t]
+    if mode != "top":
+        in_specs.append(pl.BlockSpec((None, length, head_dim), lambda r, h, g: (r, 0, h)))
+        operands.append(values_all)
+    if mode == "mix":
+        in_specs.append(pl.BlockSpec((None, tokens, head_dim * heads), lambda r, h, g: (r, 0, h * per + g)))
+        operands.append(top)
     aliases = {}
     if into is not None:
         in_specs.append(pl.BlockSpec(memory_space=pl.ANY))
+        aliases = {len(operands): 0}
         operands.append(into)
-        aliases = {4: 0}
+    if mode == "top":
+        out_specs = pl.BlockSpec((None, tokens, head_dim * heads), lambda r, h, g: (r, 0, h * per + g))
+        out_shape = jax.ShapeDtypeStruct((rows, tokens, q_width), jnp.float32)
+    else:
+        out_specs = pl.BlockSpec(
+            (None, tokens, head_dim * heads), lambda r, h, g: (r, 0, block + h * per + g)
+        )
+        out_shape = jax.ShapeDtypeStruct((rows, tokens, out_width), jnp.bfloat16)
+    passes = {"both": 3, "top": 1, "mix": 2}[mode]
     return pl.pallas_call(
         kernel,
         grid=(rows, kv_heads, per),
         in_specs=in_specs,
-        out_specs=pl.BlockSpec(
-            (None, tokens, head_dim * heads), lambda r, h, g: (r, 0, block + h * per + g)
-        ),
-        out_shape=jax.ShapeDtypeStruct((rows, tokens, out_width), jnp.bfloat16),
+        out_specs=out_specs,
+        out_shape=out_shape,
         input_output_aliases=aliases,
         cost_estimate=pl.CostEstimate(
-            flops=6 * rows * tokens * q_width * length,
+            flops=2 * passes * rows * tokens * q_width * length,
             transcendentals=rows * tokens * (q_width // head_dim) * length,
-            bytes_accessed=2 * rows * (2 * tokens * q_width + 2 * length * width),
+            bytes_accessed=2 * rows * (2 * tokens * q_width + 2 * length * head_dim),
         ),
     )(*operands)
 

time: 246 us -> 244 us (level)
  waiting for transfers between devices: 148 us -> 130 us
  Pallas kernels: 32.9 us -> 41.9 us
  starting transfers between devices: 16.5 us -> 20.8 us
    all_to_all x2 -> x3, waiting for transfers between devices: 143 us -> 125 us  [the longest x1 84.5 us: shards(): lax.all_to_all(store[head][chosen], 'stretch', split_axis=0, concat_axis=...]
    pallas_call x2 -> x3, Pallas kernels: 32.9 us -> 41.9 us  [flash(): pl.pallas_call(kernel, grid=(rows, kv_heads, per), in_specs=in_specs, out...]
    gather x4 -> x2, local copies, waits for them, and re-layouts: 14.8 us -> 7.44 us  [shards(): got = got.reshape(flat, span, 2 * head_dim)[index]]
    gather x2 -> x5, local copies, waits for them, and re-layouts: 5.55 us -> 10.9 us  [the longest x2 3 us: shards(): raw_k = got_keys.reshape(flat, span, head_dim)[index]]
    slice x1 -> x2, local copies, waits for them, and re-layouts: 1.07 us -> 5.86 us  [the longest x1 4.74 us: shards(): store[head][chosen][..., head_dim:]]
    all_to_all x2 -> x3, starting transfers between devices: 9.27 us -> 13.5 us  [the longest x1 4.54 us: shards(): lax.all_to_all(store[head][chosen], 'stretch', split_axis=0, concat_axis=...]
  transfers between devices with their start and end apart: 3 -> 4, of which waited for: 3 -> 4; matrix products, arithmetic and copies ran while one was open for 11% -> 16% of each run, Pallas kernels for 7% -> 10%
where the time goes in v7:
time: 244 us; the launch traced here: 243 us
  waiting for transfers between devices  130 us (53%)
  Pallas kernels  41.9 us (17%)
  local copies, waits for them, and re-layouts  29.7 us (12%)
  starting transfers between devices  20.8 us (9%)
  other arithmetic  19.9 us (8%)
    all_to_all x1, waiting for transfers between devices, shards(): lax.all_to_all(store[head][chosen], 'stretch', split_axis=0, concat_axis=...  84.5 us
    pallas_call x3, Pallas kernels, flash(): pl.pallas_call(kernel, grid=(rows, kv_heads, per), in_specs=in_specs, out...  41.9 us
    all_to_all x1, waiting for transfers between devices, shards(): lax.all_to_all(store[head][chosen][..., :head_dim], 'stretch', split_axis...  33.5 us
    unnamed x3, other arithmetic  8.78 us
    all_to_all x1, waiting for transfers between devices, shards(): lax.all_to_all(store[head][chosen][..., head_dim:], 'stretch', split_axis...  7.52 us
    gather x2, local copies, waits for them, and re-layouts, shards(): got = got.reshape(flat, span, 2 * head_dim)[index]  7.44 us
    all_to_all x1, starting transfers between devices, shards(): lax.all_to_all(requests, 'stretch', split_axis=0, concat_axis=0, tiled=True)  7.28 us
  transfers between devices with their start and end apart: 4, of which 4 were waited for; matrix products, arithmetic and copies ran while one was open for 16% of the time, Pallas kernels for 10%

profile of v7, /device:TPU:0, one launch (start us, length us, event | category | flops | bytes accessed | tf_op | source)
XLA Modules:
  0.0 243.3 jit_solution(5201506558547857424)
XLA Ops:
  0.0 0.8 fusion.44
  1.4 0.1 convert_reduce_fusion
  1.5 0.1 select_reduce_fusion
  1.6 0.1 sub.30
  1.7 0.7 multiply_convert_fusion.1
  2.4 0.1 copy.41
  2.5 0.1 reshape.830
  2.6 0.1 pad.15.clone
  2.7 0.6 pad_add_fusion
  3.3 7.3 %all-to-all-start = ((s32[8,1,72]{2,1,0:T(1,128)}), s32[8,1,72]{2,1,0:T(1,128)S(1)}, u32[]{:S(2)}, u32[]{:S(2)}) async-start(s32[8,1,72]{2,1,0:T(1,128)} %pad_add_fusion), calls=%async_computation | async-start | bytes 8192 | tf_op jit(solution)/shard_map/all_to_all | solution.py:82
  10.6 1.3 fusion.50
  11.9 0.3 fusion.51
  12.2 0.3 pad_maximum_fusion.2
  12.4 4.5 %all-to-all-done = s32[8,1,72]{2,1,0:T(1,128)S(1)} async-done(((s32[8,1,72]{2,1,0:T(1,128)}), s32[8,1,72]{2,1,0:T(1,128)S(1)}, u32[]{:S(2)}, u32[]{:S(2)}) %all-to-all-start) | async-done | bytes 2336 | tf_op jit(solution)/shard_map/all_to_all | solution.py:82
  17.0 0.1 reshape.759
  17.1 2.8 %gather_fusion.1 = bf16[64,128,256]{2,1,0:T(8,128)(2,1)} fusion(bf16[16,128,256]{2,1,0:T(8,128)(2,1)S(1)} %get-tuple-element.51, s32[1024]{0:T(1024)S(1)} %pad_clamp_fusion.2), kind=kCustom, calls=%fused_computation.1 | custom fusion | bytes 8388864 | tf_op jit(solution)/shard_map/gather | solution.py:136
  19.9 4.5 %all-to-all-start.2 = ((bf16[8,1,8,128,256]{4,3,2,1,0:T(8,128)(2,1)}), bf16[8,1,8,128,256]{4,3,2,1,0:T(8,128)(2,1)}, u32[]{:S(2)}, u32[]{:S(2)}) async-start(bf16[8,1,8,128,256]{4,3,2,1,0:T(8,128)(2,1)} %bitcast.78), calls=%async_computation.2 | async-start | bytes 8388608 | tf_op jit(solution)/shard_map/all_to_all | solution.py:136
  24.4 2.8 %gather_fusion = bf16[64,128,256]{2,1,0:T(8,128)(2,1)} fusion(bf16[16,128,256]{2,1,0:T(8,128)(2,1)S(1)} %get-tuple-element.50, s32[1024]{0:T(1024)S(1)} %pad_clamp_fusion.2), kind=kCustom, calls=%fused_computation | custom fusion | bytes 8388864 | tf_op jit(solution)/shard_map/gather | solution.py:126
  27.2 4.7 %fusion.49 = (bf16[8,1,8,128,128]{4,3,2,1,0:T(8,128)(2,1)}, bf16[8,1,8,128,128]{4,3,2,1,0:T(8,128)(2,1)}) fusion(bf16[8,1,8,128,256]{4,3,2,1,0:T(8,128)(2,1)} %bitcast.79), kind=kLoop, calls=%fused_computation.110 | loop fusion | bytes 8388608 | tf_op jit(solution)/shard_map/slice | solution.py:132
  32.0 84.5 %all-to-all-done.2 = bf16[8,1,8,128,256]{4,3,2,1,0:T(8,128)(2,1)} async-done(((bf16[8,1,8,128,256]{4,3,2,1,0:T(8,128)(2,1)}), bf16[8,1,8,128,256]{4,3,2,1,0:T(8,128)(2,1)}, u32[]{:S(2)}, u32[]{:S(2)}) %all-to-all-start.2) | async-done | bytes 4194336 | tf_op jit(solution)/shard_map/all_to_all | solution.py:136
  116.5 4.5 %all-to-all-start.1 = ((bf16[8,1,8,128,128]{4,3,2,1,0:T(8,128)(2,1)}), bf16[8,1,8,128,128]{4,3,2,1,0:T(8,128)(2,1)}, u32[]{:S(2)}, u32[]{:S(2)}) async-start(bf16[8,1,8,128,128]{4,3,2,1,0:T(8,128)(2,1)} %get-tuple-element.14), calls=%async_computation.1 | async-start | bytes 4194304 | tf_op jit(solution)/shard_map/all_to_all | solution.py:125
  121.0 0.1 copy.53
  121.1 0.1 copy.54
  121.3 0.2 convert_bitcast_fusion
  121.5 0.4 copy.59
  121.9 0.5 multiply_cosine_fusion.1
  122.5 0.6 multiply_subtract_fusion
  123.1 0.6 fusion
  123.7 0.5 convert_element_type.194
  124.2 0.1 copy-done.4
  124.4 0.2 copy-done.3
  124.6 0.3 fusion.31
  125.0 1.1 fusion.52
  126.1 0.6 compare_select_fusion.refs_0_
  126.7 0.1 fusion.42
  126.8 0.2 mul.363
  127.1 0.6 gather_fusion.3
  127.7 0.1 copy.44
  127.8 0.1 broadcast_bitcast_fusion
  127.8 4.2 %gather_fusion.2 = bf16[32,128,256]{2,1,0:T(8,128)(2,1)} fusion(bf16[64,128,256]{2,1,0:T(8,128)(2,1)} %bitcast.9, s32[1024]{0:T(1024)S(1)} %pad_clamp_fusion.1), kind=kCustom, calls=%fused_computation.2 | custom fusion | bytes 4194432 | tf_op jit(solution)/shard_map/gather | solution.py:140
  132.1 3.2 %copy.43 = bf16[32,128,256]{1,2,0:T(8,128)(2,1)S(1)} copy(bf16[32,128,256]{2,1,0:T(8,128)(2,1)} %gather_fusion.2) | data formatting | bytes 4194304 | tf_op jit(solution)/shard_map/gather | solution.py:140
  135.3 33.5 %all-to-all-done.1 = bf16[8,1,8,128,128]{4,3,2,1,0:T(8,128)(2,1)} async-done(((bf16[8,1,8,128,128]{4,3,2,1,0:T(8,128)(2,1)}), bf16[8,1,8,128,128]{4,3,2,1,0:T(8,128)(2,1)}, u32[]{:S(2)}, u32[]{:S(2)}) %all-to-all-start.1) | async-done | bytes 2097184 | tf_op jit(solution)/shard_map/all_to_all | solution.py:125
  168.7 4.5 %all-to-all-start.3 = ((bf16[8,1,8,128,128]{4,3,2,1,0:T(8,128)(2,1)}), bf16[8,1,8,128,128]{4,3,2,1,0:T(8,128)(2,1)}, u32[]{:S(2)}, u32[]{:S(2)}) async-start(bf16[8,1,8,128,128]{4,3,2,1,0:T(8,128)(2,1)} %get-tuple-element.13), calls=%async_computation.3 | async-start | bytes 4194304 | tf_op jit(solution)/shard_map/all_to_all | solution.py:131
  173.3 0.4 multiply_convert_fusion
  173.7 4.3 %fusion.21 = (bf16[1,32,8,8,128]{4,3,2,1,0:T(8,128)(2,1)S(1)}, bf16[1,32,8,8,128]{4,3,2,1,0:T(8,128)(2,1)S(1)}) fusion(f32[1,32,128,128]{2,3,1,0:T(8,128)S(1)} %get-tuple-element.22, f32[64]{0:T(128)S(1)} %negate_power_fusion, f32[32,128]{1,0:T(8,128)S(1)} %add_convert_fusion), kind=kLoop, calls=%fused_computation.47 | loop fusion | flops 2359296 | bytes 3162368
  178.0 0.1 copy.66
  178.1 0.1 copy.67
  178.2 0.7 copy.48
  178.8 1.1 pad_maximum_fusion.refs_3_
  179.9 1.1 maximum_bitcast_fusion.refs_2_
  181.0 16.4 %shard_map.91.refs_5_ = bf16[1,256,2048]{2,1,0:T(8,128)(2,1)} custom-call(f32[1,1,4096]{2,1,0:T(1,128)} %compare_select_fusion.refs_0_, bf16[1,256,1024]{2,1,0:T(8,128)(2,1)} %get-tuple-element.27.refs_1_, bf16[1,128,4352]{2,1,0:T(8,128)(2,1)} %maximum_bitcast_fusion.refs_2_, bf16[1,4352,128]{2,1,0:T(8,128)(2,1)} %pad_maximum_fusion.refs_3_), custom_call_target="tpu_custom_call" | custom-call | flops 6845104128 | bytes 3276800 | tf_op jit(solution)/shard_map/pallas_call | solution.py:273
  197.4 2.3 gather_fusion.4
  199.8 0.7 copy.49
  200.4 0.2 convert_multiply_fusion.1
  200.6 4.3 %fusion.19 = (bf16[1,32,8,8,128]{4,3,2,1,0:T(8,128)(2,1)S(1)}, bf16[1,32,8,8,128]{4,3,2,1,0:T(8,128)(2,1)S(1)}) fusion(f32[1,32,128,128]{2,3,1,0:T(8,128)S(1)} %convert_multiply_fusion.1, f32[64]{0:T(128)S(1)} %negate_power_fusion, f32[32,128]{1,0:T(8,128)S(1)} %add_convert_fusion), kind=kLoop, calls=%fused_computation.45 | loop fusion | flops 2359296 | bytes 3162368
  204.9 0.1 copy.64
  205.0 0.1 copy.65
  205.1 1.1 maximum_bitcast_fusion.1.refs_2_
  206.2 7.3 %shard_map.92.refs_4_ = f32[1,256,1024]{2,1,0:T(8,128)} custom-call(f32[1,1,4096]{2,1,0:T(1,128)} %compare_select_fusion.refs_0_, bf16[1,256,1024]{2,1,0:T(8,128)(2,1)} %get-tuple-element.28.refs_1_, bf16[1,128,4352]{2,1,0:T(8,128)(2,1)} %maximum_bitcast_fusion.1.refs_2_), custom_call_target="tpu_custom_call" | custom-call | flops 2281701376 | bytes 3276800 | tf_op jit(solution)/shard_map/pallas_call | solution.py:273
  213.5 7.5 %all-to-all-done.3 = bf16[8,1,8,128,128]{4,3,2,1,0:T(8,128)(2,1)} async-done(((bf16[8,1,8,128,128]{4,3,2,1,0:T(8,128)(2,1)}), bf16[8,1,8,128,128]{4,3,2,1,0:T(8,128)(2,1)}, u32[]{:S(2)}, u32[]{:S(2)}) %all-to-all-start.3) | async-done | bytes 2097184 | tf_op jit(solution)/shard_map/all_to_all | solution.py:131
  221.0 2.3 gather_fusion.5
  223.3 0.7 fusion.1
  224.1 1.1 pad_maximum_fusion.1.refs_3_
  225.1 18.2 %shard_map.93 = bf16[1,256,2048]{2,1,0:T(8,128)(2,1)} custom-call(f32[1,1,4096]{2,1,0:T(1,128)} %compare_select_fusion.refs_0_, bf16[1,256,1024]{2,1,0:T(8,128)(2,1)} %get-tuple-element.28.refs_1_, bf16[1,128,4352]{2,1,0:T(8,128)(2,1)} %maximum_bitcast_fusion.1.refs_2_, ...), custom_call_target="tpu_custom_call", output_to_operand_aliasing={{}: (5, {})} | custom-call | flops 4563402752 | bytes 3276800 | tf_op jit(solution)/shard_map/pallas_call | solution.py:273
  (23 shorter events, 0.2 us)
Async XLA Ops:
  0.0 11.9 %copy-start.1 = (bf16[16,128,256]{2,1,0:T(8,128)(2,1)S(1)}, bf16[16,128,256]{2,1,0:T(8,128)(2,1)}, u32[]{:S(2)}) copy-start(bf16[16,128,256]{2,1,0:T(8,128)(2,1)} %param.13) | copy-start | bytes 3145732
  3.3 13.7 %all-to-all-start = ((s32[8,1,72]{2,1,0:T(1,128)}), s32[8,1,72]{2,1,0:T(1,128)S(1)}, u32[]{:S(2)}, u32[]{:S(2)}) async-start(s32[8,1,72]{2,1,0:T(1,128)} %pad_add_fusion), calls=%async_computation | async-start | bytes 8192 | tf_op jit(solution)/shard_map/all_to_all | solution.py:82
  19.9 96.6 %all-to-all-start.2 = ((bf16[8,1,8,128,256]{4,3,2,1,0:T(8,128)(2,1)}), bf16[8,1,8,128,256]{4,3,2,1,0:T(8,128)(2,1)}, u32[]{:S(2)}, u32[]{:S(2)}) async-start(bf16[8,1,8,128,256]{4,3,2,1,0:T(8,128)(2,1)} %bitcast.78), calls=%async_computation.2 | async-start | bytes 8388608 | tf_op jit(solution)/shard_map/all_to_all | solution.py:136
  116.4 4.5 %copy-start.2 = (bf16[1,256,256]{2,1,0:T(8,128)(2,1)S(1)}, bf16[1,256,256]{2,1,0:T(8,128)(2,1)}, u32[]{:S(2)}) copy-start(bf16[1,256,256]{2,1,0:T(8,128)(2,1)} %param.10) | copy-start | bytes 393220
  116.5 4.8 %copy-start = (bf16[1,256,2048]{2,1,0:T(8,128)(2,1)S(1)}, bf16[1,256,2048]{2,1,0:T(8,128)(2,1)}, u32[]{:S(2)}) copy-start(bf16[1,256,2048]{2,1,0:T(8,128)(2,1)} %param.9) | copy-start | bytes 3145732
  116.5 52.3 %all-to-all-start.1 = ((bf16[8,1,8,128,128]{4,3,2,1,0:T(8,128)(2,1)}), bf16[8,1,8,128,128]{4,3,2,1,0:T(8,128)(2,1)}, u32[]{:S(2)}, u32[]{:S(2)}) async-start(bf16[8,1,8,128,128]{4,3,2,1,0:T(8,128)(2,1)} %get-tuple-element.14), calls=%async_computation.1 | async-start | bytes 4194304 | tf_op jit(solution)/shard_map/all_to_all | solution.py:125
  123.7 0.7 copy-start.4
  123.7 0.9 copy-start.3
  168.7 52.3 %all-to-all-start.3 = ((bf16[8,1,8,128,128]{4,3,2,1,0:T(8,128)(2,1)}), bf16[8,1,8,128,128]{4,3,2,1,0:T(8,128)(2,1)}, u32[]{:S(2)}, u32[]{:S(2)}) async-start(bf16[8,1,8,128,128]{4,3,2,1,0:T(8,128)(2,1)} %get-tuple-element.13), calls=%async_computation.3 | async-start | bytes 4194304 | tf_op jit(solution)/shard_map/all_to_all | solution.py:131

commit v8 on v5

v8 whole, which is shorter than its diff:
```python
import functools

import jax
import jax.numpy as jnp
from jax import lax
from jax.experimental import pallas as pl
from jax.experimental.pallas import tpu as pltpu
from jax.sharding import PartitionSpec as P

rope_base = 500000.0


def apply_rotary(x, pos):
    half = x.shape[-1] // 2
    inv = rope_base ** (-(jnp.arange(half, dtype=jnp.float32) * 2.0 / x.shape[-1]))
    angle = pos.astype(jnp.float32)[..., None] * inv
    cosine = jnp.cos(angle)
    sine = jnp.sin(angle)
    first = x[..., :half]
    second = x[..., half:]
    return jnp.concatenate(
        [first * cosine - second * sine, second * cosine + first * sine], axis=-1
    )


def slot_tables(slot_stretch_ids, counts, positions, owners, capacity, per_owner):
    rows, slots = slot_stretch_ids.shape
    owner = slot_stretch_ids // per_owner
    local = slot_stretch_ids % per_owner
    slot_iota = jnp.arange(slots, dtype=jnp.int32)
    live = slot_iota[None, :] < counts[:, None]
    same = owner[:, :, None] == owner[:, None, :]
    earlier = slot_iota[:, None] < slot_iota[None, :]
    rank = jnp.sum((same & earlier[None, :, :] & live[:, :, None]).astype(jnp.int32), axis=1)
    target = owner * capacity + rank
    hits = (
        target[:, :, None] == jnp.arange(owners * capacity, dtype=jnp.int32)[None, None, :]
    ) & live[:, :, None]
    hits = hits.astype(jnp.int32)
    local_table = jnp.sum(hits * (local + 1)[:, :, None], axis=1) - 1
    place_table = jnp.sum(hits * positions[:, :, None], axis=1)
    return (
        local_table.reshape(rows, owners, capacity),
        place_table.reshape(rows, owners, capacity),
        owner,
        rank,
        live,
    )


def shards(
    queries,
    fresh_keys,
    fresh_values,
    stored_stretch_keys,
    stored_stretch_values,
    scales,
    stretch_ids,
    counts,
    stretch_pos,
):
    owners = lax.axis_size("stretch")
    half = owners // 2
    rows, slots = stretch_ids.shape
    per_owner, span, width = stored_stretch_keys.shape
    kv_heads = scales.shape[2]
    head_dim = width // kv_heads
    q_heads = queries.shape[2] // head_dim
    request_group = q_heads // kv_heads
    tokens = queries.shape[1]
    capacity = 2 * slots // owners
    cache_length = slots * span
    me = lax.axis_index("stretch")
    across = [(i, (i + half) % owners) for i in range(owners)]
    mine = slot_tables(stretch_ids, counts, stretch_pos, owners, capacity, per_owner)
    owner, rank, live = (mine[2], mine[3], mine[4])
    scale_code = (scales.astype(jnp.float32) * 65536.0).astype(jnp.int32).reshape(1, 1, -1)
    requests = jnp.concatenate(
        [
            jnp.transpose(mine[0], (1, 0, 2)),
            jnp.broadcast_to(scale_code, (owners, rows, scale_code.shape[2])),
        ],
        axis=2,
    )
    answers = lax.all_to_all(requests, "stretch", split_axis=0, concat_axis=0, tiled=True)
    wanted = jnp.maximum(answers[:, :, :capacity], 0)
    all_scales = (answers[:, 0, capacity:].astype(jnp.float32) * (1.0 / 65536.0)).reshape(
        owners * per_owner, 2, kv_heads
    )
    meta = jnp.concatenate([stretch_ids, stretch_pos, counts[:, None]], axis=1)
    meta_far = lax.ppermute(meta, "stretch", across)
    ids_far, pos_far, counts_far = (
        meta_far[:, :slots], meta_far[:, slots:2 * slots], meta_far[:, 2 * slots]
    )
    queries_far = lax.ppermute(queries, "stretch", across)
    far = slot_tables(ids_far, counts_far, pos_far, owners, capacity, per_owner)
    owner_far, rank_far, live_far = (far[2], far[3], far[4])

    store = jnp.concatenate(
        [
            jnp.concatenate(
                [
                    stored_stretch_keys[..., h * head_dim:(h + 1) * head_dim],
                    stored_stretch_values[..., h * head_dim:(h + 1) * head_dim],
                ],
                axis=-1,
            )
            for h in range(kv_heads)
        ],
        axis=-1,
    )
    side = me // half
    local = me % half
    received = []
    for shift in range(half):
        target_local = (local + shift) % half
        target = side * half + target_local
        partner = (target + half) % owners
        choice = jnp.concatenate(
            [
                lax.dynamic_index_in_dim(wanted, target, 0, keepdims=False),
                lax.dynamic_index_in_dim(wanted, partner, 0, keepdims=False),
            ],
            axis=1,
        )
        payload = store[choice]
        if shift:
            pairs = [
                (i, (i // half) * half + (i % half + shift) % half) for i in range(owners)
            ]
            payload = lax.ppermute(payload, "stretch", pairs)
        received.append(payload)
    received = jnp.stack(received, axis=0).reshape(half * rows * 2 * capacity, span, 2 * width)

    def entries(owner_of, rank_of, live_of, second):
        near = (owner_of // half) == side
        shift = (local - owner_of % half) % half
        position = ((shift * rows + jnp.arange(rows, dtype=jnp.int32)[:, None]) * 2 + second) * capacity + rank_of
        use = live_of & near
        return jnp.where(use, position, 0), use

    token_positions = cache_length + jnp.arange(tokens, dtype=jnp.int32)

    def rotate_queries(raw):
        rotated = (
            apply_rotary(
                raw.reshape(rows, tokens, q_heads, head_dim).astype(jnp.float32),
                token_positions[:, None],
            )
            * head_dim ** (-0.5)
        ).astype(jnp.bfloat16)
        return rotated.reshape(rows, tokens, q_heads * head_dim)

    def partial(raw_queries, ids_of, pos_of, owner_of, rank_of, live_of, second, with_fresh, out_dtype):
        position, use = entries(owner_of, rank_of, live_of, second)
        got = received[position]
        slot_scale = all_scales[ids_of]
        placement = pos_of[:, :, None] + jnp.arange(span, dtype=jnp.int32)
        query_rot = rotate_queries(raw_queries)
        bias = jnp.where(jnp.repeat(use, span, axis=1), 0.0, -1e30).astype(jnp.float32)[:, None, :]
        outs = []
        for head in range(kv_heads):
            base = head * 2 * head_dim
            keys = got[..., base:base + head_dim].astype(jnp.float32) * slot_scale[:, :, 0, head][:, :, None, None]
            keys = apply_rotary(keys, placement).astype(jnp.bfloat16).reshape(rows, cache_length, head_dim)
            vals = got[..., base + head_dim:base + 2 * head_dim].astype(jnp.float32)
            vals = (vals * slot_scale[:, :, 1, head][:, :, None, None]).astype(jnp.bfloat16)
            vals = vals.reshape(rows, cache_length, head_dim)
            if with_fresh:
                cols = slice(head * head_dim, (head + 1) * head_dim)
                new_keys = apply_rotary(
                    fresh_keys[..., cols].astype(jnp.float32), token_positions
                ).astype(jnp.bfloat16)
                keys = jnp.concatenate([keys, new_keys], axis=1)
                vals = jnp.concatenate([vals, fresh_values[..., cols]], axis=1)
            group_cols = slice(head * request_group * head_dim, (head + 1) * request_group * head_dim)
            outs.append(
                flash(query_rot[..., group_cols], jnp.swapaxes(keys, 1, 2), vals, bias,
                      request_group, cache_length, out_dtype)
            )
        return [jnp.concatenate([o[i] for o in outs], axis=-1) for i in range(3)]

    far_out, far_top, far_total = partial(
        queries_far, ids_far, pos_far, owner_far, rank_far, live_far, 1, False, jnp.bfloat16
    )
    far_stats = jnp.concatenate([far_top[..., ::head_dim], far_total[..., ::head_dim]], axis=-1)
    back_out = lax.ppermute(far_out, "stretch", across)
    back_stats = lax.ppermute(far_stats, "stretch", across)
    near_out, near_top, near_total = partial(
        queries, stretch_ids, stretch_pos, owner, rank, live, 0, True, jnp.float32
    )
    back_top = jnp.repeat(back_stats[..., :q_heads], head_dim, axis=-1)
    back_total = jnp.repeat(back_stats[..., q_heads:], head_dim, axis=-1)
    top = jnp.maximum(near_top, back_top)
    near_weight = near_total * jnp.exp(near_top - top)
    back_weight = back_total * jnp.exp(back_top - top)
    mixed = near_out * near_weight + back_out.astype(jnp.float32) * back_weight
    return (mixed / (near_weight + back_weight)).astype(jnp.bfloat16)


def flash_kernel(*refs, cache_length, chunk, heads, fresh):
    bias_ref, q_ref, k_ref, v_ref = refs[:4]
    o_ref, m_ref, l_ref = refs[-3:]
    tokens = q_ref.shape[0]
    lanes = 128
    new_mask = lax.broadcasted_iota(jnp.int32, (tokens, tokens), 1) <= lax.broadcasted_iota(
        jnp.int32, (tokens, tokens), 0
    )

    def fold(acc, s, op):
        for b in range(s.shape[1] // lanes):
            acc = op(acc, s[:, b * lanes:(b + 1) * lanes])
        return acc

    for head in range(heads):
        q = q_ref[:, head * lanes:(head + 1) * lanes]

        def scores(first, size):
            return lax.dot_general(
                q, k_ref[:, first:first + size], (((1,), (0,)), ((), ())),
                preferred_element_type=jnp.float32,
            )

        def masked(first, size):
            return scores(first, size) + bias_ref[:, first:first + size]

        top = jnp.full((tokens, lanes), -1e30, jnp.float32)
        if fresh:
            recent = jnp.where(new_mask, scores(cache_length, tokens), -1e30)
            top = fold(top, recent, jnp.maximum)
        for first in range(0, cache_length, chunk):
            top = fold(top, masked(first, chunk), jnp.maximum)
        top = jnp.max(top, axis=1, keepdims=True)

        def mix(s, first, size):
            p = jnp.exp(s - top)
            return p, lax.dot_general(
                p.astype(jnp.bfloat16), v_ref[first:first + size, :], (((1,), (0,)), ((), ())),
                preferred_element_type=jnp.float32,
            )

        total = jnp.zeros((tokens, lanes), jnp.float32)
        acc = jnp.zeros((tokens, lanes), jnp.float32)
        if fresh:
            p, acc = mix(recent, cache_length, tokens)
            total = fold(total, p, jnp.add)
        for first in range(0, cache_length, chunk):
            p, part = mix(masked(first, chunk), first, chunk)
            total = fold(total, p, jnp.add)
            acc = acc + part
        total = jnp.sum(total, axis=1, keepdims=True)
        cols = slice(head * lanes, (head + 1) * lanes)
        o_ref[:, cols] = (acc / total).astype(o_ref.dtype)
        m_ref[:, cols] = jnp.broadcast_to(top, (tokens, lanes))
        l_ref[:, cols] = jnp.broadcast_to(total, (tokens, lanes))


CHUNK = 512
HEADS = 4


def flash(query_rot, keys_t, values_all, bias, request_group, cache_length, out_dtype):
    rows, tokens, q_width = query_rot.shape
    head_dim, length = keys_t.shape[1:]
    fresh = length > cache_length
    chunk = CHUNK if cache_length % CHUNK == 0 else 128
    heads = HEADS
    kernel = functools.partial(
        flash_kernel, cache_length=cache_length, chunk=chunk, heads=heads, fresh=fresh
    )
    per = request_group // heads
    q_spec = pl.BlockSpec((None, tokens, head_dim * heads), lambda r, g: (r, 0, g))
    passes = 3
    return pl.pallas_call(
        kernel,
        grid=(rows, per),
        in_specs=[
            pl.BlockSpec((None, 1, cache_length), lambda r, g: (r, 0, 0)),
            q_spec,
            pl.BlockSpec((None, head_dim, length), lambda r, g: (r, 0, 0)),
            pl.BlockSpec((None, length, head_dim), lambda r, g: (r, 0, 0)),
        ],
        out_specs=[q_spec, q_spec, q_spec],
        out_shape=[
            jax.ShapeDtypeStruct((rows, tokens, q_width), out_dtype),
            jax.ShapeDtypeStruct((rows, tokens, q_width), jnp.float32),
            jax.ShapeDtypeStruct((rows, tokens, q_width), jnp.float32),
        ],
        cost_estimate=pl.CostEstimate(
            flops=2 * passes * rows * tokens * q_width * length,
            transcendentals=rows * tokens * (q_width // head_dim) * length,
            bytes_accessed=2 * rows * (2 * tokens * q_width + 2 * length * head_dim),
        ),
    )(bias, query_rot, keys_t, values_all)


def solution(mesh):
    return jax.shard_map(
        shards,
        mesh=mesh,
        in_specs=(
            P(("grp", "stretch"), None, "req"),
            P(("grp", "stretch"), None, "req"),
            P(("grp", "stretch"), None, "req"),
            P(("grp", "stretch"), None, "req"),
            P(("grp", "stretch"), None, "req"),
            P(("grp", "stretch"), None, "req"),
            P(("grp", "stretch"), None),
            P(("grp", "stretch")),
            P(("grp", "stretch"), None),
        ),
        out_specs=P(("grp", "stretch"), None, "req"),
        check_vma=False,
    )
```

time: 258 us -> 325 us (1.26); the launches traced: 258 us -> 320 us
  local copies, waits for them, and re-layouts: 30.8 us -> 77.1 us
  waiting for transfers between devices: 141 us -> 96.4 us
  other arithmetic: 29.4 us -> 63.1 us
  Pallas kernels: 33 us -> 65.6 us
  blocking collectives: 13.5 us -> 0 us
  starting transfers between devices: 9.14 us -> 16 us
    all_to_all x2 -> x1, waiting for transfers between devices: 141 us -> 23.1 us  [shards(): lax.all_to_all(requests, 'stretch', split_axis=0, concat_axis=0, tiled=True)]
    ppermute x0 -> x7, waiting for transfers between devices: none -> 73.3 us  [the longest x3 73.3 us: shards(): payload = lax.ppermute(payload, 'stretch', pairs)]
    pallas_call x2 -> x4, Pallas kernels: 33 us -> 65.6 us  [flash(): pl.pallas_call(kernel, grid=(rows, per), in_specs=[pl.BlockSpec((None, 1,...]
    gather x8 -> x12, local copies, waits for them, and re-layouts: 21.1 us -> 35.1 us  [the longest x4 25.6 us: partial(): got = received[position]]
    all_to_all x1 -> x0, blocking collectives: 13.5 us -> none  [shards(): lax.all_to_all(requests, 'stretch', split_axis=0, concat_axis=0, tiled=True)]
    concatenate x4 -> x8, local copies, waits for them, and re-layouts: 0.37 us -> 11.4 us  [apply_rotary(): jnp.concatenate([first * cosine - second * sine, second * cosine + first...]
    ppermute x0 -> x7, starting transfers between devices: none -> 9.83 us  [the longest x1 4.04 us: shards(): meta_far = lax.ppermute(meta, 'stretch', across)]
    convert_element_type x5 -> x6, other arithmetic: 3.24 us -> 11.2 us  [the longest x1 5.36 us: shards(): return (mixed / (near_weight + back_weight)).astype(jnp.bfloat16)]
  transfers between devices with their start and end apart: 2 -> 8, of which waited for: 2 -> 4; matrix products, arithmetic and copies ran while one was open for 10% -> 19% of each run, Pallas kernels for 6% -> 11%
where the time goes in v8:
time: 325 us; the launch traced here: 320 us
  waiting for transfers between devices  96.4 us (30%)
  local copies, waits for them, and re-layouts  77.1 us (24%)
  Pallas kernels  65.6 us (20%)
  other arithmetic  63.1 us (19%)
  starting transfers between devices  16 us (5%)
    ppermute x3, waiting for transfers between devices, shards(): payload = lax.ppermute(payload, 'stretch', pairs)  73.3 us
    pallas_call x4, Pallas kernels, flash(): pl.pallas_call(kernel, grid=(rows, per), in_specs=[pl.BlockSpec((None, 1,...  65.6 us
    gather x4, local copies, waits for them, and re-layouts, partial(): got = received[position]  25.6 us
    all_to_all x1, waiting for transfers between devices, shards(): lax.all_to_all(requests, 'stretch', split_axis=0, concat_axis=0, tiled=True)  23.1 us
    unnamed x3, other arithmetic  12.9 us
    concatenate x8, local copies, waits for them, and re-layouts, apply_rotary(): jnp.concatenate([first * cosine - second * sine, second * cosine + first...  11.4 us
    concatenate x3, other arithmetic, partial(): return [jnp.concatenate([o[i] for o in outs], axis=-1) for i in range(3)]  8.24 us
    gather x4, local copies, waits for them, and re-layouts, shards(): payload = store[choice]  8.13 us
  transfers between devices with their start and end apart: 8, of which 4 were waited for; matrix products, arithmetic and copies ran while one was open for 19% of the time, Pallas kernels for 11%

profile of v8, /device:TPU:0, one launch (start us, length us, event | category | flops | bytes accessed | tf_op | source)
XLA Modules:
  0.0 319.8 jit_solution(10450361018853012586)
XLA Ops:
  0.7 1.3 pad_add_fusion.1
  1.9 4.0 %collective-permute-start.3 = (s32[1,65]{1,0:T(1,128)}, s32[1,65]{1,0:T(1,128)}, u32[]{:S(2)}, u32[]{:S(2)}) collective-permute-start(s32[1,65]{1,0:T(1,128)} %pad_add_fusion.1), channel_id=1, source_target_pairs={{0,8},{2,10},{4,12},{6,14},{8,0},{10,2},{12,4},{14,6},{1,9},{3,11}... | collective-permute-start | bytes 788 | tf_op jit(solution)/shard_map/ppermute | solution.py:91
  6.0 1.2 fusion.72
  9.6 6.1 %all-to-all-start = ((s32[8,1,72]{2,1,0:T(1,128)}), s32[8,1,72]{2,1,0:T(1,128)}, u32[]{:S(2)}, u32[]{:S(2)}) async-start(s32[8,1,72]{2,1,0:T(1,128)} %pad_add_fusion), calls=%async_computation | async-start | bytes 8192 | tf_op jit(solution)/shard_map/all_to_all | solution.py:85
  15.7 1.5 convert_bitcast_fusion.1
  17.4 1.7 copy.127
  20.7 2.6 fusion.105
  23.3 1.0 fusion.62
  24.3 1.5 pad_maximum_fusion.1
  25.8 1.2 slice.193
  30.3 1.2 pad_clamp_fusion.1
  32.2 23.1 %all-to-all-done = s32[8,1,72]{2,1,0:T(1,128)} async-done(((s32[8,1,72]{2,1,0:T(1,128)}), s32[8,1,72]{2,1,0:T(1,128)}, u32[]{:S(2)}, u32[]{:S(2)}) %all-to-all-start) | async-done | bytes 2336 | tf_op jit(solution)/shard_map/all_to_all | solution.py:85
  56.1 2.0 gather_fusion.3
  58.7 2.0 gather_fusion.2
  60.7 1.6 collective-permute-start.1
  62.4 2.1 gather_fusion.1
  65.1 2.0 gather_fusion
  70.7 1.5 convert_bitcast_fusion
  72.6 1.2 copy-done
  73.8 1.2 multiply_subtract_fusion.1
  75.0 1.1 fusion.4
  77.2 1.1 fusion.104
  78.2 1.1 fusion.103
  79.4 25.8 %collective-permute-done.2 = bf16[1,16,128,512]{3,2,1,0:T(8,128)(2,1)} collective-permute-done((bf16[1,16,128,512]{3,2,1,0:T(8,128)(2,1)}, bf16[1,16,128,512]{3,2,1,0:T(8,128)(2,1)}, u32[]{:S(2)}, u32[]{:S(2)}) %collective-permute-start.2) | collective-permute-done | bytes 2097184 | tf_op jit(solution)/shard_map/ppermute | solution.py:131
  105.1 44.8 %collective-permute-done.1 = bf16[1,16,128,512]{3,2,1,0:T(8,128)(2,1)} collective-permute-done((bf16[1,16,128,512]{3,2,1,0:T(8,128)(2,1)}, bf16[1,16,128,512]{3,2,1,0:T(8,128)(2,1)}, u32[]{:S(2)}, u32[]{:S(2)}) %collective-permute-start.1) | collective-permute-done | bytes 2097184 | tf_op jit(solution)/shard_map/ppermute | solution.py:131
  149.9 2.7 collective-permute-done
  152.6 6.8 %pad_maximum_fusion = bf16[4,1,16,128,512]{4,3,2,1,0:T(8,128)(2,1)} fusion(bf16[1,1,16,128,512]{4,3,2,1,0:T(8,128)(2,1)} %bitcast.26, bf16[1,1,16,128,512]{4,3,2,1,0:T(8,128)(2,1)} %bitcast.21, bf16[1,1,16,128,512]{4,3,2,1,0:T(8,128)(2,1)} %bitcast.16, bf16[1,1,16,128,512]{4,3,2,1,0:T(8,128)(2,1)S(1)} %bitcast.169), kind=kLoop, calls=%fused_computation.8 | loop fusion | flops 12582912 | bytes 16777216 | tf_op jit(solution)/shard_map/stack | solution.py:133
  159.4 6.2 %gather_fusion.4 = bf16[32,128,512]{2,1,0:T(8,128)(2,1)} fusion(bf16[64,128,512]{2,1,0:T(8,128)(2,1)} %bitcast.163, s32[1024]{0:T(1024)} %get-tuple-element.119), kind=kCustom, calls=%fused_computation.4 | custom fusion | bytes 8388736 | tf_op jit(solution)/shard_map/gather | solution.py:156
  165.6 6.6 %copy.95 = bf16[32,128,512]{1,2,0:T(8,128)(2,1)} copy(bf16[32,128,512]{2,1,0:T(8,128)(2,1)} %gather_fusion.4) | data formatting | bytes 8388608 | tf_op jit(solution)/shard_map/gather | solution.py:156
  172.2 6.2 %gather_fusion.6 = bf16[32,128,512]{2,1,0:T(8,128)(2,1)} fusion(bf16[64,128,512]{2,1,0:T(8,128)(2,1)} %bitcast.164, s32[1024]{0:T(1024)} %get-tuple-element.118), kind=kCustom, calls=%fused_computation.6 | custom fusion | bytes 8388736 | tf_op jit(solution)/shard_map/gather | solution.py:156
  178.5 6.5 %copy.105 = bf16[32,128,512]{1,2,0:T(8,128)(2,1)} copy(bf16[32,128,512]{2,1,0:T(8,128)(2,1)} %gather_fusion.6) | data formatting | bytes 8388608 | tf_op jit(solution)/shard_map/gather | solution.py:156
  185.0 3.1 multiply_convert_fusion.2
  188.5 1.6 multiply_convert_fusion.1
  190.1 10.0 %fusion.46 = (bf16[1,32,8,8,128]{4,3,2,1,0:T(8,128)(2,1)}, bf16[1,32,8,8,128]{4,3,2,1,0:T(8,128)(2,1)}, bf16[1,32,8,8,128]{4,3,2,1,0:T(8,128)(2,1)}, bf16[1,32,8...) fusion(f32[1,32,128,128]{2,3,1,0:T(8,128)S(1)} %get-tuple-eleme, ...), kind=kLoop, calls=%fused_computation.96 | loop fusion | flops 8912896 | bytes 12615936
  201.0 0.9 copy.138
  201.9 2.3 copy.112
  204.2 1.9 copy.139
  206.1 1.9 copy.140
  208.1 1.3 copy.109
  209.4 2.4 maximum_bitcast_fusion.3.refs_2_
  211.7 1.1 maximum_bitcast_fusion.2.refs_2_
  213.5 15.8 %shard_map.94 = (bf16[1,256,1024]{2,1,0:T(8,128)(2,1)}, f32[1,256,1024]{2,1,0:T(8,128)}, f32[1,256,1024]{2,1,0:T(8,128)}) custom-call(f32[1,1,4096]{2,1,0:T(1,128)} %bitcast.187, bf16[1,256,1024]{2,1,0:T(8,128)(2,1)} %get-tuple-element.56.refs_1_, bf16[1,128,4096]{2,1,0:T(8,128)(2,1)} %maximum_bitcast_fusion.3.refs_2_, bf16[1,4096,128]{2,1,0:T(8,128)(2,1)} %bitcast.184), custom_call_target="tpu_custom_call" | custom-call | flops 6442450944 | bytes 3145728 | tf_op jit(solution)/shard_map/pallas_call | solution.py:274
  229.3 16.1 %shard_map.93 = (bf16[1,256,1024]{2,1,0:T(8,128)(2,1)}, f32[1,256,1024]{2,1,0:T(8,128)}, f32[1,256,1024]{2,1,0:T(8,128)}) custom-call(f32[1,1,4096]{2,1,0:T(1,128)} %bitcast.188, bf16[1,256,1024]{2,1,0:T(8,128)(2,1)} %get-tuple-element.55.refs_1_, bf16[1,128,4096]{2,1,0:T(8,128)(2,1)} %maximum_bitcast_fusion.2.refs_2_, bf16[1,4096,128]{2,1,0:T(8,128)(2,1)} %bitcast.183), custom_call_target="tpu_custom_call" | custom-call | flops 6442450944 | bytes 3145728 | tf_op jit(solution)/shard_map/pallas_call | solution.py:274
  245.4 3.2 %pad_maximum_fusion.3 = f32[1,256,2048]{2,1,0:T(8,128)} fusion(f32[1,256,1024]{2,1,0:T(8,128)} %get-tuple-element.26, f32[1,256,1024]{2,1,0:T(8,128)} %get-tuple-element.25), kind=kLoop, calls=%fused_computation.24 | loop fusion | flops 524288 | bytes 4194304 | tf_op jit(solution)/shard_map/concatenate | solution.py:181
  248.6 1.9 slice.213
  250.6 2.8 pad_maximum_fusion.2
  253.4 2.0 slice.212
  255.4 1.4 collective-permute-start.5
  256.9 2.3 pad_maximum_fusion.6
  259.1 1.5 collective-permute-start.6
  260.7 0.9 copy.143
  263.1 2.0 copy.141
  265.1 1.9 copy.142
  267.7 1.1 pad_maximum_fusion.4.refs_3_
  268.8 1.1 pad_maximum_fusion.5.refs_3_
  269.9 1.1 maximum_bitcast_fusion.refs_2_
  271.7 16.9 %shard_map.91 = (f32[1,256,1024]{2,1,0:T(8,128)}, f32[1,256,1024]{2,1,0:T(8,128)}, f32[1,256,1024]{2,1,0:T(8,128)}) custom-call(f32[1,1,4096]{2,1,0:T(1,128)} %bitcast.185, bf16[1,256,1024]{2,1,0:T(8,128)(2,1)} %get-tuple-element.54.refs_1_, bf16[1,128,4352]{2,1,0:T(8,128)(2,1)} %maximum_bitcast_fusion.refs_2_, bf16[1,4352,128]{2,1,0:T(8,128)(2,1)} %pad_maximum_fusion.4.refs_3_), custom_call_target="tpu_custom_call" | custom-call | flops 6845104128 | bytes 3276800 | tf_op jit(solution)/shard_map/pallas_call | solution.py:274
  288.6 1.1 maximum_bitcast_fusion.1.refs_2_
  290.3 16.8 %shard_map.92 = (f32[1,256,1024]{2,1,0:T(8,128)}, f32[1,256,1024]{2,1,0:T(8,128)}, f32[1,256,1024]{2,1,0:T(8,128)}) custom-call(f32[1,1,4096]{2,1,0:T(1,128)} %bitcast.186, bf16[1,256,1024]{2,1,0:T(8,128)(2,1)} %get-tuple-element.53.refs_1_, bf16[1,128,4352]{2,1,0:T(8,128)(2,1)} %maximum_bitcast_fusion.1.refs_2_, bf16[1,4352,128]{2,1,0:T(8,128)(2,1)} %pad_maximum_fusion.5.refs_3_), custom_call_target="tpu_custom_call" | custom-call | flops 6845104128 | bytes 3276800 | tf_op jit(solution)/shard_map/pallas_call | solution.py:274
  307.1 1.3 constant_dynamic-update-slice_fusion
  308.4 1.3 copy-done.3
  310.5 1.5 broadcast_in_dim.53
  312.7 1.5 broadcast_in_dim.51
  314.3 5.4 %fusion.8 = bf16[1,256,2048]{2,1,0:T(8,128)(2,1)} fusion(f32[1,256,2048]{2,1,0:T(8,128)} %broadcast_in_dim.53, f32[1,256,2048]{2,1,0:T(8,128)} %broadcast_in_dim.51, bf16[1,256,2048]{2,1,0:T(8,128)(2,1)} %collective-permute-done.6, f32[1,256,2048]{2,1,0:T(8,128)} %copy-done.3, f32[1,256,1024]{2,1,0:T(8,128)} %get-tuple-element.20, ...), kind=kLoop, calls=%fused_computation.39 | loop fusion | flops 7340032 | bytes 12582912 | tf_op jit(solution)/shard_map/convert_element_type | solution.py:198
  (146 shorter events, 21.9 us)
Async XLA Ops:
  1.9 23.9 %collective-permute-start.3 = (s32[1,65]{1,0:T(1,128)}, s32[1,65]{1,0:T(1,128)}, u32[]{:S(2)}, u32[]{:S(2)}) collective-permute-start(s32[1,65]{1,0:T(1,128)} %pad_add_fusion.1), channel_id=1, source_target_pairs={{0,8},{2,10},{4,12},{6,14},{8,0},{10,2},{12,4},{14,6},{1,9},{3,11}... | collective-permute-start | bytes 788 | tf_op jit(solution)/shard_map/ppermute | solution.py:91
  6.0 64.7 %collective-permute-start.4 = (bf16[1,256,2048]{2,1,0:T(8,128)(2,1)}, bf16[1,256,2048]{2,1,0:T(8,128)(2,1)}, u32[]{:S(2)}, u32[]{:S(2)}) collective-permute-start(bf16[1,256,2048]{2,1,0:T(8,128)(2,1)} %param.9), channel_id=1, source_target_pairs={{0,8},{2,10},{4,12},{6,14},{8,0},{10,2},{12,4},{14,6},{1,9},{3,11}... | collective-permute-start | bytes 3145736 | tf_op jit(solution)/shard_map/ppermute | solution.py:95
  9.6 45.7 %all-to-all-start = ((s32[8,1,72]{2,1,0:T(1,128)}), s32[8,1,72]{2,1,0:T(1,128)}, u32[]{:S(2)}, u32[]{:S(2)}) async-start(s32[8,1,72]{2,1,0:T(1,128)} %pad_add_fusion), calls=%async_computation | async-start | bytes 8192 | tf_op jit(solution)/shard_map/all_to_all | solution.py:85
  17.2 2.9 copy-start.23
  17.2 2.9 copy-start.26
  17.4 1.8 copy-start.36
  17.4 2.4 copy-start.20
  17.4 2.7 copy-start.21
  19.2 1.5 copy-start.14
  20.7 2.6 copy-start.24
  20.7 2.6 copy-start.27
  58.1 47.0 %collective-permute-start.2 = (bf16[1,16,128,512]{3,2,1,0:T(8,128)(2,1)}, bf16[1,16,128,512]{3,2,1,0:T(8,128)(2,1)}, u32[]{:S(2)}, u32[]{:S(2)}) collective-permute-start(bf16[1,16,128,512]{3,2,1,0:T(8,128)(2,1)} %bitcast.176), channel_id=1, source_target_pairs={{0,6},{2,0},{4,2},{6,4},{8,14},{10,8},{12,10},{14,12},{1,7},{3,1},... | collective-permute-start | bytes 6291464 | tf_op jit(solution)/shard_map/ppermute | solution.py:131
  60.7 89.2 %collective-permute-start.1 = (bf16[1,16,128,512]{3,2,1,0:T(8,128)(2,1)}, bf16[1,16,128,512]{3,2,1,0:T(8,128)(2,1)}, u32[]{:S(2)}, u32[]{:S(2)}) collective-permute-start(bf16[1,16,128,512]{3,2,1,0:T(8,128)(2,1)} %bitcast.177), channel_id=1, source_target_pairs={{0,4},{2,6},{4,0},{6,2},{8,12},{10,14},{12,8},{14,10},{1,5},{3,7},... | collective-permute-start | bytes 6291464 | tf_op jit(solution)/shard_map/ppermute | solution.py:131
  64.4 88.2 %collective-permute-start = (bf16[1,16,128,512]{3,2,1,0:T(8,128)(2,1)}, bf16[1,16,128,512]{3,2,1,0:T(8,128)(2,1)}, u32[]{:S(2)}, u32[]{:S(2)}) collective-permute-start(bf16[1,16,128,512]{3,2,1,0:T(8,128)(2,1)} %bitcast.178), channel_id=1, source_target_pairs={{0,2},{2,4},{4,6},{6,0},{8,10},{10,12},{12,14},{14,8},{1,3},{3,5},... | collective-permute-start | bytes 6291464 | tf_op jit(solution)/shard_map/ppermute | solution.py:131
  72.2 1.6 copy-start
  77.2 75.5 %copy-start.2 = (bf16[16,128,512]{2,1,0:T(8,128)(2,1)S(1)}, bf16[16,128,512]{2,1,0:T(8,128)(2,1)}, u32[]{:S(2)}) copy-start(bf16[16,128,512]{2,1,0:T(8,128)(2,1)} %gather_fusion) | copy-start | bytes 6291460
  178.4 6.5 %copy-start.32 = (f32[32]{0:T(128)S(1)}, f32[32]{0:T(128)}, u32[]{:S(2)}) copy-start(f32[32]{0:T(128)} %get-tuple-element.85) | copy-start | bytes 388
  178.4 6.5 %copy-start.33 = (f32[32]{0:T(128)S(1)}, f32[32]{0:T(128)}, u32[]{:S(2)}) copy-start(f32[32]{0:T(128)} %get-tuple-element.86) | copy-start | bytes 388
  178.4 6.5 %copy-start.34 = (f32[32]{0:T(128)S(1)}, f32[32]{0:T(128)}, u32[]{:S(2)}) copy-start(f32[32]{0:T(128)} %get-tuple-element.87) | copy-start | bytes 388
  178.5 6.5 %copy-start.35 = (f32[32]{0:T(128)S(1)}, f32[32]{0:T(128)}, u32[]{:S(2)}) copy-start(f32[32]{0:T(128)} %get-tuple-element.88) | copy-start | bytes 388
  185.0 3.5 %copy-start.1 = (bf16[32,128,512]{1,2,0:T(8,128)(2,1)S(1)}, bf16[32,128,512]{1,2,0:T(8,128)(2,1)}, u32[]{:S(2)}) copy-start(bf16[32,128,512]{1,2,0:T(8,128)(2,1)} %copy.105) | copy-start | bytes 12582916
  185.0 3.5 %copy-start.28 = (f32[32]{0:T(128)S(1)}, f32[32]{0:T(128)}, u32[]{:S(2)}) copy-start(f32[32]{0:T(128)} %get-tuple-element.89) | copy-start | bytes 388
  185.0 3.4 %copy-start.29 = (f32[32]{0:T(128)S(1)}, f32[32]{0:T(128)}, u32[]{:S(2)}) copy-start(f32[32]{0:T(128)} %get-tuple-element.90) | copy-start | bytes 388
  185.0 3.4 %copy-start.30 = (f32[32]{0:T(128)S(1)}, f32[32]{0:T(128)}, u32[]{:S(2)}) copy-start(f32[32]{0:T(128)} %get-tuple-element.91) | copy-start | bytes 388
  185.0 3.4 %copy-start.31 = (f32[32]{0:T(128)S(1)}, f32[32]{0:T(128)}, u32[]{:S(2)}) copy-start(f32[32]{0:T(128)} %get-tuple-element.92) | copy-start | bytes 388
  188.5 1.6 copy-start.22
  188.5 1.6 copy-start.25
  209.4 2.4 copy-start.10
  209.4 2.4 copy-start.11
  209.4 3.5 %copy-start.38 = (f32[32]{0:T(128)S(1)}, f32[32]{0:T(128)}, u32[]{:S(2)}) copy-start(f32[32]{0:T(128)} %select_bitcast_fusion) | copy-start | bytes 388
  245.4 5.2 %copy-start.15 = (f32[1,256,1024]{2,1,0:T(8,128)S(1)}, f32[1,256,1024]{2,1,0:T(8,128)}, u32[]{:S(2)}) copy-start(f32[1,256,1024]{2,1,0:T(8,128)} %get-tuple-element.24) | copy-start | bytes 3145732
  253.4 7.3 %copy-start.5 = (bf16[1,32,8,8,128]{4,3,2,1,0:T(8,128)(2,1)S(1)}, bf16[1,32,8,8,128]{4,3,2,1,0:T(8,128)(2,1)}, u32[]{:S(2)}) copy-start(bf16[1,32,8,8,128]{4,3,2,1,0:T(8,128)(2,1)} %get-tuple-element.73) | copy-start | bytes 1572868
  253.4 8.2 %copy-start.4 = (bf16[1,32,8,8,128]{4,3,2,1,0:T(8,128)(2,1)S(1)}, bf16[1,32,8,8,128]{4,3,2,1,0:T(8,128)(2,1)}, u32[]{:S(2)}) copy-start(bf16[1,32,8,8,128]{4,3,2,1,0:T(8,128)(2,1)} %get-tuple-element.74) | copy-start | bytes 1572868
  255.4 53.0 %collective-permute-start.5 = (f32[1,256,32]{1,2,0:T(8,128)S(1)}, f32[1,256,32]{1,2,0:T(8,128)S(1)}, u32[]{:S(2)}, u32[]{:S(2)}) collective-permute-start(f32[1,256,32]{1,2,0:T(8,128)S(1)} %pad_maximum_fusion.7), channel_id=1, source_target_pairs={{0,8},{2,10},{4,12},{6,14},{8,0},{10,2},{12,4},{14,6},{1,9},{3,11}... | collective-permute-start | bytes 98312 | tf_op jit(solution)/shard_map/ppermute | solution.py:188
  259.1 55.1 %collective-permute-start.6 = (bf16[1,256,2048]{2,1,0:T(8,128)(2,1)}, bf16[1,256,2048]{2,1,0:T(8,128)(2,1)}, u32[]{:S(2)}, u32[]{:S(2)}) collective-permute-start(bf16[1,256,2048]{2,1,0:T(8,128)(2,1)} %pad_maximum_fusion.6), channel_id=1, source_target_pairs={{0,8},{2,10},{4,12},{6,14},{8,0},{10,2},{12,4},{14,6},{1,9},{3,11}... | collective-permute-start | bytes 3145736 | tf_op jit(solution)/shard_map/ppermute | solution.py:187
  267.7 2.2 copy-start.8
  267.7 2.2 copy-start.9
  267.7 2.2 copy-start.18
  267.7 2.2 copy-start.19
  268.8 2.2 copy-start.37
  271.7 16.9 %copy-start.6 = (bf16[1,32,8,8,128]{4,3,1,2,0:T(8,128)(2,1)S(1)}, bf16[1,32,8,8,128]{4,3,1,2,0:T(8,128)(2,1)}, u32[]{:S(2)}) copy-start(bf16[1,32,8,8,128]{4,3,1,2,0:T(8,128)(2,1)} %copy.141) | copy-start | bytes 1572868
  271.7 16.9 %copy-start.7 = (bf16[1,32,8,8,128]{4,3,1,2,0:T(8,128)(2,1)S(1)}, bf16[1,32,8,8,128]{4,3,1,2,0:T(8,128)(2,1)}, u32[]{:S(2)}) copy-start(bf16[1,32,8,8,128]{4,3,1,2,0:T(8,128)(2,1)} %copy.142) | copy-start | bytes 1572868
  271.7 16.9 %copy-start.16 = (bf16[1,256,64]{1,2,0:T(8,128)(2,1)S(1)}, bf16[1,256,64]{1,2,0:T(8,128)(2,1)}, u32[]{:S(2)}) copy-start(bf16[1,256,64]{1,2,0:T(8,128)(2,1)} %get-tuple-element.63) | copy-start | bytes 98308
  271.7 16.9 %copy-start.17 = (bf16[1,256,64]{1,2,0:T(8,128)(2,1)S(1)}, bf16[1,256,64]{1,2,0:T(8,128)(2,1)}, u32[]{:S(2)}) copy-start(bf16[1,256,64]{1,2,0:T(8,128)(2,1)} %get-tuple-element.64) | copy-start | bytes 98308
  288.6 1.6 copy-start.13
  308.4 1.4 copy-start.3
  312.7 1.6 copy-start.12

commit v9 on v7

--- a/solution.py
+++ b/solution.py
@@ -198,7 +198,7 @@
 
         fresh = jnp.where(new_mask, scores(cache_length, tokens), -1e30)
         if mode == "mix":
-            top = top_ref[:, head * lanes:head * lanes + 1]
+            top = top_ref[:, head * lanes:(head + 1) * lanes]
         else:
             top = fold(jnp.full((tokens, lanes), -1e30, jnp.float32), fresh, jnp.maximum)
             for first in range(0, cache_length, chunk):
@@ -209,7 +209,10 @@
             continue
 
         def mix(s, first, size):
-            p = jnp.exp(s - top)
+            if mode == "mix":
+                p = jnp.exp(s - jnp.tile(top, (1, size // lanes)))
+            else:
+                p = jnp.exp(s - top)
             return p, lax.dot_general(
                 p.astype(jnp.bfloat16), v_ref[first:first + size, :], (((1,), (0,)), ((), ())),
                 preferred_element_type=jnp.float32,

time: 244 us -> 244 us (level)
  no operation moved by 1% of the time
where the time goes in v9:
time: 244 us; the launch traced here: 243 us
  waiting for transfers between devices  130 us (53%)
  Pallas kernels  41.7 us (17%)
  local copies, waits for them, and re-layouts  29.7 us (12%)
  starting transfers between devices  20.8 us (9%)
  other arithmetic  19.9 us (8%)
    all_to_all x1, waiting for transfers between devices, shards(): lax.all_to_all(store[head][chosen], 'stretch', split_axis=0, concat_axis=...  84.5 us
    pallas_call x3, Pallas kernels, flash(): pl.pallas_call(kernel, grid=(rows, kv_heads, per), in_specs=in_specs, out...  41.7 us
    all_to_all x1, waiting for transfers between devices, shards(): lax.all_to_all(store[head][chosen][..., :head_dim], 'stretch', split_axis...  33.5 us
    unnamed x3, other arithmetic  8.78 us
    all_to_all x1, waiting for transfers between devices, shards(): lax.all_to_all(store[head][chosen][..., head_dim:], 'stretch', split_axis...  7.52 us
    gather x2, local copies, waits for them, and re-layouts, shards(): got = got.reshape(flat, span, 2 * head_dim)[index]  7.44 us
    all_to_all x1, starting transfers between devices, shards(): lax.all_to_all(requests, 'stretch', split_axis=0, concat_axis=0, tiled=True)  7.28 us
  transfers between devices with their start and end apart: 4, of which 4 were waited for; matrix products, arithmetic and copies ran while one was open for 16% of the time, Pallas kernels for 10%

profile of v9, /device:TPU:0, one launch (start us, length us, event | category | flops | bytes accessed | tf_op | source)
XLA Modules:
  0.0 243.2 jit_solution(4500136589534237040)
XLA Ops:
  0.0 0.8 fusion.44
  1.4 0.1 convert_reduce_fusion
  1.5 0.1 select_reduce_fusion
  1.6 0.1 sub.30
  1.7 0.7 multiply_convert_fusion.1
  2.4 0.1 copy.41
  2.5 0.1 reshape.830
  2.6 0.1 pad.15.clone
  2.7 0.6 pad_add_fusion
  3.3 7.3 %all-to-all-start = ((s32[8,1,72]{2,1,0:T(1,128)}), s32[8,1,72]{2,1,0:T(1,128)S(1)}, u32[]{:S(2)}, u32[]{:S(2)}) async-start(s32[8,1,72]{2,1,0:T(1,128)} %pad_add_fusion), calls=%async_computation | async-start | bytes 8192 | tf_op jit(solution)/shard_map/all_to_all | solution.py:82
  10.6 1.3 fusion.50
  11.9 0.3 fusion.51
  12.2 0.3 pad_maximum_fusion.2
  12.4 4.5 %all-to-all-done = s32[8,1,72]{2,1,0:T(1,128)S(1)} async-done(((s32[8,1,72]{2,1,0:T(1,128)}), s32[8,1,72]{2,1,0:T(1,128)S(1)}, u32[]{:S(2)}, u32[]{:S(2)}) %all-to-all-start) | async-done | bytes 2336 | tf_op jit(solution)/shard_map/all_to_all | solution.py:82
  17.0 0.1 reshape.759
  17.1 2.8 %gather_fusion.1 = bf16[64,128,256]{2,1,0:T(8,128)(2,1)} fusion(bf16[16,128,256]{2,1,0:T(8,128)(2,1)S(1)} %get-tuple-element.51, s32[1024]{0:T(1024)S(1)} %pad_clamp_fusion.2), kind=kCustom, calls=%fused_computation.1 | custom fusion | bytes 8388864 | tf_op jit(solution)/shard_map/gather | solution.py:136
  19.9 4.5 %all-to-all-start.2 = ((bf16[8,1,8,128,256]{4,3,2,1,0:T(8,128)(2,1)}), bf16[8,1,8,128,256]{4,3,2,1,0:T(8,128)(2,1)}, u32[]{:S(2)}, u32[]{:S(2)}) async-start(bf16[8,1,8,128,256]{4,3,2,1,0:T(8,128)(2,1)} %bitcast.78), calls=%async_computation.2 | async-start | bytes 8388608 | tf_op jit(solution)/shard_map/all_to_all | solution.py:136
  24.4 2.8 %gather_fusion = bf16[64,128,256]{2,1,0:T(8,128)(2,1)} fusion(bf16[16,128,256]{2,1,0:T(8,128)(2,1)S(1)} %get-tuple-element.50, s32[1024]{0:T(1024)S(1)} %pad_clamp_fusion.2), kind=kCustom, calls=%fused_computation | custom fusion | bytes 8388864 | tf_op jit(solution)/shard_map/gather | solution.py:126
  27.2 4.7 %fusion.49 = (bf16[8,1,8,128,128]{4,3,2,1,0:T(8,128)(2,1)}, bf16[8,1,8,128,128]{4,3,2,1,0:T(8,128)(2,1)}) fusion(bf16[8,1,8,128,256]{4,3,2,1,0:T(8,128)(2,1)} %bitcast.79), kind=kLoop, calls=%fused_computation.110 | loop fusion | bytes 8388608 | tf_op jit(solution)/shard_map/slice | solution.py:132
  32.0 84.5 %all-to-all-done.2 = bf16[8,1,8,128,256]{4,3,2,1,0:T(8,128)(2,1)} async-done(((bf16[8,1,8,128,256]{4,3,2,1,0:T(8,128)(2,1)}), bf16[8,1,8,128,256]{4,3,2,1,0:T(8,128)(2,1)}, u32[]{:S(2)}, u32[]{:S(2)}) %all-to-all-start.2) | async-done | bytes 4194336 | tf_op jit(solution)/shard_map/all_to_all | solution.py:136
  116.5 4.5 %all-to-all-start.1 = ((bf16[8,1,8,128,128]{4,3,2,1,0:T(8,128)(2,1)}), bf16[8,1,8,128,128]{4,3,2,1,0:T(8,128)(2,1)}, u32[]{:S(2)}, u32[]{:S(2)}) async-start(bf16[8,1,8,128,128]{4,3,2,1,0:T(8,128)(2,1)} %get-tuple-element.14), calls=%async_computation.1 | async-start | bytes 4194304 | tf_op jit(solution)/shard_map/all_to_all | solution.py:125
  121.0 0.1 copy.53
  121.1 0.1 copy.54
  121.3 0.2 convert_bitcast_fusion
  121.5 0.4 copy.59
  121.9 0.5 multiply_cosine_fusion.1
  122.5 0.6 multiply_subtract_fusion
  123.1 0.6 fusion
  123.7 0.5 convert_element_type.194
  124.2 0.1 copy-done.4
  124.4 0.2 copy-done.3
  124.6 0.3 fusion.31
  125.0 1.1 fusion.52
  126.1 0.6 compare_select_fusion.refs_0_
  126.7 0.1 fusion.42
  126.8 0.2 mul.363
  127.1 0.6 gather_fusion.3
  127.7 0.1 copy.44
  127.8 0.1 broadcast_bitcast_fusion
  127.8 4.2 %gather_fusion.2 = bf16[32,128,256]{2,1,0:T(8,128)(2,1)} fusion(bf16[64,128,256]{2,1,0:T(8,128)(2,1)} %bitcast.9, s32[1024]{0:T(1024)S(1)} %pad_clamp_fusion.1), kind=kCustom, calls=%fused_computation.2 | custom fusion | bytes 4194432 | tf_op jit(solution)/shard_map/gather | solution.py:140
  132.1 3.2 %copy.43 = bf16[32,128,256]{1,2,0:T(8,128)(2,1)S(1)} copy(bf16[32,128,256]{2,1,0:T(8,128)(2,1)} %gather_fusion.2) | data formatting | bytes 4194304 | tf_op jit(solution)/shard_map/gather | solution.py:140
  135.3 33.5 %all-to-all-done.1 = bf16[8,1,8,128,128]{4,3,2,1,0:T(8,128)(2,1)} async-done(((bf16[8,1,8,128,128]{4,3,2,1,0:T(8,128)(2,1)}), bf16[8,1,8,128,128]{4,3,2,1,0:T(8,128)(2,1)}, u32[]{:S(2)}, u32[]{:S(2)}) %all-to-all-start.1) | async-done | bytes 2097184 | tf_op jit(solution)/shard_map/all_to_all | solution.py:125
  168.7 4.5 %all-to-all-start.3 = ((bf16[8,1,8,128,128]{4,3,2,1,0:T(8,128)(2,1)}), bf16[8,1,8,128,128]{4,3,2,1,0:T(8,128)(2,1)}, u32[]{:S(2)}, u32[]{:S(2)}) async-start(bf16[8,1,8,128,128]{4,3,2,1,0:T(8,128)(2,1)} %get-tuple-element.13), calls=%async_computation.3 | async-start | bytes 4194304 | tf_op jit(solution)/shard_map/all_to_all | solution.py:131
  173.3 0.4 multiply_convert_fusion
  173.7 4.3 %fusion.21 = (bf16[1,32,8,8,128]{4,3,2,1,0:T(8,128)(2,1)S(1)}, bf16[1,32,8,8,128]{4,3,2,1,0:T(8,128)(2,1)S(1)}) fusion(f32[1,32,128,128]{2,3,1,0:T(8,128)S(1)} %get-tuple-element.22, f32[64]{0:T(128)S(1)} %negate_power_fusion, f32[32,128]{1,0:T(8,128)S(1)} %add_convert_fusion), kind=kLoop, calls=%fused_computation.47 | loop fusion | flops 2359296 | bytes 3162368
  178.0 0.1 copy.66
  178.1 0.1 copy.67
  178.2 0.7 copy.48
  178.8 1.1 pad_maximum_fusion.refs_3_
  179.9 1.1 maximum_bitcast_fusion.refs_2_
  181.0 16.4 %shard_map.91.refs_5_ = bf16[1,256,2048]{2,1,0:T(8,128)(2,1)} custom-call(f32[1,1,4096]{2,1,0:T(1,128)} %compare_select_fusion.refs_0_, bf16[1,256,1024]{2,1,0:T(8,128)(2,1)} %get-tuple-element.27.refs_1_, bf16[1,128,4352]{2,1,0:T(8,128)(2,1)} %maximum_bitcast_fusion.refs_2_, bf16[1,4352,128]{2,1,0:T(8,128)(2,1)} %pad_maximum_fusion.refs_3_), custom_call_target="tpu_custom_call" | custom-call | flops 6845104128 | bytes 3276800 | tf_op jit(solution)/shard_map/pallas_call | solution.py:276
  197.4 2.3 gather_fusion.4
  199.8 0.7 copy.49
  200.4 0.2 convert_multiply_fusion.1
  200.6 4.3 %fusion.19 = (bf16[1,32,8,8,128]{4,3,2,1,0:T(8,128)(2,1)S(1)}, bf16[1,32,8,8,128]{4,3,2,1,0:T(8,128)(2,1)S(1)}) fusion(f32[1,32,128,128]{2,3,1,0:T(8,128)S(1)} %convert_multiply_fusion.1, f32[64]{0:T(128)S(1)} %negate_power_fusion, f32[32,128]{1,0:T(8,128)S(1)} %add_convert_fusion), kind=kLoop, calls=%fused_computation.45 | loop fusion | flops 2359296 | bytes 3162368
  204.9 0.1 copy.64
  205.0 0.1 copy.65
  205.1 1.1 maximum_bitcast_fusion.1.refs_2_
  206.2 7.3 %shard_map.92.refs_4_ = f32[1,256,1024]{2,1,0:T(8,128)} custom-call(f32[1,1,4096]{2,1,0:T(1,128)} %compare_select_fusion.refs_0_, bf16[1,256,1024]{2,1,0:T(8,128)(2,1)} %get-tuple-element.28.refs_1_, bf16[1,128,4352]{2,1,0:T(8,128)(2,1)} %maximum_bitcast_fusion.1.refs_2_), custom_call_target="tpu_custom_call" | custom-call | flops 2281701376 | bytes 3276800 | tf_op jit(solution)/shard_map/pallas_call | solution.py:276
  213.5 7.5 %all-to-all-done.3 = bf16[8,1,8,128,128]{4,3,2,1,0:T(8,128)(2,1)} async-done(((bf16[8,1,8,128,128]{4,3,2,1,0:T(8,128)(2,1)}), bf16[8,1,8,128,128]{4,3,2,1,0:T(8,128)(2,1)}, u32[]{:S(2)}, u32[]{:S(2)}) %all-to-all-start.3) | async-done | bytes 2097184 | tf_op jit(solution)/shard_map/all_to_all | solution.py:131
  221.0 2.3 gather_fusion.5
  223.3 0.7 fusion.1
  224.1 1.1 pad_maximum_fusion.1.refs_3_
  225.1 18.0 %shard_map.93 = bf16[1,256,2048]{2,1,0:T(8,128)(2,1)} custom-call(f32[1,1,4096]{2,1,0:T(1,128)} %compare_select_fusion.refs_0_, bf16[1,256,1024]{2,1,0:T(8,128)(2,1)} %get-tuple-element.28.refs_1_, bf16[1,128,4352]{2,1,0:T(8,128)(2,1)} %maximum_bitcast_fusion.1.refs_2_, ...), custom_call_target="tpu_custom_call", output_to_operand_aliasing={{}: (5, {})} | custom-call | flops 4563402752 | bytes 3276800 | tf_op jit(solution)/shard_map/pallas_call | solution.py:276
  (23 shorter events, 0.2 us)
Async XLA Ops:
  0.0 11.9 %copy-start.1 = (bf16[16,128,256]{2,1,0:T(8,128)(2,1)S(1)}, bf16[16,128,256]{2,1,0:T(8,128)(2,1)}, u32[]{:S(2)}) copy-start(bf16[16,128,256]{2,1,0:T(8,128)(2,1)} %param.13) | copy-start | bytes 3145732
  3.3 13.7 %all-to-all-start = ((s32[8,1,72]{2,1,0:T(1,128)}), s32[8,1,72]{2,1,0:T(1,128)S(1)}, u32[]{:S(2)}, u32[]{:S(2)}) async-start(s32[8,1,72]{2,1,0:T(1,128)} %pad_add_fusion), calls=%async_computation | async-start | bytes 8192 | tf_op jit(solution)/shard_map/all_to_all | solution.py:82
  19.9 96.6 %all-to-all-start.2 = ((bf16[8,1,8,128,256]{4,3,2,1,0:T(8,128)(2,1)}), bf16[8,1,8,128,256]{4,3,2,1,0:T(8,128)(2,1)}, u32[]{:S(2)}, u32[]{:S(2)}) async-start(bf16[8,1,8,128,256]{4,3,2,1,0:T(8,128)(2,1)} %bitcast.78), calls=%async_computation.2 | async-start | bytes 8388608 | tf_op jit(solution)/shard_map/all_to_all | solution.py:136
  116.4 4.5 %copy-start.2 = (bf16[1,256,256]{2,1,0:T(8,128)(2,1)S(1)}, bf16[1,256,256]{2,1,0:T(8,128)(2,1)}, u32[]{:S(2)}) copy-start(bf16[1,256,256]{2,1,0:T(8,128)(2,1)} %param.10) | copy-start | bytes 393220
  116.5 4.8 %copy-start = (bf16[1,256,2048]{2,1,0:T(8,128)(2,1)S(1)}, bf16[1,256,2048]{2,1,0:T(8,128)(2,1)}, u32[]{:S(2)}) copy-start(bf16[1,256,2048]{2,1,0:T(8,128)(2,1)} %param.9) | copy-start | bytes 3145732
  116.5 52.3 %all-to-all-start.1 = ((bf16[8,1,8,128,128]{4,3,2,1,0:T(8,128)(2,1)}), bf16[8,1,8,128,128]{4,3,2,1,0:T(8,128)(2,1)}, u32[]{:S(2)}, u32[]{:S(2)}) async-start(bf16[8,1,8,128,128]{4,3,2,1,0:T(8,128)(2,1)} %get-tuple-element.14), calls=%async_computation.1 | async-start | bytes 4194304 | tf_op jit(solution)/shard_map/all_to_all | solution.py:125
  123.7 0.7 copy-start.4
  123.7 0.9 copy-start.3
  168.7 52.3 %all-to-all-start.3 = ((bf16[8,1,8,128,128]{4,3,2,1,0:T(8,128)(2,1)}), bf16[8,1,8,128,128]{4,3,2,1,0:T(8,128)(2,1)}, u32[]{:S(2)}, u32[]{:S(2)}) async-start(bf16[8,1,8,128,128]{4,3,2,1,0:T(8,128)(2,1)} %get-tuple-element.13), calls=%async_computation.3 | async-start | bytes 4194304 | tf_op jit(solution)/shard_map/all_to_all | solution.py:131

commit v10 on v9

--- a/solution.py
+++ b/solution.py
@@ -146,10 +146,10 @@
         )
         top = None
         if last:
-            top = flash(
-                query_head, keys_t, None, counts * span, request_group, cache_length, 0, None, 0, "top"
-            )
-            got_vals, top = lax.optimization_barrier((got_vals, top))
+            probs, total = flash(
+                query_head, keys_t, None, counts * span, request_group, cache_length, 0, None, 0, "prob"
+            )
+            got_vals, probs, total = lax.optimization_barrier((got_vals, probs, total))
             raw_v = got_vals.reshape(flat, span, head_dim)[index]
         else:
             raw_v = got[..., head_dim:]
@@ -158,11 +158,21 @@
         values_all = jnp.concatenate(
             [vals.reshape(rows, cache_length, head_dim), fresh_values[..., cols]], axis=1
         )
+        if last and results:
+            mixed = jnp.einsum(
+                "rgtl,rld->rtgd", probs, values_all, preferred_element_type=jnp.float32
+            )
+            mixed = mixed / total.reshape(rows, tokens, request_group, head_dim)
+            mixed = mixed.astype(jnp.bfloat16).reshape(rows, tokens, request_group * head_dim)
+            results.append(lax.dynamic_update_slice_in_dim(
+                results[-1], mixed, head * request_group * head_dim, axis=2
+            ))
+            continue
         results.append(
             flash(
                 query_head, keys_t, values_all, counts * span, request_group,
                 cache_length, head * request_group, results[-1] if results else None, queries.shape[2],
-                "mix" if last else "both", top,
+                "both", top,
             )
         )
     return results[-1]
@@ -170,9 +180,10 @@
 
 def flash_kernel(*refs, cache_length, chunk, heads, mode):
     bias_ref, q_ref, k_ref = refs[:3]
-    v_ref = refs[3] if mode != "top" else None
+    v_ref = refs[3] if mode not in ("top", "prob") else None
     top_ref = refs[4] if mode == "mix" else None
     o_ref = refs[-1]
+    pb_ref = refs[-2] if mode == "prob" else None
     tokens = q_ref.shape[0]
     lanes = 128
     new_mask = lax.broadcasted_iota(jnp.int32, (tokens, tokens), 1) <= lax.broadcasted_iota(
@@ -217,6 +228,18 @@
                 p.astype(jnp.bfloat16), v_ref[first:first + size, :], (((1,), (0,)), ((), ())),
                 preferred_element_type=jnp.float32,
             )
+
+        if mode == "prob":
+            p = jnp.exp(fresh - top)
+            pb_ref[head, :, cache_length:cache_length + tokens] = p.astype(pb_ref.dtype)
+            total = fold(jnp.zeros((tokens, lanes), jnp.float32), p, jnp.add)
+            for first in range(0, cache_length, chunk):
+                p = jnp.exp(masked(first, chunk) - top)
+                pb_ref[head, :, first:first + chunk] = p.astype(pb_ref.dtype)
+                total = fold(total, p, jnp.add)
+            total = jnp.sum(total, axis=1, keepdims=True)
+            o_ref[:, head * lanes:(head + 1) * lanes] = jnp.broadcast_to(total, (tokens, lanes))
+            continue
 
         p, acc = mix(fresh, cache_length, tokens)
         total = fold(jnp.zeros((tokens, lanes), jnp.float32), p, jnp.add)
@@ -253,7 +276,7 @@
         pl.BlockSpec((None, head_dim, length), lambda r, h, g: (r, h, 0)),
     ]
     operands = [bias, query_rot, keys_t]
-    if mode != "top":
+    if mode not in ("top", "prob"):
         in_specs.append(pl.BlockSpec((None, length, head_dim), lambda r, h, g: (r, 0, h)))
         operands.append(values_all)
     if mode == "mix":
@@ -264,7 +287,16 @@
         in_specs.append(pl.BlockSpec(memory_space=pl.ANY))
         aliases = {len(operands): 0}
         operands.append(into)
-    if mode == "top":
+    if mode == "prob":
+        out_specs = [
+            pl.BlockSpec((None, heads, tokens, length), lambda r, h, g: (r, h * per + g, 0, 0)),
+            pl.BlockSpec((None, tokens, head_dim * heads), lambda r, h, g: (r, 0, h * per + g)),
+        ]
+        out_shape = [
+            jax.ShapeDtypeStruct((rows, q_width // head_dim, tokens, length), jnp.bfloat16),
+            jax.ShapeDtypeStruct((rows, tokens, q_width), jnp.float32),
+        ]
+    elif mode == "top":
         out_specs = pl.BlockSpec((None, tokens, head_dim * heads), lambda r, h, g: (r, 0, h * per + g))
         out_shape = jax.ShapeDtypeStruct((rows, tokens, q_width), jnp.float32)
     else:
@@ -272,7 +304,7 @@
             (None, tokens, head_dim * heads), lambda r, h, g: (r, 0, block + h * per + g)
         )
         out_shape = jax.ShapeDtypeStruct((rows, tokens, out_width), jnp.bfloat16)
-    passes = {"both": 3, "top": 1, "mix": 2}[mode]
+    passes = {"both": 3, "top": 1, "mix": 2, "prob": 2}[mode]
     return pl.pallas_call(
         kernel,
         grid=(rows, kv_heads, per),

time: 244 us -> 245 us (level)
  matrix products: 0 us -> 12.1 us
  waiting for transfers between devices: 130 us -> 121 us
  Pallas kernels: 41.7 us -> 33.8 us
  local copies, waits for them, and re-layouts: 29.7 us -> 33.7 us
  other arithmetic: 19.9 us -> 22.5 us
    dot_general x0 -> x1, matrix products: none -> 12.1 us  [shards(): jnp.einsum('rgtl,rld->rtgd', probs, values_all, preferred_element_type=jn...]
    pallas_call x3 -> x2, Pallas kernels: 41.7 us -> 33.8 us  [flash(): pl.pallas_call(kernel, grid=(rows, kv_heads, per), in_specs=in_specs, out...]
    all_to_all x1, waiting for transfers between devices: 7.52 us -> 0.01 us  [shards(): lax.all_to_all(store[head][chosen][..., head_dim:], 'stretch', split_axis...]
    reshape x0 -> x2, local copies, waits for them, and re-layouts: none -> 2.78 us  [the longest x1 2.58 us: shards(): mixed = mixed / total.reshape(rows, tokens, request_group, head_dim)]
  transfers between devices with their start and end apart: 4 -> 4, of which waited for: 4 -> 3; matrix products, arithmetic and copies ran while one was open for 16% -> 17% of each run, Pallas kernels for 10% -> 14%
where the time goes in v10:
time: 245 us
  waiting for transfers between devices  121 us (49%)
  Pallas kernels  33.8 us (14%)
  local copies, waits for them, and re-layouts  33.7 us (14%)
  other arithmetic  22.5 us (9%)
  starting transfers between devices  20.7 us (8%)
  matrix products  12.1 us (5%)
    all_to_all x1, waiting for transfers between devices, shards(): lax.all_to_all(store[head][chosen], 'stretch', split_axis=0, concat_axis=...  83 us
    pallas_call x2, Pallas kernels, flash(): pl.pallas_call(kernel, grid=(rows, kv_heads, per), in_specs=in_specs, out...  33.8 us
    all_to_all x1, waiting for transfers between devices, shards(): lax.all_to_all(store[head][chosen][..., :head_dim], 'stretch', split_axis...  33.3 us
    dot_general x1, matrix products, shards(): jnp.einsum('rgtl,rld->rtgd', probs, values_all, preferred_element_type=jn...  12.1 us
    unnamed x3, other arithmetic  10 us
    all_to_all x1, starting transfers between devices, shards(): lax.all_to_all(requests, 'stretch', split_axis=0, concat_axis=0, tiled=True)  7.28 us
    gather x2, local copies, waits for them, and re-layouts, shards(): got = got.reshape(flat, span, 2 * head_dim)[index]  5.77 us
  transfers between devices with their start and end apart: 4, of which 3 were waited for; matrix products, arithmetic and copies ran while one was open for 17% of the time, Pallas kernels for 14%

profile of v10, /device:TPU:0, one launch (start us, length us, event | category | flops | bytes accessed | tf_op | source)
XLA Modules:
  0.0 244.6 jit_solution(12330505112678120401)
XLA Ops:
  0.0 0.8 fusion.52
  1.4 0.1 convert_reduce_fusion
  1.5 0.1 select_reduce_fusion
  1.7 0.7 multiply_convert_fusion.2
  2.4 0.1 copy.55
  2.5 0.1 reshape.848
  2.7 0.6 pad_add_fusion
  3.3 7.3 %all-to-all-start = ((s32[8,1,72]{2,1,0:T(1,128)}), s32[8,1,72]{2,1,0:T(1,128)S(1)}, u32[]{:S(2)}, u32[]{:S(2)}) async-start(s32[8,1,72]{2,1,0:T(1,128)} %pad_add_fusion), calls=%async_computation | async-start | bytes 8192 | tf_op jit(solution)/shard_map/all_to_all | solution.py:82
  10.6 1.3 fusion.61
  11.9 0.3 fusion.60
  12.2 0.3 pad_maximum_fusion.1
  12.4 4.5 %all-to-all-done = s32[8,1,72]{2,1,0:T(1,128)S(1)} async-done(((s32[8,1,72]{2,1,0:T(1,128)}), s32[8,1,72]{2,1,0:T(1,128)S(1)}, u32[]{:S(2)}, u32[]{:S(2)}) %all-to-all-start) | async-done | bytes 2336 | tf_op jit(solution)/shard_map/all_to_all | solution.py:82
  17.0 0.1 reshape.776
  17.1 2.8 %gather_fusion.1 = bf16[64,128,256]{2,1,0:T(8,128)(2,1)} fusion(bf16[16,128,256]{2,1,0:T(8,128)(2,1)S(1)} %get-tuple-element.57, s32[1024]{0:T(1024)S(1)} %pad_clamp_fusion.2), kind=kCustom, calls=%fused_computation.1 | custom fusion | bytes 8388864 | tf_op jit(solution)/shard_map/gather | solution.py:136
  19.9 4.5 %all-to-all-start.2 = ((bf16[8,1,8,128,256]{4,3,2,1,0:T(8,128)(2,1)}), bf16[8,1,8,128,256]{4,3,2,1,0:T(8,128)(2,1)}, u32[]{:S(2)}, u32[]{:S(2)}) async-start(bf16[8,1,8,128,256]{4,3,2,1,0:T(8,128)(2,1)} %bitcast.99), calls=%async_computation.2 | async-start | bytes 8388608 | tf_op jit(solution)/shard_map/all_to_all | solution.py:136
  24.4 1.5 convert_bitcast_fusion
  25.9 2.8 %gather_fusion = bf16[64,128,256]{2,1,0:T(8,128)(2,1)} fusion(bf16[16,128,256]{2,1,0:T(8,128)(2,1)S(1)} %get-tuple-element.56, s32[1024]{0:T(1024)S(1)} %pad_clamp_fusion.2), kind=kCustom, calls=%fused_computation | custom fusion | bytes 8388864 | tf_op jit(solution)/shard_map/gather | solution.py:126
  28.7 4.8 %fusion.58 = (bf16[8,1,8,128,128]{4,3,2,1,0:T(8,128)(2,1)}, bf16[8,1,8,128,128]{4,3,2,1,0:T(8,128)(2,1)}) fusion(bf16[8,1,8,128,256]{4,3,2,1,0:T(8,128)(2,1)} %bitcast.100), kind=kLoop, calls=%fused_computation.118 | loop fusion | bytes 8388608 | tf_op jit(solution)/shard_map/slice | solution.py:132
  33.5 83.0 %all-to-all-done.2 = bf16[8,1,8,128,256]{4,3,2,1,0:T(8,128)(2,1)} async-done(((bf16[8,1,8,128,256]{4,3,2,1,0:T(8,128)(2,1)}), bf16[8,1,8,128,256]{4,3,2,1,0:T(8,128)(2,1)}, u32[]{:S(2)}, u32[]{:S(2)}) %all-to-all-start.2) | async-done | bytes 4194336 | tf_op jit(solution)/shard_map/all_to_all | solution.py:136
  116.4 4.4 %all-to-all-start.1 = ((bf16[8,1,8,128,128]{4,3,2,1,0:T(8,128)(2,1)}), bf16[8,1,8,128,128]{4,3,2,1,0:T(8,128)(2,1)}, u32[]{:S(2)}, u32[]{:S(2)}) async-start(bf16[8,1,8,128,128]{4,3,2,1,0:T(8,128)(2,1)} %get-tuple-element.20), calls=%async_computation.1 | async-start | bytes 4194304 | tf_op jit(solution)/shard_map/all_to_all | solution.py:125
  120.8 0.4 copy.81
  121.2 0.5 multiply_cosine_fusion.1
  121.8 0.6 multiply_subtract_fusion
  122.4 0.6 fusion.2
  123.0 0.5 convert_element_type.200
  123.5 0.4 copy-done.1
  123.9 0.1 copy.75
  124.1 0.1 copy.74
  124.2 0.1 copy.76
  124.4 0.3 fusion.43
  124.8 1.0 fusion.59
  125.8 0.6 compare_select_fusion.refs_0_
  126.5 0.1 fusion.50
  126.5 0.2 mul.362
  126.8 0.6 gather_fusion.3
  127.4 0.1 copy.58
  127.6 2.9 %gather_fusion.2 = bf16[32,128,256]{2,1,0:T(8,128)(2,1)S(1)} fusion(bf16[64,128,256]{2,1,0:T(8,128)(2,1)} %bitcast.9, s32[1024]{0:T(1024)S(1)} %pad_clamp_fusion.1), kind=kCustom, calls=%fused_computation.2 | custom fusion | bytes 4194432 | tf_op jit(solution)/shard_map/gather | solution.py:140
  130.4 2.9 %copy.57 = bf16[32,128,256]{1,2,0:T(8,128)(2,1)} copy(bf16[32,128,256]{2,1,0:T(8,128)(2,1)S(1)} %gather_fusion.2) | data formatting | bytes 4194304 | tf_op jit(solution)/shard_map/gather | solution.py:140
  133.3 1.9 multiply_convert_fusion.1
  135.3 33.3 %all-to-all-done.1 = bf16[8,1,8,128,128]{4,3,2,1,0:T(8,128)(2,1)} async-done(((bf16[8,1,8,128,128]{4,3,2,1,0:T(8,128)(2,1)}), bf16[8,1,8,128,128]{4,3,2,1,0:T(8,128)(2,1)}, u32[]{:S(2)}, u32[]{:S(2)}) %all-to-all-start.1) | async-done | bytes 2097184 | tf_op jit(solution)/shard_map/all_to_all | solution.py:125
  168.6 4.5 %all-to-all-start.3 = ((bf16[8,1,8,128,128]{4,3,2,1,0:T(8,128)(2,1)}), bf16[8,1,8,128,128]{4,3,2,1,0:T(8,128)(2,1)}, u32[]{:S(2)}, u32[]{:S(2)}) async-start(bf16[8,1,8,128,128]{4,3,2,1,0:T(8,128)(2,1)} %get-tuple-element.19), calls=%async_computation.3 | async-start | bytes 4194304 | tf_op jit(solution)/shard_map/all_to_all | solution.py:131
  173.1 4.3 %fusion.29 = (bf16[1,32,8,8,128]{4,3,2,1,0:T(8,128)(2,1)S(1)}, bf16[1,32,8,8,128]{4,3,2,1,0:T(8,128)(2,1)S(1)}) fusion(f32[1,32,128,128]{2,3,1,0:T(8,128)S(1)} %get-tuple-element.28, f32[64]{0:T(128)S(1)} %negate_power_fusion, f32[32,128]{1,0:T(8,128)S(1)} %add_convert_fusion), kind=kLoop, calls=%fused_computation.53 | loop fusion | flops 2359296 | bytes 3162368
  177.4 0.1 copy.88
  177.5 0.1 copy.89
  177.6 0.7 copy.62
  178.3 1.1 pad_maximum_fusion.refs_3_
  179.4 1.1 maximum_bitcast_fusion.refs_2_
  180.4 16.4 %shard_map.91 = bf16[1,256,2048]{2,1,0:T(8,128)(2,1)} custom-call(f32[1,1,4096]{2,1,0:T(1,128)} %compare_select_fusion.refs_0_, bf16[1,256,1024]{2,1,0:T(8,128)(2,1)} %get-tuple-element.30.refs_1_, bf16[1,128,4352]{2,1,0:T(8,128)(2,1)} %maximum_bitcast_fusion.refs_2_, bf16[1,4352,128]{2,1,0:T(8,128)(2,1)} %pad_maximum_fusion.refs_3_), custom_call_target="tpu_custom_call" | custom-call | flops 6845104128 | bytes 3276800 | tf_op jit(solution)/shard_map/pallas_call | solution.py:308
  196.9 2.3 gather_fusion.4
  199.2 0.7 copy.63
  199.9 0.2 convert_multiply_fusion
  200.1 4.3 %fusion.27 = (bf16[1,32,8,8,128]{4,3,2,1,0:T(8,128)(2,1)S(1)}, bf16[1,32,8,8,128]{4,3,2,1,0:T(8,128)(2,1)S(1)}) fusion(f32[1,32,128,128]{2,3,1,0:T(8,128)S(1)} %convert_multiply_fusion, f32[64]{0:T(128)S(1)} %negate_power_fusion, f32[32,128]{1,0:T(8,128)S(1)} %add_convert_fusion), kind=kLoop, calls=%fused_computation.51 | loop fusion | flops 2359296 | bytes 3162368
  204.4 0.1 copy.86
  204.5 0.1 copy.87
  204.6 1.1 maximum_bitcast_fusion.1.refs_2_
  205.7 17.3 %shard_map.92 = (bf16[1,8,256,4352]{3,2,1,0:T(8,128)(2,1)}, f32[1,256,1024]{2,1,0:T(8,128)}) custom-call(f32[1,1,4096]{2,1,0:T(1,128)} %compare_select_fusion.refs_0_, bf16[1,256,1024]{2,1,0:T(8,128)(2,1)} %get-tuple-element.29.refs_1_, bf16[1,128,4352]{2,1,0:T(8,128)(2,1)} %maximum_bitcast_fusion.1.refs_2_), custom_call_target="tpu_custom_call" | custom-call | flops 4563402752 | bytes 3276800 | tf_op jit(solution)/shard_map/pallas_call | solution.py:308
  223.0 2.6 %copy.72 = f32[1,256,1024]{1,2,0:T(8,128)} copy(f32[1,256,1024]{2,1,0:T(8,128)} %get-tuple-element.18) | data formatting | bytes 2097152 | tf_op jit(solution)/shard_map/reshape | solution.py:165
  225.6 2.3 gather_fusion.5
  228.0 1.5 bitcast_convert_fusion
  229.4 1.9 copy.71
  231.3 0.2 multiply_convert_fusion
  231.5 12.1 %divide_convert_fusion = bf16[1,256,8,128]{1,3,2,0:T(8,128)(2,1)S(1)} fusion(f32[1,256,8,128]{1,3,2,0:T(8,128)} %bitcast.108, bf16[1,8,256,4352]{3,2,1,0:T(8,128)(2,1)} %get-tuple-element.17, bf16[1,256,128]{1,2,0:T(8,128)(2,1)S(1)} %copy.76, bf16[1,4096,128]{1,2,0:T(8,128)(2,1)S(1)} %multiply_convert_fusion), kind=kOutput, calls=%fused_computation.45 | convolution fusion | flops 2284453888 | bytes 20512768 | tf_op jit(solution)/shard_map/rgtl,rld->rtgd/dot_general | solution.py:162
  243.6 0.2 copy.73
  243.8 0.8 constant_dynamic-update-slice_fusion
  (26 shorter events, 0.4 us)
Async XLA Ops:
  0.0 11.9 %copy-start = (bf16[16,128,256]{2,1,0:T(8,128)(2,1)S(1)}, bf16[16,128,256]{2,1,0:T(8,128)(2,1)}, u32[]{:S(2)}) copy-start(bf16[16,128,256]{2,1,0:T(8,128)(2,1)} %param.12) | copy-start | bytes 3145732
  3.3 13.7 %all-to-all-start = ((s32[8,1,72]{2,1,0:T(1,128)}), s32[8,1,72]{2,1,0:T(1,128)S(1)}, u32[]{:S(2)}, u32[]{:S(2)}) async-start(s32[8,1,72]{2,1,0:T(1,128)} %pad_add_fusion), calls=%async_computation | async-start | bytes 8192 | tf_op jit(solution)/shard_map/all_to_all | solution.py:82
  19.9 96.6 %all-to-all-start.2 = ((bf16[8,1,8,128,256]{4,3,2,1,0:T(8,128)(2,1)}), bf16[8,1,8,128,256]{4,3,2,1,0:T(8,128)(2,1)}, u32[]{:S(2)}, u32[]{:S(2)}) async-start(bf16[8,1,8,128,256]{4,3,2,1,0:T(8,128)(2,1)} %bitcast.99), calls=%async_computation.2 | async-start | bytes 8388608 | tf_op jit(solution)/shard_map/all_to_all | solution.py:136
  116.4 52.2 %all-to-all-start.1 = ((bf16[8,1,8,128,128]{4,3,2,1,0:T(8,128)(2,1)}), bf16[8,1,8,128,128]{4,3,2,1,0:T(8,128)(2,1)}, u32[]{:S(2)}, u32[]{:S(2)}) async-start(bf16[8,1,8,128,128]{4,3,2,1,0:T(8,128)(2,1)} %get-tuple-element.20), calls=%async_computation.1 | async-start | bytes 4194304 | tf_op jit(solution)/shard_map/all_to_all | solution.py:125
  123.0 0.9 copy-start.1
  123.0 1.2 copy-start.2
  123.0 1.3 copy-start.3
  168.6 54.4 %all-to-all-start.3 = ((bf16[8,1,8,128,128]{4,3,2,1,0:T(8,128)(2,1)}), bf16[8,1,8,128,128]{4,3,2,1,0:T(8,128)(2,1)}, u32[]{:S(2)}, u32[]{:S(2)}) async-start(bf16[8,1,8,128,128]{4,3,2,1,0:T(8,128)(2,1)} %get-tuple-element.19), calls=%async_computation.3 | async-start | bytes 4194304 | tf_op jit(solution)/shard_map/all_to_all | solution.py:131

commit v11 on v9

--- a/solution.py
+++ b/solution.py
@@ -99,7 +99,11 @@
         axis=0,
     )
     flat = owners * rows * capacity
-    index = (owner * rows + jnp.arange(rows, dtype=jnp.int32)[:, None]) * capacity + rank
+    me = lax.axis_index("stretch")
+    order = (me + jnp.arange(owners, dtype=jnp.int32)) % owners
+    chosen = jnp.take(chosen, order, axis=0)
+    source_shift = (me - owner) % owners
+    index = (source_shift * rows + jnp.arange(rows, dtype=jnp.int32)[:, None]) * capacity + rank
     index = jnp.where(live, index, 0)
     slot_scale = all_scales[stretch_ids]
     placement = stretch_pos[:, :, None] + jnp.arange(span, dtype=jnp.int32)
@@ -112,6 +116,15 @@
         * head_dim ** (-0.5)
     ).astype(jnp.bfloat16)
     query_rot = query_rot.reshape(rows, tokens, q_heads * head_dim)
+    def swap(by_shift, after=None):
+        if after is not None:
+            by_shift, after = lax.optimization_barrier((by_shift, after))
+        pieces = [by_shift[0]]
+        for shift in range(1, owners):
+            pairs = [(i, (i + shift) % owners) for i in range(owners)]
+            pieces.append(lax.ppermute(by_shift[shift], "stretch", pairs))
+        return jnp.stack(pieces, axis=0)
+
     results = []
     for head in range(kv_heads):
         cols = slice(head * head_dim, (head + 1) * head_dim)
@@ -122,18 +135,15 @@
         group_cols = slice(head * request_group * head_dim, (head + 1) * request_group * head_dim)
         query_head = query_rot[..., group_cols]
         if last:
-            got_keys = lax.all_to_all(
-                store[head][chosen][..., :head_dim], "stretch", split_axis=0, concat_axis=0, tiled=True
-            )
+            got_keys = swap(store[head][chosen][..., :head_dim], previous)
             if results:
                 got_keys, earlier = lax.optimization_barrier((got_keys, results[-1]))
                 results[-1] = earlier
-            got_vals = lax.all_to_all(
-                store[head][chosen][..., head_dim:], "stretch", split_axis=0, concat_axis=0, tiled=True
-            )
+            got_vals = swap(store[head][chosen][..., head_dim:], got_keys)
             raw_k = got_keys.reshape(flat, span, head_dim)[index]
         else:
-            got = lax.all_to_all(store[head][chosen], "stretch", split_axis=0, concat_axis=0, tiled=True)
+            got = swap(store[head][chosen])
+            previous = got
             if results:
                 got, earlier = lax.optimization_barrier((got, results[-1]))
                 results[-1] = earlier

time: 244 us -> 290 us (1.19); the launches traced: 243 us -> 285 us
  waiting for transfers between devices: 130 us -> 57.9 us
  starting transfers between devices: 20.8 us -> 88.5 us
  local copies, waits for them, and re-layouts: 29.7 us -> 67.4 us
  other arithmetic: 19.9 us -> 27.9 us
    all_to_all x3 -> x0, waiting for transfers between devices: 125 us -> none  [the longest x1 84.5 us: shards(): lax.all_to_all(store[head][chosen], 'stretch', split_axis=0, concat_axis=...]
    ppermute x0 -> x21, starting transfers between devices: none -> 81.3 us  [swap(): pieces.append(lax.ppermute(by_shift[shift], 'stretch', pairs))]
    ppermute x0 -> x21, waiting for transfers between devices: none -> 57.9 us  [swap(): pieces.append(lax.ppermute(by_shift[shift], 'stretch', pairs))]
    unnamed x13 -> x85, local copies, waits for them, and re-layouts: 0.91 us -> 22.9 us
    all_to_all x3 -> x0, starting transfers between devices: 13.5 us -> none  [the longest x1 4.54 us: shards(): lax.all_to_all(store[head][chosen], 'stretch', split_axis=0, concat_axis=...]
    squeeze x0 -> x4, local copies, waits for them, and re-layouts: none -> 8.21 us  [swap(): pieces.append(lax.ppermute(by_shift[shift], 'stretch', pairs))]
    all_to_all x1, waiting for transfers between devices: 4.54 us -> 0.01 us  [shards(): lax.all_to_all(requests, 'stretch', split_axis=0, concat_axis=0, tiled=True)]
    gather x2 -> x3, local copies, waits for them, and re-layouts: 5.58 us -> 6.32 us  [the longest x1 2.82 us: shards(): got = swap(store[head][chosen])]
  transfers between devices with their start and end apart: 4 -> 22, of which waited for: 4 -> 7; matrix products, arithmetic and copies ran while one was open for 16% -> 18% of each run, Pallas kernels for 10% -> 8%
where the time goes in v11:
time: 290 us; the launch traced here: 285 us
  starting transfers between devices  88.5 us (31%)
  local copies, waits for them, and re-layouts  67.4 us (23%)
  waiting for transfers between devices  57.9 us (20%)
  Pallas kernels  41.9 us (14%)
  other arithmetic  27.9 us (10%)
    ppermute x21, starting transfers between devices, swap(): pieces.append(lax.ppermute(by_shift[shift], 'stretch', pairs))  81.3 us
    ppermute x21, waiting for transfers between devices, swap(): pieces.append(lax.ppermute(by_shift[shift], 'stretch', pairs))  57.9 us
    pallas_call x3, Pallas kernels, flash(): pl.pallas_call(kernel, grid=(rows, kv_heads, per), in_specs=in_specs, out...  41.9 us
    unnamed x85, local copies, waits for them, and re-layouts  22.9 us
    unnamed x3, other arithmetic  8.73 us
    gather x2, local copies, waits for them, and re-layouts, shards(): got = got.reshape(flat, span, 2 * head_dim)[index]  8.49 us
    squeeze x4, local copies, waits for them, and re-layouts, swap(): pieces.append(lax.ppermute(by_shift[shift], 'stretch', pairs))  8.21 us
    all_to_all x1, starting transfers between devices, shards(): lax.all_to_all(requests, 'stretch', split_axis=0, concat_axis=0, tiled=True)  7.28 us
  transfers between devices with their start and end apart: 22, of which 7 were waited for; matrix products, arithmetic and copies ran while one was open for 18% of the time, Pallas kernels for 8%

profile of v11, /device:TPU:0, one launch (start us, length us, event | category | flops | bytes accessed | tf_op | source)
XLA Modules:
  0.0 285.1 jit_solution(10800358691366087114)
XLA Ops:
  0.0 1.3 fusion.44
  3.9 7.3 %all-to-all-start = ((s32[8,1,72]{2,1,0:T(1,128)}), s32[8,1,72]{2,1,0:T(1,128)}, u32[]{:S(2)}, u32[]{:S(2)}) async-start(s32[8,1,72]{2,1,0:T(1,128)} %pad_add_fusion), calls=%async_computation | async-start | bytes 8192 | tf_op jit(solution)/shard_map/all_to_all | solution.py:82
  12.8 1.3 fusion.56
  14.1 1.3 fusion.57
  20.6 1.1 fusion.55
  22.9 1.0 fusion.32
  25.7 2.8 gather_fusion.2
  28.5 3.5 %slice_bitcast_fusion = (bf16[1,8,128,256]{3,2,1,0:T(8,128)(2,1)S(1)}, bf16[1,8,128,256]{3,2,1,0:T(8,128)(2,1)S(1)}, bf16[1,8,128,256]{3,2,1,0:T(8,128)(2,1)}, b...) fusion(bf16[64,128,256]{2,1,0:T(8,128)(2,1)} %gather_fusion.2), kind=kLoop, calls=%fused_computation.45 | loop fusion | bytes 7340032 | tf_op jit(solution)/shard_map/squeeze | solution.py:125
  32.1 1.9 fusion.18
  33.9 2.0 collective-permute-start
  36.0 1.5 collective-permute-start.1
  37.4 2.4 collective-permute-start.2
  39.8 1.5 collective-permute-start.3
  41.3 2.4 collective-permute-start.4
  46.7 2.8 gather_fusion.1
  49.5 3.3 %slice.241 = bf16[8,1,8,128,128]{4,3,2,1,0:T(8,128)(2,1)} slice(bf16[8,1,8,128,256]{4,3,2,1,0:T(8,128)(2,1)} %bitcast.196), slice={[0:8], [0:1], [0:8], [0:128], [0:128]} | slice | bytes 4194304 | tf_op jit(solution)/shard_map/slice | solution.py:138
  53.2 1.5 collective-permute-start.5
  54.7 1.9 bitcast_dynamic-update-slice_fusion.6
  56.6 7.3 %collective-permute-start.6 = (bf16[1,8,128,256]{3,2,1,0:T(8,128)(2,1)S(1)}, bf16[1,8,128,256]{3,2,1,0:T(8,128)(2,1)S(1)}, u32[]{:S(2)}, u32[]{:S(2)}) collective-permute-start(bf16[1,8,128,256]{3,2,1,0:T(8,128)(2,1)S(1)} %get-tuple-element.17), channel_id=1, source_target_pairs={{0,14},{2,0},{4,2},{6,4},{8,6},{10,8},{12,10},{14,12},{1,15},{3,1}... | collective-permute-start | bytes 1572872 | tf_op jit(solution)/shard_map/ppermute | solution.py:125
  63.9 1.9 bitcast_dynamic-update-slice_fusion.5
  65.8 29.6 %collective-permute-done.2 = bf16[1,8,128,256]{3,2,1,0:T(8,128)(2,1)} collective-permute-done((bf16[1,8,128,256]{3,2,1,0:T(8,128)(2,1)}, bf16[1,8,128,256]{3,2,1,0:T(8,128)(2,1)}, u32[]{:S(2)}, u32[]{:S(2)}) %collective-permute-start.2) | collective-permute-done | bytes 524320 | tf_op jit(solution)/shard_map/ppermute | solution.py:125
  95.4 1.9 bitcast_dynamic-update-slice_fusion.4
  97.3 1.9 bitcast_dynamic-update-slice_fusion.3
  99.2 1.9 bitcast_dynamic-update-slice_fusion.2
  101.9 2.3 collective-permute-done.6
  105.1 4.3 %gather_fusion.3 = bf16[32,128,256]{2,1,0:T(8,128)(2,1)} fusion(bf16[64,128,256]{2,1,0:T(8,128)(2,1)} %bitcast.49, s32[1024]{0:T(1024)} %pad_clamp_fusion.1), kind=kCustom, calls=%fused_computation.3 | custom fusion | bytes 4194432 | tf_op jit(solution)/shard_map/gather | solution.py:150
  109.4 4.1 %copy.113 = bf16[32,128,256]{1,2,0:T(8,128)(2,1)} copy(bf16[32,128,256]{2,1,0:T(8,128)(2,1)} %gather_fusion.3) | data formatting | bytes 4194304 | tf_op jit(solution)/shard_map/gather | solution.py:150
  113.5 2.8 multiply_convert_fusion
  116.4 4.2 %fusion.22 = (bf16[1,32,8,8,128]{4,3,2,1,0:T(8,128)(2,1)S(1)}, bf16[1,32,8,8,128]{4,3,2,1,0:T(8,128)(2,1)S(1)}) fusion(f32[1,32,128,128]{2,3,1,0:T(8,128)S(1)} %get-tuple-element.38, f32[64]{0:T(128)S(1)} %copy-done.23, f32[32,128]{1,0:T(8,128)S(1)} %add_convert_fusion), kind=kLoop, calls=%fused_computation.64 | loop fusion | flops 2359296 | bytes 3162368
  122.4 1.6 copy.118
  124.1 2.7 slice_bitcast_fusion.15
  126.8 7.6 %collective-permute-start.7 = (bf16[1,8,128,128]{3,2,1,0:T(8,128)(2,1)}, bf16[1,8,128,128]{3,2,1,0:T(8,128)(2,1)}, u32[]{:S(2)}, u32[]{:S(2)}) collective-permute-start(bf16[1,8,128,128]{3,2,1,0:T(8,128)(2,1)} %get-tuple-element.45), channel_id=1, source_target_pairs={{0,2},{2,4},{4,6},{6,8},{8,10},{10,12},{12,14},{14,0},{1,3},{3,5},... | collective-permute-start | bytes 786440 | tf_op jit(solution)/shard_map/ppermute | solution.py:125
  134.4 21.3 %collective-permute-start.8 = (bf16[1,8,128,128]{3,2,1,0:T(8,128)(2,1)}, bf16[1,8,128,128]{3,2,1,0:T(8,128)(2,1)}, u32[]{:S(2)}, u32[]{:S(2)}) collective-permute-start(bf16[1,8,128,128]{3,2,1,0:T(8,128)(2,1)} %get-tuple-element.44), channel_id=1, source_target_pairs={{0,4},{2,6},{4,8},{6,10},{8,12},{10,14},{12,0},{14,2},{1,5},{3,7},... | collective-permute-start | bytes 786440 | tf_op jit(solution)/shard_map/ppermute | solution.py:125
  155.7 1.1 pad_maximum_fusion.refs_3_
  156.8 1.1 maximum_bitcast_fusion.refs_2_
  157.9 16.5 %shard_map.91.refs_5_ = bf16[1,256,2048]{2,1,0:T(8,128)(2,1)} custom-call(f32[1,1,4096]{2,1,0:T(1,128)} %compare_select_fusion.refs_0_, bf16[1,256,1024]{2,1,0:T(8,128)(2,1)} %get-tuple-element.46.refs_1_, bf16[1,128,4352]{2,1,0:T(8,128)(2,1)} %maximum_bitcast_fusion.refs_2_, bf16[1,4352,128]{2,1,0:T(8,128)(2,1)} %pad_maximum_fusion.refs_3_), custom_call_target="tpu_custom_call" | custom-call | flops 6845104128 | bytes 3276800 | tf_op jit(solution)/shard_map/pallas_call | solution.py:286
  175.5 3.4 %collective-permute-start.10 = (bf16[1,8,128,128]{3,2,1,0:T(8,128)(2,1)S(1)}, bf16[1,8,128,128]{3,2,1,0:T(8,128)(2,1)S(1)}, u32[]{:S(2)}, u32[]{:S(2)}) collective-permute-start(bf16[1,8,128,128]{3,2,1,0:T(8,128)(2,1)S(1)} %copy-done.12), channel_id=1, source_target_pairs={{0,8},{2,10},{4,12},{6,14},{8,0},{10,2},{12,4},{14,6},{1,9},{3,11}... | collective-permute-start | bytes 786440 | tf_op jit(solution)/shard_map/ppermute | solution.py:125
  178.9 3.7 %collective-permute-start.11 = (bf16[1,8,128,128]{3,2,1,0:T(8,128)(2,1)S(1)}, bf16[1,8,128,128]{3,2,1,0:T(8,128)(2,1)S(1)}, u32[]{:S(2)}, u32[]{:S(2)}) collective-permute-start(bf16[1,8,128,128]{3,2,1,0:T(8,128)(2,1)S(1)} %copy-done.11), channel_id=1, source_target_pairs={{0,10},{2,12},{4,14},{6,0},{8,2},{10,4},{12,6},{14,8},{1,11},{3,13... | collective-permute-start | bytes 786440 | tf_op jit(solution)/shard_map/ppermute | solution.py:125
  182.6 1.0 bitcast_dynamic-update-slice_fusion.12
  183.7 1.6 collective-permute-start.13
  186.2 8.3 %collective-permute-done.9 = bf16[1,8,128,128]{3,2,1,0:T(8,128)(2,1)S(1)} collective-permute-done((bf16[1,8,128,128]{3,2,1,0:T(8,128)(2,1)S(1)}, bf16[1,8,128,128]{3,2,1,0:T(8,128)(2,1)S(1)}, u32[]{:S(2)}, u32[]{:S(2)}) %collective-permute-start.9) | collective-permute-done | bytes 262176 | tf_op jit(solution)/shard_map/ppermute | solution.py:125
  194.5 5.7 %collective-permute-done.10 = bf16[1,8,128,128]{3,2,1,0:T(8,128)(2,1)S(1)} collective-permute-done((bf16[1,8,128,128]{3,2,1,0:T(8,128)(2,1)S(1)}, bf16[1,8,128,128]{3,2,1,0:T(8,128)(2,1)S(1)}, u32[]{:S(2)}, u32[]{:S(2)}) %collective-permute-start.10) | collective-permute-done | bytes 262176 | tf_op jit(solution)/shard_map/ppermute | solution.py:125
  200.4 1.4 collective-permute-done.13
  202.7 1.2 slice_bitcast_fusion.8
  203.9 6.1 %collective-permute-start.14 = (bf16[1,8,128,128]{3,2,1,0:T(8,128)(2,1)}, bf16[1,8,128,128]{3,2,1,0:T(8,128)(2,1)}, u32[]{:S(2)}, u32[]{:S(2)}) collective-permute-start(bf16[1,8,128,128]{3,2,1,0:T(8,128)(2,1)} %get-tuple-element.35), channel_id=1, source_target_pairs={{0,2},{2,4},{4,6},{6,8},{8,10},{10,12},{12,14},{14,0},{1,3},{3,5},... | collective-permute-start | bytes 786440 | tf_op jit(solution)/shard_map/ppermute | solution.py:125
  210.0 11.0 %collective-permute-start.15 = (bf16[1,8,128,128]{3,2,1,0:T(8,128)(2,1)}, bf16[1,8,128,128]{3,2,1,0:T(8,128)(2,1)}, u32[]{:S(2)}, u32[]{:S(2)}) collective-permute-start(bf16[1,8,128,128]{3,2,1,0:T(8,128)(2,1)} %get-tuple-element.34), channel_id=1, source_target_pairs={{0,4},{2,6},{4,8},{6,10},{8,12},{10,14},{12,0},{14,2},{1,5},{3,7},... | collective-permute-start | bytes 786440 | tf_op jit(solution)/shard_map/ppermute | solution.py:125
  221.0 3.0 %collective-permute-start.17 = (bf16[1,8,128,128]{3,2,1,0:T(8,128)(2,1)}, bf16[1,8,128,128]{3,2,1,0:T(8,128)(2,1)}, u32[]{:S(2)}, u32[]{:S(2)}) collective-permute-start(bf16[1,8,128,128]{3,2,1,0:T(8,128)(2,1)} %get-tuple-element.32), channel_id=1, source_target_pairs={{0,8},{2,10},{4,12},{6,14},{8,0},{10,2},{12,4},{14,6},{1,9},{3,11}... | collective-permute-start | bytes 786440 | tf_op jit(solution)/shard_map/ppermute | solution.py:125
  224.0 3.4 %collective-permute-start.18 = (bf16[1,8,128,128]{3,2,1,0:T(8,128)(2,1)}, bf16[1,8,128,128]{3,2,1,0:T(8,128)(2,1)}, u32[]{:S(2)}, u32[]{:S(2)}) collective-permute-start(bf16[1,8,128,128]{3,2,1,0:T(8,128)(2,1)} %get-tuple-element.31), channel_id=1, source_target_pairs={{0,10},{2,12},{4,14},{6,0},{8,2},{10,4},{12,6},{14,8},{1,11},{3,13... | collective-permute-start | bytes 786440 | tf_op jit(solution)/shard_map/ppermute | solution.py:125
  227.4 2.5 gather_fusion.5
  231.1 4.2 %fusion.20 = (bf16[1,32,8,8,128]{4,3,2,1,0:T(8,128)(2,1)S(1)}, bf16[1,32,8,8,128]{4,3,2,1,0:T(8,128)(2,1)S(1)}) fusion(f32[1,32,128,128]{2,3,1,0:T(8,128)S(1)} %convert_multiply_fusion.1, f32[64]{0:T(128)S(1)} %copy-done.24, f32[32,128]{1,0:T(8,128)S(1)} %add_convert_fusion), kind=kLoop, calls=%fused_computation.62 | loop fusion | flops 2359296 | bytes 3162368
  235.6 1.1 maximum_bitcast_fusion.1.refs_2_
  236.7 7.4 %shard_map.92.refs_4_ = f32[1,256,1024]{2,1,0:T(8,128)} custom-call(f32[1,1,4096]{2,1,0:T(1,128)} %compare_select_fusion.refs_0_, bf16[1,256,1024]{2,1,0:T(8,128)(2,1)} %get-tuple-element.47.refs_1_, bf16[1,128,4352]{2,1,0:T(8,128)(2,1)} %maximum_bitcast_fusion.1.refs_2_), custom_call_target="tpu_custom_call" | custom-call | flops 2281701376 | bytes 3276800 | tf_op jit(solution)/shard_map/pallas_call | solution.py:286
  244.1 1.0 bitcast_dynamic-update-slice_fusion.19
  245.1 1.7 collective-permute-start.20
  246.8 1.0 bitcast_dynamic-update-slice_fusion.18
  247.8 2.1 collective-permute-done.16
  249.9 1.0 bitcast_dynamic-update-slice_fusion.17
  250.9 1.0 bitcast_dynamic-update-slice_fusion.16
  251.9 1.0 bitcast_dynamic-update-slice_fusion.15
  252.9 8.3 %collective-permute-done.19 = bf16[1,8,128,128]{3,2,1,0:T(8,128)(2,1)S(1)} collective-permute-done((bf16[1,8,128,128]{3,2,1,0:T(8,128)(2,1)S(1)}, bf16[1,8,128,128]{3,2,1,0:T(8,128)(2,1)S(1)}, u32[]{:S(2)}, u32[]{:S(2)}) %collective-permute-start.19) | collective-permute-done | bytes 262176 | tf_op jit(solution)/shard_map/ppermute | solution.py:125
  261.4 1.3 copy-done.8
  262.7 2.5 gather_fusion.6
  265.9 1.1 pad_maximum_fusion.1.refs_3_
  267.0 18.0 %shard_map.93 = bf16[1,256,2048]{2,1,0:T(8,128)(2,1)} custom-call(f32[1,1,4096]{2,1,0:T(1,128)} %compare_select_fusion.refs_0_, bf16[1,256,1024]{2,1,0:T(8,128)(2,1)} %get-tuple-element.47.refs_1_, bf16[1,128,4352]{2,1,0:T(8,128)(2,1)} %maximum_bitcast_fusion.1.refs_2_, ...), custom_call_target="tpu_custom_call", output_to_operand_aliasing={{}: (5, {})} | custom-call | flops 4563402752 | bytes 3276800 | tf_op jit(solution)/shard_map/pallas_call | solution.py:286
  (143 shorter events, 23.8 us)
Async XLA Ops:
  0.0 14.1 %copy-start.6 = (bf16[16,128,256]{2,1,0:T(8,128)(2,1)S(1)}, bf16[16,128,256]{2,1,0:T(8,128)(2,1)}, u32[]{:S(2)}) copy-start(bf16[16,128,256]{2,1,0:T(8,128)(2,1)} %param.13) | copy-start | bytes 3145732
  3.9 20.3 %all-to-all-start = ((s32[8,1,72]{2,1,0:T(1,128)}), s32[8,1,72]{2,1,0:T(1,128)}, u32[]{:S(2)}, u32[]{:S(2)}) async-start(s32[8,1,72]{2,1,0:T(1,128)} %pad_add_fusion), calls=%async_computation | async-start | bytes 8192 | tf_op jit(solution)/shard_map/all_to_all | solution.py:82
  12.8 3.2 %copy-start.29 = (s32[1,32]{1,0:T(1,128)S(1)}, s32[1,32]{1,0:T(1,128)}, u32[]{:S(2)}) copy-start(s32[1,32]{1,0:T(1,128)} %param.17) | copy-start | bytes 388
  12.8 3.3 %copy-start.19 = (bf16[1,256,256]{2,1,0:T(8,128)(2,1)S(1)}, bf16[1,256,256]{2,1,0:T(8,128)(2,1)}, u32[]{:S(2)}) copy-start(bf16[1,256,256]{2,1,0:T(8,128)(2,1)} %param.10) | copy-start | bytes 393220
  14.1 3.1 %copy-start.5 = (bf16[1,256,2048]{2,1,0:T(8,128)(2,1)S(1)}, bf16[1,256,2048]{2,1,0:T(8,128)(2,1)}, u32[]{:S(2)}) copy-start(bf16[1,256,2048]{2,1,0:T(8,128)(2,1)} %param.9) | copy-start | bytes 3145732
  17.5 0.6 copy-start.21
  17.5 0.7 copy-start.25
  20.6 1.7 copy-start.27
  20.6 1.7 copy-start.30
  20.6 2.3 copy-start.22
  20.6 2.3 copy-start.26
  20.6 3.3 %copy-start.3 = (bf16[16,128,128]{2,1,0:T(8,128)(2,1)S(1)}, bf16[16,128,128]{2,1,0:T(8,128)(2,1)}, u32[]{:S(2)}) copy-start(bf16[16,128,128]{2,1,0:T(8,128)(2,1)} %get-tuple-element.50) | copy-start | bytes 1572868
  20.6 3.3 %copy-start.4 = (bf16[16,128,128]{2,1,0:T(8,128)(2,1)S(1)}, bf16[16,128,128]{2,1,0:T(8,128)(2,1)}, u32[]{:S(2)}) copy-start(bf16[16,128,128]{2,1,0:T(8,128)(2,1)} %get-tuple-element.51) | copy-start | bytes 1572868
  33.9 19.3 %collective-permute-start = (bf16[1,8,128,256]{3,2,1,0:T(8,128)(2,1)}, bf16[1,8,128,256]{3,2,1,0:T(8,128)(2,1)}, u32[]{:S(2)}, u32[]{:S(2)}) collective-permute-start(bf16[1,8,128,256]{3,2,1,0:T(8,128)(2,1)} %get-tuple-element.23), channel_id=1, source_target_pairs={{0,2},{2,4},{4,6},{6,8},{8,10},{10,12},{12,14},{14,0},{1,3},{3,5},... | collective-permute-start | bytes 1572872 | tf_op jit(solution)/shard_map/ppermute | solution.py:125
  36.0 20.7 %collective-permute-start.1 = (bf16[1,8,128,256]{3,2,1,0:T(8,128)(2,1)}, bf16[1,8,128,256]{3,2,1,0:T(8,128)(2,1)}, u32[]{:S(2)}, u32[]{:S(2)}) collective-permute-start(bf16[1,8,128,256]{3,2,1,0:T(8,128)(2,1)} %get-tuple-element.22), channel_id=1, source_target_pairs={{0,4},{2,6},{4,8},{6,10},{8,12},{10,14},{12,0},{14,2},{1,5},{3,7},... | collective-permute-start | bytes 1572872 | tf_op jit(solution)/shard_map/ppermute | solution.py:125
  37.4 58.0 %collective-permute-start.2 = (bf16[1,8,128,256]{3,2,1,0:T(8,128)(2,1)}, bf16[1,8,128,256]{3,2,1,0:T(8,128)(2,1)}, u32[]{:S(2)}, u32[]{:S(2)}) collective-permute-start(bf16[1,8,128,256]{3,2,1,0:T(8,128)(2,1)} %get-tuple-element.21), channel_id=1, source_target_pairs={{0,6},{2,8},{4,10},{6,12},{8,14},{10,0},{12,2},{14,4},{1,7},{3,9},... | collective-permute-start | bytes 1572872 | tf_op jit(solution)/shard_map/ppermute | solution.py:125
  39.8 57.5 %collective-permute-start.3 = (bf16[1,8,128,256]{3,2,1,0:T(8,128)(2,1)}, bf16[1,8,128,256]{3,2,1,0:T(8,128)(2,1)}, u32[]{:S(2)}, u32[]{:S(2)}) collective-permute-start(bf16[1,8,128,256]{3,2,1,0:T(8,128)(2,1)} %get-tuple-element.20), channel_id=1, source_target_pairs={{0,8},{2,10},{4,12},{6,14},{8,0},{10,2},{12,4},{14,6},{1,9},{3,11}... | collective-permute-start | bytes 1572872 | tf_op jit(solution)/shard_map/ppermute | solution.py:125
  41.3 57.9 %collective-permute-start.4 = (bf16[1,8,128,256]{3,2,1,0:T(8,128)(2,1)}, bf16[1,8,128,256]{3,2,1,0:T(8,128)(2,1)}, u32[]{:S(2)}, u32[]{:S(2)}) collective-permute-start(bf16[1,8,128,256]{3,2,1,0:T(8,128)(2,1)} %get-tuple-element.19), channel_id=1, source_target_pairs={{0,10},{2,12},{4,14},{6,0},{8,2},{10,4},{12,6},{14,8},{1,11},{3,13... | collective-permute-start | bytes 1572872 | tf_op jit(solution)/shard_map/ppermute | solution.py:125
  49.5 3.3 %copy-start = (bf16[64,128,256]{2,1,0:T(8,128)(2,1)S(1)}, bf16[64,128,256]{2,1,0:T(8,128)(2,1)}, u32[]{:S(2)}) copy-start(bf16[64,128,256]{2,1,0:T(8,128)(2,1)} %gather_fusion.1) | copy-start | bytes 12582916
  53.2 47.8 %collective-permute-start.5 = (bf16[1,8,128,256]{3,2,1,0:T(8,128)(2,1)S(1)}, bf16[1,8,128,256]{3,2,1,0:T(8,128)(2,1)S(1)}, u32[]{:S(2)}, u32[]{:S(2)}) collective-permute-start(bf16[1,8,128,256]{3,2,1,0:T(8,128)(2,1)S(1)} %get-tuple-element.18), channel_id=1, source_target_pairs={{0,12},{2,14},{4,0},{6,2},{8,4},{10,6},{12,8},{14,10},{1,13},{3,15... | collective-permute-start | bytes 1572872 | tf_op jit(solution)/shard_map/ppermute | solution.py:125
  56.6 47.6 %collective-permute-start.6 = (bf16[1,8,128,256]{3,2,1,0:T(8,128)(2,1)S(1)}, bf16[1,8,128,256]{3,2,1,0:T(8,128)(2,1)S(1)}, u32[]{:S(2)}, u32[]{:S(2)}) collective-permute-start(bf16[1,8,128,256]{3,2,1,0:T(8,128)(2,1)S(1)} %get-tuple-element.17), channel_id=1, source_target_pairs={{0,14},{2,0},{4,2},{6,4},{8,6},{10,8},{12,10},{14,12},{1,15},{3,1}... | collective-permute-start | bytes 1572872 | tf_op jit(solution)/shard_map/ppermute | solution.py:125
  113.5 2.9 %copy-start.23 = (f32[64]{0:T(128)S(1)}, f32[64]{0:T(128)}, u32[]{:S(2)}) copy-start(f32[64]{0:T(128)} %negate_power_fusion) | copy-start | bytes 772
  124.1 32.7 %copy-start.1 = (bf16[1,32,8,8,128]{4,3,1,2,0:T(8,128)(2,1)S(1)}, bf16[1,32,8,8,128]{4,3,1,2,0:T(8,128)(2,1)}, u32[]{:S(2)}) copy-start(bf16[1,32,8,8,128]{4,3,1,2,0:T(8,128)(2,1)} %copy.143) | copy-start | bytes 1572868
  124.1 32.7 %copy-start.2 = (bf16[1,32,8,8,128]{4,3,1,2,0:T(8,128)(2,1)S(1)}, bf16[1,32,8,8,128]{4,3,1,2,0:T(8,128)(2,1)}, u32[]{:S(2)}) copy-start(bf16[1,32,8,8,128]{4,3,1,2,0:T(8,128)(2,1)} %copy.144) | copy-start | bytes 1572868
  124.1 32.7 %copy-start.17 = (bf16[1,256,64]{1,2,0:T(8,128)(2,1)S(1)}, bf16[1,256,64]{1,2,0:T(8,128)(2,1)}, u32[]{:S(2)}) copy-start(bf16[1,256,64]{1,2,0:T(8,128)(2,1)} %get-tuple-element.52) | copy-start | bytes 98308
  124.1 32.7 %copy-start.18 = (bf16[1,256,64]{1,2,0:T(8,128)(2,1)S(1)}, bf16[1,256,64]{1,2,0:T(8,128)(2,1)}, u32[]{:S(2)}) copy-start(bf16[1,256,64]{1,2,0:T(8,128)(2,1)} %get-tuple-element.53) | copy-start | bytes 98308
  126.8 55.9 %collective-permute-start.7 = (bf16[1,8,128,128]{3,2,1,0:T(8,128)(2,1)}, bf16[1,8,128,128]{3,2,1,0:T(8,128)(2,1)}, u32[]{:S(2)}, u32[]{:S(2)}) collective-permute-start(bf16[1,8,128,128]{3,2,1,0:T(8,128)(2,1)} %get-tuple-element.45), channel_id=1, source_target_pairs={{0,2},{2,4},{4,6},{6,8},{8,10},{10,12},{12,14},{14,0},{1,3},{3,5},... | collective-permute-start | bytes 786440 | tf_op jit(solution)/shard_map/ppermute | solution.py:125
  134.4 49.2 %collective-permute-start.8 = (bf16[1,8,128,128]{3,2,1,0:T(8,128)(2,1)}, bf16[1,8,128,128]{3,2,1,0:T(8,128)(2,1)}, u32[]{:S(2)}, u32[]{:S(2)}) collective-permute-start(bf16[1,8,128,128]{3,2,1,0:T(8,128)(2,1)} %get-tuple-element.44), channel_id=1, source_target_pairs={{0,4},{2,6},{4,8},{6,10},{8,12},{10,14},{12,0},{14,2},{1,5},{3,7},... | collective-permute-start | bytes 786440 | tf_op jit(solution)/shard_map/ppermute | solution.py:125
  157.9 17.5 %copy-start.13 = (bf16[1,8,128,128]{3,2,1,0:T(8,128)(2,1)S(1)}, bf16[1,8,128,128]{3,2,1,0:T(8,128)(2,1)}, u32[]{:S(2)}) copy-start(bf16[1,8,128,128]{3,2,1,0:T(8,128)(2,1)} %get-tuple-element.43) | copy-start | bytes 786436
  157.9 17.6 %copy-start.12 = (bf16[1,8,128,128]{3,2,1,0:T(8,128)(2,1)S(1)}, bf16[1,8,128,128]{3,2,1,0:T(8,128)(2,1)}, u32[]{:S(2)}) copy-start(bf16[1,8,128,128]{3,2,1,0:T(8,128)(2,1)} %get-tuple-element.42) | copy-start | bytes 786436
  157.9 21.0 %copy-start.11 = (bf16[1,8,128,128]{3,2,1,0:T(8,128)(2,1)S(1)}, bf16[1,8,128,128]{3,2,1,0:T(8,128)(2,1)}, u32[]{:S(2)}) copy-start(bf16[1,8,128,128]{3,2,1,0:T(8,128)(2,1)} %get-tuple-element.41) | copy-start | bytes 786436
  157.9 24.8 %copy-start.10 = (bf16[1,8,128,128]{3,2,1,0:T(8,128)(2,1)S(1)}, bf16[1,8,128,128]{3,2,1,0:T(8,128)(2,1)}, u32[]{:S(2)}) copy-start(bf16[1,8,128,128]{3,2,1,0:T(8,128)(2,1)} %get-tuple-element.40) | copy-start | bytes 786436
  175.4 19.1 %collective-permute-start.9 = (bf16[1,8,128,128]{3,2,1,0:T(8,128)(2,1)S(1)}, bf16[1,8,128,128]{3,2,1,0:T(8,128)(2,1)S(1)}, u32[]{:S(2)}, u32[]{:S(2)}) collective-permute-start(bf16[1,8,128,128]{3,2,1,0:T(8,128)(2,1)S(1)} %copy-done.13), channel_id=1, source_target_pairs={{0,6},{2,8},{4,10},{6,12},{8,14},{10,0},{12,2},{14,4},{1,7},{3,9},... | collective-permute-start | bytes 786440 | tf_op jit(solution)/shard_map/ppermute | solution.py:125
  175.5 24.8 %collective-permute-start.10 = (bf16[1,8,128,128]{3,2,1,0:T(8,128)(2,1)S(1)}, bf16[1,8,128,128]{3,2,1,0:T(8,128)(2,1)S(1)}, u32[]{:S(2)}, u32[]{:S(2)}) collective-permute-start(bf16[1,8,128,128]{3,2,1,0:T(8,128)(2,1)S(1)} %copy-done.12), channel_id=1, source_target_pairs={{0,8},{2,10},{4,12},{6,14},{8,0},{10,2},{12,4},{14,6},{1,9},{3,11}... | collective-permute-start | bytes 786440 | tf_op jit(solution)/shard_map/ppermute | solution.py:125
  178.9 21.4 %collective-permute-start.11 = (bf16[1,8,128,128]{3,2,1,0:T(8,128)(2,1)S(1)}, bf16[1,8,128,128]{3,2,1,0:T(8,128)(2,1)S(1)}, u32[]{:S(2)}, u32[]{:S(2)}) collective-permute-start(bf16[1,8,128,128]{3,2,1,0:T(8,128)(2,1)S(1)} %copy-done.11), channel_id=1, source_target_pairs={{0,10},{2,12},{4,14},{6,0},{8,2},{10,4},{12,6},{14,8},{1,11},{3,13... | collective-permute-start | bytes 786440 | tf_op jit(solution)/shard_map/ppermute | solution.py:125
  182.6 17.7 %collective-permute-start.12 = (bf16[1,8,128,128]{3,2,1,0:T(8,128)(2,1)S(1)}, bf16[1,8,128,128]{3,2,1,0:T(8,128)(2,1)S(1)}, u32[]{:S(2)}, u32[]{:S(2)}) collective-permute-start(bf16[1,8,128,128]{3,2,1,0:T(8,128)(2,1)S(1)} %copy-done.10), channel_id=1, source_target_pairs={{0,12},{2,14},{4,0},{6,2},{8,4},{10,6},{12,8},{14,10},{1,13},{3,15... | collective-permute-start | bytes 786440 | tf_op jit(solution)/shard_map/ppermute | solution.py:125
  183.7 18.2 %collective-permute-start.13 = (bf16[1,8,128,128]{3,2,1,0:T(8,128)(2,1)S(1)}, bf16[1,8,128,128]{3,2,1,0:T(8,128)(2,1)S(1)}, u32[]{:S(2)}, u32[]{:S(2)}) collective-permute-start(bf16[1,8,128,128]{3,2,1,0:T(8,128)(2,1)S(1)} %get-tuple-element.39), channel_id=1, source_target_pairs={{0,14},{2,0},{4,2},{6,4},{8,6},{10,8},{12,10},{14,12},{1,15},{3,1}... | collective-permute-start | bytes 786440 | tf_op jit(solution)/shard_map/ppermute | solution.py:125
  201.9 2.0 copy-start.9
  203.9 40.1 %collective-permute-start.14 = (bf16[1,8,128,128]{3,2,1,0:T(8,128)(2,1)}, bf16[1,8,128,128]{3,2,1,0:T(8,128)(2,1)}, u32[]{:S(2)}, u32[]{:S(2)}) collective-permute-start(bf16[1,8,128,128]{3,2,1,0:T(8,128)(2,1)} %get-tuple-element.35), channel_id=1, source_target_pairs={{0,2},{2,4},{4,6},{6,8},{8,10},{10,12},{12,14},{14,0},{1,3},{3,5},... | collective-permute-start | bytes 786440 | tf_op jit(solution)/shard_map/ppermute | solution.py:125
  210.0 35.1 %collective-permute-start.15 = (bf16[1,8,128,128]{3,2,1,0:T(8,128)(2,1)}, bf16[1,8,128,128]{3,2,1,0:T(8,128)(2,1)}, u32[]{:S(2)}, u32[]{:S(2)}) collective-permute-start(bf16[1,8,128,128]{3,2,1,0:T(8,128)(2,1)} %get-tuple-element.34), channel_id=1, source_target_pairs={{0,4},{2,6},{4,8},{6,10},{8,12},{10,14},{12,0},{14,2},{1,5},{3,7},... | collective-permute-start | bytes 786440 | tf_op jit(solution)/shard_map/ppermute | solution.py:125
  221.0 28.9 %collective-permute-start.16 = (bf16[1,8,128,128]{3,2,1,0:T(8,128)(2,1)}, bf16[1,8,128,128]{3,2,1,0:T(8,128)(2,1)}, u32[]{:S(2)}, u32[]{:S(2)}) collective-permute-start(bf16[1,8,128,128]{3,2,1,0:T(8,128)(2,1)} %get-tuple-element.33), channel_id=1, source_target_pairs={{0,6},{2,8},{4,10},{6,12},{8,14},{10,0},{12,2},{14,4},{1,7},{3,9},... | collective-permute-start | bytes 786440 | tf_op jit(solution)/shard_map/ppermute | solution.py:125
  221.0 29.9 %collective-permute-start.17 = (bf16[1,8,128,128]{3,2,1,0:T(8,128)(2,1)}, bf16[1,8,128,128]{3,2,1,0:T(8,128)(2,1)}, u32[]{:S(2)}, u32[]{:S(2)}) collective-permute-start(bf16[1,8,128,128]{3,2,1,0:T(8,128)(2,1)} %get-tuple-element.32), channel_id=1, source_target_pairs={{0,8},{2,10},{4,12},{6,14},{8,0},{10,2},{12,4},{14,6},{1,9},{3,11}... | collective-permute-start | bytes 786440 | tf_op jit(solution)/shard_map/ppermute | solution.py:125
  224.0 28.0 %collective-permute-start.18 = (bf16[1,8,128,128]{3,2,1,0:T(8,128)(2,1)}, bf16[1,8,128,128]{3,2,1,0:T(8,128)(2,1)}, u32[]{:S(2)}, u32[]{:S(2)}) collective-permute-start(bf16[1,8,128,128]{3,2,1,0:T(8,128)(2,1)} %get-tuple-element.31), channel_id=1, source_target_pairs={{0,10},{2,12},{4,14},{6,0},{8,2},{10,4},{12,6},{14,8},{1,11},{3,13... | collective-permute-start | bytes 786440 | tf_op jit(solution)/shard_map/ppermute | solution.py:125
  227.3 3.2 %copy-start.28 = (f32[32]{0:T(128)S(1)}, f32[32]{0:T(128)}, u32[]{:S(2)}) copy-start(f32[32]{0:T(128)} %get-tuple-element.61) | copy-start | bytes 388
  230.5 0.6 copy-start.24
  231.1 4.5 %copy-start.15 = (bf16[1,256,64]{1,2,0:T(8,128)(2,1)S(1)}, bf16[1,256,64]{1,2,0:T(8,128)(2,1)}, u32[]{:S(2)}) copy-start(bf16[1,256,64]{1,2,0:T(8,128)(2,1)} %get-tuple-element.64) | copy-start | bytes 98308
  231.1 4.5 %copy-start.16 = (bf16[1,256,64]{1,2,0:T(8,128)(2,1)S(1)}, bf16[1,256,64]{1,2,0:T(8,128)(2,1)}, u32[]{:S(2)}) copy-start(bf16[1,256,64]{1,2,0:T(8,128)(2,1)} %get-tuple-element.65) | copy-start | bytes 98308
  236.7 7.4 %copy-start.7 = (bf16[8,1,8,128,128]{4,3,2,1,0:T(8,128)(2,1)S(1)}, bf16[8,1,8,128,128]{4,3,2,1,0:T(8,128)(2,1)}, u32[]{:S(2)}) copy-start(bf16[8,1,8,128,128]{4,3,2,1,0:T(8,128)(2,1)} %get-tuple-element.36) | copy-start | bytes 6291460
  236.7 8.4 %copy-start.14 = (bf16[1,8,128,128]{3,2,1,0:T(8,128)(2,1)S(1)}, bf16[1,8,128,128]{3,2,1,0:T(8,128)(2,1)}, u32[]{:S(2)}) copy-start(bf16[1,8,128,128]{3,2,1,0:T(8,128)(2,1)} %slice_bitcast_fusion.14) | copy-start | bytes 786436
  244.1 17.2 %collective-permute-start.19 = (bf16[1,8,128,128]{3,2,1,0:T(8,128)(2,1)S(1)}, bf16[1,8,128,128]{3,2,1,0:T(8,128)(2,1)S(1)}, u32[]{:S(2)}, u32[]{:S(2)}) collective-permute-start(bf16[1,8,128,128]{3,2,1,0:T(8,128)(2,1)S(1)} %get-tuple-element.30), channel_id=1, source_target_pairs={{0,12},{2,14},{4,0},{6,2},{8,4},{10,6},{12,8},{14,10},{1,13},{3,15... | collective-permute-start | bytes 786440 | tf_op jit(solution)/shard_map/ppermute | solution.py:125
  245.1 16.2 %collective-permute-start.20 = (bf16[1,8,128,128]{3,2,1,0:T(8,128)(2,1)S(1)}, bf16[1,8,128,128]{3,2,1,0:T(8,128)(2,1)S(1)}, u32[]{:S(2)}, u32[]{:S(2)}) collective-permute-start(bf16[1,8,128,128]{3,2,1,0:T(8,128)(2,1)S(1)} %copy-done.14), channel_id=1, source_target_pairs={{0,14},{2,0},{4,2},{6,4},{8,6},{10,8},{12,10},{14,12},{1,15},{3,1}... | collective-permute-start | bytes 786440 | tf_op jit(solution)/shard_map/ppermute | solution.py:125
  250.9 14.3 %copy-start.20 = (f32[4096]{0:T(1024)S(1)}, f32[4096]{0:T(1024)}, u32[]{:S(2)}) copy-start(f32[4096]{0:T(1024)} %broadcast_bitcast_fusion) | copy-start | bytes 49156
  261.4 1.3 copy-start.8

commit v12 on v9

--- a/solution.py
+++ b/solution.py
@@ -112,6 +112,17 @@
         * head_dim ** (-0.5)
     ).astype(jnp.bfloat16)
     query_rot = query_rot.reshape(rows, tokens, q_heads * head_dim)
+    early = lax.all_to_all(
+        jnp.concatenate(
+            [store[h][chosen] for h in range(kv_heads - 1)]
+            + [store[kv_heads - 1][chosen][..., :head_dim]],
+            axis=-1,
+        ),
+        "stretch", split_axis=0, concat_axis=0, tiled=True,
+    )
+    late = lax.all_to_all(
+        store[kv_heads - 1][chosen][..., head_dim:], "stretch", split_axis=0, concat_axis=0, tiled=True
+    )
     results = []
     for head in range(kv_heads):
         cols = slice(head * head_dim, (head + 1) * head_dim)
@@ -122,18 +133,14 @@
         group_cols = slice(head * request_group * head_dim, (head + 1) * request_group * head_dim)
         query_head = query_rot[..., group_cols]
         if last:
-            got_keys = lax.all_to_all(
-                store[head][chosen][..., :head_dim], "stretch", split_axis=0, concat_axis=0, tiled=True
-            )
+            got_keys = early[..., 2 * head * head_dim:]
             if results:
                 got_keys, earlier = lax.optimization_barrier((got_keys, results[-1]))
                 results[-1] = earlier
-            got_vals = lax.all_to_all(
-                store[head][chosen][..., head_dim:], "stretch", split_axis=0, concat_axis=0, tiled=True
-            )
+            got_vals = late
             raw_k = got_keys.reshape(flat, span, head_dim)[index]
         else:
-            got = lax.all_to_all(store[head][chosen], "stretch", split_axis=0, concat_axis=0, tiled=True)
+            got = early[..., 2 * head * head_dim:2 * (head + 1) * head_dim]
             if results:
                 got, earlier = lax.optimization_barrier((got, results[-1]))
                 results[-1] = earlier

time: 244 us -> 257 us (1.053)
  other arithmetic: 19.9 us -> 26.5 us
  local copies, waits for them, and re-layouts: 29.7 us -> 35.9 us
  waiting for transfers between devices: 130 us -> 135 us
  starting transfers between devices: 20.8 us -> 16.7 us
    slice x1 -> x3, local copies, waits for them, and re-layouts: 4.74 us -> 10.5 us  [the longest x1 4.74 us: shards(): got = early[..., 2 * head * head_dim:2 * (head + 1) * head_dim]]
    concatenate x0 -> x1, other arithmetic: none -> 5.61 us  [shards(): jnp.concatenate([store[h][chosen] for h in range(kv_heads - 1)] + [store[...]
    all_to_all x3 -> x2, waiting for transfers between devices: 125 us -> 130 us  [the longest x1 130 us: shards(): lax.all_to_all(jnp.concatenate([store[h][chosen] for h in range(kv_heads...]
    all_to_all x3 -> x2, starting transfers between devices: 13.5 us -> 9.43 us  [the longest x1 4.89 us: shards(): lax.all_to_all(jnp.concatenate([store[h][chosen] for h in range(kv_heads...]
  transfers between devices with their start and end apart: 4 -> 3, of which waited for: 4 -> 2; matrix products, arithmetic and copies ran while one was open for 16% -> 15% of each run, Pallas kernels for 10% -> 9%
where the time goes in v12:
time: 257 us
  waiting for transfers between devices  135 us (53%)
  Pallas kernels  41.7 us (16%)
  local copies, waits for them, and re-layouts  35.9 us (14%)
  other arithmetic  26.5 us (10%)
  starting transfers between devices  16.7 us (6%)
    all_to_all x1, waiting for transfers between devices, shards(): lax.all_to_all(jnp.concatenate([store[h][chosen] for h in range(kv_heads...  130 us
    pallas_call x3, Pallas kernels, flash(): pl.pallas_call(kernel, grid=(rows, kv_heads, per), in_specs=in_specs, out...  41.7 us
    unnamed x3, other arithmetic  8.98 us
    gather x2, local copies, waits for them, and re-layouts, shards(): got = got.reshape(flat, span, 2 * head_dim)[index]  7.38 us
    all_to_all x1, starting transfers between devices, shards(): lax.all_to_all(requests, 'stretch', split_axis=0, concat_axis=0, tiled=True)  7.28 us
    concatenate x1, other arithmetic, shards(): jnp.concatenate([store[h][chosen] for h in range(kv_heads - 1)] + [store[...  5.61 us
  transfers between devices with their start and end apart: 3, of which 2 were waited for; matrix products, arithmetic and copies ran while one was open for 15% of the time, Pallas kernels for 9%

profile of v12, /device:TPU:0, one launch (start us, length us, event | category | flops | bytes accessed | tf_op | source)
XLA Modules:
  0.0 256.5 jit_solution(4705302639514983989)
XLA Ops:
  0.7 0.7 fusion.44
  1.4 0.1 convert_reduce_fusion
  1.5 0.1 select_reduce_fusion
  1.6 0.1 sub.30
  1.7 0.7 multiply_convert_fusion.1
  2.4 0.1 copy.41
  2.5 0.1 reshape.830
  2.6 0.1 pad.17.clone
  2.7 0.6 pad_add_fusion
  3.3 7.3 %all-to-all-start = ((s32[8,1,72]{2,1,0:T(1,128)}), s32[8,1,72]{2,1,0:T(1,128)S(1)}, u32[]{:S(2)}, u32[]{:S(2)}) async-start(s32[8,1,72]{2,1,0:T(1,128)} %pad_add_fusion), calls=%async_computation | async-start | bytes 8192 | tf_op jit(solution)/shard_map/all_to_all | solution.py:82
  10.6 1.3 fusion.52
  11.9 0.3 fusion.51
  12.1 0.3 pad_maximum_fusion.3
  12.4 4.5 %all-to-all-done = s32[8,1,72]{2,1,0:T(1,128)S(1)} async-done(((s32[8,1,72]{2,1,0:T(1,128)}), s32[8,1,72]{2,1,0:T(1,128)S(1)}, u32[]{:S(2)}, u32[]{:S(2)}) %all-to-all-start) | async-done | bytes 2336 | tf_op jit(solution)/shard_map/all_to_all | solution.py:82
  17.0 0.1 reshape.759
  17.1 2.8 %gather_fusion.1 = bf16[64,128,256]{2,1,0:T(8,128)(2,1)} fusion(bf16[16,128,256]{2,1,0:T(8,128)(2,1)S(1)} %get-tuple-element.51, s32[1024]{0:T(1024)S(1)} %pad_clamp_fusion.2), kind=kCustom, calls=%fused_computation.1 | custom fusion | bytes 8388864 | tf_op jit(solution)/shard_map/gather | solution.py:118
  19.9 4.0 %fusion.49 = (bf16[8,1,8,128,128]{4,3,2,1,0:T(8,128)(2,1)}, bf16[8,1,8,128,128]{4,3,2,1,0:T(8,128)(2,1)S(1)}) fusion(bf16[8,1,8,128,256]{4,3,2,1,0:T(8,128)(2,1)} %bitcast.79), kind=kLoop, calls=%fused_computation.111 | loop fusion | bytes 8388608 | tf_op jit(solution)/shard_map/slice | solution.py:124
  23.9 2.8 %gather_fusion = bf16[64,128,256]{2,1,0:T(8,128)(2,1)} fusion(bf16[16,128,256]{2,1,0:T(8,128)(2,1)S(1)} %get-tuple-element.50, s32[1024]{0:T(1024)S(1)} %pad_clamp_fusion.2), kind=kCustom, calls=%fused_computation | custom fusion | bytes 8388864 | tf_op jit(solution)/shard_map/gather | solution.py:117
  26.6 5.6 %pad_maximum_fusion = bf16[8,1,8,128,384]{4,3,2,1,0:T(8,128)(2,1)} fusion(bf16[8,1,8,128,128]{4,3,2,1,0:T(8,128)(2,1)S(1)} %get-tuple-element.14, bf16[8,1,8,128,256]{4,3,2,1,0:T(8,128)(2,1)} %bitcast.78), kind=kLoop, calls=%fused_computation.6 | loop fusion | flops 12582912 | bytes 12582912 | tf_op jit(solution)/shard_map/concatenate | solution.py:116
  32.2 4.9 %all-to-all-start.1 = ((bf16[8,1,8,128,384]{4,3,2,1,0:T(8,128)(2,1)}), bf16[8,1,8,128,384]{4,3,2,1,0:T(8,128)(2,1)}, u32[]{:S(2)}, u32[]{:S(2)}) async-start(bf16[8,1,8,128,384]{4,3,2,1,0:T(8,128)(2,1)} %pad_maximum_fusion), calls=%async_computation.1 | async-start | bytes 12582912 | tf_op jit(solution)/shard_map/all_to_all | solution.py:115
  37.2 0.2 convert_bitcast_fusion
  37.4 0.4 copy.59
  37.8 0.5 multiply_cosine_fusion.1
  38.4 0.6 multiply_subtract_fusion
  39.0 0.6 fusion
  39.6 0.5 convert_element_type.194
  40.1 0.4 copy-done.5
  40.5 0.1 copy.53
  40.6 0.1 copy.54
  40.9 0.3 fusion.31
  41.3 1.1 fusion.50
  42.3 0.6 compare_select_fusion.refs_0_
  42.9 0.1 fusion.42
  43.0 0.2 mul.363
  43.3 0.6 gather_fusion.3
  43.9 0.1 copy.44
  44.0 0.1 broadcast_bitcast_fusion
  44.0 130.1 %all-to-all-done.1 = bf16[8,1,8,128,384]{4,3,2,1,0:T(8,128)(2,1)} async-done(((bf16[8,1,8,128,384]{4,3,2,1,0:T(8,128)(2,1)}), bf16[8,1,8,128,384]{4,3,2,1,0:T(8,128)(2,1)}, u32[]{:S(2)}, u32[]{:S(2)}) %all-to-all-start.1) | async-done | bytes 6291488 | tf_op jit(solution)/shard_map/all_to_all | solution.py:115
  174.1 4.5 %all-to-all-start.2 = ((bf16[8,1,8,128,128]{4,3,2,1,0:T(8,128)(2,1)}), bf16[8,1,8,128,128]{4,3,2,1,0:T(8,128)(2,1)}, u32[]{:S(2)}, u32[]{:S(2)}) async-start(bf16[8,1,8,128,128]{4,3,2,1,0:T(8,128)(2,1)} %get-tuple-element.13), calls=%async_computation.2 | async-start | bytes 4194304 | tf_op jit(solution)/shard_map/all_to_all | solution.py:123
  178.7 4.7 %slice.147 = bf16[8,1,8,128,256]{4,3,2,1,0:T(8,128)(2,1)} slice(bf16[8,1,8,128,384]{4,3,2,1,0:T(8,128)(2,1)} %all-to-all-done.1), slice={[0:8], [0:1], [0:8], [0:128], [0:256]} | slice | bytes 8388608 | tf_op jit(solution)/shard_map/slice | solution.py:143
  183.4 4.2 %gather_fusion.2 = bf16[32,128,256]{2,1,0:T(8,128)(2,1)} fusion(bf16[64,128,256]{2,1,0:T(8,128)(2,1)} %bitcast.80, s32[1024]{0:T(1024)S(1)} %pad_clamp_fusion.1), kind=kCustom, calls=%fused_computation.2 | custom fusion | bytes 4194432 | tf_op jit(solution)/shard_map/gather | solution.py:147
  187.6 3.2 %copy.43 = bf16[32,128,256]{1,2,0:T(8,128)(2,1)S(1)} copy(bf16[32,128,256]{2,1,0:T(8,128)(2,1)} %gather_fusion.2) | data formatting | bytes 4194304 | tf_op jit(solution)/shard_map/gather | solution.py:147
  190.8 1.3 multiply_convert_fusion
  192.1 4.2 %fusion.21 = (bf16[1,32,8,8,128]{4,3,2,1,0:T(8,128)(2,1)S(1)}, bf16[1,32,8,8,128]{4,3,2,1,0:T(8,128)(2,1)S(1)}) fusion(f32[1,32,128,128]{2,3,1,0:T(8,128)S(1)} %get-tuple-element.22, f32[64]{0:T(128)S(1)} %negate_power_fusion, f32[32,128]{1,0:T(8,128)S(1)} %add_convert_fusion), kind=kLoop, calls=%fused_computation.48 | loop fusion | flops 2359296 | bytes 3162368
  196.3 0.9 copy.66
  197.2 0.9 copy.67
  198.2 0.7 copy.48
  198.8 1.7 slice.145
  200.6 1.1 pad_maximum_fusion.1.refs_3_
  201.7 0.4 copy-done.2
  202.2 1.1 maximum_bitcast_fusion.refs_2_
  203.2 16.4 %shard_map.91.refs_5_ = bf16[1,256,2048]{2,1,0:T(8,128)(2,1)} custom-call(f32[1,1,4096]{2,1,0:T(1,128)} %compare_select_fusion.refs_0_, bf16[1,256,1024]{2,1,0:T(8,128)(2,1)} %get-tuple-element.23.refs_1_, bf16[1,128,4352]{2,1,0:T(8,128)(2,1)} %maximum_bitcast_fusion.refs_2_, bf16[1,4352,128]{2,1,0:T(8,128)(2,1)} %pad_maximum_fusion.1.refs_3_), custom_call_target="tpu_custom_call" | custom-call | flops 6845104128 | bytes 3276800 | tf_op jit(solution)/shard_map/pallas_call | solution.py:283
  219.7 0.7 gather_fusion.4
  220.4 0.7 copy.49
  221.1 0.2 convert_multiply_fusion.1
  221.3 4.5 %fusion.19 = (bf16[1,32,8,8,128]{4,3,2,1,0:T(8,128)(2,1)S(1)}, bf16[1,32,8,8,128]{4,3,2,1,0:T(8,128)(2,1)S(1)}) fusion(f32[1,32,128,128]{2,3,1,0:T(8,128)S(1)} %convert_multiply_fusion.1, f32[64]{0:T(128)S(1)} %negate_power_fusion, f32[32,128]{1,0:T(8,128)S(1)} %add_convert_fusion), kind=kLoop, calls=%fused_computation.46 | loop fusion | flops 2359296 | bytes 3162368
  225.8 0.1 copy.64
  225.9 0.1 copy.65
  226.0 1.1 maximum_bitcast_fusion.1.refs_2_
  227.1 7.3 %shard_map.92.refs_4_ = f32[1,256,1024]{2,1,0:T(8,128)} custom-call(f32[1,1,4096]{2,1,0:T(1,128)} %compare_select_fusion.refs_0_, bf16[1,256,1024]{2,1,0:T(8,128)(2,1)} %get-tuple-element.24.refs_1_, bf16[1,128,4352]{2,1,0:T(8,128)(2,1)} %maximum_bitcast_fusion.1.refs_2_), custom_call_target="tpu_custom_call" | custom-call | flops 2281701376 | bytes 3276800 | tf_op jit(solution)/shard_map/pallas_call | solution.py:283
  234.4 2.3 gather_fusion.5
  236.7 0.7 fusion.1
  237.4 1.1 pad_maximum_fusion.2.refs_3_
  238.5 18.0 %shard_map.93 = bf16[1,256,2048]{2,1,0:T(8,128)(2,1)} custom-call(f32[1,1,4096]{2,1,0:T(1,128)} %compare_select_fusion.refs_0_, bf16[1,256,1024]{2,1,0:T(8,128)(2,1)} %get-tuple-element.24.refs_1_, bf16[1,128,4352]{2,1,0:T(8,128)(2,1)} %maximum_bitcast_fusion.1.refs_2_, ...), custom_call_target="tpu_custom_call", output_to_operand_aliasing={{}: (5, {})} | custom-call | flops 4563402752 | bytes 3276800 | tf_op jit(solution)/shard_map/pallas_call | solution.py:283
  (30 shorter events, 0.3 us)
Async XLA Ops:
  0.0 11.8 %copy-start.4 = (bf16[16,128,256]{2,1,0:T(8,128)(2,1)S(1)}, bf16[16,128,256]{2,1,0:T(8,128)(2,1)}, u32[]{:S(2)}) copy-start(bf16[16,128,256]{2,1,0:T(8,128)(2,1)} %param.12) | copy-start | bytes 3145732
  3.3 13.7 %all-to-all-start = ((s32[8,1,72]{2,1,0:T(1,128)}), s32[8,1,72]{2,1,0:T(1,128)S(1)}, u32[]{:S(2)}, u32[]{:S(2)}) async-start(s32[8,1,72]{2,1,0:T(1,128)} %pad_add_fusion), calls=%async_computation | async-start | bytes 8192 | tf_op jit(solution)/shard_map/all_to_all | solution.py:82
  32.2 4.9 %copy-start.3 = (bf16[1,256,2048]{2,1,0:T(8,128)(2,1)S(1)}, bf16[1,256,2048]{2,1,0:T(8,128)(2,1)}, u32[]{:S(2)}) copy-start(bf16[1,256,2048]{2,1,0:T(8,128)(2,1)} %param.9) | copy-start | bytes 3145732
  32.2 141.9 %all-to-all-start.1 = ((bf16[8,1,8,128,384]{4,3,2,1,0:T(8,128)(2,1)}), bf16[8,1,8,128,384]{4,3,2,1,0:T(8,128)(2,1)}, u32[]{:S(2)}, u32[]{:S(2)}) async-start(bf16[8,1,8,128,384]{4,3,2,1,0:T(8,128)(2,1)} %pad_maximum_fusion), calls=%async_computation.1 | async-start | bytes 12582912 | tf_op jit(solution)/shard_map/all_to_all | solution.py:115
  39.6 0.9 copy-start.5
  39.6 1.2 copy-start.7
  39.6 1.3 copy-start.6
  174.1 60.2 %all-to-all-start.2 = ((bf16[8,1,8,128,128]{4,3,2,1,0:T(8,128)(2,1)}), bf16[8,1,8,128,128]{4,3,2,1,0:T(8,128)(2,1)}, u32[]{:S(2)}, u32[]{:S(2)}) async-start(bf16[8,1,8,128,128]{4,3,2,1,0:T(8,128)(2,1)} %get-tuple-element.13), calls=%async_computation.2 | async-start | bytes 4194304 | tf_op jit(solution)/shard_map/all_to_all | solution.py:123
  192.1 6.1 %copy-start = (bf16[1,32,128,128]{2,3,1,0:T(8,128)(2,1)S(1)}, bf16[1,32,128,128]{2,3,1,0:T(8,128)(2,1)}, u32[]{:S(2)}) copy-start(bf16[1,32,128,128]{2,3,1,0:T(8,128)(2,1)} %get-tuple-element.21) | copy-start | bytes 3145732
  200.6 1.2 copy-start.1
  200.6 1.6 copy-start.2

commit v13 on v10

--- a/solution.py
+++ b/solution.py
@@ -159,14 +159,7 @@
             [vals.reshape(rows, cache_length, head_dim), fresh_values[..., cols]], axis=1
         )
         if last and results:
-            mixed = jnp.einsum(
-                "rgtl,rld->rtgd", probs, values_all, preferred_element_type=jnp.float32
-            )
-            mixed = mixed / total.reshape(rows, tokens, request_group, head_dim)
-            mixed = mixed.astype(jnp.bfloat16).reshape(rows, tokens, request_group * head_dim)
-            results.append(lax.dynamic_update_slice_in_dim(
-                results[-1], mixed, head * request_group * head_dim, axis=2
-            ))
+            results.append(weigh(probs, values_all, total, results[-1], head * request_group))
             continue
         results.append(
             flash(
@@ -249,6 +242,37 @@
             acc = acc + part
         total = jnp.sum(total, axis=1, keepdims=True)
         o_ref[:, head * lanes:(head + 1) * lanes] = (acc / total).astype(o_ref.dtype)
+
+
+def weigh_kernel(p_ref, v_ref, t_ref, into_ref, o_ref):
+    lanes = 128
+    for head in range(p_ref.shape[0]):
+        acc = lax.dot_general(
+            p_ref[head], v_ref[...], (((1,), (0,)), ((), ())), preferred_element_type=jnp.float32
+        )
+        cols = slice(head * lanes, (head + 1) * lanes)
+        o_ref[:, cols] = (acc / t_ref[:, cols]).astype(o_ref.dtype)
+
+
+def weigh(probs, values_all, total, into, offset):
+    rows, q_heads, tokens, length = probs.shape
+    head_dim = values_all.shape[2]
+    heads = HEADS
+    per = q_heads // heads
+    block = offset // heads
+    return pl.pallas_call(
+        weigh_kernel,
+        grid=(rows, per),
+        in_specs=[
+            pl.BlockSpec((None, heads, tokens, length), lambda r, g: (r, g, 0, 0)),
+            pl.BlockSpec((None, length, head_dim), lambda r, g: (r, 0, 0)),
+            pl.BlockSpec((None, tokens, head_dim * heads), lambda r, g: (r, 0, g)),
+            pl.BlockSpec(memory_space=pl.ANY),
+        ],
+        out_specs=pl.BlockSpec((None, tokens, head_dim * heads), lambda r, g: (r, 0, block + g)),
+        out_shape=jax.ShapeDtypeStruct(into.shape, jnp.bfloat16),
+        input_output_aliases={3: 0},
+    )(probs, values_all, total, into)
 
 
 CHUNK = 512

time: 245 us -> 238 us (0.971)
  matrix products: 12.1 us -> 0 us
  Pallas kernels: 33.8 us -> 43.6 us
  local copies, waits for them, and re-layouts: 33.7 us -> 28.1 us
    dot_general x1 -> x0, matrix products: 12.1 us -> none  [shards(): jnp.einsum('rgtl,rld->rtgd', probs, values_all, preferred_element_type=jn...]
    pallas_call x0 -> x1, Pallas kernels: none -> 9.8 us  [weigh(): pl.pallas_call(weigh_kernel, grid=(rows, per), in_specs=[pl.BlockSpec((No...]
    reshape x2 -> x0, local copies, waits for them, and re-layouts: 2.78 us -> none  [the longest x1 2.58 us: shards(): mixed = mixed / total.reshape(rows, tokens, request_group, head_dim)]
where the time goes in v13:
time: 238 us; the launch traced here: 237 us
  waiting for transfers between devices  121 us (51%)
  Pallas kernels  43.6 us (18%)
  local copies, waits for them, and re-layouts  28.1 us (12%)
  other arithmetic  22.7 us (10%)
  starting transfers between devices  20.7 us (9%)
    all_to_all x1, waiting for transfers between devices, shards(): lax.all_to_all(store[head][chosen], 'stretch', split_axis=0, concat_axis=...  83 us
    pallas_call x2, Pallas kernels, flash(): pl.pallas_call(kernel, grid=(rows, kv_heads, per), in_specs=in_specs, out...  33.8 us
    all_to_all x1, waiting for transfers between devices, shards(): lax.all_to_all(store[head][chosen][..., :head_dim], 'stretch', split_axis...  33.4 us
    unnamed x3, other arithmetic  10 us
    pallas_call x1, Pallas kernels, weigh(): pl.pallas_call(weigh_kernel, grid=(rows, per), in_specs=[pl.BlockSpec((No...  9.8 us
    all_to_all x1, starting transfers between devices, shards(): lax.all_to_all(requests, 'stretch', split_axis=0, concat_axis=0, tiled=True)  7.28 us
    gather x2, local copies, waits for them, and re-layouts, shards(): got = got.reshape(flat, span, 2 * head_dim)[index]  5.77 us
    slice x1, local copies, waits for them, and re-layouts, shards(): store[head][chosen][..., :head_dim]  4.82 us
  transfers between devices with their start and end apart: 4, of which 3 were waited for; matrix products, arithmetic and copies ran while one was open for 17% of the time, Pallas kernels for 14%

profile of v13, /device:TPU:0, one launch (start us, length us, event | category | flops | bytes accessed | tf_op | source)
XLA Modules:
  0.0 237.0 jit_solution(18255132659635236712)
XLA Ops:
  0.0 0.8 fusion.44
  1.4 0.1 convert_reduce_fusion
  1.5 0.1 select_reduce_fusion
  1.6 0.1 sub.29
  1.7 0.7 multiply_convert_fusion.1
  2.4 0.1 copy.41
  2.5 0.1 reshape.830
  2.6 0.1 pad.17.clone
  2.7 0.6 pad_add_fusion
  3.3 7.3 %all-to-all-start = ((s32[8,1,72]{2,1,0:T(1,128)}), s32[8,1,72]{2,1,0:T(1,128)S(1)}, u32[]{:S(2)}, u32[]{:S(2)}) async-start(s32[8,1,72]{2,1,0:T(1,128)} %pad_add_fusion), calls=%async_computation | async-start | bytes 8192 | tf_op jit(solution)/shard_map/all_to_all | solution.py:82
  10.6 1.3 fusion.51
  11.9 0.3 fusion.50
  12.2 0.3 pad_maximum_fusion.2
  12.4 4.5 %all-to-all-done = s32[8,1,72]{2,1,0:T(1,128)S(1)} async-done(((s32[8,1,72]{2,1,0:T(1,128)}), s32[8,1,72]{2,1,0:T(1,128)S(1)}, u32[]{:S(2)}, u32[]{:S(2)}) %all-to-all-start) | async-done | bytes 2336 | tf_op jit(solution)/shard_map/all_to_all | solution.py:82
  17.0 0.1 reshape.759
  17.1 2.8 %gather_fusion.1 = bf16[64,128,256]{2,1,0:T(8,128)(2,1)} fusion(bf16[16,128,256]{2,1,0:T(8,128)(2,1)S(1)} %get-tuple-element.57, s32[1024]{0:T(1024)S(1)} %pad_clamp_fusion.2), kind=kCustom, calls=%fused_computation.1 | custom fusion | bytes 8388864 | tf_op jit(solution)/shard_map/gather | solution.py:136
  19.9 4.5 %all-to-all-start.3 = ((bf16[8,1,8,128,256]{4,3,2,1,0:T(8,128)(2,1)}), bf16[8,1,8,128,256]{4,3,2,1,0:T(8,128)(2,1)}, u32[]{:S(2)}, u32[]{:S(2)}) async-start(bf16[8,1,8,128,256]{4,3,2,1,0:T(8,128)(2,1)} %bitcast.78), calls=%async_computation.3 | async-start | bytes 8388608 | tf_op jit(solution)/shard_map/all_to_all | solution.py:136
  24.4 1.5 convert_bitcast_fusion
  25.9 2.8 %gather_fusion = bf16[64,128,256]{2,1,0:T(8,128)(2,1)} fusion(bf16[16,128,256]{2,1,0:T(8,128)(2,1)S(1)} %get-tuple-element.56, s32[1024]{0:T(1024)S(1)} %pad_clamp_fusion.2), kind=kCustom, calls=%fused_computation | custom fusion | bytes 8388864 | tf_op jit(solution)/shard_map/gather | solution.py:132
  28.7 4.8 %fusion.49 = (bf16[8,1,8,128,128]{4,3,2,1,0:T(8,128)(2,1)}, bf16[8,1,8,128,128]{4,3,2,1,0:T(8,128)(2,1)}) fusion(bf16[8,1,8,128,256]{4,3,2,1,0:T(8,128)(2,1)} %bitcast.79), kind=kLoop, calls=%fused_computation.110 | loop fusion | bytes 8388608 | tf_op jit(solution)/shard_map/slice | solution.py:126
  33.5 83.0 %all-to-all-done.3 = bf16[8,1,8,128,256]{4,3,2,1,0:T(8,128)(2,1)} async-done(((bf16[8,1,8,128,256]{4,3,2,1,0:T(8,128)(2,1)}), bf16[8,1,8,128,256]{4,3,2,1,0:T(8,128)(2,1)}, u32[]{:S(2)}, u32[]{:S(2)}) %all-to-all-start.3) | async-done | bytes 4194336 | tf_op jit(solution)/shard_map/all_to_all | solution.py:136
  116.4 4.4 %all-to-all-start.2 = ((bf16[8,1,8,128,128]{4,3,2,1,0:T(8,128)(2,1)}), bf16[8,1,8,128,128]{4,3,2,1,0:T(8,128)(2,1)}, u32[]{:S(2)}, u32[]{:S(2)}) async-start(bf16[8,1,8,128,128]{4,3,2,1,0:T(8,128)(2,1)} %get-tuple-element.19), calls=%async_computation.2 | async-start | bytes 4194304 | tf_op jit(solution)/shard_map/all_to_all | solution.py:125
  120.8 0.4 copy.59
  121.2 0.5 multiply_cosine_fusion.1
  121.8 0.6 multiply_subtract_fusion
  122.4 0.6 fusion
  123.0 0.0 copy-start.1
  123.0 0.5 convert_element_type.197
  123.5 0.4 copy-done.1
  123.9 0.1 copy.53
  124.1 0.1 copy.54
  124.2 0.1 add_convert_fusion
  124.3 0.3 fusion.31
  124.7 1.1 fusion.52
  125.7 0.6 compare_select_fusion.refs_0_
  126.3 0.1 fusion.42
  126.4 0.2 mul.362
  126.7 0.6 gather_fusion.3
  127.3 0.1 copy.44
  127.4 0.1 broadcast_bitcast_fusion
  127.4 2.9 %gather_fusion.2 = bf16[32,128,256]{2,1,0:T(8,128)(2,1)S(1)} fusion(bf16[64,128,256]{2,1,0:T(8,128)(2,1)} %bitcast.9, s32[1024]{0:T(1024)S(1)} %pad_clamp_fusion.1), kind=kCustom, calls=%fused_computation.2 | custom fusion | bytes 4194432 | tf_op jit(solution)/shard_map/gather | solution.py:140
  130.3 2.9 %copy.43 = bf16[32,128,256]{1,2,0:T(8,128)(2,1)} copy(bf16[32,128,256]{2,1,0:T(8,128)(2,1)S(1)} %gather_fusion.2) | data formatting | bytes 4194304 | tf_op jit(solution)/shard_map/gather | solution.py:140
  133.2 1.9 multiply_convert_fusion
  135.2 33.4 %all-to-all-done.2 = bf16[8,1,8,128,128]{4,3,2,1,0:T(8,128)(2,1)} async-done(((bf16[8,1,8,128,128]{4,3,2,1,0:T(8,128)(2,1)}), bf16[8,1,8,128,128]{4,3,2,1,0:T(8,128)(2,1)}, u32[]{:S(2)}, u32[]{:S(2)}) %all-to-all-start.2) | async-done | bytes 2097184 | tf_op jit(solution)/shard_map/all_to_all | solution.py:125
  168.6 4.5 %all-to-all-start.1 = ((bf16[8,1,8,128,128]{4,3,2,1,0:T(8,128)(2,1)}), bf16[8,1,8,128,128]{4,3,2,1,0:T(8,128)(2,1)}, u32[]{:S(2)}, u32[]{:S(2)}) async-start(bf16[8,1,8,128,128]{4,3,2,1,0:T(8,128)(2,1)} %get-tuple-element.20), calls=%async_computation.1 | async-start | bytes 4194304 | tf_op jit(solution)/shard_map/all_to_all | solution.py:131
  173.1 4.3 %fusion.21 = (bf16[1,32,8,8,128]{4,3,2,1,0:T(8,128)(2,1)S(1)}, bf16[1,32,8,8,128]{4,3,2,1,0:T(8,128)(2,1)S(1)}) fusion(f32[1,32,128,128]{2,3,1,0:T(8,128)S(1)} %get-tuple-element.28, f32[64]{0:T(128)S(1)} %negate_power_fusion, f32[32,128]{1,0:T(8,128)S(1)} %add_convert_fusion), kind=kLoop, calls=%fused_computation.47 | loop fusion | flops 2359296 | bytes 3162368
  177.4 0.1 copy.66
  177.5 0.1 copy.67
  177.6 0.7 copy.48
  178.3 1.1 pad_maximum_fusion.refs_3_
  179.4 1.1 maximum_bitcast_fusion.refs_2_
  180.4 16.4 %shard_map.91.into_ref = bf16[1,256,2048]{2,1,0:T(8,128)(2,1)} custom-call(f32[1,1,4096]{2,1,0:T(1,128)} %compare_select_fusion.refs_0_, bf16[1,256,1024]{2,1,0:T(8,128)(2,1)} %get-tuple-element.33.refs_1_, bf16[1,128,4352]{2,1,0:T(8,128)(2,1)} %maximum_bitcast_fusion.refs_2_, bf16[1,4352,128]{2,1,0:T(8,128)(2,1)} %pad_maximum_fusion.refs_3_), custom_call_target="tpu_custom_call" | custom-call | flops 6845104128 | bytes 3276800 | tf_op jit(solution)/shard_map/pallas_call | solution.py:332
  196.9 2.3 gather_fusion.4
  199.2 0.7 copy.49
  199.9 0.2 convert_multiply_fusion.1
  200.1 4.3 %fusion.19 = (bf16[1,32,8,8,128]{4,3,2,1,0:T(8,128)(2,1)S(1)}, bf16[1,32,8,8,128]{4,3,2,1,0:T(8,128)(2,1)S(1)}) fusion(f32[1,32,128,128]{2,3,1,0:T(8,128)S(1)} %convert_multiply_fusion.1, f32[64]{0:T(128)S(1)} %negate_power_fusion, f32[32,128]{1,0:T(8,128)S(1)} %add_convert_fusion), kind=kLoop, calls=%fused_computation.45 | loop fusion | flops 2359296 | bytes 3162368
  204.4 0.1 copy.64
  204.5 0.1 copy.65
  204.6 1.1 maximum_bitcast_fusion.1.refs_2_
  205.7 17.3 %shard_map.92 = (bf16[1,8,256,4352]{3,2,1,0:T(8,128)(2,1)}, f32[1,256,1024]{2,1,0:T(8,128)}) custom-call(f32[1,1,4096]{2,1,0:T(1,128)} %compare_select_fusion.refs_0_, bf16[1,256,1024]{2,1,0:T(8,128)(2,1)} %get-tuple-element.34.refs_1_, bf16[1,128,4352]{2,1,0:T(8,128)(2,1)} %maximum_bitcast_fusion.1.refs_2_), custom_call_target="tpu_custom_call" | custom-call | flops 4563402752 | bytes 3276800 | tf_op jit(solution)/shard_map/pallas_call | solution.py:332
  223.0 2.3 gather_fusion.5
  225.4 0.7 fusion.1
  226.1 1.1 pad_maximum_fusion.1.v_ref
  227.2 9.8 %shard_map.93 = bf16[1,256,2048]{2,1,0:T(8,128)(2,1)} custom-call(bf16[1,8,256,4352]{3,2,1,0:T(8,128)(2,1)} %get-tuple-element.15.p_ref, bf16[1,4352,128]{2,1,0:T(8,128)(2,1)} %pad_maximum_fusion.1.v_ref, f32[1,256,1024]{2,1,0:T(8,128)} %get-tuple-element.17.t_ref, bf16[1,256,2048]{2,1,0:T(8,128)(2,1)} %shard_map.91.into_ref), custom_call_target="tpu_custom_call", output_to_operand_aliasing={{}: (3, {})} | custom-call | tf_op jit(solution)/shard_map/pallas_call | solution.py:263
  (21 shorter events, 0.1 us)
Async XLA Ops:
  0.0 11.9 %copy-start = (bf16[16,128,256]{2,1,0:T(8,128)(2,1)S(1)}, bf16[16,128,256]{2,1,0:T(8,128)(2,1)}, u32[]{:S(2)}) copy-start(bf16[16,128,256]{2,1,0:T(8,128)(2,1)} %param.12) | copy-start | bytes 3145732
  3.3 13.7 %all-to-all-start = ((s32[8,1,72]{2,1,0:T(1,128)}), s32[8,1,72]{2,1,0:T(1,128)S(1)}, u32[]{:S(2)}, u32[]{:S(2)}) async-start(s32[8,1,72]{2,1,0:T(1,128)} %pad_add_fusion), calls=%async_computation | async-start | bytes 8192 | tf_op jit(solution)/shard_map/all_to_all | solution.py:82
  19.9 96.6 %all-to-all-start.3 = ((bf16[8,1,8,128,256]{4,3,2,1,0:T(8,128)(2,1)}), bf16[8,1,8,128,256]{4,3,2,1,0:T(8,128)(2,1)}, u32[]{:S(2)}, u32[]{:S(2)}) async-start(bf16[8,1,8,128,256]{4,3,2,1,0:T(8,128)(2,1)} %bitcast.78), calls=%async_computation.3 | async-start | bytes 8388608 | tf_op jit(solution)/shard_map/all_to_all | solution.py:136
  116.4 52.2 %all-to-all-start.2 = ((bf16[8,1,8,128,128]{4,3,2,1,0:T(8,128)(2,1)}), bf16[8,1,8,128,128]{4,3,2,1,0:T(8,128)(2,1)}, u32[]{:S(2)}, u32[]{:S(2)}) async-start(bf16[8,1,8,128,128]{4,3,2,1,0:T(8,128)(2,1)} %get-tuple-element.19), calls=%async_computation.2 | async-start | bytes 4194304 | tf_op jit(solution)/shard_map/all_to_all | solution.py:125
  123.0 0.9 copy-start.1
  123.0 1.2 copy-start.3
  123.0 1.3 copy-start.2
  168.6 54.4 %all-to-all-start.1 = ((bf16[8,1,8,128,128]{4,3,2,1,0:T(8,128)(2,1)}), bf16[8,1,8,128,128]{4,3,2,1,0:T(8,128)(2,1)}, u32[]{:S(2)}, u32[]{:S(2)}) async-start(bf16[8,1,8,128,128]{4,3,2,1,0:T(8,128)(2,1)} %get-tuple-element.20), calls=%async_computation.1 | async-start | bytes 4194304 | tf_op jit(solution)/shard_map/all_to_all | solution.py:131

commit v14 on v13

--- a/solution.py
+++ b/solution.py
@@ -128,9 +128,11 @@
             if results:
                 got_keys, earlier = lax.optimization_barrier((got_keys, results[-1]))
                 results[-1] = earlier
-            got_vals = lax.all_to_all(
-                store[head][chosen][..., head_dim:], "stretch", split_axis=0, concat_axis=0, tiled=True
-            )
+            send_vals = store[head][chosen][..., head_dim:]
+            if results:
+                send_vals, earlier = lax.optimization_barrier((send_vals, results[-1]))
+                results[-1] = earlier
+            got_vals = lax.all_to_all(send_vals, "stretch", split_axis=0, concat_axis=0, tiled=True)
             raw_k = got_keys.reshape(flat, span, head_dim)[index]
         else:
             got = lax.all_to_all(store[head][chosen], "stretch", split_axis=0, concat_axis=0, tiled=True)

time: 238 us -> 234 us (0.983)
  waiting for transfers between devices: 121 us -> 118 us
    all_to_all x1, waiting for transfers between devices: 0.01 us -> 20.3 us  [shards(): lax.all_to_all(send_vals, 'stretch', split_axis=0, concat_axis=0, tiled=T...]
    all_to_all x1, waiting for transfers between devices: 33.4 us -> 13.3 us  [shards(): lax.all_to_all(store[head][chosen][..., :head_dim], 'stretch', split_axis...]
    all_to_all x1, waiting for transfers between devices: 83 us -> 80.4 us  [shards(): lax.all_to_all(store[head][chosen], 'stretch', split_axis=0, concat_axis=...]
  transfers between devices with their start and end apart: 4 -> 4, of which waited for: 3 -> 4; matrix products, arithmetic and copies ran while one was open for 17% -> 18% of each run, Pallas kernels for 14% -> 14%
where the time goes in v14:
time: 234 us; the launch traced here: 233 us
  waiting for transfers between devices  118 us (50%)
  Pallas kernels  43.4 us (19%)
  local copies, waits for them, and re-layouts  28.9 us (12%)
  other arithmetic  21.1 us (9%)
  starting transfers between devices  20.5 us (9%)
    all_to_all x1, waiting for transfers between devices, shards(): lax.all_to_all(store[head][chosen], 'stretch', split_axis=0, concat_axis=...  80.4 us
    pallas_call x2, Pallas kernels, flash(): pl.pallas_call(kernel, grid=(rows, kv_heads, per), in_specs=in_specs, out...  33.7 us
    all_to_all x1, waiting for transfers between devices, shards(): lax.all_to_all(send_vals, 'stretch', split_axis=0, concat_axis=0, tiled=T...  20.3 us
    all_to_all x1, waiting for transfers between devices, shards(): lax.all_to_all(store[head][chosen][..., :head_dim], 'stretch', split_axis...  13.3 us
    pallas_call x1, Pallas kernels, weigh(): pl.pallas_call(weigh_kernel, grid=(rows, per), in_specs=[pl.BlockSpec((No...  9.76 us
    unnamed x3, other arithmetic  8.78 us
    gather x2, local copies, waits for them, and re-layouts, shards(): got = got.reshape(flat, span, 2 * head_dim)[index]  7.45 us
    all_to_all x1, starting transfers between devices, shards(): lax.all_to_all(requests, 'stretch', split_axis=0, concat_axis=0, tiled=True)  7.28 us
  transfers between devices with their start and end apart: 4, of which 4 were waited for; matrix products, arithmetic and copies ran while one was open for 18% of the time, Pallas kernels for 14%

profile of v14, /device:TPU:0, one launch (start us, length us, event | category | flops | bytes accessed | tf_op | source)
XLA Modules:
  0.0 233.4 jit_solution(611726154715758261)
XLA Ops:
  0.0 0.8 fusion.44
  1.4 0.1 convert_reduce_fusion
  1.5 0.1 select_reduce_fusion
  1.6 0.1 sub.29
  1.7 0.7 multiply_convert_fusion.1
  2.4 0.1 copy.41
  2.5 0.1 reshape.830
  2.6 0.1 pad.17.clone
  2.7 0.6 pad_add_fusion
  3.3 7.3 %all-to-all-start = ((s32[8,1,72]{2,1,0:T(1,128)}), s32[8,1,72]{2,1,0:T(1,128)S(1)}, u32[]{:S(2)}, u32[]{:S(2)}) async-start(s32[8,1,72]{2,1,0:T(1,128)} %pad_add_fusion), calls=%async_computation | async-start | bytes 8192 | tf_op jit(solution)/shard_map/all_to_all | solution.py:82
  10.6 1.3 fusion.52
  11.9 0.3 fusion.51
  12.2 0.3 pad_maximum_fusion.2
  12.4 4.5 %all-to-all-done = s32[8,1,72]{2,1,0:T(1,128)S(1)} async-done(((s32[8,1,72]{2,1,0:T(1,128)}), s32[8,1,72]{2,1,0:T(1,128)S(1)}, u32[]{:S(2)}, u32[]{:S(2)}) %all-to-all-start) | async-done | bytes 2336 | tf_op jit(solution)/shard_map/all_to_all | solution.py:82
  17.0 0.1 reshape.759
  17.1 2.8 %gather_fusion.1 = bf16[64,128,256]{2,1,0:T(8,128)(2,1)} fusion(bf16[16,128,256]{2,1,0:T(8,128)(2,1)S(1)} %get-tuple-element.61, s32[1024]{0:T(1024)S(1)} %pad_clamp_fusion.2), kind=kCustom, calls=%fused_computation.1 | custom fusion | bytes 8388864 | tf_op jit(solution)/shard_map/gather | solution.py:138
  19.9 4.7 %all-to-all-start.2 = ((bf16[8,1,8,128,256]{4,3,2,1,0:T(8,128)(2,1)}), bf16[8,1,8,128,256]{4,3,2,1,0:T(8,128)(2,1)}, u32[]{:S(2)}, u32[]{:S(2)}) async-start(bf16[8,1,8,128,256]{4,3,2,1,0:T(8,128)(2,1)} %bitcast.78), calls=%async_computation.2 | async-start | bytes 8388608 | tf_op jit(solution)/shard_map/all_to_all | solution.py:138
  24.6 0.2 convert_bitcast_fusion
  24.8 0.4 copy.59
  25.3 0.5 multiply_cosine_fusion.1
  25.8 0.6 multiply_subtract_fusion
  26.4 0.6 fusion
  27.1 0.5 convert_element_type.197
  27.6 0.4 copy-done.2
  28.0 0.1 copy.54
  28.1 0.1 copy.53
  28.3 0.3 fusion.35
  28.6 2.8 %gather_fusion = bf16[64,128,256]{2,1,0:T(8,128)(2,1)} fusion(bf16[16,128,256]{2,1,0:T(8,128)(2,1)S(1)} %get-tuple-element.60, s32[1024]{0:T(1024)S(1)} %pad_clamp_fusion.2), kind=kCustom, calls=%fused_computation | custom fusion | bytes 8388864 | tf_op jit(solution)/shard_map/gather | solution.py:131
  31.4 4.8 %fusion.49 = (bf16[8,1,8,128,128]{4,3,2,1,0:T(8,128)(2,1)}, bf16[8,1,8,128,128]{4,3,2,1,0:T(8,128)(2,1)}) fusion(bf16[8,1,8,128,256]{4,3,2,1,0:T(8,128)(2,1)} %bitcast.79), kind=kLoop, calls=%fused_computation.110 | loop fusion | bytes 8388608 | tf_op jit(solution)/shard_map/slice | solution.py:126
  36.2 80.4 %all-to-all-done.2 = bf16[8,1,8,128,256]{4,3,2,1,0:T(8,128)(2,1)} async-done(((bf16[8,1,8,128,256]{4,3,2,1,0:T(8,128)(2,1)}), bf16[8,1,8,128,256]{4,3,2,1,0:T(8,128)(2,1)}, u32[]{:S(2)}, u32[]{:S(2)}) %all-to-all-start.2) | async-done | bytes 4194336 | tf_op jit(solution)/shard_map/all_to_all | solution.py:138
  116.6 4.7 %all-to-all-start.1 = ((bf16[8,1,8,128,128]{4,3,2,1,0:T(8,128)(2,1)}), bf16[8,1,8,128,128]{4,3,2,1,0:T(8,128)(2,1)}, u32[]{:S(2)}, u32[]{:S(2)}) async-start(bf16[8,1,8,128,128]{4,3,2,1,0:T(8,128)(2,1)} %get-tuple-element.23), calls=%async_computation.1 | async-start | bytes 4194304 | tf_op jit(solution)/shard_map/all_to_all | solution.py:125
  121.3 0.1 add_convert_fusion
  121.4 1.1 fusion.50
  122.5 0.6 compare_select_fusion.refs_0_
  123.1 0.1 fusion.42
  123.2 0.2 mul.362
  123.4 0.6 gather_fusion.3
  124.0 0.1 copy.44
  124.1 4.2 %gather_fusion.2 = bf16[32,128,256]{2,1,0:T(8,128)(2,1)} fusion(bf16[64,128,256]{2,1,0:T(8,128)(2,1)} %bitcast.9, s32[1024]{0:T(1024)S(1)} %pad_clamp_fusion.1), kind=kCustom, calls=%fused_computation.2 | custom fusion | bytes 4194432 | tf_op jit(solution)/shard_map/gather | solution.py:142
  128.3 3.2 %copy.43 = bf16[32,128,256]{1,2,0:T(8,128)(2,1)S(1)} copy(bf16[32,128,256]{2,1,0:T(8,128)(2,1)} %gather_fusion.2) | data formatting | bytes 4194304 | tf_op jit(solution)/shard_map/gather | solution.py:142
  131.6 0.4 multiply_convert_fusion
  132.0 4.3 %fusion.21 = (bf16[1,32,8,8,128]{4,3,2,1,0:T(8,128)(2,1)S(1)}, bf16[1,32,8,8,128]{4,3,2,1,0:T(8,128)(2,1)S(1)}) fusion(f32[1,32,128,128]{2,3,1,0:T(8,128)S(1)} %get-tuple-element.32, f32[64]{0:T(128)S(1)} %negate_power_fusion, f32[32,128]{1,0:T(8,128)S(1)} %add_convert_fusion), kind=kLoop, calls=%fused_computation.47 | loop fusion | flops 2359296 | bytes 3162368
  136.3 0.1 copy.66
  136.4 0.1 copy.67
  136.5 0.7 copy.48
  137.1 1.1 pad_maximum_fusion.refs_3_
  138.2 1.1 maximum_bitcast_fusion.refs_2_
  139.3 16.4 %shard_map.91.into_ref = bf16[1,256,2048]{2,1,0:T(8,128)(2,1)} custom-call(f32[1,1,4096]{2,1,0:T(1,128)} %compare_select_fusion.refs_0_, bf16[1,256,1024]{2,1,0:T(8,128)(2,1)} %get-tuple-element.34.refs_1_, bf16[1,128,4352]{2,1,0:T(8,128)(2,1)} %maximum_bitcast_fusion.refs_2_, bf16[1,4352,128]{2,1,0:T(8,128)(2,1)} %pad_maximum_fusion.refs_3_), custom_call_target="tpu_custom_call" | custom-call | flops 6845104128 | bytes 3276800 | tf_op jit(solution)/shard_map/pallas_call | solution.py:334
  155.7 13.3 %all-to-all-done.1 = bf16[8,1,8,128,128]{4,3,2,1,0:T(8,128)(2,1)} async-done(((bf16[8,1,8,128,128]{4,3,2,1,0:T(8,128)(2,1)}), bf16[8,1,8,128,128]{4,3,2,1,0:T(8,128)(2,1)}, u32[]{:S(2)}, u32[]{:S(2)}) %all-to-all-start.1) | async-done | bytes 2097184 | tf_op jit(solution)/shard_map/all_to_all | solution.py:125
  169.0 3.8 %all-to-all-start.3 = ((bf16[8,1,8,128,128]{4,3,2,1,0:T(8,128)(2,1)}), bf16[8,1,8,128,128]{4,3,2,1,0:T(8,128)(2,1)S(1)}, u32[]{:S(2)}, u32[]{:S(2)}) async-start(bf16[8,1,8,128,128]{4,3,2,1,0:T(8,128)(2,1)} %get-tuple-element.15), calls=%async_computation.3 | async-start | bytes 4194304 | tf_op jit(solution)/shard_map/all_to_all | solution.py:135
  172.8 0.1 broadcast_bitcast_fusion
  172.9 2.3 %gather_fusion.4 = bf16[32,128,128]{2,1,0:T(8,128)(2,1)S(1)} fusion(bf16[64,128,128]{2,1,0:T(8,128)(2,1)} %bitcast.19, s32[1024]{0:T(1024)S(1)} %pad_clamp_fusion.1), kind=kCustom, calls=%fused_computation.4 | custom fusion | bytes 2097280 | tf_op jit(solution)/shard_map/gather | solution.py:136
  175.2 1.3 copy.49
  176.6 1.4 convert_multiply_fusion.1
  178.0 4.3 %fusion.19 = (bf16[1,32,8,8,128]{4,3,2,1,0:T(8,128)(2,1)S(1)}, bf16[1,32,8,8,128]{4,3,2,1,0:T(8,128)(2,1)S(1)}) fusion(f32[1,32,128,128]{2,3,1,0:T(8,128)S(1)} %convert_multiply_fusion.1, f32[64]{0:T(128)S(1)} %negate_power_fusion, f32[32,128]{1,0:T(8,128)S(1)} %add_convert_fusion), kind=kLoop, calls=%fused_computation.45 | loop fusion | flops 2359296 | bytes 3162368
  182.3 0.1 copy.64
  182.4 0.1 copy.65
  182.5 1.1 maximum_bitcast_fusion.1.refs_2_
  183.5 17.2 %shard_map.92 = (bf16[1,8,256,4352]{3,2,1,0:T(8,128)(2,1)}, f32[1,256,1024]{2,1,0:T(8,128)}) custom-call(f32[1,1,4096]{2,1,0:T(1,128)} %compare_select_fusion.refs_0_, bf16[1,256,1024]{2,1,0:T(8,128)(2,1)} %get-tuple-element.33.refs_1_, bf16[1,128,4352]{2,1,0:T(8,128)(2,1)} %maximum_bitcast_fusion.1.refs_2_), custom_call_target="tpu_custom_call" | custom-call | flops 4563402752 | bytes 3276800 | tf_op jit(solution)/shard_map/pallas_call | solution.py:334
  200.8 20.3 %all-to-all-done.3 = bf16[8,1,8,128,128]{4,3,2,1,0:T(8,128)(2,1)S(1)} async-done(((bf16[8,1,8,128,128]{4,3,2,1,0:T(8,128)(2,1)}), bf16[8,1,8,128,128]{4,3,2,1,0:T(8,128)(2,1)S(1)}, u32[]{:S(2)}, u32[]{:S(2)}) %all-to-all-start.3) | async-done | bytes 2097184 | tf_op jit(solution)/shard_map/all_to_all | solution.py:135
  221.1 0.7 gather_fusion.5
  221.8 0.7 fusion.1
  222.5 1.1 pad_maximum_fusion.1.v_ref
  223.6 9.8 %shard_map.93 = bf16[1,256,2048]{2,1,0:T(8,128)(2,1)} custom-call(bf16[1,8,256,4352]{3,2,1,0:T(8,128)(2,1)} %get-tuple-element.19.p_ref, bf16[1,4352,128]{2,1,0:T(8,128)(2,1)} %pad_maximum_fusion.1.v_ref, f32[1,256,1024]{2,1,0:T(8,128)} %get-tuple-element.21.t_ref, bf16[1,256,2048]{2,1,0:T(8,128)(2,1)} %shard_map.91.into_ref), custom_call_target="tpu_custom_call", output_to_operand_aliasing={{}: (3, {})} | custom-call | tf_op jit(solution)/shard_map/pallas_call | solution.py:265
  (23 shorter events, 0.1 us)
Async XLA Ops:
  0.0 11.9 %copy-start.1 = (bf16[16,128,256]{2,1,0:T(8,128)(2,1)S(1)}, bf16[16,128,256]{2,1,0:T(8,128)(2,1)}, u32[]{:S(2)}) copy-start(bf16[16,128,256]{2,1,0:T(8,128)(2,1)} %param.12) | copy-start | bytes 3145732
  3.3 13.7 %all-to-all-start = ((s32[8,1,72]{2,1,0:T(1,128)}), s32[8,1,72]{2,1,0:T(1,128)S(1)}, u32[]{:S(2)}, u32[]{:S(2)}) async-start(s32[8,1,72]{2,1,0:T(1,128)} %pad_add_fusion), calls=%async_computation | async-start | bytes 8192 | tf_op jit(solution)/shard_map/all_to_all | solution.py:82
  19.9 4.7 %copy-start = (bf16[1,256,2048]{2,1,0:T(8,128)(2,1)S(1)}, bf16[1,256,2048]{2,1,0:T(8,128)(2,1)}, u32[]{:S(2)}) copy-start(bf16[1,256,2048]{2,1,0:T(8,128)(2,1)} %param.9) | copy-start | bytes 3145732
  19.9 96.7 %all-to-all-start.2 = ((bf16[8,1,8,128,256]{4,3,2,1,0:T(8,128)(2,1)}), bf16[8,1,8,128,256]{4,3,2,1,0:T(8,128)(2,1)}, u32[]{:S(2)}, u32[]{:S(2)}) async-start(bf16[8,1,8,128,256]{4,3,2,1,0:T(8,128)(2,1)} %bitcast.78), calls=%async_computation.2 | async-start | bytes 8388608 | tf_op jit(solution)/shard_map/all_to_all | solution.py:138
  27.0 0.9 copy-start.2
  27.0 1.2 copy-start.3
  116.6 4.7 %copy-start.4 = (s32[1,32]{1,0:T(1,128)S(1)}, s32[1,32]{1,0:T(1,128)}, u32[]{:S(2)}) copy-start(s32[1,32]{1,0:T(1,128)} %param.17) | copy-start | bytes 388
  116.6 52.4 %all-to-all-start.1 = ((bf16[8,1,8,128,128]{4,3,2,1,0:T(8,128)(2,1)}), bf16[8,1,8,128,128]{4,3,2,1,0:T(8,128)(2,1)}, u32[]{:S(2)}, u32[]{:S(2)}) async-start(bf16[8,1,8,128,128]{4,3,2,1,0:T(8,128)(2,1)} %get-tuple-element.23), calls=%async_computation.1 | async-start | bytes 4194304 | tf_op jit(solution)/shard_map/all_to_all | solution.py:125
  169.0 52.1 %all-to-all-start.3 = ((bf16[8,1,8,128,128]{4,3,2,1,0:T(8,128)(2,1)}), bf16[8,1,8,128,128]{4,3,2,1,0:T(8,128)(2,1)S(1)}, u32[]{:S(2)}, u32[]{:S(2)}) async-start(bf16[8,1,8,128,128]{4,3,2,1,0:T(8,128)(2,1)} %get-tuple-element.15), calls=%async_computation.3 | async-start | bytes 4194304 | tf_op jit(solution)/shard_map/all_to_all | solution.py:135

commit v15 on v14

--- a/solution.py
+++ b/solution.py
@@ -259,7 +259,7 @@
 def weigh(probs, values_all, total, into, offset):
     rows, q_heads, tokens, length = probs.shape
     head_dim = values_all.shape[2]
-    heads = HEADS
+    heads = 1
     per = q_heads // heads
     block = offset // heads
     return pl.pallas_call(

time: 234 us -> 236 us (level)
  no operation moved by 1% of the time
where the time goes in v15:
time: 236 us; the launch traced here: 235 us
  waiting for transfers between devices  118 us (50%)
  Pallas kernels  45.5 us (19%)
  local copies, waits for them, and re-layouts  28.9 us (12%)
  other arithmetic  21.1 us (9%)
  starting transfers between devices  20.5 us (9%)
    all_to_all x1, waiting for transfers between devices, shards(): lax.all_to_all(store[head][chosen], 'stretch', split_axis=0, concat_axis=...  80.4 us
    pallas_call x2, Pallas kernels, flash(): pl.pallas_call(kernel, grid=(rows, kv_heads, per), in_specs=in_specs, out...  33.7 us
    all_to_all x1, waiting for transfers between devices, shards(): lax.all_to_all(send_vals, 'stretch', split_axis=0, concat_axis=0, tiled=T...  20.3 us
    all_to_all x1, waiting for transfers between devices, shards(): lax.all_to_all(store[head][chosen][..., :head_dim], 'stretch', split_axis...  13.3 us
    pallas_call x1, Pallas kernels, weigh(): pl.pallas_call(weigh_kernel, grid=(rows, per), in_specs=[pl.BlockSpec((No...  11.8 us
    unnamed x3, other arithmetic  8.78 us
    gather x2, local copies, waits for them, and re-layouts, shards(): got = got.reshape(flat, span, 2 * head_dim)[index]  7.45 us
    all_to_all x1, starting transfers between devices, shards(): lax.all_to_all(requests, 'stretch', split_axis=0, concat_axis=0, tiled=True)  7.28 us
  transfers between devices with their start and end apart: 4, of which 4 were waited for; matrix products, arithmetic and copies ran while one was open for 18% of the time, Pallas kernels for 14%

profile of v15, /device:TPU:0, one launch (start us, length us, event | category | flops | bytes accessed | tf_op | source)
XLA Modules:
  0.0 235.4 jit_solution(7404018451315086215)
XLA Ops:
  0.0 0.8 fusion.44
  1.4 0.1 convert_reduce_fusion
  1.5 0.1 select_reduce_fusion
  1.6 0.1 sub.29
  1.7 0.7 multiply_convert_fusion.1
  2.4 0.1 copy.41
  2.5 0.1 reshape.830
  2.6 0.1 pad.17.clone
  2.7 0.6 pad_add_fusion
  3.3 7.3 %all-to-all-start = ((s32[8,1,72]{2,1,0:T(1,128)}), s32[8,1,72]{2,1,0:T(1,128)S(1)}, u32[]{:S(2)}, u32[]{:S(2)}) async-start(s32[8,1,72]{2,1,0:T(1,128)} %pad_add_fusion), calls=%async_computation | async-start | bytes 8192 | tf_op jit(solution)/shard_map/all_to_all | solution.py:82
  10.6 1.3 fusion.52
  11.9 0.3 fusion.51
  12.2 0.3 pad_maximum_fusion.2
  12.4 4.5 %all-to-all-done = s32[8,1,72]{2,1,0:T(1,128)S(1)} async-done(((s32[8,1,72]{2,1,0:T(1,128)}), s32[8,1,72]{2,1,0:T(1,128)S(1)}, u32[]{:S(2)}, u32[]{:S(2)}) %all-to-all-start) | async-done | bytes 2336 | tf_op jit(solution)/shard_map/all_to_all | solution.py:82
  17.0 0.1 reshape.759
  17.1 2.8 %gather_fusion.1 = bf16[64,128,256]{2,1,0:T(8,128)(2,1)} fusion(bf16[16,128,256]{2,1,0:T(8,128)(2,1)S(1)} %get-tuple-element.61, s32[1024]{0:T(1024)S(1)} %pad_clamp_fusion.2), kind=kCustom, calls=%fused_computation.1 | custom fusion | bytes 8388864 | tf_op jit(solution)/shard_map/gather | solution.py:138
  19.9 4.7 %all-to-all-start.2 = ((bf16[8,1,8,128,256]{4,3,2,1,0:T(8,128)(2,1)}), bf16[8,1,8,128,256]{4,3,2,1,0:T(8,128)(2,1)}, u32[]{:S(2)}, u32[]{:S(2)}) async-start(bf16[8,1,8,128,256]{4,3,2,1,0:T(8,128)(2,1)} %bitcast.78), calls=%async_computation.2 | async-start | bytes 8388608 | tf_op jit(solution)/shard_map/all_to_all | solution.py:138
  24.6 0.2 convert_bitcast_fusion
  24.8 0.4 copy.59
  25.3 0.5 multiply_cosine_fusion.1
  25.8 0.6 multiply_subtract_fusion
  26.4 0.6 fusion
  27.1 0.5 convert_element_type.197
  27.6 0.4 copy-done.2
  28.0 0.1 copy.54
  28.1 0.1 copy.53
  28.3 0.3 fusion.35
  28.6 2.8 %gather_fusion = bf16[64,128,256]{2,1,0:T(8,128)(2,1)} fusion(bf16[16,128,256]{2,1,0:T(8,128)(2,1)S(1)} %get-tuple-element.60, s32[1024]{0:T(1024)S(1)} %pad_clamp_fusion.2), kind=kCustom, calls=%fused_computation | custom fusion | bytes 8388864 | tf_op jit(solution)/shard_map/gather | solution.py:131
  31.4 4.8 %fusion.49 = (bf16[8,1,8,128,128]{4,3,2,1,0:T(8,128)(2,1)}, bf16[8,1,8,128,128]{4,3,2,1,0:T(8,128)(2,1)}) fusion(bf16[8,1,8,128,256]{4,3,2,1,0:T(8,128)(2,1)} %bitcast.79), kind=kLoop, calls=%fused_computation.110 | loop fusion | bytes 8388608 | tf_op jit(solution)/shard_map/slice | solution.py:126
  36.2 80.4 %all-to-all-done.2 = bf16[8,1,8,128,256]{4,3,2,1,0:T(8,128)(2,1)} async-done(((bf16[8,1,8,128,256]{4,3,2,1,0:T(8,128)(2,1)}), bf16[8,1,8,128,256]{4,3,2,1,0:T(8,128)(2,1)}, u32[]{:S(2)}, u32[]{:S(2)}) %all-to-all-start.2) | async-done | bytes 4194336 | tf_op jit(solution)/shard_map/all_to_all | solution.py:138
  116.6 4.7 %all-to-all-start.1 = ((bf16[8,1,8,128,128]{4,3,2,1,0:T(8,128)(2,1)}), bf16[8,1,8,128,128]{4,3,2,1,0:T(8,128)(2,1)}, u32[]{:S(2)}, u32[]{:S(2)}) async-start(bf16[8,1,8,128,128]{4,3,2,1,0:T(8,128)(2,1)} %get-tuple-element.23), calls=%async_computation.1 | async-start | bytes 4194304 | tf_op jit(solution)/shard_map/all_to_all | solution.py:125
  121.3 0.1 add_convert_fusion
  121.4 1.1 fusion.50
  122.5 0.6 compare_select_fusion.refs_0_
  123.1 0.1 fusion.42
  123.2 0.2 mul.362
  123.4 0.6 gather_fusion.3
  124.0 0.1 copy.44
  124.1 4.2 %gather_fusion.2 = bf16[32,128,256]{2,1,0:T(8,128)(2,1)} fusion(bf16[64,128,256]{2,1,0:T(8,128)(2,1)} %bitcast.9, s32[1024]{0:T(1024)S(1)} %pad_clamp_fusion.1), kind=kCustom, calls=%fused_computation.2 | custom fusion | bytes 4194432 | tf_op jit(solution)/shard_map/gather | solution.py:142
  128.3 3.2 %copy.43 = bf16[32,128,256]{1,2,0:T(8,128)(2,1)S(1)} copy(bf16[32,128,256]{2,1,0:T(8,128)(2,1)} %gather_fusion.2) | data formatting | bytes 4194304 | tf_op jit(solution)/shard_map/gather | solution.py:142
  131.6 0.4 multiply_convert_fusion
  132.0 4.3 %fusion.21 = (bf16[1,32,8,8,128]{4,3,2,1,0:T(8,128)(2,1)S(1)}, bf16[1,32,8,8,128]{4,3,2,1,0:T(8,128)(2,1)S(1)}) fusion(f32[1,32,128,128]{2,3,1,0:T(8,128)S(1)} %get-tuple-element.32, f32[64]{0:T(128)S(1)} %negate_power_fusion, f32[32,128]{1,0:T(8,128)S(1)} %add_convert_fusion), kind=kLoop, calls=%fused_computation.47 | loop fusion | flops 2359296 | bytes 3162368
  136.3 0.1 copy.66
  136.4 0.1 copy.67
  136.5 0.7 copy.48
  137.1 1.1 pad_maximum_fusion.refs_3_
  138.2 1.1 maximum_bitcast_fusion.refs_2_
  139.3 16.4 %shard_map.91.into_ref = bf16[1,256,2048]{2,1,0:T(8,128)(2,1)} custom-call(f32[1,1,4096]{2,1,0:T(1,128)} %compare_select_fusion.refs_0_, bf16[1,256,1024]{2,1,0:T(8,128)(2,1)} %get-tuple-element.34.refs_1_, bf16[1,128,4352]{2,1,0:T(8,128)(2,1)} %maximum_bitcast_fusion.refs_2_, bf16[1,4352,128]{2,1,0:T(8,128)(2,1)} %pad_maximum_fusion.refs_3_), custom_call_target="tpu_custom_call" | custom-call | flops 6845104128 | bytes 3276800 | tf_op jit(solution)/shard_map/pallas_call | solution.py:334
  155.7 13.3 %all-to-all-done.1 = bf16[8,1,8,128,128]{4,3,2,1,0:T(8,128)(2,1)} async-done(((bf16[8,1,8,128,128]{4,3,2,1,0:T(8,128)(2,1)}), bf16[8,1,8,128,128]{4,3,2,1,0:T(8,128)(2,1)}, u32[]{:S(2)}, u32[]{:S(2)}) %all-to-all-start.1) | async-done | bytes 2097184 | tf_op jit(solution)/shard_map/all_to_all | solution.py:125
  169.0 3.8 %all-to-all-start.3 = ((bf16[8,1,8,128,128]{4,3,2,1,0:T(8,128)(2,1)}), bf16[8,1,8,128,128]{4,3,2,1,0:T(8,128)(2,1)S(1)}, u32[]{:S(2)}, u32[]{:S(2)}) async-start(bf16[8,1,8,128,128]{4,3,2,1,0:T(8,128)(2,1)} %get-tuple-element.15), calls=%async_computation.3 | async-start | bytes 4194304 | tf_op jit(solution)/shard_map/all_to_all | solution.py:135
  172.8 0.1 broadcast_bitcast_fusion
  172.9 2.3 gather_fusion.4
  175.2 1.3 copy.49
  176.6 1.4 convert_multiply_fusion.1
  178.0 4.3 %fusion.19 = (bf16[1,32,8,8,128]{4,3,2,1,0:T(8,128)(2,1)S(1)}, bf16[1,32,8,8,128]{4,3,2,1,0:T(8,128)(2,1)S(1)}) fusion(f32[1,32,128,128]{2,3,1,0:T(8,128)S(1)} %convert_multiply_fusion.1, f32[64]{0:T(128)S(1)} %negate_power_fusion, f32[32,128]{1,0:T(8,128)S(1)} %add_convert_fusion), kind=kLoop, calls=%fused_computation.45 | loop fusion | flops 2359296 | bytes 3162368
  182.3 0.1 copy.64
  182.4 0.1 copy.65
  182.5 1.1 maximum_bitcast_fusion.1.refs_2_
  183.5 17.2 %shard_map.92 = (bf16[1,8,256,4352]{3,2,1,0:T(8,128)(2,1)}, f32[1,256,1024]{2,1,0:T(8,128)}) custom-call(f32[1,1,4096]{2,1,0:T(1,128)} %compare_select_fusion.refs_0_, bf16[1,256,1024]{2,1,0:T(8,128)(2,1)} %get-tuple-element.33.refs_1_, bf16[1,128,4352]{2,1,0:T(8,128)(2,1)} %maximum_bitcast_fusion.1.refs_2_), custom_call_target="tpu_custom_call" | custom-call | flops 4563402752 | bytes 3276800 | tf_op jit(solution)/shard_map/pallas_call | solution.py:334
  200.8 20.3 %all-to-all-done.3 = bf16[8,1,8,128,128]{4,3,2,1,0:T(8,128)(2,1)S(1)} async-done(((bf16[8,1,8,128,128]{4,3,2,1,0:T(8,128)(2,1)}), bf16[8,1,8,128,128]{4,3,2,1,0:T(8,128)(2,1)S(1)}, u32[]{:S(2)}, u32[]{:S(2)}) %all-to-all-start.3) | async-done | bytes 2097184 | tf_op jit(solution)/shard_map/all_to_all | solution.py:135
  221.1 0.7 gather_fusion.5
  221.8 0.7 fusion.1
  222.5 1.1 pad_maximum_fusion.1.v_ref
  223.6 11.8 %shard_map.93 = bf16[1,256,2048]{2,1,0:T(8,128)(2,1)} custom-call(bf16[1,8,256,4352]{3,2,1,0:T(8,128)(2,1)} %get-tuple-element.19.p_ref, bf16[1,4352,128]{2,1,0:T(8,128)(2,1)} %pad_maximum_fusion.1.v_ref, f32[1,256,1024]{2,1,0:T(8,128)} %get-tuple-element.21.t_ref, bf16[1,256,2048]{2,1,0:T(8,128)(2,1)} %shard_map.91.into_ref), custom_call_target="tpu_custom_call", output_to_operand_aliasing={{}: (3, {})} | custom-call | tf_op jit(solution)/shard_map/pallas_call | solution.py:265
  (23 shorter events, 0.1 us)
Async XLA Ops:
  0.0 11.9 %copy-start.1 = (bf16[16,128,256]{2,1,0:T(8,128)(2,1)S(1)}, bf16[16,128,256]{2,1,0:T(8,128)(2,1)}, u32[]{:S(2)}) copy-start(bf16[16,128,256]{2,1,0:T(8,128)(2,1)} %param.12) | copy-start | bytes 3145732
  3.3 13.7 %all-to-all-start = ((s32[8,1,72]{2,1,0:T(1,128)}), s32[8,1,72]{2,1,0:T(1,128)S(1)}, u32[]{:S(2)}, u32[]{:S(2)}) async-start(s32[8,1,72]{2,1,0:T(1,128)} %pad_add_fusion), calls=%async_computation | async-start | bytes 8192 | tf_op jit(solution)/shard_map/all_to_all | solution.py:82
  19.9 4.7 %copy-start = (bf16[1,256,2048]{2,1,0:T(8,128)(2,1)S(1)}, bf16[1,256,2048]{2,1,0:T(8,128)(2,1)}, u32[]{:S(2)}) copy-start(bf16[1,256,2048]{2,1,0:T(8,128)(2,1)} %param.9) | copy-start | bytes 3145732
  19.9 96.7 %all-to-all-start.2 = ((bf16[8,1,8,128,256]{4,3,2,1,0:T(8,128)(2,1)}), bf16[8,1,8,128,256]{4,3,2,1,0:T(8,128)(2,1)}, u32[]{:S(2)}, u32[]{:S(2)}) async-start(bf16[8,1,8,128,256]{4,3,2,1,0:T(8,128)(2,1)} %bitcast.78), calls=%async_computation.2 | async-start | bytes 8388608 | tf_op jit(solution)/shard_map/all_to_all | solution.py:138
  27.0 0.9 copy-start.2
  27.0 1.2 copy-start.3
  116.6 4.7 %copy-start.4 = (s32[1,32]{1,0:T(1,128)S(1)}, s32[1,32]{1,0:T(1,128)}, u32[]{:S(2)}) copy-start(s32[1,32]{1,0:T(1,128)} %param.17) | copy-start | bytes 388
  116.6 52.4 %all-to-all-start.1 = ((bf16[8,1,8,128,128]{4,3,2,1,0:T(8,128)(2,1)}), bf16[8,1,8,128,128]{4,3,2,1,0:T(8,128)(2,1)}, u32[]{:S(2)}, u32[]{:S(2)}) async-start(bf16[8,1,8,128,128]{4,3,2,1,0:T(8,128)(2,1)} %get-tuple-element.23), calls=%async_computation.1 | async-start | bytes 4194304 | tf_op jit(solution)/shard_map/all_to_all | solution.py:125
  169.0 52.1 %all-to-all-start.3 = ((bf16[8,1,8,128,128]{4,3,2,1,0:T(8,128)(2,1)}), bf16[8,1,8,128,128]{4,3,2,1,0:T(8,128)(2,1)S(1)}, u32[]{:S(2)}, u32[]{:S(2)}) async-start(bf16[8,1,8,128,128]{4,3,2,1,0:T(8,128)(2,1)} %get-tuple-element.15), calls=%async_computation.3 | async-start | bytes 4194304 | tf_op jit(solution)/shard_map/all_to_all | solution.py:135

commit v16 on v15

--- a/solution.py
+++ b/solution.py
@@ -259,7 +259,7 @@
 def weigh(probs, values_all, total, into, offset):
     rows, q_heads, tokens, length = probs.shape
     head_dim = values_all.shape[2]
-    heads = 1
+    heads = 2
     per = q_heads // heads
     block = offset // heads
     return pl.pallas_call(

time: 236 us -> 234 us (level)
  no operation moved by 1% of the time
where the time goes in v16:
time: 234 us
  waiting for transfers between devices  118 us (50%)
  Pallas kernels  43.6 us (19%)
  local copies, waits for them, and re-layouts  28.9 us (12%)
  other arithmetic  21.1 us (9%)
  starting transfers between devices  20.5 us (9%)
    all_to_all x1, waiting for transfers between devices, shards(): lax.all_to_all(store[head][chosen], 'stretch', split_axis=0, concat_axis=...  80.4 us
    pallas_call x2, Pallas kernels, flash(): pl.pallas_call(kernel, grid=(rows, kv_heads, per), in_specs=in_specs, out...  33.7 us
    all_to_all x1, waiting for transfers between devices, shards(): lax.all_to_all(send_vals, 'stretch', split_axis=0, concat_axis=0, tiled=T...  20.3 us
    all_to_all x1, waiting for transfers between devices, shards(): lax.all_to_all(store[head][chosen][..., :head_dim], 'stretch', split_axis...  13.3 us
    pallas_call x1, Pallas kernels, weigh(): pl.pallas_call(weigh_kernel, grid=(rows, per), in_specs=[pl.BlockSpec((No...  9.93 us
    unnamed x3, other arithmetic  8.78 us
    gather x2, local copies, waits for them, and re-layouts, shards(): got = got.reshape(flat, span, 2 * head_dim)[index]  7.45 us
    all_to_all x1, starting transfers between devices, shards(): lax.all_to_all(requests, 'stretch', split_axis=0, concat_axis=0, tiled=True)  7.28 us
  transfers between devices with their start and end apart: 4, of which 4 were waited for; matrix products, arithmetic and copies ran while one was open for 18% of the time, Pallas kernels for 14%

profile of v16, /device:TPU:0, one launch (start us, length us, event | category | flops | bytes accessed | tf_op | source)
XLA Modules:
  0.0 233.5 jit_solution(4252742727610638471)
XLA Ops:
  0.0 0.8 fusion.44
  1.4 0.1 convert_reduce_fusion
  1.5 0.1 select_reduce_fusion
  1.6 0.1 sub.29
  1.7 0.7 multiply_convert_fusion.1
  2.4 0.1 copy.41
  2.5 0.1 reshape.830
  2.6 0.1 pad.17.clone
  2.7 0.6 pad_add_fusion
  3.3 7.3 %all-to-all-start = ((s32[8,1,72]{2,1,0:T(1,128)}), s32[8,1,72]{2,1,0:T(1,128)S(1)}, u32[]{:S(2)}, u32[]{:S(2)}) async-start(s32[8,1,72]{2,1,0:T(1,128)} %pad_add_fusion), calls=%async_computation | async-start | bytes 8192 | tf_op jit(solution)/shard_map/all_to_all | solution.py:82
  10.6 1.3 fusion.52
  11.9 0.3 fusion.51
  12.2 0.3 pad_maximum_fusion.2
  12.4 4.5 %all-to-all-done = s32[8,1,72]{2,1,0:T(1,128)S(1)} async-done(((s32[8,1,72]{2,1,0:T(1,128)}), s32[8,1,72]{2,1,0:T(1,128)S(1)}, u32[]{:S(2)}, u32[]{:S(2)}) %all-to-all-start) | async-done | bytes 2336 | tf_op jit(solution)/shard_map/all_to_all | solution.py:82
  17.0 0.1 reshape.759
  17.1 2.8 %gather_fusion.1 = bf16[64,128,256]{2,1,0:T(8,128)(2,1)} fusion(bf16[16,128,256]{2,1,0:T(8,128)(2,1)S(1)} %get-tuple-element.61, s32[1024]{0:T(1024)S(1)} %pad_clamp_fusion.2), kind=kCustom, calls=%fused_computation.1 | custom fusion | bytes 8388864 | tf_op jit(solution)/shard_map/gather | solution.py:138
  19.9 4.7 %all-to-all-start.2 = ((bf16[8,1,8,128,256]{4,3,2,1,0:T(8,128)(2,1)}), bf16[8,1,8,128,256]{4,3,2,1,0:T(8,128)(2,1)}, u32[]{:S(2)}, u32[]{:S(2)}) async-start(bf16[8,1,8,128,256]{4,3,2,1,0:T(8,128)(2,1)} %bitcast.78), calls=%async_computation.2 | async-start | bytes 8388608 | tf_op jit(solution)/shard_map/all_to_all | solution.py:138
  24.6 0.2 convert_bitcast_fusion
  24.8 0.4 copy.59
  25.3 0.5 multiply_cosine_fusion.1
  25.8 0.6 multiply_subtract_fusion
  26.4 0.6 fusion
  27.1 0.5 convert_element_type.197
  27.6 0.4 copy-done.2
  28.0 0.1 copy.54
  28.1 0.1 copy.53
  28.3 0.3 fusion.35
  28.6 2.8 %gather_fusion = bf16[64,128,256]{2,1,0:T(8,128)(2,1)} fusion(bf16[16,128,256]{2,1,0:T(8,128)(2,1)S(1)} %get-tuple-element.60, s32[1024]{0:T(1024)S(1)} %pad_clamp_fusion.2), kind=kCustom, calls=%fused_computation | custom fusion | bytes 8388864 | tf_op jit(solution)/shard_map/gather | solution.py:131
  31.4 4.8 %fusion.49 = (bf16[8,1,8,128,128]{4,3,2,1,0:T(8,128)(2,1)}, bf16[8,1,8,128,128]{4,3,2,1,0:T(8,128)(2,1)}) fusion(bf16[8,1,8,128,256]{4,3,2,1,0:T(8,128)(2,1)} %bitcast.79), kind=kLoop, calls=%fused_computation.110 | loop fusion | bytes 8388608 | tf_op jit(solution)/shard_map/slice | solution.py:126
  36.2 80.4 %all-to-all-done.2 = bf16[8,1,8,128,256]{4,3,2,1,0:T(8,128)(2,1)} async-done(((bf16[8,1,8,128,256]{4,3,2,1,0:T(8,128)(2,1)}), bf16[8,1,8,128,256]{4,3,2,1,0:T(8,128)(2,1)}, u32[]{:S(2)}, u32[]{:S(2)}) %all-to-all-start.2) | async-done | bytes 4194336 | tf_op jit(solution)/shard_map/all_to_all | solution.py:138
  116.6 4.7 %all-to-all-start.1 = ((bf16[8,1,8,128,128]{4,3,2,1,0:T(8,128)(2,1)}), bf16[8,1,8,128,128]{4,3,2,1,0:T(8,128)(2,1)}, u32[]{:S(2)}, u32[]{:S(2)}) async-start(bf16[8,1,8,128,128]{4,3,2,1,0:T(8,128)(2,1)} %get-tuple-element.23), calls=%async_computation.1 | async-start | bytes 4194304 | tf_op jit(solution)/shard_map/all_to_all | solution.py:125
  121.3 0.1 add_convert_fusion
  121.4 1.1 fusion.50
  122.5 0.6 compare_select_fusion.refs_0_
  123.1 0.1 fusion.42
  123.2 0.2 mul.362
  123.4 0.6 gather_fusion.3
  124.0 0.1 copy.44
  124.1 4.2 %gather_fusion.2 = bf16[32,128,256]{2,1,0:T(8,128)(2,1)} fusion(bf16[64,128,256]{2,1,0:T(8,128)(2,1)} %bitcast.9, s32[1024]{0:T(1024)S(1)} %pad_clamp_fusion.1), kind=kCustom, calls=%fused_computation.2 | custom fusion | bytes 4194432 | tf_op jit(solution)/shard_map/gather | solution.py:142
  128.3 3.2 %copy.43 = bf16[32,128,256]{1,2,0:T(8,128)(2,1)S(1)} copy(bf16[32,128,256]{2,1,0:T(8,128)(2,1)} %gather_fusion.2) | data formatting | bytes 4194304 | tf_op jit(solution)/shard_map/gather | solution.py:142
  131.6 0.4 multiply_convert_fusion
  132.0 4.3 %fusion.21 = (bf16[1,32,8,8,128]{4,3,2,1,0:T(8,128)(2,1)S(1)}, bf16[1,32,8,8,128]{4,3,2,1,0:T(8,128)(2,1)S(1)}) fusion(f32[1,32,128,128]{2,3,1,0:T(8,128)S(1)} %get-tuple-element.32, f32[64]{0:T(128)S(1)} %negate_power_fusion, f32[32,128]{1,0:T(8,128)S(1)} %add_convert_fusion), kind=kLoop, calls=%fused_computation.47 | loop fusion | flops 2359296 | bytes 3162368
  136.3 0.1 copy.66
  136.4 0.1 copy.67
  136.5 0.7 copy.48
  137.1 1.1 pad_maximum_fusion.refs_3_
  138.2 1.1 maximum_bitcast_fusion.refs_2_
  139.3 16.4 %shard_map.91.into_ref = bf16[1,256,2048]{2,1,0:T(8,128)(2,1)} custom-call(f32[1,1,4096]{2,1,0:T(1,128)} %compare_select_fusion.refs_0_, bf16[1,256,1024]{2,1,0:T(8,128)(2,1)} %get-tuple-element.34.refs_1_, bf16[1,128,4352]{2,1,0:T(8,128)(2,1)} %maximum_bitcast_fusion.refs_2_, bf16[1,4352,128]{2,1,0:T(8,128)(2,1)} %pad_maximum_fusion.refs_3_), custom_call_target="tpu_custom_call" | custom-call | flops 6845104128 | bytes 3276800 | tf_op jit(solution)/shard_map/pallas_call | solution.py:334
  155.7 13.3 %all-to-all-done.1 = bf16[8,1,8,128,128]{4,3,2,1,0:T(8,128)(2,1)} async-done(((bf16[8,1,8,128,128]{4,3,2,1,0:T(8,128)(2,1)}), bf16[8,1,8,128,128]{4,3,2,1,0:T(8,128)(2,1)}, u32[]{:S(2)}, u32[]{:S(2)}) %all-to-all-start.1) | async-done | bytes 2097184 | tf_op jit(solution)/shard_map/all_to_all | solution.py:125
  169.0 3.8 %all-to-all-start.3 = ((bf16[8,1,8,128,128]{4,3,2,1,0:T(8,128)(2,1)}), bf16[8,1,8,128,128]{4,3,2,1,0:T(8,128)(2,1)S(1)}, u32[]{:S(2)}, u32[]{:S(2)}) async-start(bf16[8,1,8,128,128]{4,3,2,1,0:T(8,128)(2,1)} %get-tuple-element.15), calls=%async_computation.3 | async-start | bytes 4194304 | tf_op jit(solution)/shard_map/all_to_all | solution.py:135
  172.8 0.1 broadcast_bitcast_fusion
  172.9 2.3 %gather_fusion.4 = bf16[32,128,128]{2,1,0:T(8,128)(2,1)S(1)} fusion(bf16[64,128,128]{2,1,0:T(8,128)(2,1)} %bitcast.19, s32[1024]{0:T(1024)S(1)} %pad_clamp_fusion.1), kind=kCustom, calls=%fused_computation.4 | custom fusion | bytes 2097280 | tf_op jit(solution)/shard_map/gather | solution.py:136
  175.2 1.3 copy.49
  176.6 1.4 convert_multiply_fusion.1
  178.0 4.3 %fusion.19 = (bf16[1,32,8,8,128]{4,3,2,1,0:T(8,128)(2,1)S(1)}, bf16[1,32,8,8,128]{4,3,2,1,0:T(8,128)(2,1)S(1)}) fusion(f32[1,32,128,128]{2,3,1,0:T(8,128)S(1)} %convert_multiply_fusion.1, f32[64]{0:T(128)S(1)} %negate_power_fusion, f32[32,128]{1,0:T(8,128)S(1)} %add_convert_fusion), kind=kLoop, calls=%fused_computation.45 | loop fusion | flops 2359296 | bytes 3162368
  182.3 0.1 copy.64
  182.4 0.1 copy.65
  182.5 1.1 maximum_bitcast_fusion.1.refs_2_
  183.5 17.2 %shard_map.92 = (bf16[1,8,256,4352]{3,2,1,0:T(8,128)(2,1)}, f32[1,256,1024]{2,1,0:T(8,128)}) custom-call(f32[1,1,4096]{2,1,0:T(1,128)} %compare_select_fusion.refs_0_, bf16[1,256,1024]{2,1,0:T(8,128)(2,1)} %get-tuple-element.33.refs_1_, bf16[1,128,4352]{2,1,0:T(8,128)(2,1)} %maximum_bitcast_fusion.1.refs_2_), custom_call_target="tpu_custom_call" | custom-call | flops 4563402752 | bytes 3276800 | tf_op jit(solution)/shard_map/pallas_call | solution.py:334
  200.8 20.3 %all-to-all-done.3 = bf16[8,1,8,128,128]{4,3,2,1,0:T(8,128)(2,1)S(1)} async-done(((bf16[8,1,8,128,128]{4,3,2,1,0:T(8,128)(2,1)}), bf16[8,1,8,128,128]{4,3,2,1,0:T(8,128)(2,1)S(1)}, u32[]{:S(2)}, u32[]{:S(2)}) %all-to-all-start.3) | async-done | bytes 2097184 | tf_op jit(solution)/shard_map/all_to_all | solution.py:135
  221.1 0.7 gather_fusion.5
  221.8 0.7 fusion.1
  222.5 1.1 pad_maximum_fusion.1.v_ref
  223.6 9.9 %shard_map.93 = bf16[1,256,2048]{2,1,0:T(8,128)(2,1)} custom-call(bf16[1,8,256,4352]{3,2,1,0:T(8,128)(2,1)} %get-tuple-element.19.p_ref, bf16[1,4352,128]{2,1,0:T(8,128)(2,1)} %pad_maximum_fusion.1.v_ref, f32[1,256,1024]{2,1,0:T(8,128)} %get-tuple-element.21.t_ref, bf16[1,256,2048]{2,1,0:T(8,128)(2,1)} %shard_map.91.into_ref), custom_call_target="tpu_custom_call", output_to_operand_aliasing={{}: (3, {})} | custom-call | tf_op jit(solution)/shard_map/pallas_call | solution.py:265
  (23 shorter events, 0.1 us)
Async XLA Ops:
  0.0 11.9 %copy-start.1 = (bf16[16,128,256]{2,1,0:T(8,128)(2,1)S(1)}, bf16[16,128,256]{2,1,0:T(8,128)(2,1)}, u32[]{:S(2)}) copy-start(bf16[16,128,256]{2,1,0:T(8,128)(2,1)} %param.12) | copy-start | bytes 3145732
  3.3 13.7 %all-to-all-start = ((s32[8,1,72]{2,1,0:T(1,128)}), s32[8,1,72]{2,1,0:T(1,128)S(1)}, u32[]{:S(2)}, u32[]{:S(2)}) async-start(s32[8,1,72]{2,1,0:T(1,128)} %pad_add_fusion), calls=%async_computation | async-start | bytes 8192 | tf_op jit(solution)/shard_map/all_to_all | solution.py:82
  19.9 4.7 %copy-start = (bf16[1,256,2048]{2,1,0:T(8,128)(2,1)S(1)}, bf16[1,256,2048]{2,1,0:T(8,128)(2,1)}, u32[]{:S(2)}) copy-start(bf16[1,256,2048]{2,1,0:T(8,128)(2,1)} %param.9) | copy-start | bytes 3145732
  19.9 96.7 %all-to-all-start.2 = ((bf16[8,1,8,128,256]{4,3,2,1,0:T(8,128)(2,1)}), bf16[8,1,8,128,256]{4,3,2,1,0:T(8,128)(2,1)}, u32[]{:S(2)}, u32[]{:S(2)}) async-start(bf16[8,1,8,128,256]{4,3,2,1,0:T(8,128)(2,1)} %bitcast.78), calls=%async_computation.2 | async-start | bytes 8388608 | tf_op jit(solution)/shard_map/all_to_all | solution.py:138
  27.0 0.9 copy-start.2
  27.0 1.2 copy-start.3
  116.6 4.7 %copy-start.4 = (s32[1,32]{1,0:T(1,128)S(1)}, s32[1,32]{1,0:T(1,128)}, u32[]{:S(2)}) copy-start(s32[1,32]{1,0:T(1,128)} %param.17) | copy-start | bytes 388
  116.6 52.4 %all-to-all-start.1 = ((bf16[8,1,8,128,128]{4,3,2,1,0:T(8,128)(2,1)}), bf16[8,1,8,128,128]{4,3,2,1,0:T(8,128)(2,1)}, u32[]{:S(2)}, u32[]{:S(2)}) async-start(bf16[8,1,8,128,128]{4,3,2,1,0:T(8,128)(2,1)} %get-tuple-element.23), calls=%async_computation.1 | async-start | bytes 4194304 | tf_op jit(solution)/shard_map/all_to_all | solution.py:125
  169.0 52.1 %all-to-all-start.3 = ((bf16[8,1,8,128,128]{4,3,2,1,0:T(8,128)(2,1)}), bf16[8,1,8,128,128]{4,3,2,1,0:T(8,128)(2,1)S(1)}, u32[]{:S(2)}, u32[]{:S(2)}) async-start(bf16[8,1,8,128,128]{4,3,2,1,0:T(8,128)(2,1)} %get-tuple-element.15), calls=%async_computation.3 | async-start | bytes 4194304 | tf_op jit(solution)/shard_map/all_to_all | solution.py:135

commit v17 on v14

--- a/solution.py
+++ b/solution.py
@@ -157,12 +157,15 @@
             raw_v = got[..., head_dim:]
         vals = raw_v.astype(jnp.float32) * slot_scale[:, :, 1, head][:, :, None, None]
         vals = vals.astype(jnp.bfloat16)
+        if last and results:
+            results.append(weigh(
+                probs, vals.reshape(rows, cache_length, head_dim), fresh_values[..., cols],
+                total, results[-1], head * request_group,
+            ))
+            continue
         values_all = jnp.concatenate(
             [vals.reshape(rows, cache_length, head_dim), fresh_values[..., cols]], axis=1
         )
-        if last and results:
-            results.append(weigh(probs, values_all, total, results[-1], head * request_group))
-            continue
         results.append(
             flash(
                 query_head, keys_t, values_all, counts * span, request_group,
@@ -246,19 +249,24 @@
         o_ref[:, head * lanes:(head + 1) * lanes] = (acc / total).astype(o_ref.dtype)
 
 
-def weigh_kernel(p_ref, v_ref, t_ref, into_ref, o_ref):
+def weigh_kernel(p_ref, v_ref, f_ref, t_ref, into_ref, o_ref):
     lanes = 128
+    cache_length = v_ref.shape[0]
     for head in range(p_ref.shape[0]):
         acc = lax.dot_general(
-            p_ref[head], v_ref[...], (((1,), (0,)), ((), ())), preferred_element_type=jnp.float32
+            p_ref[head, :, :cache_length], v_ref[...], (((1,), (0,)), ((), ())),
+            preferred_element_type=jnp.float32,
+        ) + lax.dot_general(
+            p_ref[head, :, cache_length:], f_ref[...], (((1,), (0,)), ((), ())),
+            preferred_element_type=jnp.float32,
         )
         cols = slice(head * lanes, (head + 1) * lanes)
         o_ref[:, cols] = (acc / t_ref[:, cols]).astype(o_ref.dtype)
 
 
-def weigh(probs, values_all, total, into, offset):
+def weigh(probs, cached_values, new_values, total, into, offset):
     rows, q_heads, tokens, length = probs.shape
-    head_dim = values_all.shape[2]
+    cache_length, head_dim = cached_values.shape[1:]
     heads = HEADS
     per = q_heads // heads
     block = offset // heads
@@ -267,14 +275,15 @@
         grid=(rows, per),
         in_specs=[
             pl.BlockSpec((None, heads, tokens, length), lambda r, g: (r, g, 0, 0)),
-            pl.BlockSpec((None, length, head_dim), lambda r, g: (r, 0, 0)),
+            pl.BlockSpec((None, cache_length, head_dim), lambda r, g: (r, 0, 0)),
+            pl.BlockSpec((None, tokens, head_dim), lambda r, g: (r, 0, 0)),
             pl.BlockSpec((None, tokens, head_dim * heads), lambda r, g: (r, 0, g)),
             pl.BlockSpec(memory_space=pl.ANY),
         ],
         out_specs=pl.BlockSpec((None, tokens, head_dim * heads), lambda r, g: (r, 0, block + g)),
         out_shape=jax.ShapeDtypeStruct(into.shape, jnp.bfloat16),
-        input_output_aliases={3: 0},
-    )(probs, values_all, total, into)
+        input_output_aliases={4: 0},
+    )(probs, cached_values, new_values, total, into)
 
 
 CHUNK = 512

time: 234 us -> 234 us (level)
  no operation moved by 1% of the time
where the time goes in v17:
time: 234 us; the launch traced here: 233 us
  waiting for transfers between devices  118 us (50%)
  Pallas kernels  43.4 us (19%)
  local copies, waits for them, and re-layouts  29.5 us (13%)
  other arithmetic  20.8 us (9%)
  starting transfers between devices  20.5 us (9%)
    all_to_all x1, waiting for transfers between devices, shards(): lax.all_to_all(store[head][chosen], 'stretch', split_axis=0, concat_axis=...  79.8 us
    pallas_call x2, Pallas kernels, flash(): pl.pallas_call(kernel, grid=(rows, kv_heads, per), in_specs=in_specs, out...  33.7 us
    all_to_all x1, waiting for transfers between devices, shards(): lax.all_to_all(send_vals, 'stretch', split_axis=0, concat_axis=0, tiled=T...  20.3 us
    all_to_all x1, waiting for transfers between devices, shards(): lax.all_to_all(store[head][chosen][..., :head_dim], 'stretch', split_axis...  13.3 us
    pallas_call x1, Pallas kernels, weigh(): pl.pallas_call(weigh_kernel, grid=(rows, per), in_specs=[pl.BlockSpec((No...  9.76 us
    unnamed x3, other arithmetic  8.78 us
    gather x2, local copies, waits for them, and re-layouts, shards(): got = got.reshape(flat, span, 2 * head_dim)[index]  7.45 us
    all_to_all x1, starting transfers between devices, shards(): lax.all_to_all(requests, 'stretch', split_axis=0, concat_axis=0, tiled=True)  7.28 us
  transfers between devices with their start and end apart: 4, of which 4 were waited for; matrix products, arithmetic and copies ran while one was open for 18% of the time, Pallas kernels for 14%

profile of v17, /device:TPU:0, one launch (start us, length us, event | category | flops | bytes accessed | tf_op | source)
XLA Modules:
  0.0 233.1 jit_solution(11503811046696597745)
XLA Ops:
  0.0 0.8 fusion.44
  1.4 0.1 convert_reduce_fusion
  1.5 0.1 select_reduce_fusion
  1.6 0.1 sub.29
  1.7 0.7 multiply_convert_fusion.1
  2.4 0.1 copy.41
  2.5 0.1 reshape.830
  2.6 0.1 pad.15.clone
  2.7 0.6 pad_add_fusion
  3.3 7.3 %all-to-all-start = ((s32[8,1,72]{2,1,0:T(1,128)}), s32[8,1,72]{2,1,0:T(1,128)S(1)}, u32[]{:S(2)}, u32[]{:S(2)}) async-start(s32[8,1,72]{2,1,0:T(1,128)} %pad_add_fusion), calls=%async_computation | async-start | bytes 8192 | tf_op jit(solution)/shard_map/all_to_all | solution.py:82
  10.6 1.3 fusion.52
  11.9 0.3 fusion.51
  12.2 0.3 pad_maximum_fusion.1
  12.4 4.5 %all-to-all-done = s32[8,1,72]{2,1,0:T(1,128)S(1)} async-done(((s32[8,1,72]{2,1,0:T(1,128)}), s32[8,1,72]{2,1,0:T(1,128)S(1)}, u32[]{:S(2)}, u32[]{:S(2)}) %all-to-all-start) | async-done | bytes 2336 | tf_op jit(solution)/shard_map/all_to_all | solution.py:82
  17.0 0.1 reshape.759
  17.1 2.8 %gather_fusion.1 = bf16[64,128,256]{2,1,0:T(8,128)(2,1)} fusion(bf16[16,128,256]{2,1,0:T(8,128)(2,1)S(1)} %get-tuple-element.61, s32[1024]{0:T(1024)S(1)} %pad_clamp_fusion.2), kind=kCustom, calls=%fused_computation.1 | custom fusion | bytes 8388864 | tf_op jit(solution)/shard_map/gather | solution.py:138
  19.9 4.7 %all-to-all-start.2 = ((bf16[8,1,8,128,256]{4,3,2,1,0:T(8,128)(2,1)}), bf16[8,1,8,128,256]{4,3,2,1,0:T(8,128)(2,1)}, u32[]{:S(2)}, u32[]{:S(2)}) async-start(bf16[8,1,8,128,256]{4,3,2,1,0:T(8,128)(2,1)} %bitcast.78), calls=%async_computation.2 | async-start | bytes 8388608 | tf_op jit(solution)/shard_map/all_to_all | solution.py:138
  24.6 0.2 convert_bitcast_fusion
  24.8 0.4 copy.59
  25.3 0.5 multiply_cosine_fusion.1
  25.8 0.6 multiply_subtract_fusion
  26.4 0.6 fusion
  27.1 0.5 convert_element_type.197
  27.6 0.4 copy-done.2
  28.0 0.1 copy.54
  28.1 0.1 copy.53
  28.3 0.6 fusion.53
  28.9 0.3 fusion.35
  29.2 2.8 %gather_fusion = bf16[64,128,256]{2,1,0:T(8,128)(2,1)} fusion(bf16[16,128,256]{2,1,0:T(8,128)(2,1)S(1)} %get-tuple-element.60, s32[1024]{0:T(1024)S(1)} %pad_clamp_fusion.2), kind=kCustom, calls=%fused_computation | custom fusion | bytes 8388864 | tf_op jit(solution)/shard_map/gather | solution.py:131
  32.0 4.8 %fusion.49 = (bf16[8,1,8,128,128]{4,3,2,1,0:T(8,128)(2,1)}, bf16[8,1,8,128,128]{4,3,2,1,0:T(8,128)(2,1)}) fusion(bf16[8,1,8,128,256]{4,3,2,1,0:T(8,128)(2,1)} %bitcast.79), kind=kLoop, calls=%fused_computation.109 | loop fusion | bytes 8388608 | tf_op jit(solution)/shard_map/slice | solution.py:126
  36.8 79.8 %all-to-all-done.2 = bf16[8,1,8,128,256]{4,3,2,1,0:T(8,128)(2,1)} async-done(((bf16[8,1,8,128,256]{4,3,2,1,0:T(8,128)(2,1)}), bf16[8,1,8,128,256]{4,3,2,1,0:T(8,128)(2,1)}, u32[]{:S(2)}, u32[]{:S(2)}) %all-to-all-start.2) | async-done | bytes 4194336 | tf_op jit(solution)/shard_map/all_to_all | solution.py:138
  116.6 4.7 %all-to-all-start.1 = ((bf16[8,1,8,128,128]{4,3,2,1,0:T(8,128)(2,1)}), bf16[8,1,8,128,128]{4,3,2,1,0:T(8,128)(2,1)}, u32[]{:S(2)}, u32[]{:S(2)}) async-start(bf16[8,1,8,128,128]{4,3,2,1,0:T(8,128)(2,1)} %get-tuple-element.23), calls=%async_computation.1 | async-start | bytes 4194304 | tf_op jit(solution)/shard_map/all_to_all | solution.py:125
  121.3 0.1 add_convert_fusion
  121.4 1.1 fusion.50
  122.5 0.6 compare_select_fusion.refs_0_
  123.1 0.1 fusion.42
  123.2 0.2 mul.362
  123.4 0.6 gather_fusion.3
  124.0 0.1 copy.44
  124.1 4.2 %gather_fusion.2 = bf16[32,128,256]{2,1,0:T(8,128)(2,1)} fusion(bf16[64,128,256]{2,1,0:T(8,128)(2,1)} %bitcast.9, s32[1024]{0:T(1024)S(1)} %pad_clamp_fusion.1), kind=kCustom, calls=%fused_computation.2 | custom fusion | bytes 4194432 | tf_op jit(solution)/shard_map/gather | solution.py:142
  128.3 3.2 %copy.43 = bf16[32,128,256]{1,2,0:T(8,128)(2,1)S(1)} copy(bf16[32,128,256]{2,1,0:T(8,128)(2,1)} %gather_fusion.2) | data formatting | bytes 4194304 | tf_op jit(solution)/shard_map/gather | solution.py:142
  131.6 0.4 multiply_convert_fusion
  132.0 4.3 %fusion.21 = (bf16[1,32,8,8,128]{4,3,2,1,0:T(8,128)(2,1)S(1)}, bf16[1,32,8,8,128]{4,3,2,1,0:T(8,128)(2,1)S(1)}) fusion(f32[1,32,128,128]{2,3,1,0:T(8,128)S(1)} %get-tuple-element.32, f32[64]{0:T(128)S(1)} %negate_power_fusion, f32[32,128]{1,0:T(8,128)S(1)} %add_convert_fusion), kind=kLoop, calls=%fused_computation.46 | loop fusion | flops 2359296 | bytes 3162368
  136.3 0.1 copy.66
  136.4 0.1 copy.67
  136.5 0.7 copy.48
  137.1 1.1 pad_maximum_fusion.refs_3_
  138.2 1.1 maximum_bitcast_fusion.refs_2_
  139.3 16.4 %shard_map.91.into_ref = bf16[1,256,2048]{2,1,0:T(8,128)(2,1)} custom-call(f32[1,1,4096]{2,1,0:T(1,128)} %compare_select_fusion.refs_0_, bf16[1,256,1024]{2,1,0:T(8,128)(2,1)} %get-tuple-element.34.refs_1_, bf16[1,128,4352]{2,1,0:T(8,128)(2,1)} %maximum_bitcast_fusion.refs_2_, bf16[1,4352,128]{2,1,0:T(8,128)(2,1)} %pad_maximum_fusion.refs_3_), custom_call_target="tpu_custom_call" | custom-call | flops 6845104128 | bytes 3276800 | tf_op jit(solution)/shard_map/pallas_call | solution.py:343
  155.7 13.3 %all-to-all-done.1 = bf16[8,1,8,128,128]{4,3,2,1,0:T(8,128)(2,1)} async-done(((bf16[8,1,8,128,128]{4,3,2,1,0:T(8,128)(2,1)}), bf16[8,1,8,128,128]{4,3,2,1,0:T(8,128)(2,1)}, u32[]{:S(2)}, u32[]{:S(2)}) %all-to-all-start.1) | async-done | bytes 2097184 | tf_op jit(solution)/shard_map/all_to_all | solution.py:125
  169.0 3.8 %all-to-all-start.3 = ((bf16[8,1,8,128,128]{4,3,2,1,0:T(8,128)(2,1)}), bf16[8,1,8,128,128]{4,3,2,1,0:T(8,128)(2,1)S(1)}, u32[]{:S(2)}, u32[]{:S(2)}) async-start(bf16[8,1,8,128,128]{4,3,2,1,0:T(8,128)(2,1)} %get-tuple-element.15), calls=%async_computation.3 | async-start | bytes 4194304 | tf_op jit(solution)/shard_map/all_to_all | solution.py:135
  172.8 0.1 broadcast_bitcast_fusion
  172.9 2.3 %gather_fusion.4 = bf16[32,128,128]{2,1,0:T(8,128)(2,1)S(1)} fusion(bf16[64,128,128]{2,1,0:T(8,128)(2,1)} %bitcast.19, s32[1024]{0:T(1024)S(1)} %pad_clamp_fusion.1), kind=kCustom, calls=%fused_computation.4 | custom fusion | bytes 2097280 | tf_op jit(solution)/shard_map/gather | solution.py:136
  175.2 1.3 copy.49
  176.6 1.4 convert_multiply_fusion.1
  178.0 4.3 %fusion.19 = (bf16[1,32,8,8,128]{4,3,2,1,0:T(8,128)(2,1)S(1)}, bf16[1,32,8,8,128]{4,3,2,1,0:T(8,128)(2,1)S(1)}) fusion(f32[1,32,128,128]{2,3,1,0:T(8,128)S(1)} %convert_multiply_fusion.1, f32[64]{0:T(128)S(1)} %negate_power_fusion, f32[32,128]{1,0:T(8,128)S(1)} %add_convert_fusion), kind=kLoop, calls=%fused_computation.44 | loop fusion | flops 2359296 | bytes 3162368
  182.3 0.1 copy.64
  182.4 0.1 copy.65
  182.5 1.1 maximum_bitcast_fusion.1.refs_2_
  183.5 17.2 %shard_map.92 = (bf16[1,8,256,4352]{3,2,1,0:T(8,128)(2,1)}, f32[1,256,1024]{2,1,0:T(8,128)}) custom-call(f32[1,1,4096]{2,1,0:T(1,128)} %compare_select_fusion.refs_0_, bf16[1,256,1024]{2,1,0:T(8,128)(2,1)} %get-tuple-element.33.refs_1_, bf16[1,128,4352]{2,1,0:T(8,128)(2,1)} %maximum_bitcast_fusion.1.refs_2_), custom_call_target="tpu_custom_call" | custom-call | flops 4563402752 | bytes 3276800 | tf_op jit(solution)/shard_map/pallas_call | solution.py:343
  200.8 20.3 %all-to-all-done.3 = bf16[8,1,8,128,128]{4,3,2,1,0:T(8,128)(2,1)S(1)} async-done(((bf16[8,1,8,128,128]{4,3,2,1,0:T(8,128)(2,1)}), bf16[8,1,8,128,128]{4,3,2,1,0:T(8,128)(2,1)S(1)}, u32[]{:S(2)}, u32[]{:S(2)}) %all-to-all-start.3) | async-done | bytes 2097184 | tf_op jit(solution)/shard_map/all_to_all | solution.py:135
  221.1 0.7 gather_fusion.5
  221.8 1.5 fusion.1.v_ref
  223.3 9.8 %shard_map.93 = bf16[1,256,2048]{2,1,0:T(8,128)(2,1)} custom-call(bf16[1,8,256,4352]{3,2,1,0:T(8,128)(2,1)} %get-tuple-element.19.p_ref, bf16[1,4096,128]{2,1,0:T(8,128)(2,1)} %fusion.1.v_ref, bf16[1,256,128]{2,1,0:T(8,128)(2,1)} %get-tuple-element.43.f_ref, f32[1,256,1024]{2,1,0:T(8,128)} %get-tuple-element.21.t_ref, ...), custom_call_target="tpu_custom_call", output_to_operand_aliasing={{}: (4, {})} | custom-call | tf_op jit(solution)/shard_map/pallas_call | solution.py:273
  (22 shorter events, 0.1 us)
Async XLA Ops:
  0.0 11.9 %copy-start.1 = (bf16[16,128,256]{2,1,0:T(8,128)(2,1)S(1)}, bf16[16,128,256]{2,1,0:T(8,128)(2,1)}, u32[]{:S(2)}) copy-start(bf16[16,128,256]{2,1,0:T(8,128)(2,1)} %param.12) | copy-start | bytes 3145732
  3.3 13.7 %all-to-all-start = ((s32[8,1,72]{2,1,0:T(1,128)}), s32[8,1,72]{2,1,0:T(1,128)S(1)}, u32[]{:S(2)}, u32[]{:S(2)}) async-start(s32[8,1,72]{2,1,0:T(1,128)} %pad_add_fusion), calls=%async_computation | async-start | bytes 8192 | tf_op jit(solution)/shard_map/all_to_all | solution.py:82
  19.9 4.7 %copy-start = (bf16[1,256,2048]{2,1,0:T(8,128)(2,1)S(1)}, bf16[1,256,2048]{2,1,0:T(8,128)(2,1)}, u32[]{:S(2)}) copy-start(bf16[1,256,2048]{2,1,0:T(8,128)(2,1)} %param.9) | copy-start | bytes 3145732
  19.9 96.7 %all-to-all-start.2 = ((bf16[8,1,8,128,256]{4,3,2,1,0:T(8,128)(2,1)}), bf16[8,1,8,128,256]{4,3,2,1,0:T(8,128)(2,1)}, u32[]{:S(2)}, u32[]{:S(2)}) async-start(bf16[8,1,8,128,256]{4,3,2,1,0:T(8,128)(2,1)} %bitcast.78), calls=%async_computation.2 | async-start | bytes 8388608 | tf_op jit(solution)/shard_map/all_to_all | solution.py:138
  27.0 0.9 copy-start.2
  27.0 1.2 copy-start.3
  116.6 4.7 %copy-start.4 = (s32[1,32]{1,0:T(1,128)S(1)}, s32[1,32]{1,0:T(1,128)}, u32[]{:S(2)}) copy-start(s32[1,32]{1,0:T(1,128)} %param.17) | copy-start | bytes 388
  116.6 52.4 %all-to-all-start.1 = ((bf16[8,1,8,128,128]{4,3,2,1,0:T(8,128)(2,1)}), bf16[8,1,8,128,128]{4,3,2,1,0:T(8,128)(2,1)}, u32[]{:S(2)}, u32[]{:S(2)}) async-start(bf16[8,1,8,128,128]{4,3,2,1,0:T(8,128)(2,1)} %get-tuple-element.23), calls=%async_computation.1 | async-start | bytes 4194304 | tf_op jit(solution)/shard_map/all_to_all | solution.py:125
  169.0 52.1 %all-to-all-start.3 = ((bf16[8,1,8,128,128]{4,3,2,1,0:T(8,128)(2,1)}), bf16[8,1,8,128,128]{4,3,2,1,0:T(8,128)(2,1)S(1)}, u32[]{:S(2)}, u32[]{:S(2)}) async-start(bf16[8,1,8,128,128]{4,3,2,1,0:T(8,128)(2,1)} %get-tuple-element.15), calls=%async_computation.3 | async-start | bytes 4194304 | tf_op jit(solution)/shard_map/all_to_all | solution.py:135
